TPU v7x, 32 devices: a whole 2x2x4 slice. The times are simulated.
32 devices in a mesh: obs: 16 (over z, x, core), freq: 2 (over y).
Axes of the slice: x: 2, y: 2, z: 4, core: 2. Of those that a mesh axis runs over, the one named last changes fastest.
Arguments:
- cell_spectra: bfloat16 [8192, 512], P('obs', 'freq'), may hold values from -6 to 6
- cell_weight: float32 [8192], P('obs'), may hold values from 0.25 to 1
- cell_owner: int32 [8192, 1], P('obs'), may hold values from 0 to 15; in each aligned block of 512 rows (0 to 511, 512 to 1023, ...) at most 80 rows name the same one
- cell_local: int32 [8192], P('obs'), may hold values from 0 to 31
- panel_position: float32 [3, 512], replicated, may hold values from -8 to 8
- observer_position: float32 [3, 1024], P(None, 'obs'), may hold values from -40 to 40, as said below
Outputs:
- pressure: float32 [64, 2, 1024], P('freq', None, 'obs')
- level: float32 [1024], P('obs')
Inputs may be any that keep to these rules, and one draw needn't show every extreme that they name: `cell_owner`: among the 512 cells of one partition at most 80 name one panel group, and in every draw some partition sends exactly 80 cells to one group. `observer_position`: every observer lies between 20 and 40 from the anchor (0, 0, 0).
All inputs are finite; a program needn't handle non-finite values.
Results may differ from a plain program's by a relative error of at most 0.0029.
Values may be sent and summed in bfloat16 or wider, within the bound.
No kernel may reach another device: no remote copies, remote signals or barrier semaphores. Data moves between devices by JAX's collectives and lax.ppermute only.
A program may use at most 64 MiB of HBM per device.

v0:
```python
import math

import jax
import jax.numpy as jnp
from jax import lax
from jax.sharding import PartitionSpec as P

wave_step = 0.1
reference_radius = 10.0


def phase_powers(distance, wave_numbers):
    needed = wave_numbers.shape[0]
    cosine = jnp.cos(wave_numbers[0] * distance)[None]
    sine = jnp.sin(wave_numbers[0] * distance)[None]
    step_cos = jnp.cos(wave_step * distance)[None]
    step_sin = jnp.sin(wave_step * distance)[None]
    while cosine.shape[0] < needed:
        later_cos = cosine * step_cos - sine * step_sin
        later_sin = sine * step_cos + cosine * step_sin
        cosine = jnp.concatenate([cosine, later_cos], axis=0)
        sine = jnp.concatenate([sine, later_sin], axis=0)
        step_cos, step_sin = (step_cos * step_cos - step_sin * step_sin, 2.0 * step_cos * step_sin)
    return (cosine, sine)


def kernel_block(source, panel_points, observer_points, wave_numbers):
    offsets = observer_points[:, None, :] - panel_points[:, :, None]
    distance = jnp.sqrt(offsets[0] * offsets[0] + offsets[1] * offsets[1] + offsets[2] * offsets[2])
    inverse = 1.0 / distance
    heading = offsets * inverse[None]
    channels = jnp.transpose(source, (2, 1, 0))
    dipole_real = (
        heading[0][None] * channels[2][:, :, None]
        + heading[1][None] * channels[4][:, :, None]
        + heading[2][None] * channels[6][:, :, None]
    )
    dipole_imag = (
        heading[0][None] * channels[3][:, :, None]
        + heading[1][None] * channels[5][:, :, None]
        + heading[2][None] * channels[7][:, :, None]
    )
    waves = wave_numbers[:, None, None]
    amp_real = channels[0][:, :, None] + dipole_real * inverse[None] - waves * dipole_imag
    amp_imag = channels[1][:, :, None] + dipole_imag * inverse[None] + waves * dipole_real
    cosine, sine = phase_powers(distance, wave_numbers)
    weight_real = cosine * inverse[None]
    weight_imag = sine * inverse[None]
    real_part = jnp.sum(weight_real * amp_real + weight_imag * amp_imag, axis=1)
    imag_part = jnp.sum(weight_real * amp_imag - weight_imag * amp_real, axis=1)
    return jnp.stack([real_part, imag_part], axis=1)


def shards(cell_spectra, cell_weight, cell_owner, cell_local, panel_position, observer_position):
    cell_rows, columns = cell_spectra.shape
    freqs_dev = columns // 8
    groups = lax.axis_size("obs")
    capacity = 5 * cell_rows // (2 * groups)
    panel_total = panel_position.shape[1]
    panels_dev = panel_total // groups
    observers_dev = observer_position.shape[1]
    weighted = (cell_weight[:, None] * cell_spectra.astype(jnp.float32)).astype(jnp.bfloat16)
    owners = cell_owner[:, 0]
    ordering = jnp.argsort(owners, stable=True)
    sorted_owner = owners[ordering]
    member = sorted_owner[:, None] == jnp.arange(groups, dtype=jnp.int32)[None, :]
    counted = jnp.sum(member.astype(jnp.int32), axis=0)
    starts = jnp.cumsum(counted) - counted
    first_row = jnp.sum(jnp.where(member, starts[None, :], 0), axis=1)
    slot_index = jnp.arange(cell_rows, dtype=jnp.int32) - first_row
    target = sorted_owner * capacity + slot_index
    outgoing = (
        jnp.zeros((groups * capacity, columns), jnp.bfloat16).at[target].set(weighted[ordering])
    )
    labels = jnp.full((groups * capacity,), -1, jnp.int32).at[target].set(cell_local[ordering])
    arrived, arrived_labels = (
        lax.all_to_all(
            outgoing.reshape(groups, capacity, columns),
            "obs",
            split_axis=0,
            concat_axis=0,
            tiled=True,
        ),
        lax.all_to_all(
            labels.reshape(groups, capacity), "obs", split_axis=0, concat_axis=0, tiled=True
        ),
    )
    selector = (
        jnp.arange(panels_dev, dtype=jnp.int32)[:, None]
        == arrived_labels.reshape(1, groups * capacity)
    ).astype(jnp.bfloat16)
    panel_source = jnp.dot(
        selector, arrived.reshape(groups * capacity, columns), preferred_element_type=jnp.float32
    )
    group_first = lax.axis_index("freq") * freqs_dev
    wave_numbers = wave_step * (
        (group_first + jnp.arange(freqs_dev, dtype=jnp.int32)).astype(jnp.float32) + 1.0
    )
    start_value = jnp.zeros((freqs_dev, 2, observers_dev), jnp.float32)
    portion = lax.all_gather(panel_source, "obs", axis=0, tiled=True)
    rows_count = portion.shape[0]
    tile_rows = math.gcd(rows_count, 256)

    def advance(turn, accum):
        source = lax.dynamic_slice_in_dim(portion, turn * tile_rows, tile_rows, 0).reshape(
            tile_rows, freqs_dev, 8
        )
        points = lax.dynamic_slice_in_dim(panel_position, turn * tile_rows, tile_rows, 1)
        return accum + kernel_block(source, points, observer_position, wave_numbers)

    summed = lax.fori_loop(0, rows_count // tile_rows, advance, start_value)
    pressure = summed * (reference_radius / math.sqrt(panel_total))
    energy = jnp.sum(pressure[:, 0] * pressure[:, 0] + pressure[:, 1] * pressure[:, 1], axis=0)
    band_total = lax.psum(energy, "freq")
    level = jnp.log(band_total / (freqs_dev * lax.axis_size("freq")) + 1e-06)
    return (pressure, level)


def solution(mesh):
    in_specs = (P("obs", "freq"), P("obs"), P("obs", None), P("obs"), P(), P(None, "obs"))
    out_specs = (P("freq", None, "obs"), P("obs"))
    return jax.shard_map(shards, mesh=mesh, in_specs=in_specs, out_specs=out_specs, check_vma=False)
```

profile of v0, /device:TPU:0, one launch (start us, length us, event | category | flops | bytes accessed | tf_op | source)
XLA Modules:
  0.0 94.1 jit_solution(11356967212303534905)
XLA Ops:
  0.7 4.4 %sort.17 = (s32[512]{0:T(512)}, s32[512]{0:T(512)S(1)}) sort(s32[512]{0:T(512)} %bitcast.79, s32[512]{0:T(512)S(1)} %iota.20), dimensions={0}, to_apply=%region_0.0 | sort | flops 4608 | bytes 8192 | tf_op jit(solution)/shard_map/jit(argsort)/sort | solution.py:64
  5.1 3.7 %gather_fusion = s32[512]{0:T(512)S(1)} fusion(s32[512]{0:T(512)} %bitcast.80, s32[1024]{0:T(1024)S(1)} %pad_clamp_fusion), kind=kCustom, calls=%fused_computation | custom fusion | bytes 6144 | tf_op jit(solution)/shard_map/gather | solution.py:65
  8.8 0.1 convert_reduce_fusion
  8.9 0.1 copy.11
  9.0 0.1 reduce.1
  9.2 0.1 select_reduce_fusion
  9.3 3.5 %gather_fusion.1 = s32[512]{0:T(512)S(1)} fusion(s32[512]{0:T(512)S(1)} %copy-done, s32[1024]{0:T(1024)S(1)} %pad_clamp_fusion), kind=kCustom, calls=%fused_computation.1 | custom fusion | bytes 6144 | tf_op jit(solution)/shard_map/gather | solution.py:75
  12.8 2.5 %scatter_custom_fusion = s32[1280]{0:T(1024)S(1)} fusion(s32[512]{0:T(512)S(1)} %bitcast.89, s32[512]{0:T(512)S(1)} %gather_fusion.1, s32[]{:T(128)} %constant.73.clone.1), kind=kCustom, calls=%fused_computation.105 | custom fusion | bytes 5124 | tf_op jit(solution)/shard_map/scatter | solution.py:75
  15.3 0.7 all_to_all.9
  16.0 7.4 %all-to-all-start = ((s32[16,1,80]{2,1,0:T(1,128)}), s32[16,1,80]{2,1,0:T(1,128)S(1)}, u32[]{:S(2)}, u32[]{:S(2)}) async-start(s32[16,1,80]{2,1,0:T(1,128)} %all_to_all.9), calls=%async_computation | async-start | bytes 16384 | tf_op jit(solution)/shard_map/all_to_all | solution.py:84
  23.3 0.1 multiply_convert_fusion
  23.5 4.6 %scatter_custom_fusion.1 = bf16[1280,256]{1,0:T(8,128)(2,1)} fusion(s32[512]{0:T(512)S(1)} %bitcast.90, bf16[]{:T(256)} %constant.77.clone.1, bf16[512,256]{1,0:T(8,128)(2,1)S(1)} %multiply_convert_fusion, s32[1024]{0:T(1024)S(1)} %pad_clamp_fusion), kind=kCustom, calls=%fused_computation.88 | custom fusion | bytes 655362 | tf_op jit(solution)/shard_map/scatter | solution.py:73
  28.1 1.5 %all-to-all-done = s32[16,1,80]{2,1,0:T(1,128)S(1)} async-done(((s32[16,1,80]{2,1,0:T(1,128)}), s32[16,1,80]{2,1,0:T(1,128)S(1)}, u32[]{:S(2)}, u32[]{:S(2)}) %all-to-all-start) | async-done | bytes 5152 | tf_op jit(solution)/shard_map/all_to_all | solution.py:84
  29.7 4.5 %all-to-all-start.1 = ((bf16[16,80,256]{2,1,0:T(8,128)(2,1)}), bf16[16,80,256]{2,1,0:T(8,128)(2,1)S(1)}, u32[]{:S(2)}, u32[]{:S(2)}) async-start(bf16[16,80,256]{2,1,0:T(8,128)(2,1)} %bitcast.5), calls=%async_computation.1 | async-start | bytes 1310720 | tf_op jit(solution)/shard_map/all_to_all | solution.py:77
  34.2 0.5 broadcast.262
  34.7 0.7 reduce.5
  35.4 15.3 %all-to-all-done.1 = bf16[16,80,256]{2,1,0:T(8,128)(2,1)S(1)} async-done(((bf16[16,80,256]{2,1,0:T(8,128)(2,1)}), bf16[16,80,256]{2,1,0:T(8,128)(2,1)S(1)}, u32[]{:S(2)}, u32[]{:S(2)}) %all-to-all-start.1) | async-done | bytes 655392 | tf_op jit(solution)/shard_map/all_to_all | solution.py:77
  50.7 0.2 fusion.15
  50.9 21.9 %all_gather.3 = f32[512,256]{1,0:T(8,128)S(1)} all-gather(f32[32,256]{1,0:T(8,128)S(1)} %fusion.15), channel_id=1, replica_groups=mesh['obs'=16,'freq'=2] {'obs'}, dimensions={0}, use_global_device_ids=true | all-gather | bytes 557056 | tf_op jit(solution)/shard_map/all_gather | solution.py:100
  72.9 15.6 %while.14 = (s32[]{:T(128)}, f32[32,2,64]{2,0,1:T(8,128)S(1)}, f32[32]{0:T(128)S(1)}, f32[3,64]{1,0:T(4,128)S(1)}, f32[3,512]{1,0:T(4,128)S(1)}, /*index=5*/f32[...) while((s32[]{:T(128)}, f32[32,2,64]{2,0,1:T(8,128)S(1)}, f32[32]{0:T(128)S(1)}, ...), condition=%wide.region_9.10_spmd.clone, body=%wide.region_6.9_spmd.clone.sunk | while | flops 22880256 | bytes 33503556 | solution.py:111
  72.9 0.1 broadcast_subtract_fusion.2
  73.0 0.6 subtract_bitcast_fusion.2
  73.6 0.5 constant_dynamic-update-slice_fusion.25
  74.3 0.1 constant_dynamic-update-slice_fusion.33
  74.5 0.1 constant_dynamic-update-slice_fusion.31
  74.5 0.1 constant_dynamic-update-slice_fusion.29
  74.6 0.1 constant_dynamic-update-slice_fusion.28
  74.7 0.2 subtract_dynamic-update-slice_fusion.2
  75.0 1.3 %copy-done.1 = f32[32,256,64]{1,2,0:T(8,128)} copy-done((f32[32,256,64]{1,2,0:T(8,128)}, f32[32,256,64]{1,2,0:T(8,128)S(1)}, u32[]{:S(2)}) %copy-start.1) | copy-done | bytes 2097176 | tf_op jit(solution)/shard_map/while
  76.3 0.1 copy.41
  76.5 0.2 fusion.29
  76.7 0.1 broadcast_multiply_fusion.3
  76.8 3.8 %add_reduce_fusion.2 = (f32[32,64]{1,0:T(8,128)S(1)}, f32[32,64]{1,0:T(8,128)S(1)}) fusion(f32[32,256,64]{1,2,0:T(8,128)S(1)} %get-tuple-element.341, f32[32,256,64]{1,2,0:T(8,128)} %copy-done.1, f32[32,256]{1,0:T(8,128)S(1)} %get-tuple-element.345, f32[32,256]{1,0:T(8,128)S(1)} %get-tuple-element.346, f32[32,256]{1,0:T(8,128)S(1)} %get-tuple-element.349, ...), kind=kLoop, calls=%fused_computation.6.clone.1 | loop fusion | flops 14675968 | bytes 4735104 | tf_op jit(solution)/shard_map/while/body/eval_jaxpr/reduce_sum | solution.py:49
  80.7 0.1 broadcast_subtract_fusion.2
  80.8 0.6 subtract_bitcast_fusion.2
  81.4 0.5 constant_dynamic-update-slice_fusion.25
  82.2 0.1 constant_dynamic-update-slice_fusion.33
  82.3 0.1 constant_dynamic-update-slice_fusion.31
  82.4 0.1 constant_dynamic-update-slice_fusion.29
  82.5 0.1 constant_dynamic-update-slice_fusion.28
  82.6 0.2 subtract_dynamic-update-slice_fusion.2
  82.8 1.3 %copy-done.1 = f32[32,256,64]{1,2,0:T(8,128)} copy-done((f32[32,256,64]{1,2,0:T(8,128)}, f32[32,256,64]{1,2,0:T(8,128)S(1)}, u32[]{:S(2)}) %copy-start.1) | copy-done | bytes 2097176 | tf_op jit(solution)/shard_map/while
  84.2 0.1 copy.41
  84.3 0.2 fusion.29
  84.5 0.1 broadcast_multiply_fusion.3
  84.7 3.8 %add_reduce_fusion.2 = (f32[32,64]{1,0:T(8,128)S(1)}, f32[32,64]{1,0:T(8,128)S(1)}) fusion(f32[32,256,64]{1,2,0:T(8,128)S(1)} %get-tuple-element.341, f32[32,256,64]{1,2,0:T(8,128)} %copy-done.1, f32[32,256]{1,0:T(8,128)S(1)} %get-tuple-element.345, f32[32,256]{1,0:T(8,128)S(1)} %get-tuple-element.346, f32[32,256]{1,0:T(8,128)S(1)} %get-tuple-element.349, ...), kind=kLoop, calls=%fused_computation.6.clone.1 | loop fusion | flops 14675968 | bytes 4735104 | tf_op jit(solution)/shard_map/while/body/eval_jaxpr/reduce_sum | solution.py:49
  88.6 4.9 %psum.7 = f32[64]{0:T(128)S(1)} all-reduce(f32[64]{0:T(128)S(1)} %fusion.18), channel_id=1, replica_groups=mesh['obs'=16,'freq'=2] {'freq'}, use_global_device_ids=true, to_apply=%region_11.12 | all-reduce | flops 64 | bytes 512 | tf_op jit(solution)/shard_map/psum | solution.py:114
  93.6 0.5 add_log_fusion
  (56 shorter events, 0.9 us)
Async XLA Ops:
  0.6 8.6 %copy-start = (s32[512]{0:T(512)S(1)}, s32[512]{0:T(512)}, u32[]{:S(2)}) copy-start(s32[512]{0:T(512)} %param.11) | copy-start | bytes 6148
  5.1 18.2 %copy-start.2 = (bf16[512,256]{1,0:T(8,128)(2,1)S(1)}, bf16[512,256]{1,0:T(8,128)(2,1)}, u32[]{:S(2)}) copy-start(bf16[512,256]{1,0:T(8,128)(2,1)} %param.8) | copy-start | bytes 786436
  5.1 18.2 %copy-start.6 = (f32[512]{0:T(512)S(1)}, f32[512]{0:T(512)}, u32[]{:S(2)}) copy-start(f32[512]{0:T(512)} %param.9) | copy-start | bytes 6148
  12.8 60.1 %copy-start.3 = (f32[3,64]{1,0:T(4,128)S(1)}, f32[3,64]{1,0:T(4,128)}, u32[]{:S(2)}) copy-start(f32[3,64]{1,0:T(4,128)} %param.13) | copy-start | bytes 2308
  12.8 60.1 %copy-start.5 = (f32[3,512]{1,0:T(4,128)S(1)}, f32[3,512]{1,0:T(4,128)}, u32[]{:S(2)}) copy-start(f32[3,512]{1,0:T(4,128)} %param.12) | copy-start | bytes 18436
  16.0 13.7 %all-to-all-start = ((s32[16,1,80]{2,1,0:T(1,128)}), s32[16,1,80]{2,1,0:T(1,128)S(1)}, u32[]{:S(2)}, u32[]{:S(2)}) async-start(s32[16,1,80]{2,1,0:T(1,128)} %all_to_all.9), calls=%async_computation | async-start | bytes 16384 | tf_op jit(solution)/shard_map/all_to_all | solution.py:84
  29.7 21.1 %all-to-all-start.1 = ((bf16[16,80,256]{2,1,0:T(8,128)(2,1)}), bf16[16,80,256]{2,1,0:T(8,128)(2,1)S(1)}, u32[]{:S(2)}, u32[]{:S(2)}) async-start(bf16[16,80,256]{2,1,0:T(8,128)(2,1)} %bitcast.5), calls=%async_computation.1 | async-start | bytes 1310720 | tf_op jit(solution)/shard_map/all_to_all | solution.py:77
  75.0 1.4 %copy-start.1 = (f32[32,256,64]{1,2,0:T(8,128)}, f32[32,256,64]{1,2,0:T(8,128)S(1)}, u32[]{:S(2)}) copy-start(f32[32,256,64]{1,2,0:T(8,128)S(1)} %get-tuple-element.342) | copy-start | bytes 6291460 | tf_op jit(solution)/shard_map/while
  82.8 1.4 %copy-start.1 = (f32[32,256,64]{1,2,0:T(8,128)}, f32[32,256,64]{1,2,0:T(8,128)S(1)}, u32[]{:S(2)}) copy-start(f32[32,256,64]{1,2,0:T(8,128)S(1)} %get-tuple-element.342) | copy-start | bytes 6291460 | tf_op jit(solution)/shard_map/while
  88.6 5.5 %copy-start.4 = (f32[32,2,64]{2,1,0:T(2,128)}, f32[32,2,64]{2,1,0:T(2,128)S(1)}, u32[]{:S(2)}) copy-start(f32[32,2,64]{2,1,0:T(2,128)S(1)} %copy_multiply_fusion) | copy-start | bytes 49156
where the time goes:
time: 94.5 us; the launch traced here: 94.1 us
  blocking collectives  26.9 us (28%)
  local copies, waits for them, and re-layouts  19.2 us (20%)
  other arithmetic  17.9 us (19%)
  waiting for transfers between devices  16.8 us (18%)
  starting transfers between devices  11.8 us (12%)
    all_gather x1, blocking collectives, shards(): portion = lax.all_gather(panel_source, 'obs', axis=0, tiled=True)  21.9 us
    all_to_all x1, waiting for transfers between devices, shards(): lax.all_to_all(outgoing.reshape(groups, capacity, columns), 'obs', split_...  15.3 us
    reduce_sum x2, other arithmetic, kernel_block(): real_part = jnp.sum(weight_real * amp_real + weight_imag * amp_imag, axis=1)  7.63 us
    all_to_all x1, starting transfers between devices, shards(): lax.all_to_all(labels.reshape(groups, capacity), 'obs', split_axis=0, con...  7.36 us
    psum x1, blocking collectives, shards(): band_total = lax.psum(energy, 'freq')  4.94 us
    scatter x1, local copies, waits for them, and re-layouts, shards(): jnp.zeros((groups * capacity, columns), jnp.bfloat16).at[target]  4.64 us
    all_to_all x1, starting transfers between devices, shards(): lax.all_to_all(outgoing.reshape(groups, capacity, columns), 'obs', split_...  4.48 us
    sort x1, other arithmetic, shards(): ordering = jnp.argsort(owners, stable=True)  4.45 us
  transfers between devices with their start and end apart: 2, of which 2 were waited for; matrix products, arithmetic and copies ran while one was open for 6% of the time, Pallas kernels for 0%

commit v1 on v0

--- a/solution.py
+++ b/solution.py
@@ -60,44 +60,17 @@
     panels_dev = panel_total // groups
     observers_dev = observer_position.shape[1]
     weighted = (cell_weight[:, None] * cell_spectra.astype(jnp.float32)).astype(jnp.bfloat16)
-    owners = cell_owner[:, 0]
-    ordering = jnp.argsort(owners, stable=True)
-    sorted_owner = owners[ordering]
-    member = sorted_owner[:, None] == jnp.arange(groups, dtype=jnp.int32)[None, :]
-    counted = jnp.sum(member.astype(jnp.int32), axis=0)
-    starts = jnp.cumsum(counted) - counted
-    first_row = jnp.sum(jnp.where(member, starts[None, :], 0), axis=1)
-    slot_index = jnp.arange(cell_rows, dtype=jnp.int32) - first_row
-    target = sorted_owner * capacity + slot_index
-    outgoing = (
-        jnp.zeros((groups * capacity, columns), jnp.bfloat16).at[target].set(weighted[ordering])
-    )
-    labels = jnp.full((groups * capacity,), -1, jnp.int32).at[target].set(cell_local[ordering])
-    arrived, arrived_labels = (
-        lax.all_to_all(
-            outgoing.reshape(groups, capacity, columns),
-            "obs",
-            split_axis=0,
-            concat_axis=0,
-            tiled=True,
-        ),
-        lax.all_to_all(
-            labels.reshape(groups, capacity), "obs", split_axis=0, concat_axis=0, tiled=True
-        ),
-    )
+    panel_index = cell_owner[:, 0] * panels_dev + cell_local
     selector = (
-        jnp.arange(panels_dev, dtype=jnp.int32)[:, None]
-        == arrived_labels.reshape(1, groups * capacity)
+        jnp.arange(panel_total, dtype=jnp.int32)[:, None] == panel_index[None, :]
     ).astype(jnp.bfloat16)
-    panel_source = jnp.dot(
-        selector, arrived.reshape(groups * capacity, columns), preferred_element_type=jnp.float32
-    )
+    local_source = jnp.dot(selector, weighted, preferred_element_type=jnp.float32)
     group_first = lax.axis_index("freq") * freqs_dev
     wave_numbers = wave_step * (
         (group_first + jnp.arange(freqs_dev, dtype=jnp.int32)).astype(jnp.float32) + 1.0
     )
     start_value = jnp.zeros((freqs_dev, 2, observers_dev), jnp.float32)
-    portion = lax.all_gather(panel_source, "obs", axis=0, tiled=True)
+    portion = lax.psum(local_source, "obs")
     rows_count = portion.shape[0]
     tile_rows = math.gcd(rows_count, 256)
 

time: 94.5 us -> 136 us (1.44)
  waiting for transfers between devices: 16.8 us -> 93.4 us
  blocking collectives: 26.9 us -> 4.94 us
  local copies, waits for them, and re-layouts: 19.2 us -> 5.46 us
  between operations: 0.81 us -> 14.1 us
  starting transfers between devices: 11.8 us -> 0.04 us
  other arithmetic: 17.9 us -> 15 us
  matrix products: 0.19 us -> 2.17 us
    psum x0 -> x1, waiting for transfers between devices: none -> 93.4 us  [shards(): portion = lax.psum(local_source, 'obs')]
    all_gather x1 -> x0, blocking collectives: 21.9 us -> none  [shards(): portion = lax.all_gather(panel_source, 'obs', axis=0, tiled=True)]
    all_to_all x2 -> x0, waiting for transfers between devices: 16.8 us -> none  [the longest x1 15.3 us: shards(): lax.all_to_all(outgoing.reshape(groups, capacity, columns), 'obs', split_...]
    all_to_all x2 -> x0, starting transfers between devices: 11.8 us -> none  [the longest x1 7.36 us: shards(): lax.all_to_all(labels.reshape(groups, capacity), 'obs', split_axis=0, con...]
    gather x2 -> x0, local copies, waits for them, and re-layouts: 7.17 us -> none  [the longest x1 3.66 us: shards(): sorted_owner = owners[ordering]]
    scatter x2 -> x0, local copies, waits for them, and re-layouts: 7.09 us -> none  [the longest x1 4.64 us: shards(): jnp.zeros((groups * capacity, columns), jnp.bfloat16).at[target]]
    sort x1 -> x0, other arithmetic: 4.45 us -> none  [shards(): ordering = jnp.argsort(owners, stable=True)]
    dot_general x1, matrix products: 0.19 us -> 2.17 us  [shards(): jnp.dot(selector, weighted, preferred_element_type=jnp.float32)]
  transfers between devices with their start and end apart: 2 -> 1, of which waited for: 2 -> 1; matrix products, arithmetic and copies ran while one was open for 6% -> 0% of each run, Pallas kernels for 0% -> 0%
where the time goes in v1:
time: 136 us
  waiting for transfers between devices  93.4 us (69%)
  other arithmetic  15 us (11%)
  between operations  14.1 us (10%)
  local copies, waits for them, and re-layouts  5.46 us (4%)
  blocking collectives  4.94 us (4%)
  matrix products  2.17 us (2%)
    psum x1, waiting for transfers between devices, shards(): portion = lax.psum(local_source, 'obs')  93.4 us
    reduce_sum x2, other arithmetic, kernel_block(): real_part = jnp.sum(weight_real * amp_real + weight_imag * amp_imag, axis=1)  7.63 us
    psum x1, blocking collectives, shards(): band_total = lax.psum(energy, 'freq')  4.94 us
    while x26, local copies, waits for them, and re-layouts  3.39 us
  transfers between devices with their start and end apart: 1, of which 1 were waited for; matrix products, arithmetic and copies ran while one was open for 0% of the time, Pallas kernels for 0%

profile of v1, /device:TPU:0, one launch (start us, length us, event | category | flops | bytes accessed | tf_op | source)
XLA Modules:
  0.0 135.6 jit_solution(6641107444012159605)
XLA Ops:
  7.2 0.0 all-reduce.2.cloned.1.call-start
  7.2 0.7 broadcast_multiply_fusion.1
  7.9 0.7 add.279
  8.6 2.2 %fusion.12 = f32[512,256]{1,0:T(8,128)} fusion(s32[512]{0:T(512)S(1)} %add.279, bf16[512,256]{1,0:T(8,128)(2,1)} %param.8, f32[512]{0:T(512)} %param.9), kind=kOutput, calls=%fused_computation.83 | convolution fusion | flops 134873088 | bytes 790528 | tf_op jit(solution)/shard_map/dot_general | solution.py:67
  10.7 0.0 all-reduce.2.cloned.1.call-update
  10.8 93.4 %all-reduce.2.cloned.1.call-done = f32[512,256]{1,0:T(8,128)} async-done(((f32[512,256]{1,0:T(8,128)}), f32[512,256]{1,0:T(8,128)}) %all-reduce.2.cloned.1.call-update) | async-done | bytes 524304 | tf_op jit(solution)/shard_map/psum | solution.py:73
  104.2 18.9 %while.14 = (s32[]{:T(128)}, f32[32,2,64]{2,0,1:T(8,128)S(1)}, f32[32]{0:T(128)S(1)}, f32[3,64]{1,0:T(4,128)}, f32[3,512]{1,0:T(4,128)}, /*index=5*/f32[512,256]...) while((s32[]{:T(128)}, f32[32,2,64]{2,0,1:T(8,128)S(1)}, f32[32]{0:T(128)S(1)}, ...), condition=%wide.region_4.0_spmd.clone, body=%wide.region_1.0_spmd.clone.sunk | while | flops 22880256 | bytes 35603832 | solution.py:84
  104.2 0.7 constant_dynamic-slice_fusion.4
  104.9 0.8 broadcast_subtract_fusion.2
  105.7 0.6 subtract_bitcast_fusion.2
  106.3 0.5 constant_dynamic-update-slice_fusion.25
  106.9 0.1 constant_dynamic-update-slice_fusion.27
  107.1 0.1 constant_dynamic-update-slice_fusion.33
  107.2 0.1 constant_dynamic-update-slice_fusion.31
  107.3 0.1 constant_dynamic-update-slice_fusion.29
  107.4 0.1 constant_dynamic-update-slice_fusion.28
  107.4 0.0 copy-start.1
  107.5 0.2 subtract_dynamic-update-slice_fusion.2
  107.7 0.0 copy-start
  107.7 1.3 copy-done
  109.0 0.0 copy-done.1
  109.1 0.1 copy.38
  109.2 0.2 fusion.24
  109.4 0.3 copy-done.2
  109.7 0.1 broadcast_multiply_fusion.3
  109.8 3.8 %add_reduce_fusion.2 = (f32[32,64]{1,0:T(8,128)S(1)}, f32[32,64]{1,0:T(8,128)S(1)}) fusion(f32[32,256,64]{1,2,0:T(8,128)S(1)} %get-tuple-element.339, f32[32,256,64]{1,2,0:T(8,128)} %copy-done, f32[32,256]{1,0:T(8,128)S(1)} %get-tuple-element.343, f32[32,256]{1,0:T(8,128)S(1)} %get-tuple-element.344, f32[32,256]{1,0:T(8,128)S(1)} %get-tuple-element.347, ...), kind=kLoop, calls=%fused_computation.1.clone.1 | loop fusion | flops 14675968 | bytes 4735104 | tf_op jit(solution)/shard_map/while/body/eval_jaxpr/reduce_sum | solution.py:49
  113.7 0.7 constant_dynamic-slice_fusion.4
  114.4 0.8 broadcast_subtract_fusion.2
  115.2 0.6 subtract_bitcast_fusion.2
  115.8 0.5 constant_dynamic-update-slice_fusion.25
  116.4 0.1 constant_dynamic-update-slice_fusion.27
  116.5 0.1 constant_dynamic-update-slice_fusion.33
  116.7 0.1 constant_dynamic-update-slice_fusion.31
  116.7 0.1 constant_dynamic-update-slice_fusion.29
  116.8 0.1 constant_dynamic-update-slice_fusion.28
  116.9 0.0 copy-start.1
  116.9 0.2 subtract_dynamic-update-slice_fusion.2
  117.2 1.3 copy-done
  118.5 0.0 copy-done.1
  118.5 0.1 copy.38
  118.7 0.2 fusion.24
  118.9 0.3 copy-done.2
  119.2 0.1 broadcast_multiply_fusion.3
  119.3 3.8 %add_reduce_fusion.2 = (f32[32,64]{1,0:T(8,128)S(1)}, f32[32,64]{1,0:T(8,128)S(1)}) fusion(f32[32,256,64]{1,2,0:T(8,128)S(1)} %get-tuple-element.339, f32[32,256,64]{1,2,0:T(8,128)} %copy-done, f32[32,256]{1,0:T(8,128)S(1)} %get-tuple-element.343, f32[32,256]{1,0:T(8,128)S(1)} %get-tuple-element.344, f32[32,256]{1,0:T(8,128)S(1)} %get-tuple-element.347, ...), kind=kLoop, calls=%fused_computation.1.clone.1 | loop fusion | flops 14675968 | bytes 4735104 | tf_op jit(solution)/shard_map/while/body/eval_jaxpr/reduce_sum | solution.py:49
  123.2 0.0 copy-start.3
  123.2 0.1 fusion.16
  123.3 4.9 %psum.15 = f32[64]{0:T(128)S(1)} all-reduce(f32[64]{0:T(128)S(1)} %fusion.16), channel_id=1, replica_groups=mesh['obs'=16,'freq'=2] {'freq'}, use_global_device_ids=true, to_apply=%region_6.0 | all-reduce | flops 64 | bytes 512 | tf_op jit(solution)/shard_map/psum | solution.py:87
  128.2 0.5 add_log_fusion
  (33 shorter events, 0.5 us)
Async XLA Ops:
  7.2 97.1 %all-reduce.2.cloned.1.call-start = ((), (), s32[]{:S(2)}) async-start(), calls=%async_computation | async-start | bytes 1048576 | tf_op jit(solution)/shard_map/psum | solution.py:73
  107.4 1.6 %copy-start.1 = (f32[512,256]{1,0:T(8,128)S(1)}, f32[512,256]{1,0:T(8,128)}, u32[]{:S(2)}) copy-start(f32[512,256]{1,0:T(8,128)} %get-tuple-element.388) | copy-start | bytes 1572868 | tf_op jit(solution)/shard_map/while
  107.7 1.3 copy-start
  109.0 0.7 copy-start.2
  116.9 1.6 %copy-start.1 = (f32[512,256]{1,0:T(8,128)S(1)}, f32[512,256]{1,0:T(8,128)}, u32[]{:S(2)}) copy-start(f32[512,256]{1,0:T(8,128)} %get-tuple-element.388) | copy-start | bytes 1572868 | tf_op jit(solution)/shard_map/while
  117.2 1.3 copy-start
  118.5 0.7 copy-start.2
  123.2 5.5 %copy-start.3 = (f32[32,2,64]{2,1,0:T(2,128)}, f32[32,2,64]{2,1,0:T(2,128)S(1)}, u32[]{:S(2)}) copy-start(f32[32,2,64]{2,1,0:T(2,128)S(1)} %copy_multiply_fusion) | copy-start | bytes 49156
Sparse Core Ops, SparseCore 0:
  11.4 92.7 all-reduce.1

commit v2 on v1

--- a/solution.py
+++ b/solution.py
@@ -55,7 +55,6 @@
     cell_rows, columns = cell_spectra.shape
     freqs_dev = columns // 8
     groups = lax.axis_size("obs")
-    capacity = 5 * cell_rows // (2 * groups)
     panel_total = panel_position.shape[1]
     panels_dev = panel_total // groups
     observers_dev = observer_position.shape[1]
@@ -70,7 +69,13 @@
         (group_first + jnp.arange(freqs_dev, dtype=jnp.int32)).astype(jnp.float32) + 1.0
     )
     start_value = jnp.zeros((freqs_dev, 2, observers_dev), jnp.float32)
-    portion = lax.psum(local_source, "obs")
+    arrived = lax.all_to_all(
+        local_source.reshape(groups, panels_dev, columns), "obs", 0, 0, tiled=True
+    )
+    own_source = jnp.sum(arrived, axis=0)
+    portion = lax.all_to_all(
+        jnp.broadcast_to(own_source[None], (groups, panels_dev, columns)), "obs", 0, 0, tiled=True
+    ).reshape(panel_total, columns)
     rows_count = portion.shape[0]
     tile_rows = math.gcd(rows_count, 256)
 
@@ -84,7 +89,10 @@
     summed = lax.fori_loop(0, rows_count // tile_rows, advance, start_value)
     pressure = summed * (reference_radius / math.sqrt(panel_total))
     energy = jnp.sum(pressure[:, 0] * pressure[:, 0] + pressure[:, 1] * pressure[:, 1], axis=0)
-    band_total = lax.psum(energy, "freq")
+    if lax.axis_size("freq") == 2:
+        band_total = energy + lax.ppermute(energy, "freq", [(0, 1), (1, 0)])
+    else:
+        band_total = lax.psum(energy, "freq")
     level = jnp.log(band_total / (freqs_dev * lax.axis_size("freq")) + 1e-06)
     return (pressure, level)
 

time: 136 us -> 64.6 us (0.47)
  waiting for transfers between devices: 93.4 us -> 16.5 us
  blocking collectives: 4.94 us -> 21.6 us
  between operations: 14.1 us -> 0.71 us
  starting transfers between devices: 0.04 us -> 5.68 us
  other arithmetic: 15 us -> 13.5 us
    psum x1 -> x0, waiting for transfers between devices: 93.4 us -> none  [shards(): portion = lax.psum(local_source, 'obs')]
    all_to_all x0 -> x1, blocking collectives: none -> 21.6 us  [shards(): lax.all_to_all(local_source.reshape(groups, panels_dev, columns), 'obs',...]
    all_to_all x0 -> x1, waiting for transfers between devices: none -> 14.4 us  [shards(): lax.all_to_all(jnp.broadcast_to(own_source[None], (groups, panels_dev, co...]
    psum x1 -> x0, blocking collectives: 4.94 us -> none  [shards(): band_total = lax.psum(energy, 'freq')]
    all_to_all x0 -> x1, starting transfers between devices: none -> 4.1 us  [shards(): lax.all_to_all(jnp.broadcast_to(own_source[None], (groups, panels_dev, co...]
    ppermute x0 -> x1, waiting for transfers between devices: none -> 2.02 us  [shards(): band_total = energy + lax.ppermute(energy, 'freq', [(0, 1), (1, 0)])]
    ppermute x0 -> x1, starting transfers between devices: none -> 1.58 us  [shards(): band_total = energy + lax.ppermute(energy, 'freq', [(0, 1), (1, 0)])]
    dynamic_slice x2, local copies, waits for them, and re-layouts: 1.38 us -> 0.01 us  [advance(): lax.dynamic_slice_in_dim(panel_position, turn * tile_rows, tile_rows, 1)]
  transfers between devices with their start and end apart: 1 -> 2, of which waited for: 1 -> 2; matrix products, arithmetic and copies ran while one was open for 0% -> 0% of each run, Pallas kernels for 0% -> 0%
where the time goes in v2:
time: 64.6 us; the launch traced here: 64.2 us
  blocking collectives  21.6 us (33%)
  waiting for transfers between devices  16.5 us (26%)
  other arithmetic  13.5 us (21%)
  starting transfers between devices  5.68 us (9%)
  local copies, waits for them, and re-layouts  4.35 us (7%)
  matrix products  1.36 us (2%)
  between operations  0.71 us (1%)
    all_to_all x1, blocking collectives, shards(): lax.all_to_all(local_source.reshape(groups, panels_dev, columns), 'obs',...  21.6 us
    all_to_all x1, waiting for transfers between devices, shards(): lax.all_to_all(jnp.broadcast_to(own_source[None], (groups, panels_dev, co...  14.4 us
    reduce_sum x2, other arithmetic, kernel_block(): real_part = jnp.sum(weight_real * amp_real + weight_imag * amp_imag, axis=1)  7.48 us
    all_to_all x1, starting transfers between devices, shards(): lax.all_to_all(jnp.broadcast_to(own_source[None], (groups, panels_dev, co...  4.1 us
    while x18, local copies, waits for them, and re-layouts  2.8 us
    ppermute x1, waiting for transfers between devices, shards(): band_total = energy + lax.ppermute(energy, 'freq', [(0, 1), (1, 0)])  2.02 us
    while x12, other arithmetic  1.71 us
    ppermute x1, starting transfers between devices, shards(): band_total = energy + lax.ppermute(energy, 'freq', [(0, 1), (1, 0)])  1.58 us
  transfers between devices with their start and end apart: 2, of which 2 were waited for; matrix products, arithmetic and copies ran while one was open for 0% of the time, Pallas kernels for 0%

profile of v2, /device:TPU:0, one launch (start us, length us, event | category | flops | bytes accessed | tf_op | source)
XLA Modules:
  0.0 64.2 jit_solution(14932165219836297983)
XLA Ops:
  0.6 0.0 copy-start.3
  0.6 0.0 copy-start.1
  0.7 0.7 %broadcast_multiply_fusion.1 = s32[512,1]{0,1:T(1,128)S(1)} fusion(s32[512,1]{0,1:T(1,128)} %param.10), kind=kLoop, calls=%fused_computation.92 | loop fusion | flops 512 | bytes 4096 | tf_op jit(solution)/shard_map/mul | solution.py:62
  1.3 0.7 %add.278 = s32[512]{0:T(512)S(1)} add(s32[512]{0:T(512)S(1)} %bitcast.81, s32[512]{0:T(512)} %param.11) | non-fusion elementwise | flops 512 | bytes 6144 | tf_op jit(solution)/shard_map/add | solution.py:62
  2.0 1.4 %fusion.12 = f32[512,256]{1,0:T(8,128)S(1)} fusion(s32[512]{0:T(512)S(1)} %add.278, bf16[512,256]{1,0:T(8,128)(2,1)} %param.8, f32[512]{0:T(512)} %param.9), kind=kOutput, calls=%fused_computation.83 | convolution fusion | flops 134873088 | bytes 790528 | tf_op jit(solution)/shard_map/dot_general | solution.py:66
  3.4 21.6 %all_to_all.10 = f32[16,32,256]{2,1,0:T(8,128)S(1)} all-to-all(f32[16,32,256]{2,1,0:T(8,128)S(1)} %bitcast.78), channel_id=1, replica_groups=mesh['obs'=16,'freq'=2] {'obs'}, dimensions={0} | all-to-all | bytes 1048576 | tf_op jit(solution)/shard_map/all_to_all | solution.py:72
  25.1 0.8 %broadcast_in_dim.41 = f32[16,32,256]{2,1,0:T(8,128)} broadcast(f32[32,256]{1,0:T(8,128)S(1)} %reduce_sum.44), dimensions={1,2} | broadcast | bytes 557056 | tf_op jit(solution)/shard_map/broadcast_in_dim | solution.py:77
  25.9 4.1 %all-to-all-start.1 = ((f32[16,32,256]{2,1,0:T(8,128)}), f32[16,32,256]{2,1,0:T(8,128)S(1)}, u32[]{:S(2)}, u32[]{:S(2)}) async-start(f32[16,32,256]{2,1,0:T(8,128)} %broadcast_in_dim.41), calls=%async_computation.1 | async-start | bytes 1048576 | tf_op jit(solution)/shard_map/all_to_all | solution.py:76
  30.0 14.4 %all-to-all-done.1 = f32[16,32,256]{2,1,0:T(8,128)S(1)} async-done(((f32[16,32,256]{2,1,0:T(8,128)}), f32[16,32,256]{2,1,0:T(8,128)S(1)}, u32[]{:S(2)}, u32[]{:S(2)}) %all-to-all-start.1) | async-done | bytes 524320 | tf_op jit(solution)/shard_map/all_to_all | solution.py:76
  44.5 0.0 copy-done.3
  44.5 0.0 copy-done.1
  44.5 15.4 %while.14 = (s32[]{:T(128)}, f32[32,2,64]{2,0,1:T(8,128)S(1)}, f32[32]{0:T(128)S(1)}, f32[3,64]{1,0:T(4,128)S(1)}, f32[3,512]{1,0:T(4,128)S(1)}, /*index=5*/f32[...) while((s32[]{:T(128)}, f32[32,2,64]{2,0,1:T(8,128)S(1)}, f32[32]{0:T(128)S(1)}, ...), condition=%wide.region_4.0_spmd.clone, body=%wide.region_1.0_spmd.clone.sunk | while | flops 22880256 | bytes 33503556 | solution.py:89
  44.5 0.1 broadcast_subtract_fusion.2
  44.6 0.6 subtract_bitcast_fusion.2
  45.2 0.5 constant_dynamic-update-slice_fusion.25
  45.8 0.1 constant_dynamic-update-slice_fusion.27
  46.0 0.1 constant_dynamic-update-slice_fusion.33
  46.1 0.1 constant_dynamic-update-slice_fusion.31
  46.2 0.1 constant_dynamic-update-slice_fusion.29
  46.2 0.1 constant_dynamic-update-slice_fusion.28
  46.3 0.2 subtract_dynamic-update-slice_fusion.2
  46.6 0.0 copy-start
  46.6 1.3 %copy-done = f32[32,256,64]{1,2,0:T(8,128)} copy-done((f32[32,256,64]{1,2,0:T(8,128)}, f32[32,256,64]{1,2,0:T(8,128)S(1)}, u32[]{:S(2)}) %copy-start) | copy-done | bytes 2097176 | tf_op jit(solution)/shard_map/while
  47.9 0.1 copy.38
  48.1 0.2 fusion.24
  48.3 0.1 broadcast_multiply_fusion.3
  48.4 3.7 %add_reduce_fusion.2 = (f32[32,64]{1,0:T(8,128)S(1)}, f32[32,64]{1,0:T(8,128)S(1)}) fusion(f32[32,256,64]{1,2,0:T(8,128)S(1)} %get-tuple-element.339, f32[32,256,64]{1,2,0:T(8,128)} %copy-done, f32[32,256]{1,0:T(8,128)S(1)} %get-tuple-element.343, f32[32,256]{1,0:T(8,128)S(1)} %get-tuple-element.344, f32[32,256]{1,0:T(8,128)S(1)} %get-tuple-element.347, ...), kind=kLoop, calls=%fused_computation.1.clone.1 | loop fusion | flops 14675968 | bytes 4735104 | tf_op jit(solution)/shard_map/while/body/eval_jaxpr/reduce_sum | solution.py:49
  52.2 0.1 broadcast_subtract_fusion.2
  52.4 0.6 subtract_bitcast_fusion.2
  52.9 0.5 constant_dynamic-update-slice_fusion.25
  53.6 0.1 constant_dynamic-update-slice_fusion.27
  53.7 0.1 constant_dynamic-update-slice_fusion.33
  53.8 0.1 constant_dynamic-update-slice_fusion.31
  53.9 0.1 constant_dynamic-update-slice_fusion.29
  54.0 0.1 constant_dynamic-update-slice_fusion.28
  54.1 0.2 subtract_dynamic-update-slice_fusion.2
  54.3 0.0 copy-start
  54.3 1.3 %copy-done = f32[32,256,64]{1,2,0:T(8,128)} copy-done((f32[32,256,64]{1,2,0:T(8,128)}, f32[32,256,64]{1,2,0:T(8,128)S(1)}, u32[]{:S(2)}) %copy-start) | copy-done | bytes 2097176 | tf_op jit(solution)/shard_map/while
  55.7 0.1 copy.38
  55.8 0.2 fusion.24
  56.0 0.1 broadcast_multiply_fusion.3
  56.2 3.7 %add_reduce_fusion.2 = (f32[32,64]{1,0:T(8,128)S(1)}, f32[32,64]{1,0:T(8,128)S(1)}) fusion(f32[32,256,64]{1,2,0:T(8,128)S(1)} %get-tuple-element.339, f32[32,256,64]{1,2,0:T(8,128)} %copy-done, f32[32,256]{1,0:T(8,128)S(1)} %get-tuple-element.343, f32[32,256]{1,0:T(8,128)S(1)} %get-tuple-element.344, f32[32,256]{1,0:T(8,128)S(1)} %get-tuple-element.347, ...), kind=kLoop, calls=%fused_computation.1.clone.1 | loop fusion | flops 14675968 | bytes 4735104 | tf_op jit(solution)/shard_map/while/body/eval_jaxpr/reduce_sum | solution.py:49
  60.0 0.0 copy-start.2
  60.0 0.1 fusion.16
  60.1 1.6 %collective-permute-start = (f32[64]{0:T(128)S(1)}, f32[64]{0:T(128)S(1)}, u32[]{:S(2)}, u32[]{:S(2)}) collective-permute-start(f32[64]{0:T(128)S(1)} %fusion.16), channel_id=1, source_target_pairs={{0,1},{1,0},{2,3},{3,2},{4,5},{5,4},{6,7},{7,6},{8,9},{9,8},{10,11... | collective-permute-start | bytes 776 | tf_op jit(solution)/shard_map/ppermute | solution.py:93
  61.6 2.0 %collective-permute-done = f32[64]{0:T(128)S(1)} collective-permute-done((f32[64]{0:T(128)S(1)}, f32[64]{0:T(128)S(1)}, u32[]{:S(2)}, u32[]{:S(2)}) %collective-permute-start) | collective-permute-done | bytes 288 | tf_op jit(solution)/shard_map/ppermute | solution.py:93
  63.7 0.5 add_log_fusion
  64.2 0.0 copy-done.2
  (32 shorter events, 0.5 us)
Async XLA Ops:
  0.6 43.9 %copy-start.3 = (f32[3,512]{1,0:T(4,128)S(1)}, f32[3,512]{1,0:T(4,128)}, u32[]{:S(2)}) copy-start(f32[3,512]{1,0:T(4,128)} %param.12) | copy-start | bytes 18436
  0.6 43.8 %copy-start.1 = (f32[3,64]{1,0:T(4,128)S(1)}, f32[3,64]{1,0:T(4,128)}, u32[]{:S(2)}) copy-start(f32[3,64]{1,0:T(4,128)} %param.13) | copy-start | bytes 2308
  25.9 18.6 %all-to-all-start.1 = ((f32[16,32,256]{2,1,0:T(8,128)}), f32[16,32,256]{2,1,0:T(8,128)S(1)}, u32[]{:S(2)}, u32[]{:S(2)}) async-start(f32[16,32,256]{2,1,0:T(8,128)} %broadcast_in_dim.41), calls=%async_computation.1 | async-start | bytes 1048576 | tf_op jit(solution)/shard_map/all_to_all | solution.py:76
  46.6 1.3 %copy-start = (f32[32,256,64]{1,2,0:T(8,128)}, f32[32,256,64]{1,2,0:T(8,128)S(1)}, u32[]{:S(2)}) copy-start(f32[32,256,64]{1,2,0:T(8,128)S(1)} %get-tuple-element.340) | copy-start | bytes 6291460 | tf_op jit(solution)/shard_map/while
  54.3 1.3 %copy-start = (f32[32,256,64]{1,2,0:T(8,128)}, f32[32,256,64]{1,2,0:T(8,128)S(1)}, u32[]{:S(2)}) copy-start(f32[32,256,64]{1,2,0:T(8,128)S(1)} %get-tuple-element.340) | copy-start | bytes 6291460 | tf_op jit(solution)/shard_map/while
  60.0 4.2 %copy-start.2 = (f32[32,2,64]{2,1,0:T(2,128)}, f32[32,2,64]{2,1,0:T(2,128)S(1)}, u32[]{:S(2)}) copy-start(f32[32,2,64]{2,1,0:T(2,128)S(1)} %copy_multiply_fusion) | copy-start | bytes 49156
  60.1 3.6 %collective-permute-start = (f32[64]{0:T(128)S(1)}, f32[64]{0:T(128)S(1)}, u32[]{:S(2)}, u32[]{:S(2)}) collective-permute-start(f32[64]{0:T(128)S(1)} %fusion.16), channel_id=1, source_target_pairs={{0,1},{1,0},{2,3},{3,2},{4,5},{5,4},{6,7},{7,6},{8,9},{9,8},{10,11... | collective-permute-start | bytes 776 | tf_op jit(solution)/shard_map/ppermute | solution.py:93

commit v3 on v2

v3 whole, which is shorter than its diff:
```python
import math

import jax
import jax.numpy as jnp
from jax import lax
from jax.experimental import pallas as pl
from jax.experimental.pallas import tpu as pltpu
from jax.sharding import PartitionSpec as P

wave_step = 0.1
reference_radius = 10.0


def field_kernel(wave_ref, geo_ref, src_ref, out_ref):
    freqs = src_ref.shape[0]
    blocks = geo_ref.shape[1] // 8

    @pl.when(pl.program_id(0) == 0)
    def _():
        out_ref[...] = jnp.zeros(out_ref.shape, out_ref.dtype)

    def block_body(block, carry):
        rows = pl.ds(pl.multiple_of(block * 8, 8), 8)
        step_cos = geo_ref[2, rows, :]
        step_sin = geo_ref[3, rows, :]
        along = [geo_ref[4 + j, rows, :] for j in range(3)]
        distance = geo_ref[7, rows, :]

        def freq_body(f, phase):
            weight_real, weight_imag = phase
            channel = [jnp.broadcast_to(src_ref[f, c : c + 1, :], (8, 128)) for c in range(8)]
            wave_distance = wave_ref[f] * distance
            dipole_real = along[0] * channel[2] + along[1] * channel[4] + along[2] * channel[6]
            dipole_imag = along[0] * channel[3] + along[1] * channel[5] + along[2] * channel[7]
            amp_real = channel[0] + dipole_real - wave_distance * dipole_imag
            amp_imag = channel[1] + dipole_imag + wave_distance * dipole_real
            out_ref[f, 0, rows, :] += weight_real * amp_real + weight_imag * amp_imag
            out_ref[f, 1, rows, :] += weight_real * amp_imag - weight_imag * amp_real
            return (
                weight_real * step_cos - weight_imag * step_sin,
                weight_imag * step_cos + weight_real * step_sin,
            )

        lax.fori_loop(
            0, freqs, freq_body, (geo_ref[0, rows, :], geo_ref[1, rows, :]), unroll=2
        )
        return carry

    lax.fori_loop(0, blocks, block_body, 0)


def far_field(portion, panel_position, observer_position, wave_numbers):
    panel_total, columns = portion.shape
    freqs = columns // 8
    observers = observer_position.shape[1]
    offsets = observer_position[:, :, None] - panel_position[:, None, :]
    distance = jnp.sqrt(offsets[0] * offsets[0] + offsets[1] * offsets[1] + offsets[2] * offsets[2])
    inverse = 1.0 / distance
    first_phase = wave_numbers[0] * distance
    step_phase = wave_step * distance
    geometry = jnp.stack(
        [
            jnp.cos(first_phase) * inverse,
            jnp.sin(first_phase) * inverse,
            jnp.cos(step_phase),
            jnp.sin(step_phase),
            offsets[0] * inverse * inverse,
            offsets[1] * inverse * inverse,
            offsets[2] * inverse * inverse,
            distance,
        ]
    )
    sources = jnp.transpose(portion.reshape(panel_total, freqs, 8), (1, 2, 0))
    partial = pl.pallas_call(
        field_kernel,
        grid=(panel_total // 128,),
        in_specs=[
            pl.BlockSpec(memory_space=pltpu.SMEM),
            pl.BlockSpec((8, observers, 128), lambda chunk: (0, 0, chunk)),
            pl.BlockSpec((freqs, 8, 128), lambda chunk: (0, 0, chunk)),
        ],
        out_specs=pl.BlockSpec((freqs, 2, observers, 128), lambda chunk: (0, 0, 0, 0)),
        out_shape=jax.ShapeDtypeStruct((freqs, 2, observers, 128), jnp.float32),
        compiler_params=pltpu.CompilerParams(dimension_semantics=("arbitrary",)),
    )(wave_numbers, geometry, sources)
    return jnp.sum(partial, axis=-1)


def shards(cell_spectra, cell_weight, cell_owner, cell_local, panel_position, observer_position):
    cell_rows, columns = cell_spectra.shape
    freqs_dev = columns // 8
    groups = lax.axis_size("obs")
    panel_total = panel_position.shape[1]
    panels_dev = panel_total // groups
    weighted = (cell_weight[:, None] * cell_spectra.astype(jnp.float32)).astype(jnp.bfloat16)
    panel_index = cell_owner[:, 0] * panels_dev + cell_local
    selector = (
        jnp.arange(panel_total, dtype=jnp.int32)[:, None] == panel_index[None, :]
    ).astype(jnp.bfloat16)
    local_source = jnp.dot(selector, weighted, preferred_element_type=jnp.float32)
    group_first = lax.axis_index("freq") * freqs_dev
    wave_numbers = wave_step * (
        (group_first + jnp.arange(freqs_dev, dtype=jnp.int32)).astype(jnp.float32) + 1.0
    )
    arrived = lax.all_to_all(
        local_source.reshape(groups, panels_dev, columns), "obs", 0, 0, tiled=True
    )
    own_source = jnp.sum(arrived, axis=0)
    portion = lax.all_to_all(
        jnp.broadcast_to(own_source[None], (groups, panels_dev, columns)), "obs", 0, 0, tiled=True
    ).reshape(panel_total, columns)
    summed = far_field(portion, panel_position, observer_position, wave_numbers)
    pressure = summed * (reference_radius / math.sqrt(panel_total))
    energy = jnp.sum(pressure[:, 0] * pressure[:, 0] + pressure[:, 1] * pressure[:, 1], axis=0)
    if lax.axis_size("freq") == 2:
        band_total = energy + lax.ppermute(energy, "freq", [(0, 1), (1, 0)])
    else:
        band_total = lax.psum(energy, "freq")
    level = jnp.log(band_total / (freqs_dev * lax.axis_size("freq")) + 1e-06)
    return (pressure, level)


def solution(mesh):
    in_specs = (P("obs", "freq"), P("obs"), P("obs", None), P("obs"), P(), P(None, "obs"))
    out_specs = (P("freq", None, "obs"), P("obs"))
    return jax.shard_map(shards, mesh=mesh, in_specs=in_specs, out_specs=out_specs, check_vma=False)
```

time: 64.6 us -> 65.1 us (level)
  blocking collectives: 21.6 us -> 0 us
  waiting for transfers between devices: 16.5 us -> 27 us
  Pallas kernels: 0 us -> 9.87 us
  starting transfers between devices: 5.68 us -> 13 us
  other arithmetic: 13.5 us -> 7.08 us
  matrix products: 1.36 us -> 2.15 us
    all_to_all x1 -> x0, blocking collectives: 21.6 us -> none  [shards(): lax.all_to_all(local_source.reshape(groups, panels_dev, columns), 'obs',...]
    all_to_all x0 -> x1, waiting for transfers between devices: none -> 12.1 us  [shards(): lax.all_to_all(local_source.reshape(groups, panels_dev, columns), 'obs',...]
    pallas_call x0 -> x1, Pallas kernels: none -> 9.87 us  [far_field(): pl.pallas_call(field_kernel, grid=(panel_total // 128,), in_specs=[pl.Blo...]
    all_to_all x0 -> x1, starting transfers between devices: none -> 7.36 us  [shards(): lax.all_to_all(local_source.reshape(groups, panels_dev, columns), 'obs',...]
    reduce_sum x2 -> x1, other arithmetic: 7.48 us -> 2.22 us  [far_field(): return jnp.sum(partial, axis=-1)]
    while x18 -> x0, local copies, waits for them, and re-layouts: 2.8 us -> none
    unnamed x1 -> x7, other arithmetic: 0.01 us -> 2.06 us
    while x12 -> x0, other arithmetic: 1.71 us -> none
  transfers between devices with their start and end apart: 2 -> 3, of which waited for: 2 -> 3; matrix products, arithmetic and copies ran while one was open for 0% -> 4% of each run, Pallas kernels for 0% -> 0%
where the time goes in v3:
time: 65.1 us; the launch traced here: 64.6 us
  waiting for transfers between devices  27 us (41%)
  starting transfers between devices  13 us (20%)
  Pallas kernels  9.87 us (15%)
  other arithmetic  7.08 us (11%)
  local copies, waits for them, and re-layouts  4.75 us (7%)
  matrix products  2.15 us (3%)
  between operations  0.78 us (1%)
    all_to_all x1, waiting for transfers between devices, shards(): lax.all_to_all(jnp.broadcast_to(own_source[None], (groups, panels_dev, co...  12.8 us
    all_to_all x1, waiting for transfers between devices, shards(): lax.all_to_all(local_source.reshape(groups, panels_dev, columns), 'obs',...  12.1 us
    pallas_call x1, Pallas kernels, far_field(): pl.pallas_call(field_kernel, grid=(panel_total // 128,), in_specs=[pl.Blo...  9.87 us
    all_to_all x1, starting transfers between devices, shards(): lax.all_to_all(local_source.reshape(groups, panels_dev, columns), 'obs',...  7.36 us
    all_to_all x1, starting transfers between devices, shards(): lax.all_to_all(jnp.broadcast_to(own_source[None], (groups, panels_dev, co...  4.1 us
    reduce_sum x1, other arithmetic, far_field(): return jnp.sum(partial, axis=-1)  2.22 us
    dot_general x1, matrix products, shards(): jnp.dot(selector, weighted, preferred_element_type=jnp.float32)  2.15 us
    unnamed x7, other arithmetic  2.06 us
  transfers between devices with their start and end apart: 3, of which 3 were waited for; matrix products, arithmetic and copies ran while one was open for 4% of the time, Pallas kernels for 0%

profile of v3, /device:TPU:0, one launch (start us, length us, event | category | flops | bytes accessed | tf_op | source)
XLA Modules:
  0.0 64.6 jit_solution(826832049122939048)
XLA Ops:
  0.6 0.7 %broadcast_multiply_fusion.1 = s32[512,1]{0,1:T(1,128)S(1)} fusion(s32[512,1]{0,1:T(1,128)} %param.8), kind=kLoop, calls=%fused_computation.24 | loop fusion | flops 512 | bytes 4096 | tf_op jit(solution)/shard_map/mul | solution.py:96
  1.3 0.7 %add.56 = s32[512]{0:T(512)S(1)} add(s32[512]{0:T(512)S(1)} %bitcast.8, s32[512]{0:T(512)} %param.9) | non-fusion elementwise | flops 512 | bytes 6144 | tf_op jit(solution)/shard_map/add | solution.py:96
  2.0 2.1 %fusion = f32[512,256]{1,0:T(8,128)} fusion(s32[512]{0:T(512)S(1)} %add.56, bf16[512,256]{1,0:T(8,128)(2,1)} %param.6, f32[512]{0:T(512)} %param.7), kind=kOutput, calls=%fused_computation.1 | convolution fusion | flops 134873088 | bytes 790528 | tf_op jit(solution)/shard_map/dot_general | solution.py:100
  4.1 7.4 %all-to-all-start = ((f32[16,32,256]{2,1,0:T(8,128)}), f32[16,32,256]{2,1,0:T(8,128)S(1)}, u32[]{:S(2)}, u32[]{:S(2)}) async-start(f32[16,32,256]{2,1,0:T(8,128)} %bitcast.2), calls=%async_computation | async-start | bytes 1048576 | tf_op jit(solution)/shard_map/all_to_all | solution.py:105
  11.5 0.0 copy-start.2
  11.5 0.8 %broadcast_subtract_fusion = f32[3,64,512]{2,1,0:T(8,128)S(1)} fusion(f32[3,512]{1,0:T(4,128)} %param.10, f32[3,64]{1,0:T(4,128)} %param.11), kind=kLoop, calls=%fused_computation.8 | loop fusion | flops 98304 | bytes 400128 | tf_op jit(solution)/shard_map/sub | solution.py:56
  12.3 0.5 multiply_dynamic-update-slice_fusion.1
  12.9 0.5 multiply_dynamic-update-slice_fusion
  13.4 0.5 cosine_dynamic-update-slice_fusion
  13.9 12.1 %all-to-all-done = f32[16,32,256]{2,1,0:T(8,128)S(1)} async-done(((f32[16,32,256]{2,1,0:T(8,128)}), f32[16,32,256]{2,1,0:T(8,128)S(1)}, u32[]{:S(2)}, u32[]{:S(2)}) %all-to-all-start) | async-done | bytes 524320 | tf_op jit(solution)/shard_map/all_to_all | solution.py:105
  26.0 0.8 %broadcast_in_dim.2 = f32[16,32,256]{2,1,0:T(8,128)} broadcast(f32[32,256]{1,0:T(8,128)S(1)} %reduce_sum.27), dimensions={1,2} | broadcast | bytes 557056 | tf_op jit(solution)/shard_map/broadcast_in_dim | solution.py:110
  26.9 4.1 %all-to-all-start.1 = ((f32[16,32,256]{2,1,0:T(8,128)}), f32[16,32,256]{2,1,0:T(8,128)S(1)}, u32[]{:S(2)}, u32[]{:S(2)}) async-start(f32[16,32,256]{2,1,0:T(8,128)} %broadcast_in_dim.2), calls=%async_computation.1 | async-start | bytes 1048576 | tf_op jit(solution)/shard_map/all_to_all | solution.py:109
  31.0 0.5 sine_dynamic-update-slice_fusion
  31.5 0.0 copy-done.2
  31.6 0.0 copy-start
  31.6 1.0 %copy-done = f32[8,64,512]{2,1,0:T(8,128)} copy-done((f32[8,64,512]{2,1,0:T(8,128)}, f32[8,64,512]{2,1,0:T(8,128)S(1)}, u32[]{:S(2)}) %copy-start) | copy-done | bytes 1048600
  32.6 12.8 %all-to-all-done.1 = f32[16,32,256]{2,1,0:T(8,128)S(1)} async-done(((f32[16,32,256]{2,1,0:T(8,128)}), f32[16,32,256]{2,1,0:T(8,128)S(1)}, u32[]{:S(2)}, u32[]{:S(2)}) %all-to-all-start.1) | async-done | bytes 524320 | tf_op jit(solution)/shard_map/all_to_all | solution.py:109
  45.4 1.3 %copy.8 = f32[16,32,256]{1,0,2:T(8,128)S(1)} copy(f32[16,32,256]{2,1,0:T(8,128)S(1)} %all-to-all-done.1) | data formatting | bytes 1048576 | tf_op jit(solution)/shard_map/all_to_all | solution.py:109
  46.7 1.6 %reshape_reshape.3 = f32[512,32,8]{0,2,1:T(8,128)} reshape(f32[16,32,256]{1,0,2:T(8,128)S(1)} %copy.8) | data formatting | bytes 1048576 | tf_op jit(solution)/shard_map/reshape;reshape | solution.py:73
  48.3 9.9 %shard_map.77 = f32[32,2,64,128]{3,2,1,0:T(8,128)} custom-call(f32[32]{0:T(128)} %copy-done.2, f32[8,64,512]{2,1,0:T(8,128)} %copy-done, f32[32,8,512]{2,1,0:T(8,128)} %bitcast.7), custom_call_target="tpu_custom_call" | custom-call | tf_op jit(solution)/shard_map/pallas_call | solution.py:74
  58.2 2.2 %reduce_sum.28 = f32[32,2,64]{2,1,0:T(2,128)S(1)} reduce(f32[32,2,64,128]{3,2,1,0:T(8,128)} %shard_map.77, f32[]{:T(128)} %constant.2.clone.1), dimensions={3}, to_apply=%region_1.0 | reduce | flops 520192 | bytes 2113540 | tf_op jit(solution)/shard_map/reduce_sum | solution.py:86
  60.4 0.0 copy-start.1
  60.4 0.1 fusion.7
  60.5 1.6 %collective-permute-start = (f32[64]{0:T(128)S(1)}, f32[64]{0:T(128)S(1)}, u32[]{:S(2)}, u32[]{:S(2)}) collective-permute-start(f32[64]{0:T(128)S(1)} %fusion.7), channel_id=1, source_target_pairs={{0,1},{1,0},{2,3},{3,2},{4,5},{5,4},{6,7},{7,6},{8,9},{9,8},{10,11... | collective-permute-start | bytes 776 | tf_op jit(solution)/shard_map/ppermute | solution.py:116
  62.1 2.0 %collective-permute-done = f32[64]{0:T(128)S(1)} collective-permute-done((f32[64]{0:T(128)S(1)}, f32[64]{0:T(128)S(1)}, u32[]{:S(2)}, u32[]{:S(2)}) %collective-permute-start) | collective-permute-done | bytes 288 | tf_op jit(solution)/shard_map/ppermute | solution.py:116
  64.1 0.5 add_log_fusion
  64.6 0.0 copy-done.1
  (7 shorter events, 0.2 us)
Async XLA Ops:
  4.1 21.8 %all-to-all-start = ((f32[16,32,256]{2,1,0:T(8,128)}), f32[16,32,256]{2,1,0:T(8,128)S(1)}, u32[]{:S(2)}, u32[]{:S(2)}) async-start(f32[16,32,256]{2,1,0:T(8,128)} %bitcast.2), calls=%async_computation | async-start | bytes 1048576 | tf_op jit(solution)/shard_map/all_to_all | solution.py:105
  11.5 19.9 %copy-start.2 = (f32[32]{0:T(128)}, f32[32]{0:T(128)S(1)}, u32[]{:S(2)}) copy-start(f32[32]{0:T(128)S(1)} %add_multiply_fusion.wave_ref) | copy-start | bytes 388
  26.9 18.6 %all-to-all-start.1 = ((f32[16,32,256]{2,1,0:T(8,128)}), f32[16,32,256]{2,1,0:T(8,128)S(1)}, u32[]{:S(2)}, u32[]{:S(2)}) async-start(f32[16,32,256]{2,1,0:T(8,128)} %broadcast_in_dim.2), calls=%async_computation.1 | async-start | bytes 1048576 | tf_op jit(solution)/shard_map/all_to_all | solution.py:109
  31.6 1.0 %copy-start = (f32[8,64,512]{2,1,0:T(8,128)}, f32[8,64,512]{2,1,0:T(8,128)S(1)}, u32[]{:S(2)}) copy-start(f32[8,64,512]{2,1,0:T(8,128)S(1)} %sqrt_dynamic-update-slice_fusion.geo_ref) | copy-start | bytes 3145732
  60.4 4.2 %copy-start.1 = (f32[32,2,64]{2,1,0:T(2,128)}, f32[32,2,64]{2,1,0:T(2,128)S(1)}, u32[]{:S(2)}) copy-start(f32[32,2,64]{2,1,0:T(2,128)S(1)} %broadcast_multiply_fusion) | copy-start | bytes 49156
  60.5 3.6 %collective-permute-start = (f32[64]{0:T(128)S(1)}, f32[64]{0:T(128)S(1)}, u32[]{:S(2)}, u32[]{:S(2)}) collective-permute-start(f32[64]{0:T(128)S(1)} %fusion.7), channel_id=1, source_target_pairs={{0,1},{1,0},{2,3},{3,2},{4,5},{5,4},{6,7},{7,6},{8,9},{9,8},{10,11... | collective-permute-start | bytes 776 | tf_op jit(solution)/shard_map/ppermute | solution.py:116

commit v4 on v3

--- a/solution.py
+++ b/solution.py
@@ -11,13 +11,15 @@
 reference_radius = 10.0
 
 
-def field_kernel(wave_ref, geo_ref, src_ref, out_ref):
-    freqs = src_ref.shape[0]
-    blocks = geo_ref.shape[1] // 8
+def field_kernel(wave_ref, geo_ref, src_ref, out_ref, acc_ref, chan_ref):
+    freqs, _, observers, lanes = acc_ref.shape
+    blocks = observers // 8
 
     @pl.when(pl.program_id(0) == 0)
     def _():
-        out_ref[...] = jnp.zeros(out_ref.shape, out_ref.dtype)
+        acc_ref[...] = jnp.zeros(acc_ref.shape, acc_ref.dtype)
+
+    chan_ref[...] = jnp.transpose(src_ref[...])
 
     def block_body(block, carry):
         rows = pl.ds(pl.multiple_of(block * 8, 8), 8)
@@ -28,14 +30,17 @@
 
         def freq_body(f, phase):
             weight_real, weight_imag = phase
-            channel = [jnp.broadcast_to(src_ref[f, c : c + 1, :], (8, 128)) for c in range(8)]
+            base = f * 8
+            channel = [
+                jnp.broadcast_to(chan_ref[pl.ds(base + c, 1), :], (8, lanes)) for c in range(8)
+            ]
             wave_distance = wave_ref[f] * distance
             dipole_real = along[0] * channel[2] + along[1] * channel[4] + along[2] * channel[6]
             dipole_imag = along[0] * channel[3] + along[1] * channel[5] + along[2] * channel[7]
             amp_real = channel[0] + dipole_real - wave_distance * dipole_imag
             amp_imag = channel[1] + dipole_imag + wave_distance * dipole_real
-            out_ref[f, 0, rows, :] += weight_real * amp_real + weight_imag * amp_imag
-            out_ref[f, 1, rows, :] += weight_real * amp_imag - weight_imag * amp_real
+            acc_ref[f, 0, rows, :] += weight_real * amp_real + weight_imag * amp_imag
+            acc_ref[f, 1, rows, :] += weight_real * amp_imag - weight_imag * amp_real
             return (
                 weight_real * step_cos - weight_imag * step_sin,
                 weight_imag * step_cos + weight_real * step_sin,
@@ -47,6 +52,17 @@
         return carry
 
     lax.fori_loop(0, blocks, block_body, 0)
+
+    @pl.when(pl.program_id(0) == pl.num_programs(0) - 1)
+    def _():
+        flat = acc_ref[...].reshape(freqs * 2 * observers, lanes)
+        out_ref[...] = lax.dot_general(
+            jnp.ones((8, lanes), jnp.float32),
+            flat,
+            (((1,), (1,)), ((), ())),
+            precision=lax.Precision.HIGHEST,
+            preferred_element_type=jnp.float32,
+        )
 
 
 def far_field(portion, panel_position, observer_position, wave_numbers):
@@ -70,20 +86,23 @@
             distance,
         ]
     )
-    sources = jnp.transpose(portion.reshape(panel_total, freqs, 8), (1, 2, 0))
-    partial = pl.pallas_call(
+    summed = pl.pallas_call(
         field_kernel,
         grid=(panel_total // 128,),
         in_specs=[
             pl.BlockSpec(memory_space=pltpu.SMEM),
             pl.BlockSpec((8, observers, 128), lambda chunk: (0, 0, chunk)),
-            pl.BlockSpec((freqs, 8, 128), lambda chunk: (0, 0, chunk)),
+            pl.BlockSpec((128, columns), lambda chunk: (chunk, 0)),
         ],
-        out_specs=pl.BlockSpec((freqs, 2, observers, 128), lambda chunk: (0, 0, 0, 0)),
-        out_shape=jax.ShapeDtypeStruct((freqs, 2, observers, 128), jnp.float32),
+        out_specs=pl.BlockSpec((8, freqs * 2 * observers), lambda chunk: (0, 0)),
+        out_shape=jax.ShapeDtypeStruct((8, freqs * 2 * observers), jnp.float32),
+        scratch_shapes=[
+            pltpu.VMEM((freqs, 2, observers, 128), jnp.float32),
+            pltpu.VMEM((columns, 128), jnp.float32),
+        ],
         compiler_params=pltpu.CompilerParams(dimension_semantics=("arbitrary",)),
-    )(wave_numbers, geometry, sources)
-    return jnp.sum(partial, axis=-1)
+    )(wave_numbers, geometry, portion)
+    return summed[0].reshape(freqs, 2, observers)
 
 
 def shards(cell_spectra, cell_weight, cell_owner, cell_local, panel_position, observer_position):
@@ -93,9 +112,10 @@
     panel_total = panel_position.shape[1]
     panels_dev = panel_total // groups
     weighted = (cell_weight[:, None] * cell_spectra.astype(jnp.float32)).astype(jnp.bfloat16)
-    panel_index = cell_owner[:, 0] * panels_dev + cell_local
+    panel_number = jnp.arange(panel_total, dtype=jnp.int32)[:, None]
     selector = (
-        jnp.arange(panel_total, dtype=jnp.int32)[:, None] == panel_index[None, :]
+        (panel_number // panels_dev == cell_owner[:, 0][None, :])
+        & (panel_number % panels_dev == cell_local[None, :])
     ).astype(jnp.bfloat16)
     local_source = jnp.dot(selector, weighted, preferred_element_type=jnp.float32)
     group_first = lax.axis_index("freq") * freqs_dev

time: 65.1 us -> 62.8 us (0.965)
  other arithmetic: 7.08 us -> 3.72 us
  local copies, waits for them, and re-layouts: 4.75 us -> 3.17 us
  Pallas kernels: 9.87 us -> 11.3 us
  waiting for transfers between devices: 27 us -> 28 us
    reduce_sum x1 -> x0, other arithmetic: 2.22 us -> none  [far_field(): return jnp.sum(partial, axis=-1)]
    another operation x1 -> x0, local copies, waits for them, and re-layouts: 1.58 us -> none  [far_field(): sources = jnp.transpose(portion.reshape(panel_total, freqs, 8), (1, 2, 0))]
    pallas_call x1, Pallas kernels: 9.87 us -> 11.3 us  [far_field(): pl.pallas_call(field_kernel, grid=(panel_total // 128,), in_specs=[pl.Blo...]
    all_to_all x1 -> x0, local copies, waits for them, and re-layouts: 1.29 us -> none  [shards(): lax.all_to_all(jnp.broadcast_to(own_source[None], (groups, panels_dev, co...]
    unnamed x6 -> x18, local copies, waits for them, and re-layouts: 1 us -> 2.18 us
    all_to_all x1, waiting for transfers between devices: 12.8 us -> 13.8 us  [shards(): lax.all_to_all(jnp.broadcast_to(own_source[None], (groups, panels_dev, co...]
    mul x1, other arithmetic: 0.02 us -> 0.95 us  [shards(): pressure = summed * (reference_radius / math.sqrt(panel_total))]
    sub x1, other arithmetic: 0.79 us -> 0.09 us  [far_field(): offsets = observer_position[:, :, None] - panel_position[:, None, :]]
where the time goes in v4:
time: 62.8 us; the launch traced here: 62.4 us
  waiting for transfers between devices  28 us (45%)
  starting transfers between devices  13.2 us (21%)
  Pallas kernels  11.3 us (18%)
  other arithmetic  3.72 us (6%)
  local copies, waits for them, and re-layouts  3.17 us (5%)
  matrix products  2.21 us (4%)
  between operations  0.8 us (1%)
    all_to_all x1, waiting for transfers between devices, shards(): lax.all_to_all(jnp.broadcast_to(own_source[None], (groups, panels_dev, co...  13.8 us
    all_to_all x1, waiting for transfers between devices, shards(): lax.all_to_all(local_source.reshape(groups, panels_dev, columns), 'obs',...  12.1 us
    pallas_call x1, Pallas kernels, far_field(): pl.pallas_call(field_kernel, grid=(panel_total // 128,), in_specs=[pl.Blo...  11.3 us
    all_to_all x1, starting transfers between devices, shards(): lax.all_to_all(local_source.reshape(groups, panels_dev, columns), 'obs',...  7.49 us
    all_to_all x1, starting transfers between devices, shards(): lax.all_to_all(jnp.broadcast_to(own_source[None], (groups, panels_dev, co...  4.1 us
    dot_general x1, matrix products, shards(): jnp.dot(selector, weighted, preferred_element_type=jnp.float32)  2.21 us
    unnamed x18, local copies, waits for them, and re-layouts  2.18 us
    unnamed x7, other arithmetic  2.06 us
  transfers between devices with their start and end apart: 3, of which 3 were waited for; matrix products, arithmetic and copies ran while one was open for 4% of the time, Pallas kernels for 0%

profile of v4, /device:TPU:0, one launch (start us, length us, event | category | flops | bytes accessed | tf_op | source)
XLA Modules:
  0.0 62.4 jit_solution(16899666730012080895)
XLA Ops:
  0.6 0.0 copy-start.8
  0.6 0.0 copy-start.7
  0.7 0.0 copy-start.6
  0.7 0.6 %copy-done.8 = f32[512]{0:T(512)S(1)} copy-done((f32[512]{0:T(512)S(1)}, f32[512]{0:T(512)}, u32[]{:S(2)}) %copy-start.8) | copy-done | bytes 2072
  1.3 0.0 copy-done.7
  1.3 0.0 copy-done.6
  1.4 2.2 %fusion = f32[512,256]{1,0:T(8,128)} fusion(s32[512]{0:T(512)S(1)} %copy-done.6, s32[512]{0:T(512)S(1)} %bitcast.8, s32[512]{0:T(512)S(1)} %get-tuple-element.4, s32[512]{0:T(512)S(1)} %get-tuple-element.5, bf16[512,256]{1,0:T(8,128)(2,1)} %param.6, f32[512]{0:T(512)S(1)} %copy-done.8), kind=kOutput, calls=%fused_computation | convolution fusion | flops 135397376 | bytes 796672 | tf_op jit(solution)/shard_map/dot_general | solution.py:120
  3.6 0.0 copy-start.5
  3.6 7.5 %all-to-all-start = ((f32[16,32,256]{2,1,0:T(8,128)}), f32[16,32,256]{2,1,0:T(8,128)S(1)}, u32[]{:S(2)}, u32[]{:S(2)}) async-start(f32[16,32,256]{2,1,0:T(8,128)} %bitcast.2), calls=%async_computation | async-start | bytes 1048576 | tf_op jit(solution)/shard_map/all_to_all | solution.py:125
  11.1 0.0 copy-start.3
  11.1 0.0 copy-done.5
  11.1 0.7 %copy-done.3 = f32[3,512]{1,0:T(4,128)S(1)} copy-done((f32[3,512]{1,0:T(4,128)S(1)}, f32[3,512]{1,0:T(4,128)}, u32[]{:S(2)}) %copy-start.3) | copy-done | bytes 6168
  11.8 0.0 copy-start.4
  11.8 0.1 broadcast_subtract_fusion
  11.9 0.5 multiply_dynamic-update-slice_fusion.1
  12.4 0.0 copy-done.4
  12.4 0.5 multiply_dynamic-update-slice_fusion
  12.9 0.5 cosine_dynamic-update-slice_fusion
  13.4 12.1 %all-to-all-done = f32[16,32,256]{2,1,0:T(8,128)S(1)} async-done(((f32[16,32,256]{2,1,0:T(8,128)}), f32[16,32,256]{2,1,0:T(8,128)S(1)}, u32[]{:S(2)}, u32[]{:S(2)}) %all-to-all-start) | async-done | bytes 524320 | tf_op jit(solution)/shard_map/all_to_all | solution.py:125
  25.6 0.9 %broadcast_in_dim.2 = f32[16,32,256]{2,1,0:T(8,128)} broadcast(f32[32,256]{1,0:T(8,128)S(1)} %reduce_sum.18), dimensions={1,2} | broadcast | bytes 557056 | tf_op jit(solution)/shard_map/broadcast_in_dim | solution.py:130
  26.4 4.1 %all-to-all-start.1 = ((f32[16,32,256]{2,1,0:T(8,128)}), f32[16,32,256]{2,1,0:T(8,128)S(1)}, u32[]{:S(2)}, u32[]{:S(2)}) async-start(f32[16,32,256]{2,1,0:T(8,128)} %broadcast_in_dim.2), calls=%async_computation.1 | async-start | bytes 1048576 | tf_op jit(solution)/shard_map/all_to_all | solution.py:129
  30.5 0.5 sine_dynamic-update-slice_fusion
  31.2 0.0 copy-start.1
  31.2 13.8 %all-to-all-done.1 = f32[16,32,256]{2,1,0:T(8,128)S(1)} async-done(((f32[16,32,256]{2,1,0:T(8,128)}), f32[16,32,256]{2,1,0:T(8,128)S(1)}, u32[]{:S(2)}, u32[]{:S(2)}) %all-to-all-start.1) | async-done | bytes 524320 | tf_op jit(solution)/shard_map/all_to_all | solution.py:129
  45.0 0.0 copy-start
  45.0 0.0 copy-done.1
  45.0 0.8 %copy-done = f32[16,32,256]{2,1,0:T(8,128)} copy-done((f32[16,32,256]{2,1,0:T(8,128)}, f32[16,32,256]{2,1,0:T(8,128)S(1)}, u32[]{:S(2)}) %copy-start) | copy-done | bytes 524312
  45.8 11.3 %shard_map.77 = f32[8,4096]{1,0:T(8,128)} custom-call(f32[32]{0:T(128)} %copy-done.4, f32[8,64,512]{2,1,0:T(8,128)} %copy-done.1, f32[512,256]{1,0:T(8,128)} %bitcast.5), custom_call_target="tpu_custom_call" | custom-call | tf_op jit(solution)/shard_map/pallas_call | solution.py:89
  57.1 0.9 %fusion.13 = f32[4096]{0:T(1024)S(1)} fusion(f32[8,4096]{1,0:T(8,128)} %shard_map.77), kind=kLoop, calls=%fused_computation.28 | loop fusion | flops 4096 | bytes 32768 | tf_op jit(solution)/shard_map/mul | solution.py:133
  58.1 0.1 mul.137
  58.2 0.0 copy-start.2
  58.2 0.1 fusion.14
  58.2 1.6 %collective-permute-start = (f32[64]{0:T(128)S(1)}, f32[64]{0:T(128)S(1)}, u32[]{:S(2)}, u32[]{:S(2)}) collective-permute-start(f32[64]{0:T(128)S(1)} %fusion.14), channel_id=1, source_target_pairs={{0,1},{1,0},{2,3},{3,2},{4,5},{5,4},{6,7},{7,6},{8,9},{9,8},{10,11... | collective-permute-start | bytes 776 | tf_op jit(solution)/shard_map/ppermute | solution.py:136
  59.8 2.0 %collective-permute-done = f32[64]{0:T(128)S(1)} collective-permute-done((f32[64]{0:T(128)S(1)}, f32[64]{0:T(128)S(1)}, u32[]{:S(2)}, u32[]{:S(2)}) %collective-permute-start) | collective-permute-done | bytes 288 | tf_op jit(solution)/shard_map/ppermute | solution.py:136
  61.8 0.5 add_log_fusion
  62.4 0.0 copy-done.2
  (7 shorter events, 0.2 us)
Async XLA Ops:
  0.6 0.7 %copy-start.8 = (f32[512]{0:T(512)S(1)}, f32[512]{0:T(512)}, u32[]{:S(2)}) copy-start(f32[512]{0:T(512)} %param.7) | copy-start | bytes 6148
  0.6 0.7 %copy-start.7 = (s32[512,1]{0,1:T(1,128)S(1)}, s32[512,1]{0,1:T(1,128)}, u32[]{:S(2)}) copy-start(s32[512,1]{0,1:T(1,128)} %param.8) | copy-start | bytes 6148
  0.7 0.7 %copy-start.6 = (s32[512]{0:T(512)S(1)}, s32[512]{0:T(512)}, u32[]{:S(2)}) copy-start(s32[512]{0:T(512)} %param.9) | copy-start | bytes 6148
  3.6 7.5 %copy-start.5 = (f32[3,64]{1,0:T(4,128)S(1)}, f32[3,64]{1,0:T(4,128)}, u32[]{:S(2)}) copy-start(f32[3,64]{1,0:T(4,128)} %param.11) | copy-start | bytes 2308
  3.6 22.0 %all-to-all-start = ((f32[16,32,256]{2,1,0:T(8,128)}), f32[16,32,256]{2,1,0:T(8,128)S(1)}, u32[]{:S(2)}, u32[]{:S(2)}) async-start(f32[16,32,256]{2,1,0:T(8,128)} %bitcast.2), calls=%async_computation | async-start | bytes 1048576 | tf_op jit(solution)/shard_map/all_to_all | solution.py:125
  11.1 0.7 %copy-start.3 = (f32[3,512]{1,0:T(4,128)S(1)}, f32[3,512]{1,0:T(4,128)}, u32[]{:S(2)}) copy-start(f32[3,512]{1,0:T(4,128)} %param.10) | copy-start | bytes 18436
  11.8 0.6 %copy-start.4 = (f32[32]{0:T(128)}, f32[32]{0:T(128)S(1)}, u32[]{:S(2)}) copy-start(f32[32]{0:T(128)S(1)} %add_multiply_fusion.wave_ref) | copy-start | bytes 388
  26.4 18.6 %all-to-all-start.1 = ((f32[16,32,256]{2,1,0:T(8,128)}), f32[16,32,256]{2,1,0:T(8,128)S(1)}, u32[]{:S(2)}, u32[]{:S(2)}) async-start(f32[16,32,256]{2,1,0:T(8,128)} %broadcast_in_dim.2), calls=%async_computation.1 | async-start | bytes 1048576 | tf_op jit(solution)/shard_map/all_to_all | solution.py:129
  31.2 13.8 %copy-start.1 = (f32[8,64,512]{2,1,0:T(8,128)}, f32[8,64,512]{2,1,0:T(8,128)S(1)}, u32[]{:S(2)}) copy-start(f32[8,64,512]{2,1,0:T(8,128)S(1)} %sqrt_dynamic-update-slice_fusion.geo_ref) | copy-start | bytes 3145732
  45.0 0.8 %copy-start = (f32[16,32,256]{2,1,0:T(8,128)}, f32[16,32,256]{2,1,0:T(8,128)S(1)}, u32[]{:S(2)}) copy-start(f32[16,32,256]{2,1,0:T(8,128)S(1)} %all-to-all-done.1) | copy-start | bytes 1572868
  58.2 4.2 %copy-start.2 = (f32[32,2,64]{2,1,0:T(2,128)}, f32[32,2,64]{2,1,0:T(2,128)S(1)}, u32[]{:S(2)}) copy-start(f32[32,2,64]{2,1,0:T(2,128)S(1)} %mul.137) | copy-start | bytes 49156
  58.2 3.6 %collective-permute-start = (f32[64]{0:T(128)S(1)}, f32[64]{0:T(128)S(1)}, u32[]{:S(2)}, u32[]{:S(2)}) collective-permute-start(f32[64]{0:T(128)S(1)} %fusion.14), channel_id=1, source_target_pairs={{0,1},{1,0},{2,3},{3,2},{4,5},{5,4},{6,7},{7,6},{8,9},{9,8},{10,11... | collective-permute-start | bytes 776 | tf_op jit(solution)/shard_map/ppermute | solution.py:136

commit v5 on v4

--- a/solution.py
+++ b/solution.py
@@ -11,7 +11,7 @@
 reference_radius = 10.0
 
 
-def field_kernel(wave_ref, geo_ref, src_ref, out_ref, acc_ref, chan_ref):
+def field_kernel(wave_ref, geo_ref, src_ref, out_ref, acc_ref, chan_ref, spread_ref):
     freqs, _, observers, lanes = acc_ref.shape
     blocks = observers // 8
 
@@ -20,6 +20,12 @@
         acc_ref[...] = jnp.zeros(acc_ref.shape, acc_ref.dtype)
 
     chan_ref[...] = jnp.transpose(src_ref[...])
+
+    def spread_body(row, carry):
+        spread_ref[row] = jnp.broadcast_to(chan_ref[pl.ds(row, 1), :], (8, lanes))
+        return carry
+
+    lax.fori_loop(0, chan_ref.shape[0], spread_body, 0, unroll=8)
 
     def block_body(block, carry):
         rows = pl.ds(pl.multiple_of(block * 8, 8), 8)
@@ -31,9 +37,7 @@
         def freq_body(f, phase):
             weight_real, weight_imag = phase
             base = f * 8
-            channel = [
-                jnp.broadcast_to(chan_ref[pl.ds(base + c, 1), :], (8, lanes)) for c in range(8)
-            ]
+            channel = [spread_ref[base + c] for c in range(8)]
             wave_distance = wave_ref[f] * distance
             dipole_real = along[0] * channel[2] + along[1] * channel[4] + along[2] * channel[6]
             dipole_imag = along[0] * channel[3] + along[1] * channel[5] + along[2] * channel[7]
@@ -47,7 +51,7 @@
             )
 
         lax.fori_loop(
-            0, freqs, freq_body, (geo_ref[0, rows, :], geo_ref[1, rows, :]), unroll=2
+            0, freqs, freq_body, (geo_ref[0, rows, :], geo_ref[1, rows, :]), unroll=4
         )
         return carry
 
@@ -99,6 +103,7 @@
         scratch_shapes=[
             pltpu.VMEM((freqs, 2, observers, 128), jnp.float32),
             pltpu.VMEM((columns, 128), jnp.float32),
+            pltpu.VMEM((columns, 8, 128), jnp.float32),
         ],
         compiler_params=pltpu.CompilerParams(dimension_semantics=("arbitrary",)),
     )(wave_numbers, geometry, portion)

time: 62.8 us -> 62.3 us (level)
  no operation moved by 1% of the time
where the time goes in v5:
time: 62.3 us; the launch traced here: 61.9 us
  waiting for transfers between devices  28 us (45%)
  starting transfers between devices  13.2 us (21%)
  Pallas kernels  10.8 us (17%)
  other arithmetic  3.72 us (6%)
  local copies, waits for them, and re-layouts  3.17 us (5%)
  matrix products  2.21 us (4%)
  between operations  0.8 us (1%)
    all_to_all x1, waiting for transfers between devices, shards(): lax.all_to_all(jnp.broadcast_to(own_source[None], (groups, panels_dev, co...  13.8 us
    all_to_all x1, waiting for transfers between devices, shards(): lax.all_to_all(local_source.reshape(groups, panels_dev, columns), 'obs',...  12.1 us
    pallas_call x1, Pallas kernels, far_field(): pl.pallas_call(field_kernel, grid=(panel_total // 128,), in_specs=[pl.Blo...  10.8 us
    all_to_all x1, starting transfers between devices, shards(): lax.all_to_all(local_source.reshape(groups, panels_dev, columns), 'obs',...  7.49 us
    all_to_all x1, starting transfers between devices, shards(): lax.all_to_all(jnp.broadcast_to(own_source[None], (groups, panels_dev, co...  4.1 us
    dot_general x1, matrix products, shards(): jnp.dot(selector, weighted, preferred_element_type=jnp.float32)  2.21 us
    unnamed x18, local copies, waits for them, and re-layouts  2.18 us
    unnamed x7, other arithmetic  2.06 us
  transfers between devices with their start and end apart: 3, of which 3 were waited for; matrix products, arithmetic and copies ran while one was open for 4% of the time, Pallas kernels for 0%

profile of v5, /device:TPU:0, one launch (start us, length us, event | category | flops | bytes accessed | tf_op | source)
XLA Modules:
  0.0 61.9 jit_solution(13976851628650615504)
XLA Ops:
  0.6 0.0 copy-start.8
  0.6 0.0 copy-start.7
  0.7 0.0 copy-start.6
  0.7 0.6 %copy-done.8 = f32[512]{0:T(512)S(1)} copy-done((f32[512]{0:T(512)S(1)}, f32[512]{0:T(512)}, u32[]{:S(2)}) %copy-start.8) | copy-done | bytes 2072
  1.3 0.0 copy-done.7
  1.3 0.0 copy-done.6
  1.4 2.2 %fusion = f32[512,256]{1,0:T(8,128)} fusion(s32[512]{0:T(512)S(1)} %copy-done.6, s32[512]{0:T(512)S(1)} %bitcast.8, s32[512]{0:T(512)S(1)} %get-tuple-element.4, s32[512]{0:T(512)S(1)} %get-tuple-element.5, bf16[512,256]{1,0:T(8,128)(2,1)} %param.6, f32[512]{0:T(512)S(1)} %copy-done.8), kind=kOutput, calls=%fused_computation | convolution fusion | flops 135397376 | bytes 796672 | tf_op jit(solution)/shard_map/dot_general | solution.py:125
  3.6 0.0 copy-start.5
  3.6 7.5 %all-to-all-start = ((f32[16,32,256]{2,1,0:T(8,128)}), f32[16,32,256]{2,1,0:T(8,128)S(1)}, u32[]{:S(2)}, u32[]{:S(2)}) async-start(f32[16,32,256]{2,1,0:T(8,128)} %bitcast.2), calls=%async_computation | async-start | bytes 1048576 | tf_op jit(solution)/shard_map/all_to_all | solution.py:130
  11.1 0.0 copy-start.3
  11.1 0.0 copy-done.5
  11.1 0.7 %copy-done.3 = f32[3,512]{1,0:T(4,128)S(1)} copy-done((f32[3,512]{1,0:T(4,128)S(1)}, f32[3,512]{1,0:T(4,128)}, u32[]{:S(2)}) %copy-start.3) | copy-done | bytes 6168
  11.8 0.0 copy-start.4
  11.8 0.1 broadcast_subtract_fusion
  11.9 0.5 multiply_dynamic-update-slice_fusion.1
  12.4 0.0 copy-done.4
  12.4 0.5 multiply_dynamic-update-slice_fusion
  12.9 0.5 cosine_dynamic-update-slice_fusion
  13.4 12.1 %all-to-all-done = f32[16,32,256]{2,1,0:T(8,128)S(1)} async-done(((f32[16,32,256]{2,1,0:T(8,128)}), f32[16,32,256]{2,1,0:T(8,128)S(1)}, u32[]{:S(2)}, u32[]{:S(2)}) %all-to-all-start) | async-done | bytes 524320 | tf_op jit(solution)/shard_map/all_to_all | solution.py:130
  25.6 0.9 %broadcast_in_dim.2 = f32[16,32,256]{2,1,0:T(8,128)} broadcast(f32[32,256]{1,0:T(8,128)S(1)} %reduce_sum.18), dimensions={1,2} | broadcast | bytes 557056 | tf_op jit(solution)/shard_map/broadcast_in_dim | solution.py:135
  26.4 4.1 %all-to-all-start.1 = ((f32[16,32,256]{2,1,0:T(8,128)}), f32[16,32,256]{2,1,0:T(8,128)S(1)}, u32[]{:S(2)}, u32[]{:S(2)}) async-start(f32[16,32,256]{2,1,0:T(8,128)} %broadcast_in_dim.2), calls=%async_computation.1 | async-start | bytes 1048576 | tf_op jit(solution)/shard_map/all_to_all | solution.py:134
  30.5 0.5 sine_dynamic-update-slice_fusion
  31.2 0.0 copy-start.1
  31.2 13.8 %all-to-all-done.1 = f32[16,32,256]{2,1,0:T(8,128)S(1)} async-done(((f32[16,32,256]{2,1,0:T(8,128)}), f32[16,32,256]{2,1,0:T(8,128)S(1)}, u32[]{:S(2)}, u32[]{:S(2)}) %all-to-all-start.1) | async-done | bytes 524320 | tf_op jit(solution)/shard_map/all_to_all | solution.py:134
  45.0 0.0 copy-start
  45.0 0.0 copy-done.1
  45.0 0.8 %copy-done = f32[16,32,256]{2,1,0:T(8,128)} copy-done((f32[16,32,256]{2,1,0:T(8,128)}, f32[16,32,256]{2,1,0:T(8,128)S(1)}, u32[]{:S(2)}) %copy-start) | copy-done | bytes 524312
  45.8 10.8 %shard_map.77 = f32[8,4096]{1,0:T(8,128)} custom-call(f32[32]{0:T(128)} %copy-done.4, f32[8,64,512]{2,1,0:T(8,128)} %copy-done.1, f32[512,256]{1,0:T(8,128)} %bitcast.5), custom_call_target="tpu_custom_call" | custom-call | tf_op jit(solution)/shard_map/pallas_call | solution.py:93
  56.6 0.9 %fusion.13 = f32[4096]{0:T(1024)S(1)} fusion(f32[8,4096]{1,0:T(8,128)} %shard_map.77), kind=kLoop, calls=%fused_computation.28 | loop fusion | flops 4096 | bytes 32768 | tf_op jit(solution)/shard_map/mul | solution.py:138
  57.6 0.1 mul.137
  57.7 0.0 copy-start.2
  57.7 0.1 fusion.14
  57.7 1.6 %collective-permute-start = (f32[64]{0:T(128)S(1)}, f32[64]{0:T(128)S(1)}, u32[]{:S(2)}, u32[]{:S(2)}) collective-permute-start(f32[64]{0:T(128)S(1)} %fusion.14), channel_id=1, source_target_pairs={{0,1},{1,0},{2,3},{3,2},{4,5},{5,4},{6,7},{7,6},{8,9},{9,8},{10,11... | collective-permute-start | bytes 776 | tf_op jit(solution)/shard_map/ppermute | solution.py:141
  59.3 2.0 %collective-permute-done = f32[64]{0:T(128)S(1)} collective-permute-done((f32[64]{0:T(128)S(1)}, f32[64]{0:T(128)S(1)}, u32[]{:S(2)}, u32[]{:S(2)}) %collective-permute-start) | collective-permute-done | bytes 288 | tf_op jit(solution)/shard_map/ppermute | solution.py:141
  61.3 0.5 add_log_fusion
  61.9 0.0 copy-done.2
  (7 shorter events, 0.2 us)
Async XLA Ops:
  0.6 0.7 %copy-start.8 = (f32[512]{0:T(512)S(1)}, f32[512]{0:T(512)}, u32[]{:S(2)}) copy-start(f32[512]{0:T(512)} %param.7) | copy-start | bytes 6148
  0.6 0.7 %copy-start.7 = (s32[512,1]{0,1:T(1,128)S(1)}, s32[512,1]{0,1:T(1,128)}, u32[]{:S(2)}) copy-start(s32[512,1]{0,1:T(1,128)} %param.8) | copy-start | bytes 6148
  0.7 0.7 %copy-start.6 = (s32[512]{0:T(512)S(1)}, s32[512]{0:T(512)}, u32[]{:S(2)}) copy-start(s32[512]{0:T(512)} %param.9) | copy-start | bytes 6148
  3.6 7.5 %copy-start.5 = (f32[3,64]{1,0:T(4,128)S(1)}, f32[3,64]{1,0:T(4,128)}, u32[]{:S(2)}) copy-start(f32[3,64]{1,0:T(4,128)} %param.11) | copy-start | bytes 2308
  3.6 22.0 %all-to-all-start = ((f32[16,32,256]{2,1,0:T(8,128)}), f32[16,32,256]{2,1,0:T(8,128)S(1)}, u32[]{:S(2)}, u32[]{:S(2)}) async-start(f32[16,32,256]{2,1,0:T(8,128)} %bitcast.2), calls=%async_computation | async-start | bytes 1048576 | tf_op jit(solution)/shard_map/all_to_all | solution.py:130
  11.1 0.7 %copy-start.3 = (f32[3,512]{1,0:T(4,128)S(1)}, f32[3,512]{1,0:T(4,128)}, u32[]{:S(2)}) copy-start(f32[3,512]{1,0:T(4,128)} %param.10) | copy-start | bytes 18436
  11.8 0.6 %copy-start.4 = (f32[32]{0:T(128)}, f32[32]{0:T(128)S(1)}, u32[]{:S(2)}) copy-start(f32[32]{0:T(128)S(1)} %add_multiply_fusion.wave_ref) | copy-start | bytes 388
  26.4 18.6 %all-to-all-start.1 = ((f32[16,32,256]{2,1,0:T(8,128)}), f32[16,32,256]{2,1,0:T(8,128)S(1)}, u32[]{:S(2)}, u32[]{:S(2)}) async-start(f32[16,32,256]{2,1,0:T(8,128)} %broadcast_in_dim.2), calls=%async_computation.1 | async-start | bytes 1048576 | tf_op jit(solution)/shard_map/all_to_all | solution.py:134
  31.2 13.8 %copy-start.1 = (f32[8,64,512]{2,1,0:T(8,128)}, f32[8,64,512]{2,1,0:T(8,128)S(1)}, u32[]{:S(2)}) copy-start(f32[8,64,512]{2,1,0:T(8,128)S(1)} %sqrt_dynamic-update-slice_fusion.geo_ref) | copy-start | bytes 3145732
  45.0 0.8 %copy-start = (f32[16,32,256]{2,1,0:T(8,128)}, f32[16,32,256]{2,1,0:T(8,128)S(1)}, u32[]{:S(2)}) copy-start(f32[16,32,256]{2,1,0:T(8,128)S(1)} %all-to-all-done.1) | copy-start | bytes 1572868
  57.7 4.2 %copy-start.2 = (f32[32,2,64]{2,1,0:T(2,128)}, f32[32,2,64]{2,1,0:T(2,128)S(1)}, u32[]{:S(2)}) copy-start(f32[32,2,64]{2,1,0:T(2,128)S(1)} %mul.137) | copy-start | bytes 49156
  57.7 3.6 %collective-permute-start = (f32[64]{0:T(128)S(1)}, f32[64]{0:T(128)S(1)}, u32[]{:S(2)}, u32[]{:S(2)}) collective-permute-start(f32[64]{0:T(128)S(1)} %fusion.14), channel_id=1, source_target_pairs={{0,1},{1,0},{2,3},{3,2},{4,5},{5,4},{6,7},{7,6},{8,9},{9,8},{10,11... | collective-permute-start | bytes 776 | tf_op jit(solution)/shard_map/ppermute | solution.py:141

commit v6 on v5

--- a/solution.py
+++ b/solution.py
@@ -1,3 +1,4 @@
+import functools
 import math
 
 import jax
@@ -11,7 +12,7 @@
 reference_radius = 10.0
 
 
-def field_kernel(wave_ref, geo_ref, src_ref, out_ref, acc_ref, chan_ref, spread_ref):
+def field_kernel(block_group, freq_unroll, wave_ref, geo_ref, src_ref, out_ref, acc_ref, chan_ref, spread_ref):
     freqs, _, observers, lanes = acc_ref.shape
     blocks = observers // 8
 
@@ -27,35 +28,44 @@
 
     lax.fori_loop(0, chan_ref.shape[0], spread_body, 0, unroll=8)
 
-    def block_body(block, carry):
-        rows = pl.ds(pl.multiple_of(block * 8, 8), 8)
-        step_cos = geo_ref[2, rows, :]
-        step_sin = geo_ref[3, rows, :]
-        along = [geo_ref[4 + j, rows, :] for j in range(3)]
-        distance = geo_ref[7, rows, :]
+    def block_body(group, carry):
+        spans = [
+            pl.ds(pl.multiple_of((group * block_group + member) * 8, 8), 8)
+            for member in range(block_group)
+        ]
+        step_cos = [geo_ref[2, rows, :] for rows in spans]
+        step_sin = [geo_ref[3, rows, :] for rows in spans]
+        along = [[geo_ref[4 + j, rows, :] for j in range(3)] for rows in spans]
+        distance = [geo_ref[7, rows, :] for rows in spans]
 
         def freq_body(f, phase):
-            weight_real, weight_imag = phase
             base = f * 8
             channel = [spread_ref[base + c] for c in range(8)]
-            wave_distance = wave_ref[f] * distance
-            dipole_real = along[0] * channel[2] + along[1] * channel[4] + along[2] * channel[6]
-            dipole_imag = along[0] * channel[3] + along[1] * channel[5] + along[2] * channel[7]
-            amp_real = channel[0] + dipole_real - wave_distance * dipole_imag
-            amp_imag = channel[1] + dipole_imag + wave_distance * dipole_real
-            acc_ref[f, 0, rows, :] += weight_real * amp_real + weight_imag * amp_imag
-            acc_ref[f, 1, rows, :] += weight_real * amp_imag - weight_imag * amp_real
-            return (
-                weight_real * step_cos - weight_imag * step_sin,
-                weight_imag * step_cos + weight_real * step_sin,
-            )
+            wave = wave_ref[f]
+            turned = []
+            for member, rows in enumerate(spans):
+                weight_real, weight_imag = phase[member]
+                g = along[member]
+                wave_distance = wave * distance[member]
+                dipole_real = g[0] * channel[2] + g[1] * channel[4] + g[2] * channel[6]
+                dipole_imag = g[0] * channel[3] + g[1] * channel[5] + g[2] * channel[7]
+                amp_real = channel[0] + dipole_real - wave_distance * dipole_imag
+                amp_imag = channel[1] + dipole_imag + wave_distance * dipole_real
+                acc_ref[f, 0, rows, :] += weight_real * amp_real + weight_imag * amp_imag
+                acc_ref[f, 1, rows, :] += weight_real * amp_imag - weight_imag * amp_real
+                turned.append(
+                    (
+                        weight_real * step_cos[member] - weight_imag * step_sin[member],
+                        weight_imag * step_cos[member] + weight_real * step_sin[member],
+                    )
+                )
+            return tuple(turned)
 
-        lax.fori_loop(
-            0, freqs, freq_body, (geo_ref[0, rows, :], geo_ref[1, rows, :]), unroll=4
-        )
+        start = tuple((geo_ref[0, rows, :], geo_ref[1, rows, :]) for rows in spans)
+        lax.fori_loop(0, freqs, freq_body, start, unroll=freq_unroll)
         return carry
 
-    lax.fori_loop(0, blocks, block_body, 0)
+    lax.fori_loop(0, blocks // block_group, block_body, 0)
 
     @pl.when(pl.program_id(0) == pl.num_programs(0) - 1)
     def _():
@@ -91,7 +101,7 @@
         ]
     )
     summed = pl.pallas_call(
-        field_kernel,
+        functools.partial(field_kernel, math.gcd(observers // 8, 4), 2),
         grid=(panel_total // 128,),
         in_specs=[
             pl.BlockSpec(memory_space=pltpu.SMEM),
@@ -108,6 +118,35 @@
         compiler_params=pltpu.CompilerParams(dimension_semantics=("arbitrary",)),
     )(wave_numbers, geometry, portion)
     return summed[0].reshape(freqs, 2, observers)
+
+
+def partner_pairs(groups, bit):
+    return [(k, k ^ bit) for k in range(groups)]
+
+
+def halving_sum(blocks, bits):
+    groups = blocks.shape[0]
+    place = lax.axis_index("obs")
+    current = blocks
+    for bit in bits:
+        split = current.reshape((current.shape[0] // 2, 2) + current.shape[1:])
+        mine = (place // bit) % 2
+        keep = lax.dynamic_index_in_dim(split, mine, 1, keepdims=False)
+        send = lax.dynamic_index_in_dim(split, 1 - mine, 1, keepdims=False)
+        current = keep + lax.ppermute(send, "obs", partner_pairs(groups, bit))
+    return current
+
+
+def doubling_gather(own, bits, groups):
+    place = lax.axis_index("obs")
+    gathered = own
+    for bit in reversed(bits):
+        mine = (place // bit) % 2
+        other = lax.ppermute(gathered, "obs", partner_pairs(groups, bit))
+        low = jnp.where(mine == 0, gathered, other)
+        high = jnp.where(mine == 0, other, gathered)
+        gathered = jnp.stack([low, high], axis=1).reshape((-1,) + gathered.shape[1:])
+    return gathered
 
 
 def shards(cell_spectra, cell_weight, cell_owner, cell_local, panel_position, observer_position):
@@ -127,13 +166,16 @@
     wave_numbers = wave_step * (
         (group_first + jnp.arange(freqs_dev, dtype=jnp.int32)).astype(jnp.float32) + 1.0
     )
-    arrived = lax.all_to_all(
-        local_source.reshape(groups, panels_dev, columns), "obs", 0, 0, tiled=True
-    )
-    own_source = jnp.sum(arrived, axis=0)
-    portion = lax.all_to_all(
-        jnp.broadcast_to(own_source[None], (groups, panels_dev, columns)), "obs", 0, 0, tiled=True
-    ).reshape(panel_total, columns)
+    blocks = local_source.reshape(groups, panels_dev, columns)
+    if groups & (groups - 1) == 0:
+        bits = [1 << k for k in range(groups.bit_length() - 1)]
+        own_source = halving_sum(blocks, bits)
+        portion = doubling_gather(own_source, bits, groups).reshape(panel_total, columns)
+    else:
+        own_source = jnp.sum(lax.all_to_all(blocks, "obs", 0, 0, tiled=True), axis=0)
+        portion = lax.all_to_all(
+            jnp.broadcast_to(own_source[None], blocks.shape), "obs", 0, 0, tiled=True
+        ).reshape(panel_total, columns)
     summed = far_field(portion, panel_position, observer_position, wave_numbers)
     pressure = summed * (reference_radius / math.sqrt(panel_total))
     energy = jnp.sum(pressure[:, 0] * pressure[:, 0] + pressure[:, 1] * pressure[:, 1], axis=0)

time: 62.3 us -> 53.2 us (0.85)
  waiting for transfers between devices: 28 us -> 17.7 us
  starting transfers between devices: 13.2 us -> 16.5 us
  Pallas kernels: 10.8 us -> 9.92 us
  matrix products: 2.21 us -> 1.42 us
  local copies, waits for them, and re-layouts: 3.17 us -> 2.45 us
    all_to_all x2 -> x0, waiting for transfers between devices: 26 us -> none  [the longest x1 13.8 us: shards(): lax.all_to_all(jnp.broadcast_to(own_source[None], (groups, panels_dev, co...]
    ppermute x0 -> x8, waiting for transfers between devices: none -> 15.7 us  [the longest x4 8.67 us: doubling_gather(): other = lax.ppermute(gathered, 'obs', partner_pairs(groups, bit))]
    ppermute x0 -> x8, starting transfers between devices: none -> 14.9 us  [the longest x4 8.23 us: halving_sum(): current = keep + lax.ppermute(send, 'obs', partner_pairs(groups, bit))]
    all_to_all x2 -> x0, starting transfers between devices: 11.6 us -> none  [the longest x1 7.49 us: shards(): lax.all_to_all(local_source.reshape(groups, panels_dev, columns), 'obs',...]
    pallas_call x1, Pallas kernels: 10.8 us -> 9.92 us  [far_field(): pl.pallas_call(functools.partial(field_kernel, math.gcd(observers // 8, 4...]
    another operation x0 -> x2, local copies, waits for them, and re-layouts: none -> 0.88 us  [doubling_gather(): jnp.stack([low, high], axis=1).reshape((-1,) + gathered.shape[1:])]
    broadcast_in_dim x1 -> x0, local copies, waits for them, and re-layouts: 0.87 us -> none  [shards(): jnp.broadcast_to(own_source[None], (groups, panels_dev, columns))]
    unnamed x18 -> x16, local copies, waits for them, and re-layouts: 2.18 us -> 1.38 us
  transfers between devices with their start and end apart: 3 -> 9, of which waited for: 3 -> 9; matrix products, arithmetic and copies ran while one was open for 4% -> 4% of each run, Pallas kernels for 0% -> 0%
where the time goes in v6:
time: 53.2 us; the launch traced here: 52.9 us
  waiting for transfers between devices  17.7 us (33%)
  starting transfers between devices  16.5 us (31%)
  Pallas kernels  9.92 us (19%)
  other arithmetic  3.91 us (7%)
  local copies, waits for them, and re-layouts  2.45 us (5%)
  matrix products  1.42 us (3%)
  between operations  0.99 us (2%)
    pallas_call x1, Pallas kernels, far_field(): pl.pallas_call(functools.partial(field_kernel, math.gcd(observers // 8, 4...  9.92 us
    ppermute x4, waiting for transfers between devices, doubling_gather(): other = lax.ppermute(gathered, 'obs', partner_pairs(groups, bit))  8.67 us
    ppermute x4, starting transfers between devices, halving_sum(): current = keep + lax.ppermute(send, 'obs', partner_pairs(groups, bit))  8.23 us
    ppermute x4, waiting for transfers between devices, halving_sum(): current = keep + lax.ppermute(send, 'obs', partner_pairs(groups, bit))  6.99 us
    ppermute x4, starting transfers between devices, doubling_gather(): other = lax.ppermute(gathered, 'obs', partner_pairs(groups, bit))  6.71 us
    unnamed x7, other arithmetic  2.05 us
    ppermute x1, waiting for transfers between devices, shards(): band_total = energy + lax.ppermute(energy, 'freq', [(0, 1), (1, 0)])  2.02 us
    ppermute x1, starting transfers between devices, shards(): band_total = energy + lax.ppermute(energy, 'freq', [(0, 1), (1, 0)])  1.58 us
  transfers between devices with their start and end apart: 9, of which 9 were waited for; matrix products, arithmetic and copies ran while one was open for 4% of the time, Pallas kernels for 0%

profile of v6, /device:TPU:0, one launch (start us, length us, event | category | flops | bytes accessed | tf_op | source)
XLA Modules:
  0.0 52.9 jit_solution(15703139632161658639)
XLA Ops:
  0.7 0.0 copy-start.7
  0.7 0.0 copy-start.6
  0.7 0.0 copy-start.5
  0.7 0.6 %copy-done.7 = f32[512]{0:T(512)S(1)} copy-done((f32[512]{0:T(512)S(1)}, f32[512]{0:T(512)}, u32[]{:S(2)}) %copy-start.7) | copy-done | bytes 2072
  1.3 0.0 copy-done.6
  1.4 0.0 copy-done.5
  1.4 1.4 %fusion = f32[512,256]{1,0:T(8,128)S(1)} fusion(s32[512]{0:T(512)S(1)} %copy-done.5, s32[512]{0:T(512)S(1)} %bitcast.60, s32[512]{0:T(512)S(1)} %get-tuple-element.12, s32[512]{0:T(512)S(1)} %get-tuple-element.13, bf16[512,256]{1,0:T(8,128)(2,1)} %param.6, f32[512]{0:T(512)S(1)} %copy-done.7), kind=kOutput, calls=%fused_computation | convolution fusion | flops 135397376 | bytes 796672 | tf_op jit(solution)/shard_map/dot_general | solution.py:164
  2.8 0.5 collective-permute-start
  3.4 0.0 copy-start.3
  3.4 0.0 copy-start.2
  3.4 0.0 copy-start.4
  3.4 0.7 %copy-done.2 = f32[3,512]{1,0:T(4,128)S(1)} copy-done((f32[3,512]{1,0:T(4,128)S(1)}, f32[3,512]{1,0:T(4,128)}, u32[]{:S(2)}) %copy-start.2) | copy-done | bytes 6168
  4.1 0.0 copy-done.4
  4.1 0.1 broadcast_subtract_fusion
  4.2 0.4 collective-permute-done
  4.6 2.9 %collective-permute-start.1 = (f32[4,32,256]{2,1,0:T(8,128)S(1)}, f32[4,32,256]{2,1,0:T(8,128)S(1)}, u32[]{:S(2)}, u32[]{:S(2)}) collective-permute-start(f32[4,32,256]{2,1,0:T(8,128)S(1)} %dynamic-slice_bitcast_fusion.1), channel_id=1, source_target_pairs={{0,4},{2,6},{4,0},{6,2},{8,12},{10,14},{12,8},{14,10},{16,20},{18,... | collective-permute-start | bytes 393224 | tf_op jit(solution)/shard_map/ppermute | solution.py:136
  7.5 0.5 %multiply_dynamic-update-slice_fusion.1 = (f32[8,64,512]{2,1,0:T(8,128)S(1)}, f32[1,64,512]{2,1,0:T(8,128)S(1)}) fusion(f32[]{:T(128)S(1)} %bitcast.58, f32[3,64,512]{2,1,0:T(8,128)S(1)} %broadcast_subtract_fusion), kind=kLoop, calls=%fused_computation.31 | loop fusion | flops 262143 | bytes 655364
  8.0 3.3 %collective-permute-done.1 = f32[4,32,256]{2,1,0:T(8,128)S(1)} collective-permute-done((f32[4,32,256]{2,1,0:T(8,128)S(1)}, f32[4,32,256]{2,1,0:T(8,128)S(1)}, u32[]{:S(2)}, u32[]{:S(2)}) %collective-permute-start.1) | collective-permute-done | bytes 131104 | tf_op jit(solution)/shard_map/ppermute | solution.py:136
  11.3 1.9 %collective-permute-start.2 = (f32[2,32,256]{2,1,0:T(8,128)S(1)}, f32[2,32,256]{2,1,0:T(8,128)S(1)}, u32[]{:S(2)}, u32[]{:S(2)}) collective-permute-start(f32[2,32,256]{2,1,0:T(8,128)S(1)} %dynamic-slice_bitcast_fusion.2), channel_id=1, source_target_pairs={{0,8},{2,10},{4,12},{6,14},{8,0},{10,2},{12,4},{14,6},{16,24},{18,... | collective-permute-start | bytes 196616 | tf_op jit(solution)/shard_map/ppermute | solution.py:136
  13.2 0.0 copy-done.3
  13.2 0.5 multiply_dynamic-update-slice_fusion
  13.8 1.9 %collective-permute-done.2 = f32[2,32,256]{2,1,0:T(8,128)S(1)} collective-permute-done((f32[2,32,256]{2,1,0:T(8,128)S(1)}, f32[2,32,256]{2,1,0:T(8,128)S(1)}, u32[]{:S(2)}, u32[]{:S(2)}) %collective-permute-start.2) | collective-permute-done | bytes 65568 | tf_op jit(solution)/shard_map/ppermute | solution.py:136
  15.7 2.9 %collective-permute-start.3 = (f32[1,32,256]{2,1,0:T(8,128)S(1)}, f32[1,32,256]{2,1,0:T(8,128)S(1)}, u32[]{:S(2)}, u32[]{:S(2)}) collective-permute-start(f32[1,32,256]{2,1,0:T(8,128)S(1)} %constant_dynamic-slice_fusion), channel_id=1, source_target_pairs={{0,16},{2,18},{4,20},{6,22},{8,24},{10,26},{12,28},{14,30},{16,0},... | collective-permute-start | bytes 98312 | tf_op jit(solution)/shard_map/ppermute | solution.py:136
  18.6 0.5 cosine_dynamic-update-slice_fusion
  19.1 1.5 %collective-permute-done.3 = f32[1,32,256]{2,1,0:T(8,128)S(1)} collective-permute-done((f32[1,32,256]{2,1,0:T(8,128)S(1)}, f32[1,32,256]{2,1,0:T(8,128)S(1)}, u32[]{:S(2)}, u32[]{:S(2)}) %collective-permute-start.3) | collective-permute-done | bytes 32800 | tf_op jit(solution)/shard_map/ppermute | solution.py:136
  20.6 2.9 %collective-permute-start.4 = (f32[1,32,256]{2,1,0:T(8,128)S(1)}, f32[1,32,256]{2,1,0:T(8,128)S(1)}, u32[]{:S(2)}, u32[]{:S(2)}) collective-permute-start(f32[1,32,256]{2,1,0:T(8,128)S(1)} %dynamic-slice_add_fusion), channel_id=1, source_target_pairs={{0,16},{2,18},{4,20},{6,22},{8,24},{10,26},{12,28},{14,30},{16,0},... | collective-permute-start | bytes 98312 | tf_op jit(solution)/shard_map/ppermute | solution.py:145
  23.5 0.5 sine_dynamic-update-slice_fusion
  23.9 1.6 %collective-permute-done.4 = f32[1,32,256]{2,1,0:T(8,128)S(1)} collective-permute-done((f32[1,32,256]{2,1,0:T(8,128)S(1)}, f32[1,32,256]{2,1,0:T(8,128)S(1)}, u32[]{:S(2)}, u32[]{:S(2)}) %collective-permute-start.4) | collective-permute-done | bytes 32800 | tf_op jit(solution)/shard_map/ppermute | solution.py:145
  25.5 2.2 %collective-permute-start.5 = (f32[2,32,256]{2,1,0:T(8,128)S(1)}, f32[2,32,256]{2,1,0:T(8,128)S(1)}, u32[]{:S(2)}, u32[]{:S(2)}) collective-permute-start(f32[2,32,256]{2,1,0:T(8,128)S(1)} %maximum_bitcast_fusion), channel_id=1, source_target_pairs={{0,8},{2,10},{4,12},{6,14},{8,0},{10,2},{12,4},{14,6},{16,24},{18,... | collective-permute-start | bytes 196616 | tf_op jit(solution)/shard_map/ppermute | solution.py:145
  27.8 2.2 %collective-permute-done.5 = f32[2,32,256]{2,1,0:T(8,128)S(1)} collective-permute-done((f32[2,32,256]{2,1,0:T(8,128)S(1)}, f32[2,32,256]{2,1,0:T(8,128)S(1)}, u32[]{:S(2)}, u32[]{:S(2)}) %collective-permute-start.5) | collective-permute-done | bytes 65568 | tf_op jit(solution)/shard_map/ppermute | solution.py:145
  30.1 1.6 %collective-permute-start.6 = (f32[4,32,256]{2,1,0:T(8,128)S(1)}, f32[4,32,256]{2,1,0:T(8,128)S(1)}, u32[]{:S(2)}, u32[]{:S(2)}) collective-permute-start(f32[4,32,256]{2,1,0:T(8,128)S(1)} %bitcast.53), channel_id=1, source_target_pairs={{0,4},{2,6},{4,0},{6,2},{8,12},{10,14},{12,8},{14,10},{16,20},{18,... | collective-permute-start | bytes 393224 | tf_op jit(solution)/shard_map/ppermute | solution.py:145
  31.6 3.5 %collective-permute-done.6 = f32[4,32,256]{2,1,0:T(8,128)S(1)} collective-permute-done((f32[4,32,256]{2,1,0:T(8,128)S(1)}, f32[4,32,256]{2,1,0:T(8,128)S(1)}, u32[]{:S(2)}, u32[]{:S(2)}) %collective-permute-start.6) | collective-permute-done | bytes 131104 | tf_op jit(solution)/shard_map/ppermute | solution.py:145
  35.2 0.1 collective-permute-start.7
  35.3 0.0 copy-start
  35.3 1.4 %collective-permute-done.7 = f32[8,32,256]{2,1,0:T(8,128)S(1)} collective-permute-done((f32[8,32,256]{2,1,0:T(8,128)S(1)}, f32[8,32,256]{2,1,0:T(8,128)S(1)}, u32[]{:S(2)}, u32[]{:S(2)}) %collective-permute-start.7) | collective-permute-done | bytes 262176 | tf_op jit(solution)/shard_map/ppermute | solution.py:145
  36.9 0.0 copy-done
  36.9 0.9 %copy.17 = f32[8,2,32,256]{3,2,1,0:T(8,128)} copy(f32[8,2,32,256]{3,2,0,1:T(8,128)S(1)} %pad_maximum_fusion) | data formatting | bytes 1048576 | tf_op jit(solution)/shard_map/stack | solution.py:148
  37.7 9.9 %shard_map.77 = f32[8,4096]{1,0:T(8,128)} custom-call(f32[32]{0:T(128)} %copy-done.3, f32[8,64,512]{2,1,0:T(8,128)} %copy-done, f32[512,256]{1,0:T(8,128)} %bitcast.49), custom_call_target="tpu_custom_call" | custom-call | tf_op jit(solution)/shard_map/pallas_call | solution.py:103
  47.7 0.9 %fusion.13 = f32[4096]{0:T(1024)S(1)} fusion(f32[8,4096]{1,0:T(8,128)} %shard_map.77), kind=kLoop, calls=%fused_computation.47 | loop fusion | flops 4096 | bytes 32768 | tf_op jit(solution)/shard_map/mul | solution.py:180
  48.6 0.1 mul.137
  48.7 0.0 copy-start.1
  48.7 0.1 fusion.14
  48.8 1.6 %collective-permute-start.8 = (f32[64]{0:T(128)S(1)}, f32[64]{0:T(128)S(1)}, u32[]{:S(2)}, u32[]{:S(2)}) collective-permute-start(f32[64]{0:T(128)S(1)} %fusion.14), channel_id=1, source_target_pairs={{0,1},{1,0},{2,3},{3,2},{4,5},{5,4},{6,7},{7,6},{8,9},{9,8},{10,11... | collective-permute-start | bytes 776 | tf_op jit(solution)/shard_map/ppermute | solution.py:183
  50.4 2.0 %collective-permute-done.8 = f32[64]{0:T(128)S(1)} collective-permute-done((f32[64]{0:T(128)S(1)}, f32[64]{0:T(128)S(1)}, u32[]{:S(2)}, u32[]{:S(2)}) %collective-permute-start.8) | collective-permute-done | bytes 288 | tf_op jit(solution)/shard_map/ppermute | solution.py:183
  52.4 0.5 add_log_fusion
  52.9 0.0 copy-done.1
  (23 shorter events, 0.4 us)
Async XLA Ops:
  0.7 0.7 %copy-start.7 = (f32[512]{0:T(512)S(1)}, f32[512]{0:T(512)}, u32[]{:S(2)}) copy-start(f32[512]{0:T(512)} %param.7) | copy-start | bytes 6148
  0.7 0.7 %copy-start.6 = (s32[512,1]{0,1:T(1,128)S(1)}, s32[512,1]{0,1:T(1,128)}, u32[]{:S(2)}) copy-start(s32[512,1]{0,1:T(1,128)} %param.8) | copy-start | bytes 6148
  0.7 0.7 %copy-start.5 = (s32[512]{0:T(512)S(1)}, s32[512]{0:T(512)}, u32[]{:S(2)}) copy-start(s32[512]{0:T(512)} %param.9) | copy-start | bytes 6148
  2.8 1.7 %collective-permute-start = (f32[8,32,256]{2,1,0:T(8,128)S(1)}, f32[8,32,256]{2,1,0:T(8,128)S(1)}, u32[]{:S(2)}, u32[]{:S(2)}) collective-permute-start(f32[8,32,256]{2,1,0:T(8,128)S(1)} %dynamic-slice_bitcast_fusion), channel_id=1, source_target_pairs={{0,2},{2,0},{4,6},{6,4},{8,10},{10,8},{12,14},{14,12},{16,18},{18,... | collective-permute-start | bytes 786440 | tf_op jit(solution)/shard_map/ppermute | solution.py:136
  3.4 9.9 %copy-start.3 = (f32[32]{0:T(128)}, f32[32]{0:T(128)S(1)}, u32[]{:S(2)}) copy-start(f32[32]{0:T(128)S(1)} %add_multiply_fusion.wave_ref) | copy-start | bytes 388
  3.4 0.7 %copy-start.2 = (f32[3,512]{1,0:T(4,128)S(1)}, f32[3,512]{1,0:T(4,128)}, u32[]{:S(2)}) copy-start(f32[3,512]{1,0:T(4,128)} %param.10) | copy-start | bytes 18436
  3.4 0.7 %copy-start.4 = (f32[3,64]{1,0:T(4,128)S(1)}, f32[3,64]{1,0:T(4,128)}, u32[]{:S(2)}) copy-start(f32[3,64]{1,0:T(4,128)} %param.11) | copy-start | bytes 2308
  4.6 6.7 %collective-permute-start.1 = (f32[4,32,256]{2,1,0:T(8,128)S(1)}, f32[4,32,256]{2,1,0:T(8,128)S(1)}, u32[]{:S(2)}, u32[]{:S(2)}) collective-permute-start(f32[4,32,256]{2,1,0:T(8,128)S(1)} %dynamic-slice_bitcast_fusion.1), channel_id=1, source_target_pairs={{0,4},{2,6},{4,0},{6,2},{8,12},{10,14},{12,8},{14,10},{16,20},{18,... | collective-permute-start | bytes 393224 | tf_op jit(solution)/shard_map/ppermute | solution.py:136
  11.3 4.3 %collective-permute-start.2 = (f32[2,32,256]{2,1,0:T(8,128)S(1)}, f32[2,32,256]{2,1,0:T(8,128)S(1)}, u32[]{:S(2)}, u32[]{:S(2)}) collective-permute-start(f32[2,32,256]{2,1,0:T(8,128)S(1)} %dynamic-slice_bitcast_fusion.2), channel_id=1, source_target_pairs={{0,8},{2,10},{4,12},{6,14},{8,0},{10,2},{12,4},{14,6},{16,24},{18,... | collective-permute-start | bytes 196616 | tf_op jit(solution)/shard_map/ppermute | solution.py:136
  15.7 4.9 %collective-permute-start.3 = (f32[1,32,256]{2,1,0:T(8,128)S(1)}, f32[1,32,256]{2,1,0:T(8,128)S(1)}, u32[]{:S(2)}, u32[]{:S(2)}) collective-permute-start(f32[1,32,256]{2,1,0:T(8,128)S(1)} %constant_dynamic-slice_fusion), channel_id=1, source_target_pairs={{0,16},{2,18},{4,20},{6,22},{8,24},{10,26},{12,28},{14,30},{16,0},... | collective-permute-start | bytes 98312 | tf_op jit(solution)/shard_map/ppermute | solution.py:136
  20.6 4.9 %collective-permute-start.4 = (f32[1,32,256]{2,1,0:T(8,128)S(1)}, f32[1,32,256]{2,1,0:T(8,128)S(1)}, u32[]{:S(2)}, u32[]{:S(2)}) collective-permute-start(f32[1,32,256]{2,1,0:T(8,128)S(1)} %dynamic-slice_add_fusion), channel_id=1, source_target_pairs={{0,16},{2,18},{4,20},{6,22},{8,24},{10,26},{12,28},{14,30},{16,0},... | collective-permute-start | bytes 98312 | tf_op jit(solution)/shard_map/ppermute | solution.py:145
  25.5 4.5 %collective-permute-start.5 = (f32[2,32,256]{2,1,0:T(8,128)S(1)}, f32[2,32,256]{2,1,0:T(8,128)S(1)}, u32[]{:S(2)}, u32[]{:S(2)}) collective-permute-start(f32[2,32,256]{2,1,0:T(8,128)S(1)} %maximum_bitcast_fusion), channel_id=1, source_target_pairs={{0,8},{2,10},{4,12},{6,14},{8,0},{10,2},{12,4},{14,6},{16,24},{18,... | collective-permute-start | bytes 196616 | tf_op jit(solution)/shard_map/ppermute | solution.py:145
  30.1 5.0 %collective-permute-start.6 = (f32[4,32,256]{2,1,0:T(8,128)S(1)}, f32[4,32,256]{2,1,0:T(8,128)S(1)}, u32[]{:S(2)}, u32[]{:S(2)}) collective-permute-start(f32[4,32,256]{2,1,0:T(8,128)S(1)} %bitcast.53), channel_id=1, source_target_pairs={{0,4},{2,6},{4,0},{6,2},{8,12},{10,14},{12,8},{14,10},{16,20},{18,... | collective-permute-start | bytes 393224 | tf_op jit(solution)/shard_map/ppermute | solution.py:145
  35.2 1.6 %collective-permute-start.7 = (f32[8,32,256]{2,1,0:T(8,128)S(1)}, f32[8,32,256]{2,1,0:T(8,128)S(1)}, u32[]{:S(2)}, u32[]{:S(2)}) collective-permute-start(f32[8,32,256]{2,1,0:T(8,128)S(1)} %bitcast.50), channel_id=1, source_target_pairs={{0,2},{2,0},{4,6},{6,4},{8,10},{10,8},{12,14},{14,12},{16,18},{18,... | collective-permute-start | bytes 786440 | tf_op jit(solution)/shard_map/ppermute | solution.py:145
  35.3 1.5 %copy-start = (f32[8,64,512]{2,1,0:T(8,128)}, f32[8,64,512]{2,1,0:T(8,128)S(1)}, u32[]{:S(2)}) copy-start(f32[8,64,512]{2,1,0:T(8,128)S(1)} %sqrt_dynamic-update-slice_fusion.geo_ref) | copy-start | bytes 3145732
  48.7 4.2 %copy-start.1 = (f32[32,2,64]{2,1,0:T(2,128)}, f32[32,2,64]{2,1,0:T(2,128)S(1)}, u32[]{:S(2)}) copy-start(f32[32,2,64]{2,1,0:T(2,128)S(1)} %mul.137) | copy-start | bytes 49156
  48.8 3.6 %collective-permute-start.8 = (f32[64]{0:T(128)S(1)}, f32[64]{0:T(128)S(1)}, u32[]{:S(2)}, u32[]{:S(2)}) collective-permute-start(f32[64]{0:T(128)S(1)} %fusion.14), channel_id=1, source_target_pairs={{0,1},{1,0},{2,3},{3,2},{4,5},{5,4},{6,7},{7,6},{8,9},{9,8},{10,11... | collective-permute-start | bytes 776 | tf_op jit(solution)/shard_map/ppermute | solution.py:183

commit v7 on v6

--- a/solution.py
+++ b/solution.py
@@ -12,7 +12,9 @@
 reference_radius = 10.0
 
 
-def field_kernel(block_group, freq_unroll, wave_ref, geo_ref, src_ref, out_ref, acc_ref, chan_ref, spread_ref):
+def field_kernel(
+    block_group, freq_unroll, scale, low_chunks, wave_ref, geo_ref, low_ref, high_ref, out_ref, acc_ref, chan_ref, spread_ref
+):
     freqs, _, observers, lanes = acc_ref.shape
     blocks = observers // 8
 
@@ -20,7 +22,15 @@
     def _():
         acc_ref[...] = jnp.zeros(acc_ref.shape, acc_ref.dtype)
 
-    chan_ref[...] = jnp.transpose(src_ref[...])
+    chunk = pl.program_id(0)
+
+    @pl.when(chunk < low_chunks)
+    def _():
+        chan_ref[...] = jnp.transpose(low_ref[...])
+
+    @pl.when(chunk >= low_chunks)
+    def _():
+        chan_ref[...] = jnp.transpose(high_ref[...])
 
     def spread_body(row, carry):
         spread_ref[row] = jnp.broadcast_to(chan_ref[pl.ds(row, 1), :], (8, lanes))
@@ -70,19 +80,22 @@
     @pl.when(pl.program_id(0) == pl.num_programs(0) - 1)
     def _():
         flat = acc_ref[...].reshape(freqs * 2 * observers, lanes)
-        out_ref[...] = lax.dot_general(
+        summed = lax.dot_general(
             jnp.ones((8, lanes), jnp.float32),
             flat,
             (((1,), (1,)), ((), ())),
             precision=lax.Precision.HIGHEST,
             preferred_element_type=jnp.float32,
         )
-
-
-def far_field(portion, panel_position, observer_position, wave_numbers):
-    panel_total, columns = portion.shape
+        out_ref[...] = summed[0:1, :] * scale
+
+
+def far_field(low, high, panel_position, observer_position, wave_numbers, scale):
+    columns = low.shape[1]
     freqs = columns // 8
     observers = observer_position.shape[1]
+    low_chunks = low.shape[0] // 128
+    high_chunks = high.shape[0] // 128
     offsets = observer_position[:, :, None] - panel_position[:, None, :]
     distance = jnp.sqrt(offsets[0] * offsets[0] + offsets[1] * offsets[1] + offsets[2] * offsets[2])
     inverse = 1.0 / distance
@@ -100,24 +113,26 @@
             distance,
         ]
     )
+    kernel = functools.partial(field_kernel, math.gcd(observers // 8, 4), 2, scale, low_chunks)
     summed = pl.pallas_call(
-        functools.partial(field_kernel, math.gcd(observers // 8, 4), 2),
-        grid=(panel_total // 128,),
+        kernel,
+        grid=(low_chunks + high_chunks,),
         in_specs=[
             pl.BlockSpec(memory_space=pltpu.SMEM),
             pl.BlockSpec((8, observers, 128), lambda chunk: (0, 0, chunk)),
-            pl.BlockSpec((128, columns), lambda chunk: (chunk, 0)),
+            pl.BlockSpec((128, columns), lambda chunk: (jnp.minimum(chunk, low_chunks - 1), 0)),
+            pl.BlockSpec((128, columns), lambda chunk: (jnp.maximum(chunk - low_chunks, 0), 0)),
         ],
-        out_specs=pl.BlockSpec((8, freqs * 2 * observers), lambda chunk: (0, 0)),
-        out_shape=jax.ShapeDtypeStruct((8, freqs * 2 * observers), jnp.float32),
+        out_specs=pl.BlockSpec((1, freqs * 2 * observers), lambda chunk: (0, 0)),
+        out_shape=jax.ShapeDtypeStruct((1, freqs * 2 * observers), jnp.float32),
         scratch_shapes=[
             pltpu.VMEM((freqs, 2, observers, 128), jnp.float32),
             pltpu.VMEM((columns, 128), jnp.float32),
             pltpu.VMEM((columns, 8, 128), jnp.float32),
         ],
         compiler_params=pltpu.CompilerParams(dimension_semantics=("arbitrary",)),
-    )(wave_numbers, geometry, portion)
-    return summed[0].reshape(freqs, 2, observers)
+    )(wave_numbers, geometry, low, high)
+    return summed.reshape(freqs, 2, observers)
 
 
 def partner_pairs(groups, bit):
@@ -145,8 +160,9 @@
         other = lax.ppermute(gathered, "obs", partner_pairs(groups, bit))
         low = jnp.where(mine == 0, gathered, other)
         high = jnp.where(mine == 0, other, gathered)
+        if bit == 1:
+            return low, high
         gathered = jnp.stack([low, high], axis=1).reshape((-1,) + gathered.shape[1:])
-    return gathered
 
 
 def shards(cell_spectra, cell_weight, cell_owner, cell_local, panel_position, observer_position):
@@ -167,17 +183,29 @@
         (group_first + jnp.arange(freqs_dev, dtype=jnp.int32)).astype(jnp.float32) + 1.0
     )
     blocks = local_source.reshape(groups, panels_dev, columns)
-    if groups & (groups - 1) == 0:
+    scale = reference_radius / math.sqrt(panel_total)
+    if groups & (groups - 1) == 0 and groups >= 8:
         bits = [1 << k for k in range(groups.bit_length() - 1)]
         own_source = halving_sum(blocks, bits)
-        portion = doubling_gather(own_source, bits, groups).reshape(panel_total, columns)
+        even, odd = doubling_gather(own_source, bits, groups)
+        order = jnp.transpose(panel_position.reshape(3, groups // 2, 2, panels_dev), (0, 2, 1, 3))
+        pressure = far_field(
+            even.reshape(-1, columns),
+            odd.reshape(-1, columns),
+            order.reshape(3, panel_total),
+            observer_position,
+            wave_numbers,
+            scale,
+        )
     else:
         own_source = jnp.sum(lax.all_to_all(blocks, "obs", 0, 0, tiled=True), axis=0)
         portion = lax.all_to_all(
             jnp.broadcast_to(own_source[None], blocks.shape), "obs", 0, 0, tiled=True
         ).reshape(panel_total, columns)
-    summed = far_field(portion, panel_position, observer_position, wave_numbers)
-    pressure = summed * (reference_radius / math.sqrt(panel_total))
+        half = panel_total // 256 * 128
+        pressure = far_field(
+            portion[:half], portion[half:], panel_position, observer_position, wave_numbers, scale
+        )
     energy = jnp.sum(pressure[:, 0] * pressure[:, 0] + pressure[:, 1] * pressure[:, 1], axis=0)
     if lax.axis_size("freq") == 2:
         band_total = energy + lax.ppermute(energy, "freq", [(0, 1), (1, 0)])

time: 53.2 us -> 54.6 us (1.026)
  other arithmetic: 3.91 us -> 5.17 us
    pallas_call x0 -> x1, other arithmetic: none -> 1.4 us  [far_field(): pl.pallas_call(kernel, grid=(low_chunks + high_chunks,), in_specs=[pl.Blo...]
    mul x1 -> x0, other arithmetic: 0.95 us -> none  [shards(): pressure = summed * (reference_radius / math.sqrt(panel_total))]
    select_n x0 -> x1, other arithmetic: none -> 0.89 us  [doubling_gather(): high = jnp.where(mine == 0, other, gathered)]
    another operation x2 -> x1, local copies, waits for them, and re-layouts: 0.88 us -> 0.02 us  [doubling_gather(): jnp.stack([low, high], axis=1).reshape((-1,) + gathered.shape[1:])]
    unnamed x16, local copies, waits for them, and re-layouts: 1.38 us -> 2.06 us
  transfers between devices with their start and end apart: 9 -> 9, of which waited for: 9 -> 8; matrix products, arithmetic and copies ran while one was open for 4% -> 4% of each run, Pallas kernels for 0% -> 0%
where the time goes in v7:
time: 54.6 us; the launch traced here: 54.3 us
  waiting for transfers between devices  17.3 us (32%)
  starting transfers between devices  16.4 us (30%)
  Pallas kernels  10 us (18%)
  other arithmetic  5.17 us (9%)
  local copies, waits for them, and re-layouts  2.96 us (5%)
  matrix products  1.42 us (3%)
  between operations  0.99 us (2%)
    pallas_call x1, Pallas kernels, far_field(): pl.pallas_call(kernel, grid=(low_chunks + high_chunks,), in_specs=[pl.Blo...  10 us
    ppermute x4, waiting for transfers between devices, doubling_gather(): other = lax.ppermute(gathered, 'obs', partner_pairs(groups, bit))  8.64 us
    ppermute x4, starting transfers between devices, halving_sum(): current = keep + lax.ppermute(send, 'obs', partner_pairs(groups, bit))  7.98 us
    ppermute x4, waiting for transfers between devices, halving_sum(): current = keep + lax.ppermute(send, 'obs', partner_pairs(groups, bit))  6.9 us
    ppermute x4, starting transfers between devices, doubling_gather(): other = lax.ppermute(gathered, 'obs', partner_pairs(groups, bit))  6.6 us
    unnamed x16, local copies, waits for them, and re-layouts  2.06 us
    unnamed x7, other arithmetic  2.05 us
    ppermute x1, starting transfers between devices, shards(): band_total = energy + lax.ppermute(energy, 'freq', [(0, 1), (1, 0)])  1.84 us
  transfers between devices with their start and end apart: 9, of which 8 were waited for; matrix products, arithmetic and copies ran while one was open for 4% of the time, Pallas kernels for 0%

profile of v7, /device:TPU:0, one launch (start us, length us, event | category | flops | bytes accessed | tf_op | source)
XLA Modules:
  0.0 54.3 jit_solution(14312854848807897503)
XLA Ops:
  0.7 0.0 copy-start.7
  0.7 0.0 copy-start.6
  0.7 0.0 copy-start.5
  0.7 0.6 %copy-done.7 = f32[512]{0:T(512)S(1)} copy-done((f32[512]{0:T(512)S(1)}, f32[512]{0:T(512)}, u32[]{:S(2)}) %copy-start.7) | copy-done | bytes 2072
  1.3 0.0 copy-done.6
  1.4 0.0 copy-done.5
  1.4 1.4 %fusion = f32[512,256]{1,0:T(8,128)S(1)} fusion(s32[512]{0:T(512)S(1)} %copy-done.5, s32[512]{0:T(512)S(1)} %bitcast.62, s32[512]{0:T(512)S(1)} %get-tuple-element.12, s32[512]{0:T(512)S(1)} %get-tuple-element.13, bf16[512,256]{1,0:T(8,128)(2,1)} %param.6, f32[512]{0:T(512)S(1)} %copy-done.7), kind=kOutput, calls=%fused_computation | convolution fusion | flops 135397376 | bytes 796672 | tf_op jit(solution)/shard_map/dot_general | solution.py:180
  2.8 0.5 collective-permute-start
  3.4 0.0 copy-start.2
  3.4 0.7 %copy-done.2 = f32[3,512]{1,0:T(4,128)S(1)} copy-done((f32[3,512]{1,0:T(4,128)S(1)}, f32[3,512]{1,0:T(4,128)}, u32[]{:S(2)}) %copy-start.2) | copy-done | bytes 6168
  4.1 0.1 reshape.96
  4.2 0.1 sub.49
  4.3 0.0 copy-start.4
  4.3 0.7 %copy-done.4 = f32[3,64]{1,0:T(4,128)S(1)} copy-done((f32[3,64]{1,0:T(4,128)S(1)}, f32[3,64]{1,0:T(4,128)}, u32[]{:S(2)}) %copy-start.4) | copy-done | bytes 792
  4.9 0.1 broadcast_subtract_fusion
  5.0 0.0 collective-permute-done
  5.1 2.6 %collective-permute-start.1 = (f32[4,32,256]{2,1,0:T(8,128)S(1)}, f32[4,32,256]{2,1,0:T(8,128)S(1)}, u32[]{:S(2)}, u32[]{:S(2)}) collective-permute-start(f32[4,32,256]{2,1,0:T(8,128)S(1)} %dynamic-slice_bitcast_fusion.1), channel_id=1, source_target_pairs={{0,4},{2,6},{4,0},{6,2},{8,12},{10,14},{12,8},{14,10},{16,20},{18,... | collective-permute-start | bytes 393224 | tf_op jit(solution)/shard_map/ppermute | solution.py:151
  7.8 0.5 multiply_dynamic-update-slice_fusion.1
  8.3 3.5 %collective-permute-done.1 = f32[4,32,256]{2,1,0:T(8,128)S(1)} collective-permute-done((f32[4,32,256]{2,1,0:T(8,128)S(1)}, f32[4,32,256]{2,1,0:T(8,128)S(1)}, u32[]{:S(2)}, u32[]{:S(2)}) %collective-permute-start.1) | collective-permute-done | bytes 131104 | tf_op jit(solution)/shard_map/ppermute | solution.py:151
  11.9 1.9 %collective-permute-start.2 = (f32[2,32,256]{2,1,0:T(8,128)S(1)}, f32[2,32,256]{2,1,0:T(8,128)S(1)}, u32[]{:S(2)}, u32[]{:S(2)}) collective-permute-start(f32[2,32,256]{2,1,0:T(8,128)S(1)} %dynamic-slice_bitcast_fusion.2), channel_id=1, source_target_pairs={{0,8},{2,10},{4,12},{6,14},{8,0},{10,2},{12,4},{14,6},{16,24},{18,... | collective-permute-start | bytes 196616 | tf_op jit(solution)/shard_map/ppermute | solution.py:151
  13.8 0.0 copy-done.3
  13.8 0.5 multiply_dynamic-update-slice_fusion
  14.4 1.9 %collective-permute-done.2 = f32[2,32,256]{2,1,0:T(8,128)S(1)} collective-permute-done((f32[2,32,256]{2,1,0:T(8,128)S(1)}, f32[2,32,256]{2,1,0:T(8,128)S(1)}, u32[]{:S(2)}, u32[]{:S(2)}) %collective-permute-start.2) | collective-permute-done | bytes 65568 | tf_op jit(solution)/shard_map/ppermute | solution.py:151
  16.2 2.9 %collective-permute-start.3 = (f32[1,32,256]{2,1,0:T(8,128)S(1)}, f32[1,32,256]{2,1,0:T(8,128)S(1)}, u32[]{:S(2)}, u32[]{:S(2)}) collective-permute-start(f32[1,32,256]{2,1,0:T(8,128)S(1)} %constant_dynamic-slice_fusion), channel_id=1, source_target_pairs={{0,16},{2,18},{4,20},{6,22},{8,24},{10,26},{12,28},{14,30},{16,0},... | collective-permute-start | bytes 98312 | tf_op jit(solution)/shard_map/ppermute | solution.py:151
  19.2 0.5 cosine_dynamic-update-slice_fusion
  19.6 1.5 %collective-permute-done.3 = f32[1,32,256]{2,1,0:T(8,128)S(1)} collective-permute-done((f32[1,32,256]{2,1,0:T(8,128)S(1)}, f32[1,32,256]{2,1,0:T(8,128)S(1)}, u32[]{:S(2)}, u32[]{:S(2)}) %collective-permute-start.3) | collective-permute-done | bytes 32800 | tf_op jit(solution)/shard_map/ppermute | solution.py:151
  21.1 2.9 %collective-permute-start.4 = (f32[1,32,256]{2,1,0:T(8,128)S(1)}, f32[1,32,256]{2,1,0:T(8,128)S(1)}, u32[]{:S(2)}, u32[]{:S(2)}) collective-permute-start(f32[1,32,256]{2,1,0:T(8,128)S(1)} %dynamic-slice_add_fusion), channel_id=1, source_target_pairs={{0,16},{2,18},{4,20},{6,22},{8,24},{10,26},{12,28},{14,30},{16,0},... | collective-permute-start | bytes 98312 | tf_op jit(solution)/shard_map/ppermute | solution.py:160
  24.0 0.5 sine_dynamic-update-slice_fusion
  24.5 1.6 %collective-permute-done.4 = f32[1,32,256]{2,1,0:T(8,128)S(1)} collective-permute-done((f32[1,32,256]{2,1,0:T(8,128)S(1)}, f32[1,32,256]{2,1,0:T(8,128)S(1)}, u32[]{:S(2)}, u32[]{:S(2)}) %collective-permute-start.4) | collective-permute-done | bytes 32800 | tf_op jit(solution)/shard_map/ppermute | solution.py:160
  26.1 1.8 %collective-permute-start.5 = (f32[2,32,256]{2,1,0:T(8,128)S(1)}, f32[2,32,256]{2,1,0:T(8,128)S(1)}, u32[]{:S(2)}, u32[]{:S(2)}) collective-permute-start(f32[2,32,256]{2,1,0:T(8,128)S(1)} %maximum_bitcast_fusion), channel_id=1, source_target_pairs={{0,8},{2,10},{4,12},{6,14},{8,0},{10,2},{12,4},{14,6},{16,24},{18,... | collective-permute-start | bytes 196616 | tf_op jit(solution)/shard_map/ppermute | solution.py:160
  28.0 2.5 %collective-permute-done.5 = f32[2,32,256]{2,1,0:T(8,128)S(1)} collective-permute-done((f32[2,32,256]{2,1,0:T(8,128)S(1)}, f32[2,32,256]{2,1,0:T(8,128)S(1)}, u32[]{:S(2)}, u32[]{:S(2)}) %collective-permute-start.5) | collective-permute-done | bytes 65568 | tf_op jit(solution)/shard_map/ppermute | solution.py:160
  30.4 1.8 %collective-permute-start.6 = (f32[4,32,256]{2,1,0:T(8,128)S(1)}, f32[4,32,256]{2,1,0:T(8,128)S(1)}, u32[]{:S(2)}, u32[]{:S(2)}) collective-permute-start(f32[4,32,256]{2,1,0:T(8,128)S(1)} %bitcast.54), channel_id=1, source_target_pairs={{0,4},{2,6},{4,0},{6,2},{8,12},{10,14},{12,8},{14,10},{16,20},{18,... | collective-permute-start | bytes 393224 | tf_op jit(solution)/shard_map/ppermute | solution.py:160
  32.3 3.2 %collective-permute-done.6 = f32[4,32,256]{2,1,0:T(8,128)S(1)} collective-permute-done((f32[4,32,256]{2,1,0:T(8,128)S(1)}, f32[4,32,256]{2,1,0:T(8,128)S(1)}, u32[]{:S(2)}, u32[]{:S(2)}) %collective-permute-start.6) | collective-permute-done | bytes 131104 | tf_op jit(solution)/shard_map/ppermute | solution.py:160
  35.6 0.1 collective-permute-start.7
  35.7 0.0 copy-start
  35.7 1.4 %collective-permute-done.7 = f32[8,32,256]{2,1,0:T(8,128)S(1)} collective-permute-done((f32[8,32,256]{2,1,0:T(8,128)S(1)}, f32[8,32,256]{2,1,0:T(8,128)S(1)}, u32[]{:S(2)}, u32[]{:S(2)}) %collective-permute-start.7) | collective-permute-done | bytes 262176 | tf_op jit(solution)/shard_map/ppermute | solution.py:160
  37.2 0.9 %broadcast_select_fusion = (f32[8,32,256]{2,1,0:T(8,128)}, f32[8,32,256]{2,1,0:T(8,128)}) fusion(f32[8,32,256]{2,1,0:T(8,128)S(1)} %collective-permute-done.7, pred[]{:T(512)S(6)} %eq.55, f32[4,2,32,256]{3,2,1,0:T(8,128)S(1)} %copy.17), kind=kLoop, calls=%fused_computation.30 | loop fusion | flops 131072 | bytes 1048577 | tf_op jit(solution)/shard_map/jit(_where)/select_n | solution.py:162
  38.0 0.0 copy-done
  38.1 10.0 %shard_map.77 = f32[1,4096]{1,0:T(1,128)} custom-call(f32[32]{0:T(128)} %copy-done.3, f32[8,64,512]{2,1,0:T(8,128)} %copy-done, f32[256,256]{1,0:T(8,128)} %bitcast.53, f32[256,256]{1,0:T(8,128)} %bitcast.52), custom_call_target="tpu_custom_call" | custom-call | tf_op jit(solution)/shard_map/pallas_call | solution.py:117
  48.1 0.5 broadcast.89
  48.6 1.4 %reduce.4 = f32[4096]{0:T(1024)S(1)} reduce(f32[1,4096]{1,0:T(1,128)} %shard_map.77, f32[]{:T(128)} %broadcast.89), dimensions={0}, to_apply=%pallas_call.3.reduce_sub_computation.3 | reduce | bytes 32772 | tf_op jit(solution)/shard_map/pallas_call | solution.py:117
  50.0 0.1 reshape.104
  50.1 0.0 copy-start.1
  50.1 0.1 fusion.13
  50.2 1.8 %collective-permute-start.8 = (f32[64]{0:T(128)S(1)}, f32[64]{0:T(128)S(1)}, u32[]{:S(2)}, u32[]{:S(2)}) collective-permute-start(f32[64]{0:T(128)S(1)} %fusion.13), channel_id=1, source_target_pairs={{0,1},{1,0},{2,3},{3,2},{4,5},{5,4},{6,7},{7,6},{8,9},{9,8},{10,11... | collective-permute-start | bytes 776 | tf_op jit(solution)/shard_map/ppermute | solution.py:211
  52.0 1.8 %collective-permute-done.8 = f32[64]{0:T(128)S(1)} collective-permute-done((f32[64]{0:T(128)S(1)}, f32[64]{0:T(128)S(1)}, u32[]{:S(2)}, u32[]{:S(2)}) %collective-permute-start.8) | collective-permute-done | bytes 288 | tf_op jit(solution)/shard_map/ppermute | solution.py:211
  53.8 0.5 add_log_fusion
  54.3 0.0 copy-done.1
  (23 shorter events, 0.4 us)
Async XLA Ops:
  0.7 0.7 %copy-start.7 = (f32[512]{0:T(512)S(1)}, f32[512]{0:T(512)}, u32[]{:S(2)}) copy-start(f32[512]{0:T(512)} %param.7) | copy-start | bytes 6148
  0.7 0.7 %copy-start.6 = (s32[512,1]{0,1:T(1,128)S(1)}, s32[512,1]{0,1:T(1,128)}, u32[]{:S(2)}) copy-start(s32[512,1]{0,1:T(1,128)} %param.8) | copy-start | bytes 6148
  0.7 0.7 %copy-start.5 = (s32[512]{0:T(512)S(1)}, s32[512]{0:T(512)}, u32[]{:S(2)}) copy-start(s32[512]{0:T(512)} %param.9) | copy-start | bytes 6148
  2.8 2.2 %collective-permute-start = (f32[8,32,256]{2,1,0:T(8,128)S(1)}, f32[8,32,256]{2,1,0:T(8,128)S(1)}, u32[]{:S(2)}, u32[]{:S(2)}) collective-permute-start(f32[8,32,256]{2,1,0:T(8,128)S(1)} %dynamic-slice_bitcast_fusion), channel_id=1, source_target_pairs={{0,2},{2,0},{4,6},{6,4},{8,10},{10,8},{12,14},{14,12},{16,18},{18,... | collective-permute-start | bytes 786440 | tf_op jit(solution)/shard_map/ppermute | solution.py:151
  3.4 10.4 %copy-start.3 = (f32[32]{0:T(128)}, f32[32]{0:T(128)S(1)}, u32[]{:S(2)}) copy-start(f32[32]{0:T(128)S(1)} %add_multiply_fusion.wave_ref) | copy-start | bytes 388
  3.4 0.7 %copy-start.2 = (f32[3,512]{1,0:T(4,128)S(1)}, f32[3,512]{1,0:T(4,128)}, u32[]{:S(2)}) copy-start(f32[3,512]{1,0:T(4,128)} %param.10) | copy-start | bytes 18436
  4.3 0.7 %copy-start.4 = (f32[3,64]{1,0:T(4,128)S(1)}, f32[3,64]{1,0:T(4,128)}, u32[]{:S(2)}) copy-start(f32[3,64]{1,0:T(4,128)} %param.11) | copy-start | bytes 2308
  5.1 6.7 %collective-permute-start.1 = (f32[4,32,256]{2,1,0:T(8,128)S(1)}, f32[4,32,256]{2,1,0:T(8,128)S(1)}, u32[]{:S(2)}, u32[]{:S(2)}) collective-permute-start(f32[4,32,256]{2,1,0:T(8,128)S(1)} %dynamic-slice_bitcast_fusion.1), channel_id=1, source_target_pairs={{0,4},{2,6},{4,0},{6,2},{8,12},{10,14},{12,8},{14,10},{16,20},{18,... | collective-permute-start | bytes 393224 | tf_op jit(solution)/shard_map/ppermute | solution.py:151
  11.9 4.3 %collective-permute-start.2 = (f32[2,32,256]{2,1,0:T(8,128)S(1)}, f32[2,32,256]{2,1,0:T(8,128)S(1)}, u32[]{:S(2)}, u32[]{:S(2)}) collective-permute-start(f32[2,32,256]{2,1,0:T(8,128)S(1)} %dynamic-slice_bitcast_fusion.2), channel_id=1, source_target_pairs={{0,8},{2,10},{4,12},{6,14},{8,0},{10,2},{12,4},{14,6},{16,24},{18,... | collective-permute-start | bytes 196616 | tf_op jit(solution)/shard_map/ppermute | solution.py:151
  16.2 4.9 %collective-permute-start.3 = (f32[1,32,256]{2,1,0:T(8,128)S(1)}, f32[1,32,256]{2,1,0:T(8,128)S(1)}, u32[]{:S(2)}, u32[]{:S(2)}) collective-permute-start(f32[1,32,256]{2,1,0:T(8,128)S(1)} %constant_dynamic-slice_fusion), channel_id=1, source_target_pairs={{0,16},{2,18},{4,20},{6,22},{8,24},{10,26},{12,28},{14,30},{16,0},... | collective-permute-start | bytes 98312 | tf_op jit(solution)/shard_map/ppermute | solution.py:151
  21.1 4.9 %collective-permute-start.4 = (f32[1,32,256]{2,1,0:T(8,128)S(1)}, f32[1,32,256]{2,1,0:T(8,128)S(1)}, u32[]{:S(2)}, u32[]{:S(2)}) collective-permute-start(f32[1,32,256]{2,1,0:T(8,128)S(1)} %dynamic-slice_add_fusion), channel_id=1, source_target_pairs={{0,16},{2,18},{4,20},{6,22},{8,24},{10,26},{12,28},{14,30},{16,0},... | collective-permute-start | bytes 98312 | tf_op jit(solution)/shard_map/ppermute | solution.py:160
  26.1 4.3 %collective-permute-start.5 = (f32[2,32,256]{2,1,0:T(8,128)S(1)}, f32[2,32,256]{2,1,0:T(8,128)S(1)}, u32[]{:S(2)}, u32[]{:S(2)}) collective-permute-start(f32[2,32,256]{2,1,0:T(8,128)S(1)} %maximum_bitcast_fusion), channel_id=1, source_target_pairs={{0,8},{2,10},{4,12},{6,14},{8,0},{10,2},{12,4},{14,6},{16,24},{18,... | collective-permute-start | bytes 196616 | tf_op jit(solution)/shard_map/ppermute | solution.py:160
  30.4 5.0 %collective-permute-start.6 = (f32[4,32,256]{2,1,0:T(8,128)S(1)}, f32[4,32,256]{2,1,0:T(8,128)S(1)}, u32[]{:S(2)}, u32[]{:S(2)}) collective-permute-start(f32[4,32,256]{2,1,0:T(8,128)S(1)} %bitcast.54), channel_id=1, source_target_pairs={{0,4},{2,6},{4,0},{6,2},{8,12},{10,14},{12,8},{14,10},{16,20},{18,... | collective-permute-start | bytes 393224 | tf_op jit(solution)/shard_map/ppermute | solution.py:160
  35.6 1.6 %collective-permute-start.7 = (f32[8,32,256]{2,1,0:T(8,128)S(1)}, f32[8,32,256]{2,1,0:T(8,128)S(1)}, u32[]{:S(2)}, u32[]{:S(2)}) collective-permute-start(f32[8,32,256]{2,1,0:T(8,128)S(1)} %bitcast.49), channel_id=1, source_target_pairs={{0,2},{2,0},{4,6},{6,4},{8,10},{10,8},{12,14},{14,12},{16,18},{18,... | collective-permute-start | bytes 786440 | tf_op jit(solution)/shard_map/ppermute | solution.py:160
  35.7 2.3 %copy-start = (f32[8,64,512]{2,1,0:T(8,128)}, f32[8,64,512]{2,1,0:T(8,128)S(1)}, u32[]{:S(2)}) copy-start(f32[8,64,512]{2,1,0:T(8,128)S(1)} %sqrt_dynamic-update-slice_fusion.geo_ref) | copy-start | bytes 3145732
  50.1 4.2 %copy-start.1 = (f32[32,2,64]{2,1,0:T(2,128)}, f32[32,2,64]{2,1,0:T(2,128)S(1)}, u32[]{:S(2)}) copy-start(f32[32,2,64]{2,1,0:T(2,128)S(1)} %reshape.104) | copy-start | bytes 49156
  50.2 3.6 %collective-permute-start.8 = (f32[64]{0:T(128)S(1)}, f32[64]{0:T(128)S(1)}, u32[]{:S(2)}, u32[]{:S(2)}) collective-permute-start(f32[64]{0:T(128)S(1)} %fusion.13), channel_id=1, source_target_pairs={{0,1},{1,0},{2,3},{3,2},{4,5},{5,4},{6,7},{7,6},{8,9},{9,8},{10,11... | collective-permute-start | bytes 776 | tf_op jit(solution)/shard_map/ppermute | solution.py:211

commit v8 on v6

--- a/solution.py
+++ b/solution.py
@@ -124,6 +124,11 @@
     return [(k, k ^ bit) for k in range(groups)]
 
 
+def quad_pairs(groups, shift):
+    low = groups // 4
+    return [(k, ((k // low + shift) % 4) * low + k % low) for k in range(groups)]
+
+
 def halving_sum(blocks, bits):
     groups = blocks.shape[0]
     place = lax.axis_index("obs")
@@ -134,12 +139,23 @@
         keep = lax.dynamic_index_in_dim(split, mine, 1, keepdims=False)
         send = lax.dynamic_index_in_dim(split, 1 - mine, 1, keepdims=False)
         current = keep + lax.ppermute(send, "obs", partner_pairs(groups, bit))
-    return current
+    quarter = place // (groups // 4)
+    total = lax.dynamic_index_in_dim(current, quarter, 0, keepdims=False)
+    for shift in (1, 2, 3):
+        piece = lax.dynamic_index_in_dim(current, (quarter + shift) % 4, 0, keepdims=False)
+        total = total + lax.ppermute(piece, "obs", quad_pairs(groups, shift))
+    return total
 
 
 def doubling_gather(own, bits, groups):
     place = lax.axis_index("obs")
-    gathered = own
+    quarter = place // (groups // 4)
+    arrived = jnp.stack(
+        [own] + [lax.ppermute(own, "obs", quad_pairs(groups, shift)) for shift in (1, 2, 3)]
+    )
+    gathered = jnp.stack(
+        [lax.dynamic_index_in_dim(arrived, (quarter - k) % 4, 0, keepdims=False) for k in range(4)]
+    )
     for bit in reversed(bits):
         mine = (place // bit) % 2
         other = lax.ppermute(gathered, "obs", partner_pairs(groups, bit))
@@ -167,8 +183,8 @@
         (group_first + jnp.arange(freqs_dev, dtype=jnp.int32)).astype(jnp.float32) + 1.0
     )
     blocks = local_source.reshape(groups, panels_dev, columns)
-    if groups & (groups - 1) == 0:
-        bits = [1 << k for k in range(groups.bit_length() - 1)]
+    if groups & (groups - 1) == 0 and groups >= 4:
+        bits = [1 << k for k in range(groups.bit_length() - 3)]
         own_source = halving_sum(blocks, bits)
         portion = doubling_gather(own_source, bits, groups).reshape(panel_total, columns)
     else:

time: 53.2 us -> 51.9 us (0.976)
  starting transfers between devices: 16.5 us -> 14.4 us
  local copies, waits for them, and re-layouts: 2.45 us -> 1.59 us
  other arithmetic: 3.91 us -> 4.74 us
  waiting for transfers between devices: 17.7 us -> 18.4 us
    ppermute x0 -> x6, starting transfers between devices: none -> 8.12 us  [the longest x3 4.91 us: halving_sum(): total = total + lax.ppermute(piece, 'obs', quad_pairs(groups, shift))]
    ppermute x0 -> x6, waiting for transfers between devices: none -> 7.87 us  [the longest x3 4.22 us: halving_sum(): total = total + lax.ppermute(piece, 'obs', quad_pairs(groups, shift))]
    ppermute x4 -> x2, starting transfers between devices: 8.23 us -> 3.09 us  [halving_sum(): current = keep + lax.ppermute(send, 'obs', partner_pairs(groups, bit))]
    ppermute x4 -> x2, starting transfers between devices: 6.71 us -> 1.63 us  [doubling_gather(): other = lax.ppermute(gathered, 'obs', partner_pairs(groups, bit))]
    ppermute x4 -> x2, waiting for transfers between devices: 8.67 us -> 4.87 us  [doubling_gather(): other = lax.ppermute(gathered, 'obs', partner_pairs(groups, bit))]
    ppermute x4 -> x2, waiting for transfers between devices: 6.99 us -> 3.69 us  [halving_sum(): current = keep + lax.ppermute(send, 'obs', partner_pairs(groups, bit))]
    another operation x2 -> x0, local copies, waits for them, and re-layouts: 0.88 us -> none  [doubling_gather(): jnp.stack([low, high], axis=1).reshape((-1,) + gathered.shape[1:])]
    another operation x7 -> x4, other arithmetic: 0.16 us -> 0.97 us  [doubling_gather(): jnp.stack([low, high], axis=1).reshape((-1,) + gathered.shape[1:])]
  transfers between devices with their start and end apart: 9 -> 11, of which waited for: 9 -> 10; matrix products, arithmetic and copies ran while one was open for 4% -> 4% of each run, Pallas kernels for 0% -> 0%
where the time goes in v8:
time: 51.9 us; the launch traced here: 51.6 us
  waiting for transfers between devices  18.4 us (35%)
  starting transfers between devices  14.4 us (28%)
  Pallas kernels  9.93 us (19%)
  other arithmetic  4.74 us (9%)
  local copies, waits for them, and re-layouts  1.59 us (3%)
  matrix products  1.42 us (3%)
  between operations  1.11 us (2%)
    pallas_call x1, Pallas kernels, far_field(): pl.pallas_call(functools.partial(field_kernel, math.gcd(observers // 8, 4...  9.93 us
    ppermute x3, starting transfers between devices, halving_sum(): total = total + lax.ppermute(piece, 'obs', quad_pairs(groups, shift))  4.91 us
    ppermute x2, waiting for transfers between devices, doubling_gather(): other = lax.ppermute(gathered, 'obs', partner_pairs(groups, bit))  4.87 us
    ppermute x3, waiting for transfers between devices, halving_sum(): total = total + lax.ppermute(piece, 'obs', quad_pairs(groups, shift))  4.22 us
    ppermute x2, waiting for transfers between devices, halving_sum(): current = keep + lax.ppermute(send, 'obs', partner_pairs(groups, bit))  3.69 us
    ppermute x3, waiting for transfers between devices, doubling_gather(): lax.ppermute(own, 'obs', quad_pairs(groups, shift))  3.65 us
    ppermute x3, starting transfers between devices, doubling_gather(): lax.ppermute(own, 'obs', quad_pairs(groups, shift))  3.2 us
    ppermute x2, starting transfers between devices, halving_sum(): current = keep + lax.ppermute(send, 'obs', partner_pairs(groups, bit))  3.09 us
  transfers between devices with their start and end apart: 11, of which 10 were waited for; matrix products, arithmetic and copies ran while one was open for 4% of the time, Pallas kernels for 0%

profile of v8, /device:TPU:0, one launch (start us, length us, event | category | flops | bytes accessed | tf_op | source)
XLA Modules:
  0.0 51.6 jit_solution(11954477657905453928)
XLA Ops:
  0.7 0.0 copy-start.7
  0.7 0.0 copy-start.6
  0.7 0.0 copy-start.5
  0.7 0.6 %copy-done.7 = f32[512]{0:T(512)S(1)} copy-done((f32[512]{0:T(512)S(1)}, f32[512]{0:T(512)}, u32[]{:S(2)}) %copy-start.7) | copy-done | bytes 2072
  1.3 0.0 copy-done.6
  1.4 0.0 copy-done.5
  1.4 1.4 %fusion = f32[512,256]{1,0:T(8,128)S(1)} fusion(s32[512]{0:T(512)S(1)} %copy-done.5, s32[512]{0:T(512)S(1)} %bitcast.57, s32[512]{0:T(512)S(1)} %get-tuple-element.15, s32[512]{0:T(512)S(1)} %get-tuple-element.16, bf16[512,256]{1,0:T(8,128)(2,1)} %param.6, f32[512]{0:T(512)S(1)} %copy-done.7), kind=kOutput, calls=%fused_computation | convolution fusion | flops 135397376 | bytes 796672 | tf_op jit(solution)/shard_map/dot_general | solution.py:180
  2.8 0.0 copy-start.2
  2.8 0.5 %collective-permute-start = (f32[8,32,256]{2,1,0:T(8,128)S(1)}, f32[8,32,256]{2,1,0:T(8,128)S(1)}, u32[]{:S(2)}, u32[]{:S(2)}) collective-permute-start(f32[8,32,256]{2,1,0:T(8,128)S(1)} %dynamic-slice_bitcast_fusion), channel_id=1, source_target_pairs={{0,2},{2,0},{4,6},{6,4},{8,10},{10,8},{12,14},{14,12},{16,18},{18,... | collective-permute-start | bytes 786440 | tf_op jit(solution)/shard_map/ppermute | solution.py:141
  3.4 0.1 copy-done.2
  3.5 0.5 %copy-done.4 = f32[3,64]{1,0:T(4,128)S(1)} copy-done((f32[3,64]{1,0:T(4,128)S(1)}, f32[3,64]{1,0:T(4,128)}, u32[]{:S(2)}) %copy-start.4) | copy-done | bytes 792
  4.1 0.1 broadcast_subtract_fusion
  4.1 0.5 %multiply_dynamic-update-slice_fusion.1 = (f32[8,64,512]{2,1,0:T(8,128)S(1)}, f32[1,64,512]{2,1,0:T(8,128)S(1)}) fusion(f32[]{:T(128)S(1)} %bitcast.55, f32[3,64,512]{2,1,0:T(8,128)S(1)} %broadcast_subtract_fusion), kind=kLoop, calls=%fused_computation.32 | loop fusion | flops 262143 | bytes 655364
  4.8 0.0 copy-done.3
  4.8 0.5 multiply_dynamic-update-slice_fusion
  5.3 0.0 collective-permute-done
  5.4 2.6 %collective-permute-start.1 = (f32[4,32,256]{2,1,0:T(8,128)S(1)}, f32[4,32,256]{2,1,0:T(8,128)S(1)}, u32[]{:S(2)}, u32[]{:S(2)}) collective-permute-start(f32[4,32,256]{2,1,0:T(8,128)S(1)} %dynamic-slice_bitcast_fusion.1), channel_id=1, source_target_pairs={{0,4},{2,6},{4,0},{6,2},{8,12},{10,14},{12,8},{14,10},{16,20},{18,... | collective-permute-start | bytes 393224 | tf_op jit(solution)/shard_map/ppermute | solution.py:141
  8.0 0.5 cosine_dynamic-update-slice_fusion
  8.5 3.7 %collective-permute-done.1 = f32[4,32,256]{2,1,0:T(8,128)S(1)} collective-permute-done((f32[4,32,256]{2,1,0:T(8,128)S(1)}, f32[4,32,256]{2,1,0:T(8,128)S(1)}, u32[]{:S(2)}, u32[]{:S(2)}) %collective-permute-start.1) | collective-permute-done | bytes 131104 | tf_op jit(solution)/shard_map/ppermute | solution.py:141
  12.2 3.9 %collective-permute-start.4 = (f32[32,256]{1,0:T(8,128)S(1)}, f32[32,256]{1,0:T(8,128)S(1)}, u32[]{:S(2)}, u32[]{:S(2)}) collective-permute-start(f32[32,256]{1,0:T(8,128)S(1)} %get-tuple-element.13), channel_id=1, source_target_pairs={{0,24},{2,26},{4,28},{6,30},{8,0},{10,2},{12,4},{14,6},{16,8},{18,... | collective-permute-start | bytes 98312 | tf_op jit(solution)/shard_map/ppermute | solution.py:146
  16.1 0.0 collective-permute-start.3
  16.1 1.0 %collective-permute-start.2 = (f32[32,256]{1,0:T(8,128)S(1)}, f32[32,256]{1,0:T(8,128)S(1)}, u32[]{:S(2)}, u32[]{:S(2)}) collective-permute-start(f32[32,256]{1,0:T(8,128)S(1)} %get-tuple-element.12), channel_id=1, source_target_pairs={{0,8},{2,10},{4,12},{6,14},{8,16},{10,18},{12,20},{14,22},{16,24},... | collective-permute-start | bytes 98312 | tf_op jit(solution)/shard_map/ppermute | solution.py:146
  17.1 0.5 sine_dynamic-update-slice_fusion
  17.6 0.1 collective-permute-done.4
  17.7 3.2 %collective-permute-done.3 = f32[32,256]{1,0:T(8,128)S(1)} collective-permute-done((f32[32,256]{1,0:T(8,128)S(1)}, f32[32,256]{1,0:T(8,128)S(1)}, u32[]{:S(2)}, u32[]{:S(2)}) %collective-permute-start.3) | collective-permute-done | bytes 32800 | tf_op jit(solution)/shard_map/ppermute | solution.py:146
  20.9 0.9 %collective-permute-done.2 = f32[32,256]{1,0:T(8,128)S(1)} collective-permute-done((f32[32,256]{1,0:T(8,128)S(1)}, f32[32,256]{1,0:T(8,128)S(1)}, u32[]{:S(2)}, u32[]{:S(2)}) %collective-permute-start.2) | collective-permute-done | bytes 32800 | tf_op jit(solution)/shard_map/ppermute | solution.py:146
  21.8 0.6 %collective-permute-start.7 = (f32[32,256]{1,0:T(8,128)S(1)}, f32[32,256]{1,0:T(8,128)S(1)}, u32[]{:S(2)}, u32[]{:S(2)}) collective-permute-start(f32[32,256]{1,0:T(8,128)S(1)} %fusion.13), channel_id=1, source_target_pairs={{0,24},{2,26},{4,28},{6,30},{8,0},{10,2},{12,4},{14,6},{16,8},{18,... | collective-permute-start | bytes 98312 | tf_op jit(solution)/shard_map/ppermute | solution.py:154
  22.4 0.6 %collective-permute-start.6 = (f32[32,256]{1,0:T(8,128)S(1)}, f32[32,256]{1,0:T(8,128)S(1)}, u32[]{:S(2)}, u32[]{:S(2)}) collective-permute-start(f32[32,256]{1,0:T(8,128)S(1)} %fusion.13), channel_id=1, source_target_pairs={{0,16},{2,18},{4,20},{6,22},{8,24},{10,26},{12,28},{14,30},{16,0},... | collective-permute-start | bytes 98312 | tf_op jit(solution)/shard_map/ppermute | solution.py:154
  23.1 1.9 %collective-permute-start.5 = (f32[32,256]{1,0:T(8,128)S(1)}, f32[32,256]{1,0:T(8,128)S(1)}, u32[]{:S(2)}, u32[]{:S(2)}) collective-permute-start(f32[32,256]{1,0:T(8,128)S(1)} %fusion.13), channel_id=1, source_target_pairs={{0,8},{2,10},{4,12},{6,14},{8,16},{10,18},{12,20},{14,22},{16,24},... | collective-permute-start | bytes 98312 | tf_op jit(solution)/shard_map/ppermute | solution.py:154
  25.1 0.7 %collective-permute-done.7 = f32[32,256]{1,0:T(8,128)S(1)} collective-permute-done((f32[32,256]{1,0:T(8,128)S(1)}, f32[32,256]{1,0:T(8,128)S(1)}, u32[]{:S(2)}, u32[]{:S(2)}) %collective-permute-start.7) | collective-permute-done | bytes 32800 | tf_op jit(solution)/shard_map/ppermute | solution.py:154
  25.8 1.5 %collective-permute-done.6 = f32[32,256]{1,0:T(8,128)S(1)} collective-permute-done((f32[32,256]{1,0:T(8,128)S(1)}, f32[32,256]{1,0:T(8,128)S(1)}, u32[]{:S(2)}, u32[]{:S(2)}) %collective-permute-start.6) | collective-permute-done | bytes 32800 | tf_op jit(solution)/shard_map/ppermute | solution.py:154
  27.2 1.5 %collective-permute-done.5 = f32[32,256]{1,0:T(8,128)S(1)} collective-permute-done((f32[32,256]{1,0:T(8,128)S(1)}, f32[32,256]{1,0:T(8,128)S(1)}, u32[]{:S(2)}, u32[]{:S(2)}) %collective-permute-start.5) | collective-permute-done | bytes 32800 | tf_op jit(solution)/shard_map/ppermute | solution.py:154
  28.8 1.6 %collective-permute-start.8 = (f32[4,32,256]{2,1,0:T(8,128)S(1)}, f32[4,32,256]{2,1,0:T(8,128)S(1)}, u32[]{:S(2)}, u32[]{:S(2)}) collective-permute-start(f32[4,32,256]{2,1,0:T(8,128)S(1)} %pad_maximum_fusion.3), channel_id=1, source_target_pairs={{0,4},{2,6},{4,0},{6,2},{8,12},{10,14},{12,8},{14,10},{16,20},{18,... | collective-permute-start | bytes 393224 | tf_op jit(solution)/shard_map/ppermute | solution.py:161
  30.4 3.4 %collective-permute-done.8 = f32[4,32,256]{2,1,0:T(8,128)S(1)} collective-permute-done((f32[4,32,256]{2,1,0:T(8,128)S(1)}, f32[4,32,256]{2,1,0:T(8,128)S(1)}, u32[]{:S(2)}, u32[]{:S(2)}) %collective-permute-start.8) | collective-permute-done | bytes 131104 | tf_op jit(solution)/shard_map/ppermute | solution.py:161
  33.9 0.1 collective-permute-start.9
  34.1 0.0 copy-start
  34.1 1.4 %collective-permute-done.9 = f32[8,32,256]{2,1,0:T(8,128)S(1)} collective-permute-done((f32[8,32,256]{2,1,0:T(8,128)S(1)}, f32[8,32,256]{2,1,0:T(8,128)S(1)}, u32[]{:S(2)}, u32[]{:S(2)}) %collective-permute-start.9) | collective-permute-done | bytes 262176 | tf_op jit(solution)/shard_map/ppermute | solution.py:161
  35.5 0.1 select_bitcast_fusion.1
  35.6 0.9 %pad_maximum_fusion = f32[8,2,32,256]{3,2,1,0:T(8,128)} fusion(f32[8,1,32,256]{3,2,1,0:T(8,128)S(1)} %get-tuple-element.5, f32[8,1,32,256]{3,2,1,0:T(8,128)S(1)} %get-tuple-element.4), kind=kLoop, calls=%fused_computation.4 | loop fusion | flops 131072 | bytes 1048576 | tf_op jit(solution)/shard_map/stack | solution.py:164
  36.5 9.9 %shard_map.77 = f32[8,4096]{1,0:T(8,128)} custom-call(f32[32]{0:T(128)} %copy-done.3, f32[8,64,512]{2,1,0:T(8,128)} %copy-done, f32[512,256]{1,0:T(8,128)} %bitcast.45), custom_call_target="tpu_custom_call" | custom-call | tf_op jit(solution)/shard_map/pallas_call | solution.py:103
  46.4 0.9 %fusion.15 = f32[4096]{0:T(1024)S(1)} fusion(f32[8,4096]{1,0:T(8,128)} %shard_map.77), kind=kLoop, calls=%fused_computation.46 | loop fusion | flops 4096 | bytes 32768 | tf_op jit(solution)/shard_map/mul | solution.py:196
  47.4 0.1 mul.137
  47.4 0.0 copy-start.1
  47.5 0.1 fusion.16
  47.5 1.6 %collective-permute-start.10 = (f32[64]{0:T(128)S(1)}, f32[64]{0:T(128)S(1)}, u32[]{:S(2)}, u32[]{:S(2)}) collective-permute-start(f32[64]{0:T(128)S(1)} %fusion.16), channel_id=1, source_target_pairs={{0,1},{1,0},{2,3},{3,2},{4,5},{5,4},{6,7},{7,6},{8,9},{9,8},{10,11... | collective-permute-start | bytes 776 | tf_op jit(solution)/shard_map/ppermute | solution.py:199
  49.1 2.0 %collective-permute-done.10 = f32[64]{0:T(128)S(1)} collective-permute-done((f32[64]{0:T(128)S(1)}, f32[64]{0:T(128)S(1)}, u32[]{:S(2)}, u32[]{:S(2)}) %collective-permute-start.10) | collective-permute-done | bytes 288 | tf_op jit(solution)/shard_map/ppermute | solution.py:199
  51.1 0.5 %add_log_fusion = f32[64]{0:T(128)} fusion(f32[64]{0:T(128)S(1)} %fusion.16, f32[64]{0:T(128)S(1)} %collective-permute-done.10), kind=kLoop, calls=%fused_computation.63 | loop fusion | flops 192 | bytes 768 | tf_op jit(solution)/shard_map/log | solution.py:202
  51.6 0.0 copy-done.1
  (20 shorter events, 0.3 us)
Async XLA Ops:
  0.7 0.7 %copy-start.7 = (f32[512]{0:T(512)S(1)}, f32[512]{0:T(512)}, u32[]{:S(2)}) copy-start(f32[512]{0:T(512)} %param.7) | copy-start | bytes 6148
  0.7 0.7 %copy-start.6 = (s32[512,1]{0,1:T(1,128)S(1)}, s32[512,1]{0,1:T(1,128)}, u32[]{:S(2)}) copy-start(s32[512,1]{0,1:T(1,128)} %param.8) | copy-start | bytes 6148
  0.7 0.7 %copy-start.5 = (s32[512]{0:T(512)S(1)}, s32[512]{0:T(512)}, u32[]{:S(2)}) copy-start(s32[512]{0:T(512)} %param.9) | copy-start | bytes 6148
  2.8 0.7 %copy-start.2 = (f32[3,512]{1,0:T(4,128)S(1)}, f32[3,512]{1,0:T(4,128)}, u32[]{:S(2)}) copy-start(f32[3,512]{1,0:T(4,128)} %param.10) | copy-start | bytes 18436
  2.8 2.5 %collective-permute-start = (f32[8,32,256]{2,1,0:T(8,128)S(1)}, f32[8,32,256]{2,1,0:T(8,128)S(1)}, u32[]{:S(2)}, u32[]{:S(2)}) collective-permute-start(f32[8,32,256]{2,1,0:T(8,128)S(1)} %dynamic-slice_bitcast_fusion), channel_id=1, source_target_pairs={{0,2},{2,0},{4,6},{6,4},{8,10},{10,8},{12,14},{14,12},{16,18},{18,... | collective-permute-start | bytes 786440 | tf_op jit(solution)/shard_map/ppermute | solution.py:141
  3.4 0.7 %copy-start.4 = (f32[3,64]{1,0:T(4,128)S(1)}, f32[3,64]{1,0:T(4,128)}, u32[]{:S(2)}) copy-start(f32[3,64]{1,0:T(4,128)} %param.11) | copy-start | bytes 2308
  4.0 0.8 %copy-start.3 = (f32[32]{0:T(128)}, f32[32]{0:T(128)S(1)}, u32[]{:S(2)}) copy-start(f32[32]{0:T(128)S(1)} %add_multiply_fusion.wave_ref) | copy-start | bytes 388
  5.4 6.7 %collective-permute-start.1 = (f32[4,32,256]{2,1,0:T(8,128)S(1)}, f32[4,32,256]{2,1,0:T(8,128)S(1)}, u32[]{:S(2)}, u32[]{:S(2)}) collective-permute-start(f32[4,32,256]{2,1,0:T(8,128)S(1)} %dynamic-slice_bitcast_fusion.1), channel_id=1, source_target_pairs={{0,4},{2,6},{4,0},{6,2},{8,12},{10,14},{12,8},{14,10},{16,20},{18,... | collective-permute-start | bytes 393224 | tf_op jit(solution)/shard_map/ppermute | solution.py:141
  12.2 5.5 %collective-permute-start.4 = (f32[32,256]{1,0:T(8,128)S(1)}, f32[32,256]{1,0:T(8,128)S(1)}, u32[]{:S(2)}, u32[]{:S(2)}) collective-permute-start(f32[32,256]{1,0:T(8,128)S(1)} %get-tuple-element.13), channel_id=1, source_target_pairs={{0,24},{2,26},{4,28},{6,30},{8,0},{10,2},{12,4},{14,6},{16,8},{18,... | collective-permute-start | bytes 98312 | tf_op jit(solution)/shard_map/ppermute | solution.py:146
  16.1 4.8 %collective-permute-start.3 = (f32[32,256]{1,0:T(8,128)S(1)}, f32[32,256]{1,0:T(8,128)S(1)}, u32[]{:S(2)}, u32[]{:S(2)}) collective-permute-start(f32[32,256]{1,0:T(8,128)S(1)} %get-tuple-element.14), channel_id=1, source_target_pairs={{0,16},{2,18},{4,20},{6,22},{8,24},{10,26},{12,28},{14,30},{16,0},... | collective-permute-start | bytes 98312 | tf_op jit(solution)/shard_map/ppermute | solution.py:146
  16.1 5.7 %collective-permute-start.2 = (f32[32,256]{1,0:T(8,128)S(1)}, f32[32,256]{1,0:T(8,128)S(1)}, u32[]{:S(2)}, u32[]{:S(2)}) collective-permute-start(f32[32,256]{1,0:T(8,128)S(1)} %get-tuple-element.12), channel_id=1, source_target_pairs={{0,8},{2,10},{4,12},{6,14},{8,16},{10,18},{12,20},{14,22},{16,24},... | collective-permute-start | bytes 98312 | tf_op jit(solution)/shard_map/ppermute | solution.py:146
  21.8 4.0 %collective-permute-start.7 = (f32[32,256]{1,0:T(8,128)S(1)}, f32[32,256]{1,0:T(8,128)S(1)}, u32[]{:S(2)}, u32[]{:S(2)}) collective-permute-start(f32[32,256]{1,0:T(8,128)S(1)} %fusion.13), channel_id=1, source_target_pairs={{0,24},{2,26},{4,28},{6,30},{8,0},{10,2},{12,4},{14,6},{16,8},{18,... | collective-permute-start | bytes 98312 | tf_op jit(solution)/shard_map/ppermute | solution.py:154
  22.4 4.8 %collective-permute-start.6 = (f32[32,256]{1,0:T(8,128)S(1)}, f32[32,256]{1,0:T(8,128)S(1)}, u32[]{:S(2)}, u32[]{:S(2)}) collective-permute-start(f32[32,256]{1,0:T(8,128)S(1)} %fusion.13), channel_id=1, source_target_pairs={{0,16},{2,18},{4,20},{6,22},{8,24},{10,26},{12,28},{14,30},{16,0},... | collective-permute-start | bytes 98312 | tf_op jit(solution)/shard_map/ppermute | solution.py:154
  23.1 5.7 %collective-permute-start.5 = (f32[32,256]{1,0:T(8,128)S(1)}, f32[32,256]{1,0:T(8,128)S(1)}, u32[]{:S(2)}, u32[]{:S(2)}) collective-permute-start(f32[32,256]{1,0:T(8,128)S(1)} %fusion.13), channel_id=1, source_target_pairs={{0,8},{2,10},{4,12},{6,14},{8,16},{10,18},{12,20},{14,22},{16,24},... | collective-permute-start | bytes 98312 | tf_op jit(solution)/shard_map/ppermute | solution.py:154
  28.8 5.0 %collective-permute-start.8 = (f32[4,32,256]{2,1,0:T(8,128)S(1)}, f32[4,32,256]{2,1,0:T(8,128)S(1)}, u32[]{:S(2)}, u32[]{:S(2)}) collective-permute-start(f32[4,32,256]{2,1,0:T(8,128)S(1)} %pad_maximum_fusion.3), channel_id=1, source_target_pairs={{0,4},{2,6},{4,0},{6,2},{8,12},{10,14},{12,8},{14,10},{16,20},{18,... | collective-permute-start | bytes 393224 | tf_op jit(solution)/shard_map/ppermute | solution.py:161
  33.9 1.6 %collective-permute-start.9 = (f32[8,32,256]{2,1,0:T(8,128)S(1)}, f32[8,32,256]{2,1,0:T(8,128)S(1)}, u32[]{:S(2)}, u32[]{:S(2)}) collective-permute-start(f32[8,32,256]{2,1,0:T(8,128)S(1)} %bitcast.46), channel_id=1, source_target_pairs={{0,2},{2,0},{4,6},{6,4},{8,10},{10,8},{12,14},{14,12},{16,18},{18,... | collective-permute-start | bytes 786440 | tf_op jit(solution)/shard_map/ppermute | solution.py:161
  34.1 2.4 %copy-start = (f32[8,64,512]{2,1,0:T(8,128)}, f32[8,64,512]{2,1,0:T(8,128)S(1)}, u32[]{:S(2)}) copy-start(f32[8,64,512]{2,1,0:T(8,128)S(1)} %sqrt_dynamic-update-slice_fusion.geo_ref) | copy-start | bytes 3145732
  47.4 4.2 %copy-start.1 = (f32[32,2,64]{2,1,0:T(2,128)}, f32[32,2,64]{2,1,0:T(2,128)S(1)}, u32[]{:S(2)}) copy-start(f32[32,2,64]{2,1,0:T(2,128)S(1)} %mul.137) | copy-start | bytes 49156
  47.5 3.6 %collective-permute-start.10 = (f32[64]{0:T(128)S(1)}, f32[64]{0:T(128)S(1)}, u32[]{:S(2)}, u32[]{:S(2)}) collective-permute-start(f32[64]{0:T(128)S(1)} %fusion.16), channel_id=1, source_target_pairs={{0,1},{1,0},{2,3},{3,2},{4,5},{5,4},{6,7},{7,6},{8,9},{9,8},{10,11... | collective-permute-start | bytes 776 | tf_op jit(solution)/shard_map/ppermute | solution.py:199

commit v9 on v8

--- a/solution.py
+++ b/solution.py
@@ -12,7 +12,9 @@
 reference_radius = 10.0
 
 
-def field_kernel(block_group, freq_unroll, wave_ref, geo_ref, src_ref, out_ref, acc_ref, chan_ref, spread_ref):
+def field_kernel(
+    block_group, freq_unroll, chunk_ref, wave_ref, geo_ref, src_ref, out_ref, acc_ref, chan_ref, spread_ref
+):
     freqs, _, observers, lanes = acc_ref.shape
     blocks = observers // 8
 
@@ -79,16 +81,13 @@
         )
 
 
-def far_field(portion, panel_position, observer_position, wave_numbers):
-    panel_total, columns = portion.shape
-    freqs = columns // 8
-    observers = observer_position.shape[1]
+def field_geometry(panel_position, observer_position, wave_numbers):
     offsets = observer_position[:, :, None] - panel_position[:, None, :]
     distance = jnp.sqrt(offsets[0] * offsets[0] + offsets[1] * offsets[1] + offsets[2] * offsets[2])
     inverse = 1.0 / distance
     first_phase = wave_numbers[0] * distance
     step_phase = wave_step * distance
-    geometry = jnp.stack(
+    return jnp.stack(
         [
             jnp.cos(first_phase) * inverse,
             jnp.sin(first_phase) * inverse,
@@ -100,24 +99,33 @@
             distance,
         ]
     )
-    summed = pl.pallas_call(
-        functools.partial(field_kernel, math.gcd(observers // 8, 4), 2),
-        grid=(panel_total // 128,),
-        in_specs=[
-            pl.BlockSpec(memory_space=pltpu.SMEM),
-            pl.BlockSpec((8, observers, 128), lambda chunk: (0, 0, chunk)),
-            pl.BlockSpec((128, columns), lambda chunk: (chunk, 0)),
-        ],
-        out_specs=pl.BlockSpec((8, freqs * 2 * observers), lambda chunk: (0, 0)),
+
+
+def field_chunks(sources, chunk_ids, geometry, wave_numbers):
+    rows, columns = sources.shape
+    freqs = columns // 8
+    observers = geometry.shape[1]
+    kernel = functools.partial(field_kernel, math.gcd(observers // 8, 4), 2)
+    return pl.pallas_call(
+        kernel,
+        grid_spec=pltpu.PrefetchScalarGridSpec(
+            num_scalar_prefetch=1,
+            grid=(rows // 128,),
+            in_specs=[
+                pl.BlockSpec(memory_space=pltpu.SMEM),
+                pl.BlockSpec((8, observers, 128), lambda step, ids: (0, 0, ids[step])),
+                pl.BlockSpec((128, columns), lambda step, ids: (step, 0)),
+            ],
+            out_specs=pl.BlockSpec((8, freqs * 2 * observers), lambda step, ids: (0, 0)),
+            scratch_shapes=[
+                pltpu.VMEM((freqs, 2, observers, 128), jnp.float32),
+                pltpu.VMEM((columns, 128), jnp.float32),
+                pltpu.VMEM((columns, 8, 128), jnp.float32),
+            ],
+        ),
         out_shape=jax.ShapeDtypeStruct((8, freqs * 2 * observers), jnp.float32),
-        scratch_shapes=[
-            pltpu.VMEM((freqs, 2, observers, 128), jnp.float32),
-            pltpu.VMEM((columns, 128), jnp.float32),
-            pltpu.VMEM((columns, 8, 128), jnp.float32),
-        ],
         compiler_params=pltpu.CompilerParams(dimension_semantics=("arbitrary",)),
-    )(wave_numbers, geometry, portion)
-    return summed[0].reshape(freqs, 2, observers)
+    )(chunk_ids, wave_numbers, geometry, sources)
 
 
 def partner_pairs(groups, bit):
@@ -147,22 +155,30 @@
     return total
 
 
-def doubling_gather(own, bits, groups):
+def gather_and_sum(own, bits, groups, geometry, wave_numbers):
     place = lax.axis_index("obs")
-    quarter = place // (groups // 4)
+    columns = own.shape[-1]
+    low = groups // 4
+    quarter = place // low
     arrived = jnp.stack(
         [own] + [lax.ppermute(own, "obs", quad_pairs(groups, shift)) for shift in (1, 2, 3)]
     )
-    gathered = jnp.stack(
+    known = jnp.stack(
         [lax.dynamic_index_in_dim(arrived, (quarter - k) % 4, 0, keepdims=False) for k in range(4)]
-    )
-    for bit in reversed(bits):
-        mine = (place // bit) % 2
-        other = lax.ppermute(gathered, "obs", partner_pairs(groups, bit))
-        low = jnp.where(mine == 0, gathered, other)
-        high = jnp.where(mine == 0, other, gathered)
-        gathered = jnp.stack([low, high], axis=1).reshape((-1,) + gathered.shape[1:])
-    return gathered
+    )[None]
+    known_ids = (place % low)[None].astype(jnp.int32)
+    partials = [field_chunks(known.reshape(-1, columns), known_ids, geometry, wave_numbers)]
+    for turn, bit in enumerate(reversed(bits)):
+        other = lax.ppermute(known, "obs", partner_pairs(groups, bit))
+        other_ids = jnp.bitwise_xor(known_ids, bit)
+        partials.append(field_chunks(other.reshape(-1, columns), other_ids, geometry, wave_numbers))
+        if turn + 1 < len(bits):
+            known = jnp.concatenate([known, other], axis=0)
+            known_ids = jnp.concatenate([known_ids, other_ids], axis=0)
+    total = partials[0]
+    for part in partials[1:]:
+        total = total + part
+    return total
 
 
 def shards(cell_spectra, cell_weight, cell_owner, cell_local, panel_position, observer_position):
@@ -183,17 +199,23 @@
         (group_first + jnp.arange(freqs_dev, dtype=jnp.int32)).astype(jnp.float32) + 1.0
     )
     blocks = local_source.reshape(groups, panels_dev, columns)
-    if groups & (groups - 1) == 0 and groups >= 4:
+    geometry = field_geometry(panel_position, observer_position, wave_numbers)
+    observers = observer_position.shape[1]
+    if groups & (groups - 1) == 0 and groups >= 16 and 4 * panels_dev == 128:
         bits = [1 << k for k in range(groups.bit_length() - 3)]
         own_source = halving_sum(blocks, bits)
-        portion = doubling_gather(own_source, bits, groups).reshape(panel_total, columns)
+        chunked = jnp.transpose(
+            geometry.reshape(8, observers, 4, groups // 4, panels_dev), (0, 1, 3, 2, 4)
+        ).reshape(geometry.shape)
+        summed = gather_and_sum(own_source, bits, groups, chunked, wave_numbers)
     else:
         own_source = jnp.sum(lax.all_to_all(blocks, "obs", 0, 0, tiled=True), axis=0)
         portion = lax.all_to_all(
             jnp.broadcast_to(own_source[None], blocks.shape), "obs", 0, 0, tiled=True
         ).reshape(panel_total, columns)
-    summed = far_field(portion, panel_position, observer_position, wave_numbers)
-    pressure = summed * (reference_radius / math.sqrt(panel_total))
+        chunk_ids = jnp.arange(panel_total // 128, dtype=jnp.int32)
+        summed = field_chunks(portion, chunk_ids, geometry, wave_numbers)
+    pressure = summed[0].reshape(freqs_dev, 2, observers) * (reference_radius / math.sqrt(panel_total))
     energy = jnp.sum(pressure[:, 0] * pressure[:, 0] + pressure[:, 1] * pressure[:, 1], axis=0)
     if lax.axis_size("freq") == 2:
         band_total = energy + lax.ppermute(energy, "freq", [(0, 1), (1, 0)])

time: 51.9 us -> 69.6 us (1.34)
  Pallas kernels: 9.93 us -> 17.4 us
  local copies, waits for them, and re-layouts: 1.59 us -> 8.32 us
  other arithmetic: 4.74 us -> 10.1 us
  waiting for transfers between devices: 18.4 us -> 16.4 us
    pallas_call x1 -> x3, Pallas kernels: 9.93 us -> 17.4 us  [field_chunks(): pl.pallas_call(kernel, grid_spec=pltpu.PrefetchScalarGridSpec(num_scalar_...]
    mul x1 -> x2, other arithmetic: 0.95 us -> 3.96 us  [the longest x1 2.88 us: field_geometry(): offsets[2] * inverse * inverse]
    unnamed x16 -> x19, local copies, waits for them, and re-layouts: 1.38 us -> 4.1 us
    unnamed x7 -> x0, other arithmetic: 2.05 us -> none
    transpose x0 -> x1, local copies, waits for them, and re-layouts: none -> 1.83 us  [shards(): jnp.transpose(geometry.reshape(8, observers, 4, groups // 4, panels_dev),...]
    reshape x0 -> x1, local copies, waits for them, and re-layouts: none -> 1.58 us  [shards(): chunked = jnp.transpose(geometry.reshape(8, observers, 4, groups // 4, pa...]
    add x1, other arithmetic: 0.01 us -> 1.41 us  [halving_sum(): total = total + lax.ppermute(piece, 'obs', quad_pairs(groups, shift))]
    ppermute x5, waiting for transfers between devices: 8.52 us -> 7.22 us  [the longest x3 3.79 us: gather_and_sum(): lax.ppermute(own, 'obs', quad_pairs(groups, shift))]
  transfers between devices with their start and end apart: 11 -> 11, of which waited for: 10 -> 8; matrix products, arithmetic and copies ran while one was open for 4% -> 14% of each run, Pallas kernels for 0% -> 15%
where the time goes in v9:
time: 69.6 us; the launch traced here: 69 us
  Pallas kernels  17.4 us (25%)
  waiting for transfers between devices  16.4 us (24%)
  starting transfers between devices  14.3 us (21%)
  other arithmetic  10.1 us (15%)
  local copies, waits for them, and re-layouts  8.32 us (12%)
  matrix products  1.46 us (2%)
  between operations  1.04 us (1%)
    pallas_call x3, Pallas kernels, field_chunks(): pl.pallas_call(kernel, grid_spec=pltpu.PrefetchScalarGridSpec(num_scalar_...  17.4 us
    ppermute x3, starting transfers between devices, halving_sum(): total = total + lax.ppermute(piece, 'obs', quad_pairs(groups, shift))  4.86 us
    unnamed x19, local copies, waits for them, and re-layouts  4.1 us
    ppermute x3, waiting for transfers between devices, halving_sum(): total = total + lax.ppermute(piece, 'obs', quad_pairs(groups, shift))  4.03 us
    ppermute x3, waiting for transfers between devices, gather_and_sum(): lax.ppermute(own, 'obs', quad_pairs(groups, shift))  3.79 us
    ppermute x2, waiting for transfers between devices, gather_and_sum(): other = lax.ppermute(known, 'obs', partner_pairs(groups, bit))  3.43 us
    ppermute x3, starting transfers between devices, gather_and_sum(): lax.ppermute(own, 'obs', quad_pairs(groups, shift))  3.15 us
    ppermute x2, starting transfers between devices, halving_sum(): current = keep + lax.ppermute(send, 'obs', partner_pairs(groups, bit))  3.14 us
  transfers between devices with their start and end apart: 11, of which 8 were waited for; matrix products, arithmetic and copies ran while one was open for 14% of the time, Pallas kernels for 15%

profile of v9, /device:TPU:0, one launch (start us, length us, event | category | flops | bytes accessed | tf_op | source)
XLA Modules:
  0.0 69.0 jit_solution(3253346422096609467)
XLA Ops:
  0.7 1.5 %fusion = f32[512,256]{1,0:T(8,128)S(1)} fusion(s32[512]{0:T(512)} %param.9, s32[512]{0:T(512)} %bitcast.66, s32[512]{0:T(512)S(1)} %get-tuple-element.20, s32[512]{0:T(512)S(1)} %get-tuple-element.21, bf16[512,256]{1,0:T(8,128)(2,1)} %param.6, f32[512]{0:T(512)} %param.7), kind=kOutput, calls=%fused_computation | convolution fusion | flops 135397376 | bytes 796672 | tf_op jit(solution)/shard_map/dot_general | solution.py:196
  2.2 0.5 collective-permute-start
  2.7 1.0 %broadcast_subtract_fusion = f32[3,64,512]{1,2,0:T(8,128)S(1)} fusion(f32[3,512]{1,0:T(4,128)} %param.10, f32[3,64]{1,0:T(4,128)} %param.11), kind=kLoop, calls=%fused_computation.12 | loop fusion | flops 98304 | bytes 400128 | tf_op jit(solution)/shard_map/sub | solution.py:85
  3.7 0.1 fusion.23
  3.8 2.9 %multiply_multiply_fusion = (f32[1,64,512]{1,2,0:T(8,128)S(1)}, f32[1,64,512]{1,2,0:T(8,128)S(1)}, f32[1,64,512]{1,2,0:T(8,128)S(1)}, f32[1,64,512]{1,2,0:T(8,12...) fusion(f32[3,64,512]{1,2,0:T(8,128)S(1)} %broadcast_subtract_fusion, ...), kind=kLoop, calls=%fused_computation.9 | loop fusion | flops 360448 | bytes 1441796 | tf_op jit(solution)/shard_map/mul | solution.py:98
  6.7 0.0 copy-done.5
  6.7 0.0 collective-permute-done
  6.7 0.0 copy-start.1
  6.7 2.6 %collective-permute-start.1 = (f32[4,32,256]{2,1,0:T(8,128)S(1)}, f32[4,32,256]{2,1,0:T(8,128)}, u32[]{:S(2)}, u32[]{:S(2)}) collective-permute-start(f32[4,32,256]{2,1,0:T(8,128)S(1)} %dynamic-slice_bitcast_fusion.1), channel_id=1, source_target_pairs={{0,4},{2,6},{4,0},{6,2},{8,12},{10,14},{12,8},{14,10},{16,20},{18,... | collective-permute-start | bytes 393224 | tf_op jit(solution)/shard_map/ppermute | solution.py:149
  9.5 1.0 %constant_dynamic-update-slice_fusion.6 = f32[8,64,4,4,32]{1,4,3,2,0:T(8,128)S(1)} fusion(f32[8,64,4,4,32]{1,4,3,2,0:T(8,128)S(1)} %constant_dynamic-update-slice_fusion.7, f32[1,64,4,4,32]{1,4,3,2,0:T(8,128)} %bitcast.53), kind=kLoop, calls=%fused_computation.39 | loop fusion | bytes 393216
  10.4 3.1 %collective-permute-done.1 = f32[4,32,256]{2,1,0:T(8,128)} collective-permute-done((f32[4,32,256]{2,1,0:T(8,128)S(1)}, f32[4,32,256]{2,1,0:T(8,128)}, u32[]{:S(2)}, u32[]{:S(2)}) %collective-permute-start.1) | collective-permute-done | bytes 131104 | tf_op jit(solution)/shard_map/ppermute | solution.py:149
  13.6 1.0 %bitcast_add_fusion.1 = f32[4,32,256]{2,1,0:T(8,128)S(1)} fusion(f32[4,32,256]{2,1,0:T(8,128)} %collective-permute-done.1, f32[4,2,32,256]{3,2,1,0:T(8,128)} %bitcast.56, s32[]{:T(128)S(6)} %select_n.120), kind=kLoop, calls=%fused_computation.24 | loop fusion | flops 32768 | bytes 393220 | tf_op jit(solution)/shard_map/add | solution.py:149
  14.6 0.6 dynamic-slice_bitcast_fusion.4
  15.2 3.8 %collective-permute-start.4 = (f32[32,256]{1,0:T(8,128)}, f32[32,256]{1,0:T(8,128)}, u32[]{:S(2)}, u32[]{:S(2)}) collective-permute-start(f32[32,256]{1,0:T(8,128)} %get-tuple-element.18), channel_id=1, source_target_pairs={{0,24},{2,26},{4,28},{6,30},{8,0},{10,2},{12,4},{14,6},{16,8},{18,... | collective-permute-start | bytes 98312 | tf_op jit(solution)/shard_map/ppermute | solution.py:154
  19.1 0.0 collective-permute-start.3
  19.1 1.0 %collective-permute-start.2 = (f32[32,256]{1,0:T(8,128)}, f32[32,256]{1,0:T(8,128)}, u32[]{:S(2)}, u32[]{:S(2)}) collective-permute-start(f32[32,256]{1,0:T(8,128)} %get-tuple-element.17), channel_id=1, source_target_pairs={{0,8},{2,10},{4,12},{6,14},{8,16},{10,18},{12,20},{14,22},{16,24},... | collective-permute-start | bytes 98312 | tf_op jit(solution)/shard_map/ppermute | solution.py:154
  20.1 1.0 %constant_dynamic-update-slice_fusion.5 = f32[8,64,4,4,32]{1,4,3,2,0:T(8,128)S(1)} fusion(f32[8,64,4,4,32]{1,4,3,2,0:T(8,128)S(1)} %constant_dynamic-update-slice_fusion.6, f32[1,64,4,4,32]{1,4,3,2,0:T(8,128)} %bitcast.52), kind=kLoop, calls=%fused_computation.38 | loop fusion | bytes 393216
  21.0 0.0 collective-permute-done.4
  21.1 3.1 %collective-permute-done.3 = f32[32,256]{1,0:T(8,128)} collective-permute-done((f32[32,256]{1,0:T(8,128)}, f32[32,256]{1,0:T(8,128)}, u32[]{:S(2)}, u32[]{:S(2)}) %collective-permute-start.3) | collective-permute-done | bytes 32800 | tf_op jit(solution)/shard_map/ppermute | solution.py:154
  24.2 0.9 %collective-permute-done.2 = f32[32,256]{1,0:T(8,128)} collective-permute-done((f32[32,256]{1,0:T(8,128)}, f32[32,256]{1,0:T(8,128)}, u32[]{:S(2)}, u32[]{:S(2)}) %collective-permute-start.2) | collective-permute-done | bytes 32800 | tf_op jit(solution)/shard_map/ppermute | solution.py:154
  25.1 1.4 %fusion.10 = f32[32,256]{1,0:T(8,128)} fusion(f32[32,256]{1,0:T(8,128)} %collective-permute-done.4, f32[32,256]{1,0:T(8,128)} %collective-permute-done.3, f32[32,256]{1,0:T(8,128)} %collective-permute-done.2, f32[4,32,256]{2,1,0:T(8,128)S(1)} %bitcast_add_fusion.1, s32[]{:T(128)S(6)} %select_n.123), kind=kLoop, calls=%fused_computation.29 | loop fusion | flops 24576 | bytes 163844 | tf_op jit(solution)/shard_map/add | solution.py:154
  26.5 0.6 collective-permute-start.7
  27.1 0.6 collective-permute-start.6
  27.6 2.0 %collective-permute-start.5 = (f32[32,256]{1,0:T(8,128)}, f32[32,256]{1,0:T(8,128)S(1)}, u32[]{:S(2)}, u32[]{:S(2)}) collective-permute-start(f32[32,256]{1,0:T(8,128)} %fusion.10), channel_id=1, source_target_pairs={{0,8},{2,10},{4,12},{6,14},{8,16},{10,18},{12,20},{14,22},{16,24},... | collective-permute-start | bytes 98312 | tf_op jit(solution)/shard_map/ppermute | solution.py:164
  29.8 1.2 %collective-permute-done.7 = f32[32,256]{1,0:T(8,128)S(1)} collective-permute-done((f32[32,256]{1,0:T(8,128)}, f32[32,256]{1,0:T(8,128)S(1)}, u32[]{:S(2)}, u32[]{:S(2)}) %collective-permute-start.7) | collective-permute-done | bytes 32800 | tf_op jit(solution)/shard_map/ppermute | solution.py:164
  31.0 1.1 %collective-permute-done.6 = f32[32,256]{1,0:T(8,128)S(1)} collective-permute-done((f32[32,256]{1,0:T(8,128)}, f32[32,256]{1,0:T(8,128)S(1)}, u32[]{:S(2)}, u32[]{:S(2)}) %collective-permute-start.6) | collective-permute-done | bytes 32800 | tf_op jit(solution)/shard_map/ppermute | solution.py:164
  32.1 1.5 %collective-permute-done.5 = f32[32,256]{1,0:T(8,128)S(1)} collective-permute-done((f32[32,256]{1,0:T(8,128)}, f32[32,256]{1,0:T(8,128)S(1)}, u32[]{:S(2)}, u32[]{:S(2)}) %collective-permute-start.5) | collective-permute-done | bytes 32800 | tf_op jit(solution)/shard_map/ppermute | solution.py:164
  33.6 0.8 %pad_maximum_fusion.1 = f32[4,32,256]{2,1,0:T(8,128)S(1)} fusion(f32[1,32,256]{2,1,0:T(8,128)S(1)} %bitcast.62, f32[1,32,256]{2,1,0:T(8,128)S(1)} %bitcast.63, f32[1,32,256]{2,1,0:T(8,128)S(1)} %bitcast.64, f32[1,32,256]{2,1,0:T(8,128)} %bitcast.23), kind=kLoop, calls=%fused_computation.22 | loop fusion | flops 98304 | bytes 262144 | tf_op jit(solution)/shard_map/stack | solution.py:163
  34.4 0.7 pad_maximum_fusion.2
  35.0 1.5 %collective-permute-start.8 = (f32[1,4,32,256]{3,2,1,0:T(8,128)S(1)}, f32[1,4,32,256]{3,2,1,0:T(8,128)S(1)}, u32[]{:S(2)}, u32[]{:S(2)}) collective-permute-start(f32[1,4,32,256]{3,2,1,0:T(8,128)S(1)} %get-tuple-element.12), channel_id=1, source_target_pairs={{0,4},{2,6},{4,0},{6,2},{8,12},{10,14},{12,8},{14,10},{16,20},{18,... | collective-permute-start | bytes 393224 | tf_op jit(solution)/shard_map/ppermute | solution.py:172
  36.6 3.4 %collective-permute-done.8 = f32[1,4,32,256]{3,2,1,0:T(8,128)S(1)} collective-permute-done((f32[1,4,32,256]{3,2,1,0:T(8,128)S(1)}, f32[1,4,32,256]{3,2,1,0:T(8,128)S(1)}, u32[]{:S(2)}, u32[]{:S(2)}) %collective-permute-start.8) | collective-permute-done | bytes 131104 | tf_op jit(solution)/shard_map/ppermute | solution.py:172
  40.0 0.1 collective-permute-start.9
  40.2 1.3 %copy-done = f32[8,64,4,4,32]{1,4,3,2,0:T(8,128)} copy-done((f32[8,64,4,4,32]{1,4,3,2,0:T(8,128)}, f32[8,64,4,4,32]{1,4,3,2,0:T(8,128)S(1)}, u32[]{:S(2)}) %copy-start) | copy-done | bytes 1048600
  41.5 1.8 %copy.8 = f32[8,64,4,4,32]{1,4,3,2,0:T(8,128)S(1)} copy(f32[8,64,4,4,32]{1,4,2,3,0:T(8,128)} %bitcast.46) | data formatting | bytes 2097152 | tf_op jit(solution)/shard_map/transpose | solution.py:207
  43.4 1.6 %copy.9.geo_ref = f32[8,64,512]{2,1,0:T(8,128)} copy(f32[8,64,512]{1,2,0:T(8,128)S(1)} %bitcast.45) | data formatting | bytes 2097152 | tf_op jit(solution)/shard_map/reshape | solution.py:209
  44.9 0.6 add_xor_fusion.chunk_ref
  45.5 5.0 %shard_map.77 = f32[8,4096]{1,0:T(8,128)} custom-call(s32[1]{0:T(128)} %bitcast.chunk_ref, f32[32]{0:T(128)} %copy-done.5, f32[8,64,512]{2,1,0:T(8,128)} %copy.9.geo_ref, f32[128,256]{1,0:T(8,128)} %bitcast.57), custom_call_target="tpu_custom_call" | custom-call | tf_op jit(solution)/shard_map/pallas_call | solution.py:109
  50.5 5.0 %shard_map.78 = f32[8,4096]{1,0:T(8,128)} custom-call(s32[1]{0:T(128)S(6)} %xor.6.chunk_ref, f32[32]{0:T(128)} %copy-done.5, f32[8,64,512]{2,1,0:T(8,128)} %copy.9.geo_ref, f32[128,256]{1,0:T(8,128)} %bitcast.60), custom_call_target="tpu_custom_call" | custom-call | tf_op jit(solution)/shard_map/pallas_call | solution.py:109
  55.6 0.0 collective-permute-done.9
  55.6 0.7 %copy-done.3 = f32[2,4,32,256]{3,2,1,0:T(8,128)} copy-done((f32[2,4,32,256]{3,2,1,0:T(8,128)}, f32[2,4,32,256]{3,2,1,0:T(8,128)S(1)}, u32[]{:S(2)}) %copy-start.3) | copy-done | bytes 262168
  56.3 7.4 %shard_map.79 = f32[8,4096]{1,0:T(8,128)} custom-call(s32[2]{0:T(128)} %add_xor_fusion.chunk_ref, f32[32]{0:T(128)} %copy-done.5, f32[8,64,512]{2,1,0:T(8,128)} %copy.9.geo_ref, f32[256,256]{1,0:T(8,128)} %bitcast.61), custom_call_target="tpu_custom_call" | custom-call | tf_op jit(solution)/shard_map/pallas_call | solution.py:109
  63.7 1.1 %fusion.14 = f32[4096]{0:T(1024)S(1)} fusion(f32[8,4096]{1,0:T(8,128)} %shard_map.79, f32[8,4096]{1,0:T(8,128)} %shard_map.78, f32[8,4096]{1,0:T(8,128)} %shard_map.77), kind=kLoop, calls=%fused_computation.48 | loop fusion | flops 12288 | bytes 65536 | tf_op jit(solution)/shard_map/mul | solution.py:218
  64.8 0.1 mul.137
  64.8 0.0 copy-start.4
  64.9 0.1 fusion.13
  64.9 1.6 %collective-permute-start.10 = (f32[64]{0:T(128)S(1)}, f32[64]{0:T(128)S(1)}, u32[]{:S(2)}, u32[]{:S(2)}) collective-permute-start(f32[64]{0:T(128)S(1)} %fusion.13), channel_id=1, source_target_pairs={{0,1},{1,0},{2,3},{3,2},{4,5},{5,4},{6,7},{7,6},{8,9},{9,8},{10,11... | collective-permute-start | bytes 776 | tf_op jit(solution)/shard_map/ppermute | solution.py:221
  66.5 2.0 %collective-permute-done.10 = f32[64]{0:T(128)S(1)} collective-permute-done((f32[64]{0:T(128)S(1)}, f32[64]{0:T(128)S(1)}, u32[]{:S(2)}, u32[]{:S(2)}) %collective-permute-start.10) | collective-permute-done | bytes 288 | tf_op jit(solution)/shard_map/ppermute | solution.py:221
  68.5 0.5 add_log_fusion
  (20 shorter events, 0.3 us)
Async XLA Ops:
  2.2 4.5 %collective-permute-start = (f32[8,32,256]{2,1,0:T(8,128)S(1)}, f32[8,32,256]{2,1,0:T(8,128)S(1)}, u32[]{:S(2)}, u32[]{:S(2)}) collective-permute-start(f32[8,32,256]{2,1,0:T(8,128)S(1)} %dynamic-slice_bitcast_fusion), channel_id=1, source_target_pairs={{0,2},{2,0},{4,6},{6,4},{8,10},{10,8},{12,14},{14,12},{16,18},{18,... | collective-permute-start | bytes 786440 | tf_op jit(solution)/shard_map/ppermute | solution.py:149
  2.7 4.0 %copy-start.5 = (f32[32]{0:T(128)}, f32[32]{0:T(128)S(1)}, u32[]{:S(2)}) copy-start(f32[32]{0:T(128)S(1)} %add_multiply_fusion.wave_ref) | copy-start | bytes 388
  6.7 2.7 %copy-start.1 = (f32[8,32,256]{2,1,0:T(8,128)}, f32[8,32,256]{2,1,0:T(8,128)S(1)}, u32[]{:S(2)}) copy-start(f32[8,32,256]{2,1,0:T(8,128)S(1)} %bitcast_add_fusion) | copy-start | bytes 786436
  6.7 6.8 %collective-permute-start.1 = (f32[4,32,256]{2,1,0:T(8,128)S(1)}, f32[4,32,256]{2,1,0:T(8,128)}, u32[]{:S(2)}, u32[]{:S(2)}) collective-permute-start(f32[4,32,256]{2,1,0:T(8,128)S(1)} %dynamic-slice_bitcast_fusion.1), channel_id=1, source_target_pairs={{0,4},{2,6},{4,0},{6,2},{8,12},{10,14},{12,8},{14,10},{16,20},{18,... | collective-permute-start | bytes 393224 | tf_op jit(solution)/shard_map/ppermute | solution.py:149
  15.2 5.8 %collective-permute-start.4 = (f32[32,256]{1,0:T(8,128)}, f32[32,256]{1,0:T(8,128)}, u32[]{:S(2)}, u32[]{:S(2)}) collective-permute-start(f32[32,256]{1,0:T(8,128)} %get-tuple-element.18), channel_id=1, source_target_pairs={{0,24},{2,26},{4,28},{6,30},{8,0},{10,2},{12,4},{14,6},{16,8},{18,... | collective-permute-start | bytes 98312 | tf_op jit(solution)/shard_map/ppermute | solution.py:154
  19.1 5.1 %collective-permute-start.3 = (f32[32,256]{1,0:T(8,128)}, f32[32,256]{1,0:T(8,128)}, u32[]{:S(2)}, u32[]{:S(2)}) collective-permute-start(f32[32,256]{1,0:T(8,128)} %get-tuple-element.19), channel_id=1, source_target_pairs={{0,16},{2,18},{4,20},{6,22},{8,24},{10,26},{12,28},{14,30},{16,0},... | collective-permute-start | bytes 98312 | tf_op jit(solution)/shard_map/ppermute | solution.py:154
  19.1 6.0 %collective-permute-start.2 = (f32[32,256]{1,0:T(8,128)}, f32[32,256]{1,0:T(8,128)}, u32[]{:S(2)}, u32[]{:S(2)}) collective-permute-start(f32[32,256]{1,0:T(8,128)} %get-tuple-element.17), channel_id=1, source_target_pairs={{0,8},{2,10},{4,12},{6,14},{8,16},{10,18},{12,20},{14,22},{16,24},... | collective-permute-start | bytes 98312 | tf_op jit(solution)/shard_map/ppermute | solution.py:154
  26.5 4.5 %collective-permute-start.7 = (f32[32,256]{1,0:T(8,128)}, f32[32,256]{1,0:T(8,128)S(1)}, u32[]{:S(2)}, u32[]{:S(2)}) collective-permute-start(f32[32,256]{1,0:T(8,128)} %fusion.10), channel_id=1, source_target_pairs={{0,24},{2,26},{4,28},{6,30},{8,0},{10,2},{12,4},{14,6},{16,8},{18,... | collective-permute-start | bytes 98312 | tf_op jit(solution)/shard_map/ppermute | solution.py:164
  27.1 5.0 %collective-permute-start.6 = (f32[32,256]{1,0:T(8,128)}, f32[32,256]{1,0:T(8,128)S(1)}, u32[]{:S(2)}, u32[]{:S(2)}) collective-permute-start(f32[32,256]{1,0:T(8,128)} %fusion.10), channel_id=1, source_target_pairs={{0,16},{2,18},{4,20},{6,22},{8,24},{10,26},{12,28},{14,30},{16,0},... | collective-permute-start | bytes 98312 | tf_op jit(solution)/shard_map/ppermute | solution.py:164
  27.6 5.9 %collective-permute-start.5 = (f32[32,256]{1,0:T(8,128)}, f32[32,256]{1,0:T(8,128)S(1)}, u32[]{:S(2)}, u32[]{:S(2)}) collective-permute-start(f32[32,256]{1,0:T(8,128)} %fusion.10), channel_id=1, source_target_pairs={{0,8},{2,10},{4,12},{6,14},{8,16},{10,18},{12,20},{14,22},{16,24},... | collective-permute-start | bytes 98312 | tf_op jit(solution)/shard_map/ppermute | solution.py:164
  35.0 5.0 %collective-permute-start.8 = (f32[1,4,32,256]{3,2,1,0:T(8,128)S(1)}, f32[1,4,32,256]{3,2,1,0:T(8,128)S(1)}, u32[]{:S(2)}, u32[]{:S(2)}) collective-permute-start(f32[1,4,32,256]{3,2,1,0:T(8,128)S(1)} %get-tuple-element.12), channel_id=1, source_target_pairs={{0,4},{2,6},{4,0},{6,2},{8,12},{10,14},{12,8},{14,10},{16,20},{18,... | collective-permute-start | bytes 393224 | tf_op jit(solution)/shard_map/ppermute | solution.py:172
  40.0 3.4 %copy-start.2 = (f32[1,4,32,256]{3,2,1,0:T(8,128)}, f32[1,4,32,256]{3,2,1,0:T(8,128)S(1)}, u32[]{:S(2)}) copy-start(f32[1,4,32,256]{3,2,1,0:T(8,128)S(1)} %collective-permute-done.8) | copy-start | bytes 393220
  40.0 15.5 %collective-permute-start.9 = (f32[2,4,32,256]{3,2,1,0:T(8,128)S(1)}, f32[2,4,32,256]{3,2,1,0:T(8,128)S(1)}, u32[]{:S(2)}, u32[]{:S(2)}) collective-permute-start(f32[2,4,32,256]{3,2,1,0:T(8,128)S(1)} %pad_maximum_fusion), channel_id=1, source_target_pairs={{0,2},{2,0},{4,6},{6,4},{8,10},{10,8},{12,14},{14,12},{16,18},{18,... | collective-permute-start | bytes 786440 | tf_op jit(solution)/shard_map/ppermute | solution.py:172
  40.2 1.3 %copy-start = (f32[8,64,4,4,32]{1,4,3,2,0:T(8,128)}, f32[8,64,4,4,32]{1,4,3,2,0:T(8,128)S(1)}, u32[]{:S(2)}) copy-start(f32[8,64,4,4,32]{1,4,3,2,0:T(8,128)S(1)} %constant_dynamic-update-slice_fusion) | copy-start | bytes 3145732
  55.6 0.7 %copy-start.3 = (f32[2,4,32,256]{3,2,1,0:T(8,128)}, f32[2,4,32,256]{3,2,1,0:T(8,128)S(1)}, u32[]{:S(2)}) copy-start(f32[2,4,32,256]{3,2,1,0:T(8,128)S(1)} %collective-permute-done.9) | copy-start | bytes 786436
  64.8 4.2 %copy-start.4 = (f32[32,2,64]{2,1,0:T(2,128)}, f32[32,2,64]{2,1,0:T(2,128)S(1)}, u32[]{:S(2)}) copy-start(f32[32,2,64]{2,1,0:T(2,128)S(1)} %mul.137) | copy-start | bytes 49156
  64.9 3.6 %collective-permute-start.10 = (f32[64]{0:T(128)S(1)}, f32[64]{0:T(128)S(1)}, u32[]{:S(2)}, u32[]{:S(2)}) collective-permute-start(f32[64]{0:T(128)S(1)} %fusion.13), channel_id=1, source_target_pairs={{0,1},{1,0},{2,3},{3,2},{4,5},{5,4},{6,7},{7,6},{8,9},{9,8},{10,11... | collective-permute-start | bytes 776 | tf_op jit(solution)/shard_map/ppermute | solution.py:221

commit v10 on v8

--- a/solution.py
+++ b/solution.py
@@ -12,13 +12,10 @@
 reference_radius = 10.0
 
 
-def field_kernel(block_group, freq_unroll, wave_ref, geo_ref, src_ref, out_ref, acc_ref, chan_ref, spread_ref):
+def field_kernel(block_group, freq_unroll, scale, wave_ref, geo_ref, src_ref, out_ref, acc_ref, chan_ref, spread_ref):
     freqs, _, observers, lanes = acc_ref.shape
     blocks = observers // 8
-
-    @pl.when(pl.program_id(0) == 0)
-    def _():
-        acc_ref[...] = jnp.zeros(acc_ref.shape, acc_ref.dtype)
+    chunk = pl.program_id(0)
 
     chan_ref[...] = jnp.transpose(src_ref[...])
 
@@ -28,58 +25,73 @@
 
     lax.fori_loop(0, chan_ref.shape[0], spread_body, 0, unroll=8)
 
-    def block_body(group, carry):
-        spans = [
-            pl.ds(pl.multiple_of((group * block_group + member) * 8, 8), 8)
-            for member in range(block_group)
-        ]
-        step_cos = [geo_ref[2, rows, :] for rows in spans]
-        step_sin = [geo_ref[3, rows, :] for rows in spans]
-        along = [[geo_ref[4 + j, rows, :] for j in range(3)] for rows in spans]
-        distance = [geo_ref[7, rows, :] for rows in spans]
-
-        def freq_body(f, phase):
-            base = f * 8
-            channel = [spread_ref[base + c] for c in range(8)]
-            wave = wave_ref[f]
-            turned = []
-            for member, rows in enumerate(spans):
-                weight_real, weight_imag = phase[member]
-                g = along[member]
-                wave_distance = wave * distance[member]
-                dipole_real = g[0] * channel[2] + g[1] * channel[4] + g[2] * channel[6]
-                dipole_imag = g[0] * channel[3] + g[1] * channel[5] + g[2] * channel[7]
-                amp_real = channel[0] + dipole_real - wave_distance * dipole_imag
-                amp_imag = channel[1] + dipole_imag + wave_distance * dipole_real
-                acc_ref[f, 0, rows, :] += weight_real * amp_real + weight_imag * amp_imag
-                acc_ref[f, 1, rows, :] += weight_real * amp_imag - weight_imag * amp_real
-                turned.append(
-                    (
-                        weight_real * step_cos[member] - weight_imag * step_sin[member],
-                        weight_imag * step_cos[member] + weight_real * step_sin[member],
+    def sweep(first):
+        def block_body(group, carry):
+            spans = [
+                pl.ds(pl.multiple_of((group * block_group + member) * 8, 8), 8)
+                for member in range(block_group)
+            ]
+            step_cos = [geo_ref[2, rows, :] for rows in spans]
+            step_sin = [geo_ref[3, rows, :] for rows in spans]
+            along = [[geo_ref[4 + j, rows, :] for j in range(3)] for rows in spans]
+            distance = [geo_ref[7, rows, :] for rows in spans]
+
+            def freq_body(f, phase):
+                base = f * 8
+                channel = [spread_ref[base + c] for c in range(8)]
+                wave = wave_ref[f]
+                turned = []
+                for member, rows in enumerate(spans):
+                    weight_real, weight_imag = phase[member]
+                    g = along[member]
+                    wave_distance = wave * distance[member]
+                    dipole_real = g[0] * channel[2] + g[1] * channel[4] + g[2] * channel[6]
+                    dipole_imag = g[0] * channel[3] + g[1] * channel[5] + g[2] * channel[7]
+                    amp_real = channel[0] + dipole_real - wave_distance * dipole_imag
+                    amp_imag = channel[1] + dipole_imag + wave_distance * dipole_real
+                    real_term = weight_real * amp_real + weight_imag * amp_imag
+                    imag_term = weight_real * amp_imag - weight_imag * amp_real
+                    if first:
+                        acc_ref[f, 0, rows, :] = real_term
+                        acc_ref[f, 1, rows, :] = imag_term
+                    else:
+                        acc_ref[f, 0, rows, :] += real_term
+                        acc_ref[f, 1, rows, :] += imag_term
+                    turned.append(
+                        (
+                            weight_real * step_cos[member] - weight_imag * step_sin[member],
+                            weight_imag * step_cos[member] + weight_real * step_sin[member],
+                        )
                     )
-                )
-            return tuple(turned)
-
-        start = tuple((geo_ref[0, rows, :], geo_ref[1, rows, :]) for rows in spans)
-        lax.fori_loop(0, freqs, freq_body, start, unroll=freq_unroll)
-        return carry
-
-    lax.fori_loop(0, blocks // block_group, block_body, 0)
-
-    @pl.when(pl.program_id(0) == pl.num_programs(0) - 1)
+                return tuple(turned)
+
+            start = tuple((geo_ref[0, rows, :], geo_ref[1, rows, :]) for rows in spans)
+            lax.fori_loop(0, freqs, freq_body, start, unroll=freq_unroll)
+            return carry
+
+        lax.fori_loop(0, blocks // block_group, block_body, 0)
+
+    @pl.when(chunk == 0)
     def _():
-        flat = acc_ref[...].reshape(freqs * 2 * observers, lanes)
-        out_ref[...] = lax.dot_general(
-            jnp.ones((8, lanes), jnp.float32),
-            flat,
-            (((1,), (1,)), ((), ())),
-            precision=lax.Precision.HIGHEST,
-            preferred_element_type=jnp.float32,
-        )
-
-
-def far_field(portion, panel_position, observer_position, wave_numbers):
+        sweep(True)
+
+    @pl.when(chunk > 0)
+    def _():
+        sweep(False)
+
+    @pl.when(chunk == pl.num_programs(0) - 1)
+    def _():
+        def fold_body(row, carry):
+            f = row // 2
+            part = row % 2
+            flipped = jnp.transpose(acc_ref[f, part])
+            out_ref[f, pl.ds(part, 1), :] = jnp.sum(flipped, axis=0, keepdims=True) * scale
+            return carry
+
+        lax.fori_loop(0, freqs * 2, fold_body, 0)
+
+
+def far_field(portion, panel_position, observer_position, wave_numbers, scale):
     panel_total, columns = portion.shape
     freqs = columns // 8
     observers = observer_position.shape[1]
@@ -101,15 +113,15 @@
         ]
     )
     summed = pl.pallas_call(
-        functools.partial(field_kernel, math.gcd(observers // 8, 4), 2),
+        functools.partial(field_kernel, math.gcd(observers // 8, 4), 2, scale),
         grid=(panel_total // 128,),
         in_specs=[
             pl.BlockSpec(memory_space=pltpu.SMEM),
             pl.BlockSpec((8, observers, 128), lambda chunk: (0, 0, chunk)),
             pl.BlockSpec((128, columns), lambda chunk: (chunk, 0)),
         ],
-        out_specs=pl.BlockSpec((8, freqs * 2 * observers), lambda chunk: (0, 0)),
-        out_shape=jax.ShapeDtypeStruct((8, freqs * 2 * observers), jnp.float32),
+        out_specs=pl.BlockSpec((freqs, 2, observers), lambda chunk: (0, 0, 0)),
+        out_shape=jax.ShapeDtypeStruct((freqs, 2, observers), jnp.float32),
         scratch_shapes=[
             pltpu.VMEM((freqs, 2, observers, 128), jnp.float32),
             pltpu.VMEM((columns, 128), jnp.float32),
@@ -117,7 +129,7 @@
         ],
         compiler_params=pltpu.CompilerParams(dimension_semantics=("arbitrary",)),
     )(wave_numbers, geometry, portion)
-    return summed[0].reshape(freqs, 2, observers)
+    return summed
 
 
 def partner_pairs(groups, bit):
@@ -192,8 +204,9 @@
         portion = lax.all_to_all(
             jnp.broadcast_to(own_source[None], blocks.shape), "obs", 0, 0, tiled=True
         ).reshape(panel_total, columns)
-    summed = far_field(portion, panel_position, observer_position, wave_numbers)
-    pressure = summed * (reference_radius / math.sqrt(panel_total))
+    pressure = far_field(
+        portion, panel_position, observer_position, wave_numbers, reference_radius / math.sqrt(panel_total)
+    )
     energy = jnp.sum(pressure[:, 0] * pressure[:, 0] + pressure[:, 1] * pressure[:, 1], axis=0)
     if lax.axis_size("freq") == 2:
         band_total = energy + lax.ppermute(energy, "freq", [(0, 1), (1, 0)])

time: 51.9 us -> 56.7 us (1.092)
  Pallas kernels: 9.93 us -> 14.9 us
    pallas_call x1, Pallas kernels: 9.93 us -> 14.9 us  [far_field(): pl.pallas_call(functools.partial(field_kernel, math.gcd(observers // 8, 4...]
    mul x1 -> x0, other arithmetic: 0.95 us -> none  [shards(): pressure = summed * (reference_radius / math.sqrt(panel_total))]
    reduce_sum x1, other arithmetic: 0.05 us -> 0.89 us  [shards(): jnp.sum(pressure[:, 0] * pressure[:, 0] + pressure[:, 1] * pressure[:, 1]...]
    unnamed x16 -> x14, local copies, waits for them, and re-layouts: 1.38 us -> 1.38 us
where the time goes in v10:
time: 56.7 us; the launch traced here: 56.4 us
  waiting for transfers between devices  18.4 us (32%)
  Pallas kernels  14.9 us (26%)
  starting transfers between devices  14.4 us (25%)
  other arithmetic  4.6 us (8%)
  local copies, waits for them, and re-layouts  1.5 us (3%)
  matrix products  1.42 us (3%)
  between operations  1.09 us (2%)
    pallas_call x1, Pallas kernels, far_field(): pl.pallas_call(functools.partial(field_kernel, math.gcd(observers // 8, 4...  14.9 us
    ppermute x3, starting transfers between devices, halving_sum(): total = total + lax.ppermute(piece, 'obs', quad_pairs(groups, shift))  4.91 us
    ppermute x2, waiting for transfers between devices, doubling_gather(): other = lax.ppermute(gathered, 'obs', partner_pairs(groups, bit))  4.87 us
    ppermute x3, waiting for transfers between devices, halving_sum(): total = total + lax.ppermute(piece, 'obs', quad_pairs(groups, shift))  4.22 us
    ppermute x2, waiting for transfers between devices, halving_sum(): current = keep + lax.ppermute(send, 'obs', partner_pairs(groups, bit))  3.69 us
    ppermute x3, waiting for transfers between devices, doubling_gather(): lax.ppermute(own, 'obs', quad_pairs(groups, shift))  3.65 us
    ppermute x3, starting transfers between devices, doubling_gather(): lax.ppermute(own, 'obs', quad_pairs(groups, shift))  3.2 us
    ppermute x2, starting transfers between devices, halving_sum(): current = keep + lax.ppermute(send, 'obs', partner_pairs(groups, bit))  3.09 us
  transfers between devices with their start and end apart: 11, of which 10 were waited for; matrix products, arithmetic and copies ran while one was open for 4% of the time, Pallas kernels for 0%

profile of v10, /device:TPU:0, one launch (start us, length us, event | category | flops | bytes accessed | tf_op | source)
XLA Modules:
  0.0 56.4 jit_solution(16802132837766605163)
XLA Ops:
  0.7 0.0 copy-start.6
  0.7 0.0 copy-start.5
  0.7 0.0 copy-start.4
  0.7 0.6 %copy-done.6 = f32[512]{0:T(512)S(1)} copy-done((f32[512]{0:T(512)S(1)}, f32[512]{0:T(512)}, u32[]{:S(2)}) %copy-start.6) | copy-done | bytes 2072
  1.3 0.0 copy-done.5
  1.4 0.0 copy-done.4
  1.4 1.4 %fusion = f32[512,256]{1,0:T(8,128)S(1)} fusion(s32[512]{0:T(512)S(1)} %copy-done.4, s32[512]{0:T(512)S(1)} %bitcast.57, s32[512]{0:T(512)S(1)} %get-tuple-element.15, s32[512]{0:T(512)S(1)} %get-tuple-element.16, bf16[512,256]{1,0:T(8,128)(2,1)} %param.6, f32[512]{0:T(512)S(1)} %copy-done.6), kind=kOutput, calls=%fused_computation | convolution fusion | flops 135397376 | bytes 796672 | tf_op jit(solution)/shard_map/dot_general | solution.py:192
  2.8 0.0 copy-start.1
  2.8 0.5 collective-permute-start
  3.4 0.0 copy-start.3
  3.4 0.1 copy-done.1
  3.5 0.5 copy-done.3
  4.0 0.0 copy-start.2
  4.1 0.1 broadcast_subtract_fusion
  4.1 0.5 multiply_dynamic-update-slice_fusion.1
  4.8 0.0 copy-done.2
  4.8 0.5 multiply_dynamic-update-slice_fusion
  5.3 0.0 collective-permute-done
  5.4 2.6 %collective-permute-start.1 = (f32[4,32,256]{2,1,0:T(8,128)S(1)}, f32[4,32,256]{2,1,0:T(8,128)S(1)}, u32[]{:S(2)}, u32[]{:S(2)}) collective-permute-start(f32[4,32,256]{2,1,0:T(8,128)S(1)} %dynamic-slice_bitcast_fusion.1), channel_id=1, source_target_pairs={{0,4},{2,6},{4,0},{6,2},{8,12},{10,14},{12,8},{14,10},{16,20},{18,... | collective-permute-start | bytes 393224 | tf_op jit(solution)/shard_map/ppermute | solution.py:153
  8.0 0.5 cosine_dynamic-update-slice_fusion
  8.5 3.7 %collective-permute-done.1 = f32[4,32,256]{2,1,0:T(8,128)S(1)} collective-permute-done((f32[4,32,256]{2,1,0:T(8,128)S(1)}, f32[4,32,256]{2,1,0:T(8,128)S(1)}, u32[]{:S(2)}, u32[]{:S(2)}) %collective-permute-start.1) | collective-permute-done | bytes 131104 | tf_op jit(solution)/shard_map/ppermute | solution.py:153
  12.2 3.9 %collective-permute-start.4 = (f32[32,256]{1,0:T(8,128)S(1)}, f32[32,256]{1,0:T(8,128)S(1)}, u32[]{:S(2)}, u32[]{:S(2)}) collective-permute-start(f32[32,256]{1,0:T(8,128)S(1)} %get-tuple-element.13), channel_id=1, source_target_pairs={{0,24},{2,26},{4,28},{6,30},{8,0},{10,2},{12,4},{14,6},{16,8},{18,... | collective-permute-start | bytes 98312 | tf_op jit(solution)/shard_map/ppermute | solution.py:158
  16.1 0.0 collective-permute-start.3
  16.1 1.0 %collective-permute-start.2 = (f32[32,256]{1,0:T(8,128)S(1)}, f32[32,256]{1,0:T(8,128)S(1)}, u32[]{:S(2)}, u32[]{:S(2)}) collective-permute-start(f32[32,256]{1,0:T(8,128)S(1)} %get-tuple-element.12), channel_id=1, source_target_pairs={{0,8},{2,10},{4,12},{6,14},{8,16},{10,18},{12,20},{14,22},{16,24},... | collective-permute-start | bytes 98312 | tf_op jit(solution)/shard_map/ppermute | solution.py:158
  17.1 0.5 sine_dynamic-update-slice_fusion
  17.6 0.1 collective-permute-done.4
  17.7 3.2 %collective-permute-done.3 = f32[32,256]{1,0:T(8,128)S(1)} collective-permute-done((f32[32,256]{1,0:T(8,128)S(1)}, f32[32,256]{1,0:T(8,128)S(1)}, u32[]{:S(2)}, u32[]{:S(2)}) %collective-permute-start.3) | collective-permute-done | bytes 32800 | tf_op jit(solution)/shard_map/ppermute | solution.py:158
  20.9 0.9 %collective-permute-done.2 = f32[32,256]{1,0:T(8,128)S(1)} collective-permute-done((f32[32,256]{1,0:T(8,128)S(1)}, f32[32,256]{1,0:T(8,128)S(1)}, u32[]{:S(2)}, u32[]{:S(2)}) %collective-permute-start.2) | collective-permute-done | bytes 32800 | tf_op jit(solution)/shard_map/ppermute | solution.py:158
  21.8 0.6 %collective-permute-start.7 = (f32[32,256]{1,0:T(8,128)S(1)}, f32[32,256]{1,0:T(8,128)S(1)}, u32[]{:S(2)}, u32[]{:S(2)}) collective-permute-start(f32[32,256]{1,0:T(8,128)S(1)} %fusion.13), channel_id=1, source_target_pairs={{0,24},{2,26},{4,28},{6,30},{8,0},{10,2},{12,4},{14,6},{16,8},{18,... | collective-permute-start | bytes 98312 | tf_op jit(solution)/shard_map/ppermute | solution.py:166
  22.4 0.6 %collective-permute-start.6 = (f32[32,256]{1,0:T(8,128)S(1)}, f32[32,256]{1,0:T(8,128)S(1)}, u32[]{:S(2)}, u32[]{:S(2)}) collective-permute-start(f32[32,256]{1,0:T(8,128)S(1)} %fusion.13), channel_id=1, source_target_pairs={{0,16},{2,18},{4,20},{6,22},{8,24},{10,26},{12,28},{14,30},{16,0},... | collective-permute-start | bytes 98312 | tf_op jit(solution)/shard_map/ppermute | solution.py:166
  23.1 1.9 %collective-permute-start.5 = (f32[32,256]{1,0:T(8,128)S(1)}, f32[32,256]{1,0:T(8,128)S(1)}, u32[]{:S(2)}, u32[]{:S(2)}) collective-permute-start(f32[32,256]{1,0:T(8,128)S(1)} %fusion.13), channel_id=1, source_target_pairs={{0,8},{2,10},{4,12},{6,14},{8,16},{10,18},{12,20},{14,22},{16,24},... | collective-permute-start | bytes 98312 | tf_op jit(solution)/shard_map/ppermute | solution.py:166
  25.1 0.7 %collective-permute-done.7 = f32[32,256]{1,0:T(8,128)S(1)} collective-permute-done((f32[32,256]{1,0:T(8,128)S(1)}, f32[32,256]{1,0:T(8,128)S(1)}, u32[]{:S(2)}, u32[]{:S(2)}) %collective-permute-start.7) | collective-permute-done | bytes 32800 | tf_op jit(solution)/shard_map/ppermute | solution.py:166
  25.8 1.5 %collective-permute-done.6 = f32[32,256]{1,0:T(8,128)S(1)} collective-permute-done((f32[32,256]{1,0:T(8,128)S(1)}, f32[32,256]{1,0:T(8,128)S(1)}, u32[]{:S(2)}, u32[]{:S(2)}) %collective-permute-start.6) | collective-permute-done | bytes 32800 | tf_op jit(solution)/shard_map/ppermute | solution.py:166
  27.2 1.5 %collective-permute-done.5 = f32[32,256]{1,0:T(8,128)S(1)} collective-permute-done((f32[32,256]{1,0:T(8,128)S(1)}, f32[32,256]{1,0:T(8,128)S(1)}, u32[]{:S(2)}, u32[]{:S(2)}) %collective-permute-start.5) | collective-permute-done | bytes 32800 | tf_op jit(solution)/shard_map/ppermute | solution.py:166
  28.8 1.6 %collective-permute-start.8 = (f32[4,32,256]{2,1,0:T(8,128)S(1)}, f32[4,32,256]{2,1,0:T(8,128)S(1)}, u32[]{:S(2)}, u32[]{:S(2)}) collective-permute-start(f32[4,32,256]{2,1,0:T(8,128)S(1)} %pad_maximum_fusion.3), channel_id=1, source_target_pairs={{0,4},{2,6},{4,0},{6,2},{8,12},{10,14},{12,8},{14,10},{16,20},{18,... | collective-permute-start | bytes 393224 | tf_op jit(solution)/shard_map/ppermute | solution.py:173
  30.4 3.4 %collective-permute-done.8 = f32[4,32,256]{2,1,0:T(8,128)S(1)} collective-permute-done((f32[4,32,256]{2,1,0:T(8,128)S(1)}, f32[4,32,256]{2,1,0:T(8,128)S(1)}, u32[]{:S(2)}, u32[]{:S(2)}) %collective-permute-start.8) | collective-permute-done | bytes 131104 | tf_op jit(solution)/shard_map/ppermute | solution.py:173
  33.9 0.1 collective-permute-start.9
  34.1 0.0 copy-start
  34.1 1.4 %collective-permute-done.9 = f32[8,32,256]{2,1,0:T(8,128)S(1)} collective-permute-done((f32[8,32,256]{2,1,0:T(8,128)S(1)}, f32[8,32,256]{2,1,0:T(8,128)S(1)}, u32[]{:S(2)}, u32[]{:S(2)}) %collective-permute-start.9) | collective-permute-done | bytes 262176 | tf_op jit(solution)/shard_map/ppermute | solution.py:173
  35.5 0.1 select_bitcast_fusion.1
  35.6 0.9 %pad_maximum_fusion = f32[8,2,32,256]{3,2,1,0:T(8,128)} fusion(f32[8,1,32,256]{3,2,1,0:T(8,128)S(1)} %get-tuple-element.5, f32[8,1,32,256]{3,2,1,0:T(8,128)S(1)} %get-tuple-element.4), kind=kLoop, calls=%fused_computation.4 | loop fusion | flops 131072 | bytes 1048576 | tf_op jit(solution)/shard_map/stack | solution.py:176
  36.5 0.0 copy-done
  36.5 14.9 %shard_map.77 = f32[32,2,64]{2,1,0:T(2,128)} custom-call(f32[32]{0:T(128)} %copy-done.2, f32[8,64,512]{2,1,0:T(8,128)} %copy-done, f32[512,256]{1,0:T(8,128)} %bitcast.45), custom_call_target="tpu_custom_call" | custom-call | tf_op jit(solution)/shard_map/pallas_call | solution.py:115
  51.3 0.9 %fusion.15 = f32[64]{0:T(128)S(1)} fusion(f32[32,2,64]{2,1,0:T(2,128)} %shard_map.77), kind=kLoop, calls=%fused_computation.45 | loop fusion | flops 8128 | bytes 16640 | tf_op jit(solution)/shard_map/reduce_sum | solution.py:210
  52.2 1.6 %collective-permute-start.10 = (f32[64]{0:T(128)S(1)}, f32[64]{0:T(128)S(1)}, u32[]{:S(2)}, u32[]{:S(2)}) collective-permute-start(f32[64]{0:T(128)S(1)} %fusion.15), channel_id=1, source_target_pairs={{0,1},{1,0},{2,3},{3,2},{4,5},{5,4},{6,7},{7,6},{8,9},{9,8},{10,11... | collective-permute-start | bytes 776 | tf_op jit(solution)/shard_map/ppermute | solution.py:212
  53.8 2.0 %collective-permute-done.10 = f32[64]{0:T(128)S(1)} collective-permute-done((f32[64]{0:T(128)S(1)}, f32[64]{0:T(128)S(1)}, u32[]{:S(2)}, u32[]{:S(2)}) %collective-permute-start.10) | collective-permute-done | bytes 288 | tf_op jit(solution)/shard_map/ppermute | solution.py:212
  55.8 0.5 add_log_fusion
  (17 shorter events, 0.3 us)
Async XLA Ops:
  0.7 0.7 %copy-start.6 = (f32[512]{0:T(512)S(1)}, f32[512]{0:T(512)}, u32[]{:S(2)}) copy-start(f32[512]{0:T(512)} %param.7) | copy-start | bytes 6148
  0.7 0.7 %copy-start.5 = (s32[512,1]{0,1:T(1,128)S(1)}, s32[512,1]{0,1:T(1,128)}, u32[]{:S(2)}) copy-start(s32[512,1]{0,1:T(1,128)} %param.8) | copy-start | bytes 6148
  0.7 0.7 %copy-start.4 = (s32[512]{0:T(512)S(1)}, s32[512]{0:T(512)}, u32[]{:S(2)}) copy-start(s32[512]{0:T(512)} %param.9) | copy-start | bytes 6148
  2.8 0.7 %copy-start.1 = (f32[3,512]{1,0:T(4,128)S(1)}, f32[3,512]{1,0:T(4,128)}, u32[]{:S(2)}) copy-start(f32[3,512]{1,0:T(4,128)} %param.10) | copy-start | bytes 18436
  2.8 2.5 %collective-permute-start = (f32[8,32,256]{2,1,0:T(8,128)S(1)}, f32[8,32,256]{2,1,0:T(8,128)S(1)}, u32[]{:S(2)}, u32[]{:S(2)}) collective-permute-start(f32[8,32,256]{2,1,0:T(8,128)S(1)} %dynamic-slice_bitcast_fusion), channel_id=1, source_target_pairs={{0,2},{2,0},{4,6},{6,4},{8,10},{10,8},{12,14},{14,12},{16,18},{18,... | collective-permute-start | bytes 786440 | tf_op jit(solution)/shard_map/ppermute | solution.py:153
  3.4 0.7 %copy-start.3 = (f32[3,64]{1,0:T(4,128)S(1)}, f32[3,64]{1,0:T(4,128)}, u32[]{:S(2)}) copy-start(f32[3,64]{1,0:T(4,128)} %param.11) | copy-start | bytes 2308
  4.0 0.8 %copy-start.2 = (f32[32]{0:T(128)}, f32[32]{0:T(128)S(1)}, u32[]{:S(2)}) copy-start(f32[32]{0:T(128)S(1)} %add_multiply_fusion.wave_ref) | copy-start | bytes 388
  5.4 6.7 %collective-permute-start.1 = (f32[4,32,256]{2,1,0:T(8,128)S(1)}, f32[4,32,256]{2,1,0:T(8,128)S(1)}, u32[]{:S(2)}, u32[]{:S(2)}) collective-permute-start(f32[4,32,256]{2,1,0:T(8,128)S(1)} %dynamic-slice_bitcast_fusion.1), channel_id=1, source_target_pairs={{0,4},{2,6},{4,0},{6,2},{8,12},{10,14},{12,8},{14,10},{16,20},{18,... | collective-permute-start | bytes 393224 | tf_op jit(solution)/shard_map/ppermute | solution.py:153
  12.2 5.5 %collective-permute-start.4 = (f32[32,256]{1,0:T(8,128)S(1)}, f32[32,256]{1,0:T(8,128)S(1)}, u32[]{:S(2)}, u32[]{:S(2)}) collective-permute-start(f32[32,256]{1,0:T(8,128)S(1)} %get-tuple-element.13), channel_id=1, source_target_pairs={{0,24},{2,26},{4,28},{6,30},{8,0},{10,2},{12,4},{14,6},{16,8},{18,... | collective-permute-start | bytes 98312 | tf_op jit(solution)/shard_map/ppermute | solution.py:158
  16.1 4.8 %collective-permute-start.3 = (f32[32,256]{1,0:T(8,128)S(1)}, f32[32,256]{1,0:T(8,128)S(1)}, u32[]{:S(2)}, u32[]{:S(2)}) collective-permute-start(f32[32,256]{1,0:T(8,128)S(1)} %get-tuple-element.14), channel_id=1, source_target_pairs={{0,16},{2,18},{4,20},{6,22},{8,24},{10,26},{12,28},{14,30},{16,0},... | collective-permute-start | bytes 98312 | tf_op jit(solution)/shard_map/ppermute | solution.py:158
  16.1 5.7 %collective-permute-start.2 = (f32[32,256]{1,0:T(8,128)S(1)}, f32[32,256]{1,0:T(8,128)S(1)}, u32[]{:S(2)}, u32[]{:S(2)}) collective-permute-start(f32[32,256]{1,0:T(8,128)S(1)} %get-tuple-element.12), channel_id=1, source_target_pairs={{0,8},{2,10},{4,12},{6,14},{8,16},{10,18},{12,20},{14,22},{16,24},... | collective-permute-start | bytes 98312 | tf_op jit(solution)/shard_map/ppermute | solution.py:158
  21.8 4.0 %collective-permute-start.7 = (f32[32,256]{1,0:T(8,128)S(1)}, f32[32,256]{1,0:T(8,128)S(1)}, u32[]{:S(2)}, u32[]{:S(2)}) collective-permute-start(f32[32,256]{1,0:T(8,128)S(1)} %fusion.13), channel_id=1, source_target_pairs={{0,24},{2,26},{4,28},{6,30},{8,0},{10,2},{12,4},{14,6},{16,8},{18,... | collective-permute-start | bytes 98312 | tf_op jit(solution)/shard_map/ppermute | solution.py:166
  22.4 4.8 %collective-permute-start.6 = (f32[32,256]{1,0:T(8,128)S(1)}, f32[32,256]{1,0:T(8,128)S(1)}, u32[]{:S(2)}, u32[]{:S(2)}) collective-permute-start(f32[32,256]{1,0:T(8,128)S(1)} %fusion.13), channel_id=1, source_target_pairs={{0,16},{2,18},{4,20},{6,22},{8,24},{10,26},{12,28},{14,30},{16,0},... | collective-permute-start | bytes 98312 | tf_op jit(solution)/shard_map/ppermute | solution.py:166
  23.1 5.7 %collective-permute-start.5 = (f32[32,256]{1,0:T(8,128)S(1)}, f32[32,256]{1,0:T(8,128)S(1)}, u32[]{:S(2)}, u32[]{:S(2)}) collective-permute-start(f32[32,256]{1,0:T(8,128)S(1)} %fusion.13), channel_id=1, source_target_pairs={{0,8},{2,10},{4,12},{6,14},{8,16},{10,18},{12,20},{14,22},{16,24},... | collective-permute-start | bytes 98312 | tf_op jit(solution)/shard_map/ppermute | solution.py:166
  28.8 5.0 %collective-permute-start.8 = (f32[4,32,256]{2,1,0:T(8,128)S(1)}, f32[4,32,256]{2,1,0:T(8,128)S(1)}, u32[]{:S(2)}, u32[]{:S(2)}) collective-permute-start(f32[4,32,256]{2,1,0:T(8,128)S(1)} %pad_maximum_fusion.3), channel_id=1, source_target_pairs={{0,4},{2,6},{4,0},{6,2},{8,12},{10,14},{12,8},{14,10},{16,20},{18,... | collective-permute-start | bytes 393224 | tf_op jit(solution)/shard_map/ppermute | solution.py:173
  33.9 1.6 %collective-permute-start.9 = (f32[8,32,256]{2,1,0:T(8,128)S(1)}, f32[8,32,256]{2,1,0:T(8,128)S(1)}, u32[]{:S(2)}, u32[]{:S(2)}) collective-permute-start(f32[8,32,256]{2,1,0:T(8,128)S(1)} %bitcast.46), channel_id=1, source_target_pairs={{0,2},{2,0},{4,6},{6,4},{8,10},{10,8},{12,14},{14,12},{16,18},{18,... | collective-permute-start | bytes 786440 | tf_op jit(solution)/shard_map/ppermute | solution.py:173
  34.1 2.4 %copy-start = (f32[8,64,512]{2,1,0:T(8,128)}, f32[8,64,512]{2,1,0:T(8,128)S(1)}, u32[]{:S(2)}) copy-start(f32[8,64,512]{2,1,0:T(8,128)S(1)} %sqrt_dynamic-update-slice_fusion.geo_ref) | copy-start | bytes 3145732
  52.2 3.6 %collective-permute-start.10 = (f32[64]{0:T(128)S(1)}, f32[64]{0:T(128)S(1)}, u32[]{:S(2)}, u32[]{:S(2)}) collective-permute-start(f32[64]{0:T(128)S(1)} %fusion.15), channel_id=1, source_target_pairs={{0,1},{1,0},{2,3},{3,2},{4,5},{5,4},{6,7},{7,6},{8,9},{9,8},{10,11... | collective-permute-start | bytes 776 | tf_op jit(solution)/shard_map/ppermute | solution.py:212

commit v11 on v8

--- a/solution.py
+++ b/solution.py
@@ -12,7 +12,9 @@
 reference_radius = 10.0
 
 
-def field_kernel(block_group, freq_unroll, wave_ref, geo_ref, src_ref, out_ref, acc_ref, chan_ref, spread_ref):
+def field_kernel(
+    block_group, freq_unroll, low_chunks, wave_ref, geo_ref, low_ref, high_ref, out_ref, acc_ref, chan_ref, spread_ref
+):
     freqs, _, observers, lanes = acc_ref.shape
     blocks = observers // 8
 
@@ -20,7 +22,15 @@
     def _():
         acc_ref[...] = jnp.zeros(acc_ref.shape, acc_ref.dtype)
 
-    chan_ref[...] = jnp.transpose(src_ref[...])
+    chunk = pl.program_id(0)
+
+    @pl.when(chunk < low_chunks)
+    def _():
+        chan_ref[...] = jnp.transpose(low_ref[...])
+
+    @pl.when(chunk >= low_chunks)
+    def _():
+        chan_ref[...] = jnp.transpose(high_ref[...])
 
     def spread_body(row, carry):
         spread_ref[row] = jnp.broadcast_to(chan_ref[pl.ds(row, 1), :], (8, lanes))
@@ -79,8 +89,10 @@
         )
 
 
-def far_field(portion, panel_position, observer_position, wave_numbers):
-    panel_total, columns = portion.shape
+def far_field(low, high, panel_position, observer_position, wave_numbers):
+    columns = low.shape[1]
+    low_chunks = low.shape[0] // 128
+    panel_total = low.shape[0] + high.shape[0]
     freqs = columns // 8
     observers = observer_position.shape[1]
     offsets = observer_position[:, :, None] - panel_position[:, None, :]
@@ -101,12 +113,13 @@
         ]
     )
     summed = pl.pallas_call(
-        functools.partial(field_kernel, math.gcd(observers // 8, 4), 2),
+        functools.partial(field_kernel, math.gcd(observers // 8, 4), 2, low_chunks),
         grid=(panel_total // 128,),
         in_specs=[
             pl.BlockSpec(memory_space=pltpu.SMEM),
             pl.BlockSpec((8, observers, 128), lambda chunk: (0, 0, chunk)),
-            pl.BlockSpec((128, columns), lambda chunk: (chunk, 0)),
+            pl.BlockSpec((128, columns), lambda chunk: (jnp.minimum(chunk, low_chunks - 1), 0)),
+            pl.BlockSpec((128, columns), lambda chunk: (jnp.maximum(chunk - low_chunks, 0), 0)),
         ],
         out_specs=pl.BlockSpec((8, freqs * 2 * observers), lambda chunk: (0, 0)),
         out_shape=jax.ShapeDtypeStruct((8, freqs * 2 * observers), jnp.float32),
@@ -116,7 +129,7 @@
             pltpu.VMEM((columns, 8, 128), jnp.float32),
         ],
         compiler_params=pltpu.CompilerParams(dimension_semantics=("arbitrary",)),
-    )(wave_numbers, geometry, portion)
+    )(wave_numbers, geometry, low, high)
     return summed[0].reshape(freqs, 2, observers)
 
 
@@ -159,6 +172,8 @@
     for bit in reversed(bits):
         mine = (place // bit) % 2
         other = lax.ppermute(gathered, "obs", partner_pairs(groups, bit))
+        if bit == 1:
+            return gathered, other
         low = jnp.where(mine == 0, gathered, other)
         high = jnp.where(mine == 0, other, gathered)
         gathered = jnp.stack([low, high], axis=1).reshape((-1,) + gathered.shape[1:])
@@ -183,16 +198,33 @@
         (group_first + jnp.arange(freqs_dev, dtype=jnp.int32)).astype(jnp.float32) + 1.0
     )
     blocks = local_source.reshape(groups, panels_dev, columns)
-    if groups & (groups - 1) == 0 and groups >= 4:
+    if groups & (groups - 1) == 0 and groups >= 8:
         bits = [1 << k for k in range(groups.bit_length() - 3)]
         own_source = halving_sum(blocks, bits)
-        portion = doubling_gather(own_source, bits, groups).reshape(panel_total, columns)
+        mine_half, other_half = doubling_gather(own_source, bits, groups)
+        mine = lax.axis_index("obs") % 2
+        paired = panel_position.reshape(3, groups // 2, 2, panels_dev)
+        ordered = jnp.concatenate(
+            [
+                lax.dynamic_index_in_dim(paired, mine, 2, keepdims=False),
+                lax.dynamic_index_in_dim(paired, 1 - mine, 2, keepdims=False),
+            ],
+            axis=1,
+        ).reshape(3, panel_total)
+        summed = far_field(
+            mine_half.reshape(-1, columns),
+            other_half.reshape(-1, columns),
+            ordered,
+            observer_position,
+            wave_numbers,
+        )
     else:
         own_source = jnp.sum(lax.all_to_all(blocks, "obs", 0, 0, tiled=True), axis=0)
         portion = lax.all_to_all(
             jnp.broadcast_to(own_source[None], blocks.shape), "obs", 0, 0, tiled=True
         ).reshape(panel_total, columns)
-    summed = far_field(portion, panel_position, observer_position, wave_numbers)
+        half = panel_total // 256 * 128
+        summed = far_field(portion[:half], portion[half:], panel_position, observer_position, wave_numbers)
     pressure = summed * (reference_radius / math.sqrt(panel_total))
     energy = jnp.sum(pressure[:, 0] * pressure[:, 0] + pressure[:, 1] * pressure[:, 1], axis=0)
     if lax.axis_size("freq") == 2:

time: 51.9 us -> 52 us (level)
  local copies, waits for them, and re-layouts: 1.59 us -> 3.1 us
  waiting for transfers between devices: 18.4 us -> 17.3 us
  other arithmetic: 4.74 us -> 3.81 us
    unnamed x16 -> x20, local copies, waits for them, and re-layouts: 1.38 us -> 2.69 us
    another operation x4 -> x2, other arithmetic: 0.97 us -> 0.04 us  [doubling_gather(): jnp.stack([low, high], axis=1).reshape((-1,) + gathered.shape[1:])]
    ppermute x2, waiting for transfers between devices: 3.69 us -> 3.1 us  [halving_sum(): current = keep + lax.ppermute(send, 'obs', partner_pairs(groups, bit))]
  transfers between devices with their start and end apart: 11 -> 11, of which waited for: 10 -> 10; matrix products, arithmetic and copies ran while one was open for 4% -> 5% of each run, Pallas kernels for 0% -> 0%
where the time goes in v11:
time: 52 us; the launch traced here: 51.7 us
  waiting for transfers between devices  17.3 us (33%)
  starting transfers between devices  14.9 us (29%)
  Pallas kernels  10.1 us (19%)
  other arithmetic  3.81 us (7%)
  local copies, waits for them, and re-layouts  3.1 us (6%)
  matrix products  1.41 us (3%)
  between operations  1.12 us (2%)
    pallas_call x1, Pallas kernels, far_field(): pl.pallas_call(functools.partial(field_kernel, math.gcd(observers // 8, 4...  10.1 us
    ppermute x3, starting transfers between devices, halving_sum(): total = total + lax.ppermute(piece, 'obs', quad_pairs(groups, shift))  4.92 us
    ppermute x2, waiting for transfers between devices, doubling_gather(): other = lax.ppermute(gathered, 'obs', partner_pairs(groups, bit))  4.35 us
    ppermute x3, waiting for transfers between devices, halving_sum(): total = total + lax.ppermute(piece, 'obs', quad_pairs(groups, shift))  4.22 us
    ppermute x3, waiting for transfers between devices, doubling_gather(): lax.ppermute(own, 'obs', quad_pairs(groups, shift))  3.65 us
    ppermute x2, starting transfers between devices, halving_sum(): current = keep + lax.ppermute(send, 'obs', partner_pairs(groups, bit))  3.52 us
    ppermute x3, starting transfers between devices, doubling_gather(): lax.ppermute(own, 'obs', quad_pairs(groups, shift))  3.2 us
    ppermute x2, waiting for transfers between devices, halving_sum(): current = keep + lax.ppermute(send, 'obs', partner_pairs(groups, bit))  3.1 us
  transfers between devices with their start and end apart: 11, of which 10 were waited for; matrix products, arithmetic and copies ran while one was open for 5% of the time, Pallas kernels for 0%

profile of v11, /device:TPU:0, one launch (start us, length us, event | category | flops | bytes accessed | tf_op | source)
XLA Modules:
  0.0 51.7 jit_solution(17914639827849812670)
XLA Ops:
  0.7 0.0 copy-start.9
  0.7 0.0 copy-start.8
  0.7 0.0 copy-start.7
  0.7 0.6 %copy-done.9 = f32[512]{0:T(512)S(1)} copy-done((f32[512]{0:T(512)S(1)}, f32[512]{0:T(512)}, u32[]{:S(2)}) %copy-start.9) | copy-done | bytes 2072
  1.3 0.0 copy-done.8
  1.4 0.0 copy-done.7
  1.4 1.4 %fusion = f32[512,256]{1,0:T(8,128)S(1)} fusion(s32[512]{0:T(512)S(1)} %copy-done.7, s32[512]{0:T(512)S(1)} %bitcast.55, s32[512]{0:T(512)S(1)} %get-tuple-element.15, s32[512]{0:T(512)S(1)} %get-tuple-element.16, bf16[512,256]{1,0:T(8,128)(2,1)} %param.6, f32[512]{0:T(512)S(1)} %copy-done.9), kind=kOutput, calls=%fused_computation | convolution fusion | flops 135397376 | bytes 796672 | tf_op jit(solution)/shard_map/dot_general | solution.py:195
  2.8 0.0 copy-start.4
  2.8 0.5 %collective-permute-start = (f32[8,32,256]{2,1,0:T(8,128)S(1)}, f32[8,32,256]{2,1,0:T(8,128)S(1)}, u32[]{:S(2)}, u32[]{:S(2)}) collective-permute-start(f32[8,32,256]{2,1,0:T(8,128)S(1)} %dynamic-slice_bitcast_fusion), channel_id=1, source_target_pairs={{0,2},{2,0},{4,6},{6,4},{8,10},{10,8},{12,14},{14,12},{16,18},{18,... | collective-permute-start | bytes 786440 | tf_op jit(solution)/shard_map/ppermute | solution.py:154
  3.4 0.2 copy-done.4
  3.5 0.1 reshape.78
  3.7 0.0 copy-start.6
  3.7 0.1 sub.49
  3.8 0.6 %copy-done.6 = f32[3,64]{1,0:T(4,128)S(1)} copy-done((f32[3,64]{1,0:T(4,128)S(1)}, f32[3,64]{1,0:T(4,128)}, u32[]{:S(2)}) %copy-start.6) | copy-done | bytes 792
  4.4 0.1 broadcast_subtract_fusion
  4.5 0.5 %multiply_dynamic-update-slice_fusion.1 = (f32[8,64,512]{2,1,0:T(8,128)S(1)}, f32[1,64,512]{2,1,0:T(8,128)S(1)}) fusion(f32[]{:T(128)S(1)} %bitcast.53, f32[3,64,512]{2,1,0:T(8,128)S(1)} %broadcast_subtract_fusion), kind=kLoop, calls=%fused_computation.29 | loop fusion | flops 262143 | bytes 655364
  5.1 0.5 multiply_dynamic-update-slice_fusion
  5.7 3.0 %collective-permute-start.1 = (f32[4,32,256]{2,1,0:T(8,128)S(1)}, f32[4,32,256]{2,1,0:T(8,128)S(1)}, u32[]{:S(2)}, u32[]{:S(2)}) collective-permute-start(f32[4,32,256]{2,1,0:T(8,128)S(1)} %dynamic-slice_bitcast_fusion.1), channel_id=1, source_target_pairs={{0,4},{2,6},{4,0},{6,2},{8,12},{10,14},{12,8},{14,10},{16,20},{18,... | collective-permute-start | bytes 393224 | tf_op jit(solution)/shard_map/ppermute | solution.py:154
  8.7 0.5 cosine_dynamic-update-slice_fusion
  9.2 3.1 %collective-permute-done.1 = f32[4,32,256]{2,1,0:T(8,128)S(1)} collective-permute-done((f32[4,32,256]{2,1,0:T(8,128)S(1)}, f32[4,32,256]{2,1,0:T(8,128)S(1)}, u32[]{:S(2)}, u32[]{:S(2)}) %collective-permute-start.1) | collective-permute-done | bytes 131104 | tf_op jit(solution)/shard_map/ppermute | solution.py:154
  12.3 3.9 %collective-permute-start.4 = (f32[32,256]{1,0:T(8,128)S(1)}, f32[32,256]{1,0:T(8,128)S(1)}, u32[]{:S(2)}, u32[]{:S(2)}) collective-permute-start(f32[32,256]{1,0:T(8,128)S(1)} %get-tuple-element.11), channel_id=1, source_target_pairs={{0,24},{2,26},{4,28},{6,30},{8,0},{10,2},{12,4},{14,6},{16,8},{18,... | collective-permute-start | bytes 98312 | tf_op jit(solution)/shard_map/ppermute | solution.py:159
  16.2 0.0 collective-permute-start.3
  16.2 1.0 %collective-permute-start.2 = (f32[32,256]{1,0:T(8,128)S(1)}, f32[32,256]{1,0:T(8,128)S(1)}, u32[]{:S(2)}, u32[]{:S(2)}) collective-permute-start(f32[32,256]{1,0:T(8,128)S(1)} %get-tuple-element.10), channel_id=1, source_target_pairs={{0,8},{2,10},{4,12},{6,14},{8,16},{10,18},{12,20},{14,22},{16,24},... | collective-permute-start | bytes 98312 | tf_op jit(solution)/shard_map/ppermute | solution.py:159
  17.3 0.5 sine_dynamic-update-slice_fusion
  17.7 0.1 collective-permute-done.4
  17.8 3.2 %collective-permute-done.3 = f32[32,256]{1,0:T(8,128)S(1)} collective-permute-done((f32[32,256]{1,0:T(8,128)S(1)}, f32[32,256]{1,0:T(8,128)S(1)}, u32[]{:S(2)}, u32[]{:S(2)}) %collective-permute-start.3) | collective-permute-done | bytes 32800 | tf_op jit(solution)/shard_map/ppermute | solution.py:159
  21.1 0.9 %collective-permute-done.2 = f32[32,256]{1,0:T(8,128)S(1)} collective-permute-done((f32[32,256]{1,0:T(8,128)S(1)}, f32[32,256]{1,0:T(8,128)S(1)}, u32[]{:S(2)}, u32[]{:S(2)}) %collective-permute-start.2) | collective-permute-done | bytes 32800 | tf_op jit(solution)/shard_map/ppermute | solution.py:159
  22.0 0.7 %collective-permute-start.7 = (f32[32,256]{1,0:T(8,128)S(1)}, f32[32,256]{1,0:T(8,128)S(1)}, u32[]{:S(2)}, u32[]{:S(2)}) collective-permute-start(f32[32,256]{1,0:T(8,128)S(1)} %fusion.13), channel_id=1, source_target_pairs={{0,24},{2,26},{4,28},{6,30},{8,0},{10,2},{12,4},{14,6},{16,8},{18,... | collective-permute-start | bytes 98312 | tf_op jit(solution)/shard_map/ppermute | solution.py:167
  22.7 0.6 %collective-permute-start.6 = (f32[32,256]{1,0:T(8,128)S(1)}, f32[32,256]{1,0:T(8,128)S(1)}, u32[]{:S(2)}, u32[]{:S(2)}) collective-permute-start(f32[32,256]{1,0:T(8,128)S(1)} %fusion.13), channel_id=1, source_target_pairs={{0,16},{2,18},{4,20},{6,22},{8,24},{10,26},{12,28},{14,30},{16,0},... | collective-permute-start | bytes 98312 | tf_op jit(solution)/shard_map/ppermute | solution.py:167
  23.2 1.9 %collective-permute-start.5 = (f32[32,256]{1,0:T(8,128)S(1)}, f32[32,256]{1,0:T(8,128)S(1)}, u32[]{:S(2)}, u32[]{:S(2)}) collective-permute-start(f32[32,256]{1,0:T(8,128)S(1)} %fusion.13), channel_id=1, source_target_pairs={{0,8},{2,10},{4,12},{6,14},{8,16},{10,18},{12,20},{14,22},{16,24},... | collective-permute-start | bytes 98312 | tf_op jit(solution)/shard_map/ppermute | solution.py:167
  25.3 1.0 %collective-permute-done.7 = f32[32,256]{1,0:T(8,128)S(1)} collective-permute-done((f32[32,256]{1,0:T(8,128)S(1)}, f32[32,256]{1,0:T(8,128)S(1)}, u32[]{:S(2)}, u32[]{:S(2)}) %collective-permute-start.7) | collective-permute-done | bytes 32800 | tf_op jit(solution)/shard_map/ppermute | solution.py:167
  26.3 1.2 %collective-permute-done.6 = f32[32,256]{1,0:T(8,128)S(1)} collective-permute-done((f32[32,256]{1,0:T(8,128)S(1)}, f32[32,256]{1,0:T(8,128)S(1)}, u32[]{:S(2)}, u32[]{:S(2)}) %collective-permute-start.6) | collective-permute-done | bytes 32800 | tf_op jit(solution)/shard_map/ppermute | solution.py:167
  27.5 1.5 %collective-permute-done.5 = f32[32,256]{1,0:T(8,128)S(1)} collective-permute-done((f32[32,256]{1,0:T(8,128)S(1)}, f32[32,256]{1,0:T(8,128)S(1)}, u32[]{:S(2)}, u32[]{:S(2)}) %collective-permute-start.5) | collective-permute-done | bytes 32800 | tf_op jit(solution)/shard_map/ppermute | solution.py:167
  29.0 1.6 %collective-permute-start.8 = (f32[4,32,256]{2,1,0:T(8,128)S(1)}, f32[4,32,256]{2,1,0:T(8,128)S(1)}, u32[]{:S(2)}, u32[]{:S(2)}) collective-permute-start(f32[4,32,256]{2,1,0:T(8,128)S(1)} %pad_maximum_fusion.2), channel_id=1, source_target_pairs={{0,4},{2,6},{4,0},{6,2},{8,12},{10,14},{12,8},{14,10},{16,20},{18,... | collective-permute-start | bytes 393224 | tf_op jit(solution)/shard_map/ppermute | solution.py:174
  30.6 3.4 %collective-permute-done.8 = f32[4,32,256]{2,1,0:T(8,128)S(1)} collective-permute-done((f32[4,32,256]{2,1,0:T(8,128)S(1)}, f32[4,32,256]{2,1,0:T(8,128)S(1)}, u32[]{:S(2)}, u32[]{:S(2)}) %collective-permute-start.8) | collective-permute-done | bytes 131104 | tf_op jit(solution)/shard_map/ppermute | solution.py:174
  34.1 0.1 collective-permute-start.9
  34.3 0.5 %copy-done.1 = f32[4,2,32,256]{3,2,1,0:T(8,128)} copy-done((f32[4,2,32,256]{3,2,1,0:T(8,128)}, f32[4,2,32,256]{3,2,1,0:T(8,128)S(1)}, u32[]{:S(2)}) %copy-start.1) | copy-done | bytes 262168
  34.8 0.9 %collective-permute-done.9 = f32[8,32,256]{2,1,0:T(8,128)S(1)} collective-permute-done((f32[8,32,256]{2,1,0:T(8,128)S(1)}, f32[8,32,256]{2,1,0:T(8,128)S(1)}, u32[]{:S(2)}, u32[]{:S(2)}) %collective-permute-start.9) | collective-permute-done | bytes 262176 | tf_op jit(solution)/shard_map/ppermute | solution.py:174
  35.7 0.1 copy-done
  35.8 0.6 %copy-done.2 = f32[8,32,256]{2,1,0:T(8,128)} copy-done((f32[8,32,256]{2,1,0:T(8,128)}, f32[8,32,256]{2,1,0:T(8,128)S(1)}, u32[]{:S(2)}) %copy-start.2) | copy-done | bytes 262168
  36.4 10.1 %shard_map.77 = f32[8,4096]{1,0:T(8,128)} custom-call(f32[32]{0:T(128)} %copy-done.5, f32[8,64,512]{2,1,0:T(8,128)} %copy-done, f32[256,256]{1,0:T(8,128)} %bitcast.41, f32[256,256]{1,0:T(8,128)} %bitcast.46), custom_call_target="tpu_custom_call" | custom-call | tf_op jit(solution)/shard_map/pallas_call | solution.py:115
  46.5 0.9 %fusion.15 = f32[4096]{0:T(1024)S(1)} fusion(f32[8,4096]{1,0:T(8,128)} %shard_map.77), kind=kLoop, calls=%fused_computation.44 | loop fusion | flops 4096 | bytes 32768 | tf_op jit(solution)/shard_map/mul | solution.py:228
  47.4 0.1 mul.137
  47.5 0.0 copy-start.3
  47.5 0.1 fusion.16
  47.6 1.6 %collective-permute-start.10 = (f32[64]{0:T(128)S(1)}, f32[64]{0:T(128)S(1)}, u32[]{:S(2)}, u32[]{:S(2)}) collective-permute-start(f32[64]{0:T(128)S(1)} %fusion.16), channel_id=1, source_target_pairs={{0,1},{1,0},{2,3},{3,2},{4,5},{5,4},{6,7},{7,6},{8,9},{9,8},{10,11... | collective-permute-start | bytes 776 | tf_op jit(solution)/shard_map/ppermute | solution.py:231
  49.2 2.0 %collective-permute-done.10 = f32[64]{0:T(128)S(1)} collective-permute-done((f32[64]{0:T(128)S(1)}, f32[64]{0:T(128)S(1)}, u32[]{:S(2)}, u32[]{:S(2)}) %collective-permute-start.10) | collective-permute-done | bytes 288 | tf_op jit(solution)/shard_map/ppermute | solution.py:231
  51.2 0.5 %add_log_fusion = f32[64]{0:T(128)} fusion(f32[64]{0:T(128)S(1)} %fusion.16, f32[64]{0:T(128)S(1)} %collective-permute-done.10), kind=kLoop, calls=%fused_computation.63 | loop fusion | flops 192 | bytes 768 | tf_op jit(solution)/shard_map/log | solution.py:234
  (26 shorter events, 0.4 us)
Async XLA Ops:
  0.7 0.7 %copy-start.9 = (f32[512]{0:T(512)S(1)}, f32[512]{0:T(512)}, u32[]{:S(2)}) copy-start(f32[512]{0:T(512)} %param.7) | copy-start | bytes 6148
  0.7 0.7 %copy-start.8 = (s32[512,1]{0,1:T(1,128)S(1)}, s32[512,1]{0,1:T(1,128)}, u32[]{:S(2)}) copy-start(s32[512,1]{0,1:T(1,128)} %param.8) | copy-start | bytes 6148
  0.7 0.7 %copy-start.7 = (s32[512]{0:T(512)S(1)}, s32[512]{0:T(512)}, u32[]{:S(2)}) copy-start(s32[512]{0:T(512)} %param.9) | copy-start | bytes 6148
  2.8 0.7 %copy-start.4 = (f32[3,512]{1,0:T(4,128)S(1)}, f32[3,512]{1,0:T(4,128)}, u32[]{:S(2)}) copy-start(f32[3,512]{1,0:T(4,128)} %param.10) | copy-start | bytes 18436
  2.8 2.8 %collective-permute-start = (f32[8,32,256]{2,1,0:T(8,128)S(1)}, f32[8,32,256]{2,1,0:T(8,128)S(1)}, u32[]{:S(2)}, u32[]{:S(2)}) collective-permute-start(f32[8,32,256]{2,1,0:T(8,128)S(1)} %dynamic-slice_bitcast_fusion), channel_id=1, source_target_pairs={{0,2},{2,0},{4,6},{6,4},{8,10},{10,8},{12,14},{14,12},{16,18},{18,... | collective-permute-start | bytes 786440 | tf_op jit(solution)/shard_map/ppermute | solution.py:154
  3.5 1.6 %copy-start.5 = (f32[32]{0:T(128)}, f32[32]{0:T(128)S(1)}, u32[]{:S(2)}) copy-start(f32[32]{0:T(128)S(1)} %add_multiply_fusion.wave_ref) | copy-start | bytes 388
  3.7 0.7 %copy-start.6 = (f32[3,64]{1,0:T(4,128)S(1)}, f32[3,64]{1,0:T(4,128)}, u32[]{:S(2)}) copy-start(f32[3,64]{1,0:T(4,128)} %param.11) | copy-start | bytes 2308
  5.7 6.6 %collective-permute-start.1 = (f32[4,32,256]{2,1,0:T(8,128)S(1)}, f32[4,32,256]{2,1,0:T(8,128)S(1)}, u32[]{:S(2)}, u32[]{:S(2)}) collective-permute-start(f32[4,32,256]{2,1,0:T(8,128)S(1)} %dynamic-slice_bitcast_fusion.1), channel_id=1, source_target_pairs={{0,4},{2,6},{4,0},{6,2},{8,12},{10,14},{12,8},{14,10},{16,20},{18,... | collective-permute-start | bytes 393224 | tf_op jit(solution)/shard_map/ppermute | solution.py:154
  12.3 5.5 %collective-permute-start.4 = (f32[32,256]{1,0:T(8,128)S(1)}, f32[32,256]{1,0:T(8,128)S(1)}, u32[]{:S(2)}, u32[]{:S(2)}) collective-permute-start(f32[32,256]{1,0:T(8,128)S(1)} %get-tuple-element.11), channel_id=1, source_target_pairs={{0,24},{2,26},{4,28},{6,30},{8,0},{10,2},{12,4},{14,6},{16,8},{18,... | collective-permute-start | bytes 98312 | tf_op jit(solution)/shard_map/ppermute | solution.py:159
  16.2 4.8 %collective-permute-start.3 = (f32[32,256]{1,0:T(8,128)S(1)}, f32[32,256]{1,0:T(8,128)S(1)}, u32[]{:S(2)}, u32[]{:S(2)}) collective-permute-start(f32[32,256]{1,0:T(8,128)S(1)} %get-tuple-element.12), channel_id=1, source_target_pairs={{0,16},{2,18},{4,20},{6,22},{8,24},{10,26},{12,28},{14,30},{16,0},... | collective-permute-start | bytes 98312 | tf_op jit(solution)/shard_map/ppermute | solution.py:159
  16.2 5.7 %collective-permute-start.2 = (f32[32,256]{1,0:T(8,128)S(1)}, f32[32,256]{1,0:T(8,128)S(1)}, u32[]{:S(2)}, u32[]{:S(2)}) collective-permute-start(f32[32,256]{1,0:T(8,128)S(1)} %get-tuple-element.10), channel_id=1, source_target_pairs={{0,8},{2,10},{4,12},{6,14},{8,16},{10,18},{12,20},{14,22},{16,24},... | collective-permute-start | bytes 98312 | tf_op jit(solution)/shard_map/ppermute | solution.py:159
  22.0 4.3 %collective-permute-start.7 = (f32[32,256]{1,0:T(8,128)S(1)}, f32[32,256]{1,0:T(8,128)S(1)}, u32[]{:S(2)}, u32[]{:S(2)}) collective-permute-start(f32[32,256]{1,0:T(8,128)S(1)} %fusion.13), channel_id=1, source_target_pairs={{0,24},{2,26},{4,28},{6,30},{8,0},{10,2},{12,4},{14,6},{16,8},{18,... | collective-permute-start | bytes 98312 | tf_op jit(solution)/shard_map/ppermute | solution.py:167
  22.7 4.8 %collective-permute-start.6 = (f32[32,256]{1,0:T(8,128)S(1)}, f32[32,256]{1,0:T(8,128)S(1)}, u32[]{:S(2)}, u32[]{:S(2)}) collective-permute-start(f32[32,256]{1,0:T(8,128)S(1)} %fusion.13), channel_id=1, source_target_pairs={{0,16},{2,18},{4,20},{6,22},{8,24},{10,26},{12,28},{14,30},{16,0},... | collective-permute-start | bytes 98312 | tf_op jit(solution)/shard_map/ppermute | solution.py:167
  23.2 5.7 %collective-permute-start.5 = (f32[32,256]{1,0:T(8,128)S(1)}, f32[32,256]{1,0:T(8,128)S(1)}, u32[]{:S(2)}, u32[]{:S(2)}) collective-permute-start(f32[32,256]{1,0:T(8,128)S(1)} %fusion.13), channel_id=1, source_target_pairs={{0,8},{2,10},{4,12},{6,14},{8,16},{10,18},{12,20},{14,22},{16,24},... | collective-permute-start | bytes 98312 | tf_op jit(solution)/shard_map/ppermute | solution.py:167
  29.0 5.0 %collective-permute-start.8 = (f32[4,32,256]{2,1,0:T(8,128)S(1)}, f32[4,32,256]{2,1,0:T(8,128)S(1)}, u32[]{:S(2)}, u32[]{:S(2)}) collective-permute-start(f32[4,32,256]{2,1,0:T(8,128)S(1)} %pad_maximum_fusion.2), channel_id=1, source_target_pairs={{0,4},{2,6},{4,0},{6,2},{8,12},{10,14},{12,8},{14,10},{16,20},{18,... | collective-permute-start | bytes 393224 | tf_op jit(solution)/shard_map/ppermute | solution.py:174
  34.1 0.7 %copy-start.1 = (f32[4,2,32,256]{3,2,1,0:T(8,128)}, f32[4,2,32,256]{3,2,1,0:T(8,128)S(1)}, u32[]{:S(2)}) copy-start(f32[4,2,32,256]{3,2,1,0:T(8,128)S(1)} %pad_maximum_fusion) | copy-start | bytes 786436
  34.1 1.6 %collective-permute-start.9 = (f32[8,32,256]{2,1,0:T(8,128)S(1)}, f32[8,32,256]{2,1,0:T(8,128)S(1)}, u32[]{:S(2)}, u32[]{:S(2)}) collective-permute-start(f32[8,32,256]{2,1,0:T(8,128)S(1)} %bitcast.40), channel_id=1, source_target_pairs={{0,2},{2,0},{4,6},{6,4},{8,10},{10,8},{12,14},{14,12},{16,18},{18,... | collective-permute-start | bytes 786440 | tf_op jit(solution)/shard_map/ppermute | solution.py:174
  34.8 1.0 %copy-start = (f32[8,64,512]{2,1,0:T(8,128)}, f32[8,64,512]{2,1,0:T(8,128)S(1)}, u32[]{:S(2)}) copy-start(f32[8,64,512]{2,1,0:T(8,128)S(1)} %sqrt_dynamic-update-slice_fusion.geo_ref) | copy-start | bytes 3145732
  35.7 0.7 %copy-start.2 = (f32[8,32,256]{2,1,0:T(8,128)}, f32[8,32,256]{2,1,0:T(8,128)S(1)}, u32[]{:S(2)}) copy-start(f32[8,32,256]{2,1,0:T(8,128)S(1)} %collective-permute-done.9) | copy-start | bytes 786436
  47.5 4.2 %copy-start.3 = (f32[32,2,64]{2,1,0:T(2,128)}, f32[32,2,64]{2,1,0:T(2,128)S(1)}, u32[]{:S(2)}) copy-start(f32[32,2,64]{2,1,0:T(2,128)S(1)} %mul.137) | copy-start | bytes 49156
  47.6 3.6 %collective-permute-start.10 = (f32[64]{0:T(128)S(1)}, f32[64]{0:T(128)S(1)}, u32[]{:S(2)}, u32[]{:S(2)}) collective-permute-start(f32[64]{0:T(128)S(1)} %fusion.16), channel_id=1, source_target_pairs={{0,1},{1,0},{2,3},{3,2},{4,5},{5,4},{6,7},{7,6},{8,9},{9,8},{10,11... | collective-permute-start | bytes 776 | tf_op jit(solution)/shard_map/ppermute | solution.py:231

commit v12 on v8

--- a/solution.py
+++ b/solution.py
@@ -129,11 +129,10 @@
     return [(k, ((k // low + shift) % 4) * low + k % low) for k in range(groups)]
 
 
-def halving_sum(blocks, bits):
-    groups = blocks.shape[0]
+def halving_sum(keep_first, send_first, bits, groups):
     place = lax.axis_index("obs")
-    current = blocks
-    for bit in bits:
+    current = keep_first + lax.ppermute(send_first, "obs", partner_pairs(groups, bits[0]))
+    for bit in bits[1:]:
         split = current.reshape((current.shape[0] // 2, 2) + current.shape[1:])
         mine = (place // bit) % 2
         keep = lax.dynamic_index_in_dim(split, mine, 1, keepdims=False)
@@ -172,22 +171,35 @@
     panel_total = panel_position.shape[1]
     panels_dev = panel_total // groups
     weighted = (cell_weight[:, None] * cell_spectra.astype(jnp.float32)).astype(jnp.bfloat16)
-    panel_number = jnp.arange(panel_total, dtype=jnp.int32)[:, None]
-    selector = (
-        (panel_number // panels_dev == cell_owner[:, 0][None, :])
-        & (panel_number % panels_dev == cell_local[None, :])
-    ).astype(jnp.bfloat16)
-    local_source = jnp.dot(selector, weighted, preferred_element_type=jnp.float32)
+    owners = cell_owner[:, 0][None, :]
+    slots = cell_local[None, :]
     group_first = lax.axis_index("freq") * freqs_dev
     wave_numbers = wave_step * (
         (group_first + jnp.arange(freqs_dev, dtype=jnp.int32)).astype(jnp.float32) + 1.0
     )
-    blocks = local_source.reshape(groups, panels_dev, columns)
-    if groups & (groups - 1) == 0 and groups >= 4:
+
+    def source_of(panel_number):
+        selector = (
+            (panel_number // panels_dev == owners) & (panel_number % panels_dev == slots)
+        ).astype(jnp.bfloat16)
+        return jnp.dot(selector, weighted, preferred_element_type=jnp.float32)
+
+    if groups & (groups - 1) == 0 and groups >= 8:
         bits = [1 << k for k in range(groups.bit_length() - 3)]
-        own_source = halving_sum(blocks, bits)
+        mine = lax.axis_index("obs") % 2
+
+        def half_panels(parity):
+            pair = 2 * jnp.arange(groups // 2, dtype=jnp.int32)[:, None] + parity
+            return (pair * panels_dev + jnp.arange(panels_dev, dtype=jnp.int32)[None, :]).reshape(-1, 1)
+
+        send_first = source_of(half_panels(1 - mine)).reshape(groups // 2, panels_dev, columns)
+        keep_first = source_of(half_panels(mine)).reshape(groups // 2, panels_dev, columns)
+        own_source = halving_sum(keep_first, send_first, bits, groups)
         portion = doubling_gather(own_source, bits, groups).reshape(panel_total, columns)
     else:
+        blocks = source_of(jnp.arange(panel_total, dtype=jnp.int32)[:, None]).reshape(
+            groups, panels_dev, columns
+        )
         own_source = jnp.sum(lax.all_to_all(blocks, "obs", 0, 0, tiled=True), axis=0)
         portion = lax.all_to_all(
             jnp.broadcast_to(own_source[None], blocks.shape), "obs", 0, 0, tiled=True

time: 51.9 us -> 52.1 us (level)
    ppermute x2 -> x1, waiting for transfers between devices: 3.69 us -> 3.11 us  [halving_sum(): current = keep + lax.ppermute(send, 'obs', partner_pairs(groups, bit))]
    dot_general x1 -> x2, matrix products: 1.42 us -> 1.69 us  [source_of(): return jnp.dot(selector, weighted, preferred_element_type=jnp.float32)]
    unnamed x16 -> x18, local copies, waits for them, and re-layouts: 1.38 us -> 1.18 us
    ppermute x2 -> x1, starting transfers between devices: 3.09 us -> 3.01 us  [halving_sum(): current = keep + lax.ppermute(send, 'obs', partner_pairs(groups, bit))]
  transfers between devices with their start and end apart: 11 -> 11, of which waited for: 10 -> 10; matrix products, arithmetic and copies ran while one was open for 4% -> 5% of each run, Pallas kernels for 0% -> 0%
where the time goes in v12:
time: 52.1 us; the launch traced here: 51.9 us
  waiting for transfers between devices  17.9 us (34%)
  starting transfers between devices  14.9 us (29%)
  Pallas kernels  9.94 us (19%)
  other arithmetic  4.9 us (9%)
  matrix products  1.69 us (3%)
  local copies, waits for them, and re-layouts  1.52 us (3%)
  between operations  1.1 us (2%)
    pallas_call x1, Pallas kernels, far_field(): pl.pallas_call(functools.partial(field_kernel, math.gcd(observers // 8, 4...  9.94 us
    ppermute x3, starting transfers between devices, halving_sum(): total = total + lax.ppermute(piece, 'obs', quad_pairs(groups, shift))  4.92 us
    ppermute x2, waiting for transfers between devices, doubling_gather(): other = lax.ppermute(gathered, 'obs', partner_pairs(groups, bit))  4.87 us
    ppermute x3, waiting for transfers between devices, halving_sum(): total = total + lax.ppermute(piece, 'obs', quad_pairs(groups, shift))  4.22 us
    ppermute x3, waiting for transfers between devices, doubling_gather(): lax.ppermute(own, 'obs', quad_pairs(groups, shift))  3.65 us
    ppermute x3, starting transfers between devices, doubling_gather(): lax.ppermute(own, 'obs', quad_pairs(groups, shift))  3.2 us
    ppermute x1, waiting for transfers between devices, halving_sum(): current = keep + lax.ppermute(send, 'obs', partner_pairs(groups, bit))  3.11 us
    ppermute x1, starting transfers between devices, halving_sum(): current = keep + lax.ppermute(send, 'obs', partner_pairs(groups, bit))  3.01 us
  transfers between devices with their start and end apart: 11, of which 10 were waited for; matrix products, arithmetic and copies ran while one was open for 5% of the time, Pallas kernels for 0%

profile of v12, /device:TPU:0, one launch (start us, length us, event | category | flops | bytes accessed | tf_op | source)
XLA Modules:
  0.0 51.9 jit_solution(10379441409032984748)
XLA Ops:
  0.7 0.1 iota_add_fusion
  0.7 0.1 add.288
  0.8 0.1 iota_add_fusion.1
  0.9 0.1 add.281
  1.0 0.0 copy-start.7
  1.0 0.0 copy-start.6
  1.0 0.6 %copy-done.8 = f32[512]{0:T(512)S(1)} copy-done((f32[512]{0:T(512)S(1)}, f32[512]{0:T(512)}, u32[]{:S(2)}) %copy-start.8) | copy-done | bytes 2072
  1.7 0.0 copy-done.7
  1.7 0.0 copy-done.6
  1.7 1.3 %fusion = f32[256,256]{1,0:T(8,128)S(1)} fusion(s32[512]{0:T(512)S(1)} %copy-done.6, s32[512]{0:T(512)S(1)} %bitcast.54, s32[256]{0:T(256)S(1)} %get-tuple-element.16, s32[256]{0:T(256)S(1)} %get-tuple-element.15, bf16[512,256]{1,0:T(8,128)(2,1)} %param.6, f32[512]{0:T(512)S(1)} %copy-done.8), kind=kOutput, calls=%fused_computation.2 | convolution fusion | flops 67895296 | bytes 532480 | tf_op jit(solution)/shard_map/dot_general | solution.py:185
  3.0 0.0 copy-start.2
  3.0 0.5 %collective-permute-start = (f32[8,32,256]{2,1,0:T(8,128)S(1)}, f32[8,32,256]{2,1,0:T(8,128)S(1)}, u32[]{:S(2)}, u32[]{:S(2)}) collective-permute-start(f32[8,32,256]{2,1,0:T(8,128)S(1)} %bitcast.53), channel_id=1, source_target_pairs={{0,2},{2,0},{4,6},{6,4},{8,10},{10,8},{12,14},{14,12},{16,18},{18,... | collective-permute-start | bytes 786440 | tf_op jit(solution)/shard_map/ppermute | solution.py:134
  3.6 0.2 copy-done.2
  3.7 0.1 broadcast_subtract_fusion
  3.8 0.5 %multiply_dynamic-update-slice_fusion.1 = (f32[8,64,512]{2,1,0:T(8,128)S(1)}, f32[1,64,512]{2,1,0:T(8,128)S(1)}) fusion(f32[]{:T(128)S(1)} %bitcast.51, f32[3,64,512]{2,1,0:T(8,128)S(1)} %broadcast_subtract_fusion), kind=kLoop, calls=%fused_computation.37 | loop fusion | flops 262143 | bytes 655364
  4.4 0.0 copy-start.5
  4.4 0.5 multiply_dynamic-update-slice_fusion
  5.0 0.3 copy-done.5
  5.3 0.4 fusion.4
  5.8 3.0 %collective-permute-start.1 = (f32[4,32,256]{2,1,0:T(8,128)S(1)}, f32[4,32,256]{2,1,0:T(8,128)S(1)}, u32[]{:S(2)}, u32[]{:S(2)}) collective-permute-start(f32[4,32,256]{2,1,0:T(8,128)S(1)} %dynamic-slice_bitcast_fusion), channel_id=1, source_target_pairs={{0,4},{2,6},{4,0},{6,2},{8,12},{10,14},{12,8},{14,10},{16,20},{18,... | collective-permute-start | bytes 393224 | tf_op jit(solution)/shard_map/ppermute | solution.py:140
  8.8 0.5 cosine_dynamic-update-slice_fusion
  9.2 3.1 %collective-permute-done.1 = f32[4,32,256]{2,1,0:T(8,128)S(1)} collective-permute-done((f32[4,32,256]{2,1,0:T(8,128)S(1)}, f32[4,32,256]{2,1,0:T(8,128)S(1)}, u32[]{:S(2)}, u32[]{:S(2)}) %collective-permute-start.1) | collective-permute-done | bytes 131104 | tf_op jit(solution)/shard_map/ppermute | solution.py:140
  12.4 3.9 %collective-permute-start.4 = (f32[32,256]{1,0:T(8,128)S(1)}, f32[32,256]{1,0:T(8,128)S(1)}, u32[]{:S(2)}, u32[]{:S(2)}) collective-permute-start(f32[32,256]{1,0:T(8,128)S(1)} %get-tuple-element.13), channel_id=1, source_target_pairs={{0,24},{2,26},{4,28},{6,30},{8,0},{10,2},{12,4},{14,6},{16,8},{18,... | collective-permute-start | bytes 98312 | tf_op jit(solution)/shard_map/ppermute | solution.py:145
  16.3 1.0 %collective-permute-start.2 = (f32[32,256]{1,0:T(8,128)S(1)}, f32[32,256]{1,0:T(8,128)S(1)}, u32[]{:S(2)}, u32[]{:S(2)}) collective-permute-start(f32[32,256]{1,0:T(8,128)S(1)} %get-tuple-element.12), channel_id=1, source_target_pairs={{0,8},{2,10},{4,12},{6,14},{8,16},{10,18},{12,20},{14,22},{16,24},... | collective-permute-start | bytes 98312 | tf_op jit(solution)/shard_map/ppermute | solution.py:145
  17.3 0.5 sine_dynamic-update-slice_fusion
  17.8 0.1 collective-permute-done.4
  17.9 3.2 %collective-permute-done.3 = f32[32,256]{1,0:T(8,128)S(1)} collective-permute-done((f32[32,256]{1,0:T(8,128)S(1)}, f32[32,256]{1,0:T(8,128)S(1)}, u32[]{:S(2)}, u32[]{:S(2)}) %collective-permute-start.3) | collective-permute-done | bytes 32800 | tf_op jit(solution)/shard_map/ppermute | solution.py:145
  21.1 0.9 %collective-permute-done.2 = f32[32,256]{1,0:T(8,128)S(1)} collective-permute-done((f32[32,256]{1,0:T(8,128)S(1)}, f32[32,256]{1,0:T(8,128)S(1)}, u32[]{:S(2)}, u32[]{:S(2)}) %collective-permute-start.2) | collective-permute-done | bytes 32800 | tf_op jit(solution)/shard_map/ppermute | solution.py:145
  22.0 0.7 %collective-permute-start.7 = (f32[32,256]{1,0:T(8,128)S(1)}, f32[32,256]{1,0:T(8,128)S(1)}, u32[]{:S(2)}, u32[]{:S(2)}) collective-permute-start(f32[32,256]{1,0:T(8,128)S(1)} %fusion.20), channel_id=1, source_target_pairs={{0,24},{2,26},{4,28},{6,30},{8,0},{10,2},{12,4},{14,6},{16,8},{18,... | collective-permute-start | bytes 98312 | tf_op jit(solution)/shard_map/ppermute | solution.py:153
  22.7 0.6 %collective-permute-start.6 = (f32[32,256]{1,0:T(8,128)S(1)}, f32[32,256]{1,0:T(8,128)S(1)}, u32[]{:S(2)}, u32[]{:S(2)}) collective-permute-start(f32[32,256]{1,0:T(8,128)S(1)} %fusion.20), channel_id=1, source_target_pairs={{0,16},{2,18},{4,20},{6,22},{8,24},{10,26},{12,28},{14,30},{16,0},... | collective-permute-start | bytes 98312 | tf_op jit(solution)/shard_map/ppermute | solution.py:153
  23.3 1.9 %collective-permute-start.5 = (f32[32,256]{1,0:T(8,128)S(1)}, f32[32,256]{1,0:T(8,128)S(1)}, u32[]{:S(2)}, u32[]{:S(2)}) collective-permute-start(f32[32,256]{1,0:T(8,128)S(1)} %fusion.20), channel_id=1, source_target_pairs={{0,8},{2,10},{4,12},{6,14},{8,16},{10,18},{12,20},{14,22},{16,24},... | collective-permute-start | bytes 98312 | tf_op jit(solution)/shard_map/ppermute | solution.py:153
  25.4 1.0 %collective-permute-done.7 = f32[32,256]{1,0:T(8,128)S(1)} collective-permute-done((f32[32,256]{1,0:T(8,128)S(1)}, f32[32,256]{1,0:T(8,128)S(1)}, u32[]{:S(2)}, u32[]{:S(2)}) %collective-permute-start.7) | collective-permute-done | bytes 32800 | tf_op jit(solution)/shard_map/ppermute | solution.py:153
  26.4 1.2 %collective-permute-done.6 = f32[32,256]{1,0:T(8,128)S(1)} collective-permute-done((f32[32,256]{1,0:T(8,128)S(1)}, f32[32,256]{1,0:T(8,128)S(1)}, u32[]{:S(2)}, u32[]{:S(2)}) %collective-permute-start.6) | collective-permute-done | bytes 32800 | tf_op jit(solution)/shard_map/ppermute | solution.py:153
  27.5 1.5 %collective-permute-done.5 = f32[32,256]{1,0:T(8,128)S(1)} collective-permute-done((f32[32,256]{1,0:T(8,128)S(1)}, f32[32,256]{1,0:T(8,128)S(1)}, u32[]{:S(2)}, u32[]{:S(2)}) %collective-permute-start.5) | collective-permute-done | bytes 32800 | tf_op jit(solution)/shard_map/ppermute | solution.py:153
  29.1 1.6 %collective-permute-start.8 = (f32[4,32,256]{2,1,0:T(8,128)S(1)}, f32[4,32,256]{2,1,0:T(8,128)S(1)}, u32[]{:S(2)}, u32[]{:S(2)}) collective-permute-start(f32[4,32,256]{2,1,0:T(8,128)S(1)} %pad_maximum_fusion.3), channel_id=1, source_target_pairs={{0,4},{2,6},{4,0},{6,2},{8,12},{10,14},{12,8},{14,10},{16,20},{18,... | collective-permute-start | bytes 393224 | tf_op jit(solution)/shard_map/ppermute | solution.py:160
  30.6 3.4 %collective-permute-done.8 = f32[4,32,256]{2,1,0:T(8,128)S(1)} collective-permute-done((f32[4,32,256]{2,1,0:T(8,128)S(1)}, f32[4,32,256]{2,1,0:T(8,128)S(1)}, u32[]{:S(2)}, u32[]{:S(2)}) %collective-permute-start.8) | collective-permute-done | bytes 131104 | tf_op jit(solution)/shard_map/ppermute | solution.py:160
  34.1 0.1 collective-permute-start.9
  34.3 1.4 %collective-permute-done.9 = f32[8,32,256]{2,1,0:T(8,128)S(1)} collective-permute-done((f32[8,32,256]{2,1,0:T(8,128)S(1)}, f32[8,32,256]{2,1,0:T(8,128)S(1)}, u32[]{:S(2)}, u32[]{:S(2)}) %collective-permute-start.9) | collective-permute-done | bytes 262176 | tf_op jit(solution)/shard_map/ppermute | solution.py:160
  35.8 0.1 select_bitcast_fusion.1
  35.8 0.9 %pad_maximum_fusion = f32[8,2,32,256]{3,2,1,0:T(8,128)} fusion(f32[8,1,32,256]{3,2,1,0:T(8,128)S(1)} %get-tuple-element.5, f32[8,1,32,256]{3,2,1,0:T(8,128)S(1)} %get-tuple-element.4), kind=kLoop, calls=%fused_computation | loop fusion | flops 131072 | bytes 1048576 | tf_op jit(solution)/shard_map/stack | solution.py:163
  36.7 9.9 %shard_map.77 = f32[8,4096]{1,0:T(8,128)} custom-call(f32[32]{0:T(128)} %copy-done.3, f32[8,64,512]{2,1,0:T(8,128)} %copy-done, f32[512,256]{1,0:T(8,128)} %bitcast.42), custom_call_target="tpu_custom_call" | custom-call | tf_op jit(solution)/shard_map/pallas_call | solution.py:103
  46.6 0.9 %fusion.22 = f32[4096]{0:T(1024)S(1)} fusion(f32[8,4096]{1,0:T(8,128)} %shard_map.77), kind=kLoop, calls=%fused_computation.51 | loop fusion | flops 4096 | bytes 32768 | tf_op jit(solution)/shard_map/mul | solution.py:208
  47.6 0.1 mul.170
  47.7 0.0 copy-start.1
  47.7 0.1 fusion.23
  47.7 1.6 %collective-permute-start.10 = (f32[64]{0:T(128)S(1)}, f32[64]{0:T(128)S(1)}, u32[]{:S(2)}, u32[]{:S(2)}) collective-permute-start(f32[64]{0:T(128)S(1)} %fusion.23), channel_id=1, source_target_pairs={{0,1},{1,0},{2,3},{3,2},{4,5},{5,4},{6,7},{7,6},{8,9},{9,8},{10,11... | collective-permute-start | bytes 776 | tf_op jit(solution)/shard_map/ppermute | solution.py:211
  49.3 2.0 %collective-permute-done.10 = f32[64]{0:T(128)S(1)} collective-permute-done((f32[64]{0:T(128)S(1)}, f32[64]{0:T(128)S(1)}, u32[]{:S(2)}, u32[]{:S(2)}) %collective-permute-start.10) | collective-permute-done | bytes 288 | tf_op jit(solution)/shard_map/ppermute | solution.py:211
  51.3 0.5 %add_log_fusion = f32[64]{0:T(128)} fusion(f32[64]{0:T(128)S(1)} %fusion.23, f32[64]{0:T(128)S(1)} %collective-permute-done.10), kind=kLoop, calls=%fused_computation.69 | loop fusion | flops 192 | bytes 768 | tf_op jit(solution)/shard_map/log | solution.py:214
  (28 shorter events, 0.4 us)
Async XLA Ops:
  1.0 0.7 %copy-start.8 = (f32[512]{0:T(512)S(1)}, f32[512]{0:T(512)}, u32[]{:S(2)}) copy-start(f32[512]{0:T(512)} %param.7) | copy-start | bytes 6148
  1.0 0.7 %copy-start.7 = (s32[512,1]{0,1:T(1,128)S(1)}, s32[512,1]{0,1:T(1,128)}, u32[]{:S(2)}) copy-start(s32[512,1]{0,1:T(1,128)} %param.8) | copy-start | bytes 6148
  1.0 0.7 %copy-start.6 = (s32[512]{0:T(512)S(1)}, s32[512]{0:T(512)}, u32[]{:S(2)}) copy-start(s32[512]{0:T(512)} %param.9) | copy-start | bytes 6148
  1.7 1.9 %copy-start.4 = (f32[3,64]{1,0:T(4,128)S(1)}, f32[3,64]{1,0:T(4,128)}, u32[]{:S(2)}) copy-start(f32[3,64]{1,0:T(4,128)} %param.11) | copy-start | bytes 2308
  3.0 0.7 %copy-start.2 = (f32[3,512]{1,0:T(4,128)S(1)}, f32[3,512]{1,0:T(4,128)}, u32[]{:S(2)}) copy-start(f32[3,512]{1,0:T(4,128)} %param.10) | copy-start | bytes 18436
  3.0 2.6 %collective-permute-start = (f32[8,32,256]{2,1,0:T(8,128)S(1)}, f32[8,32,256]{2,1,0:T(8,128)S(1)}, u32[]{:S(2)}, u32[]{:S(2)}) collective-permute-start(f32[8,32,256]{2,1,0:T(8,128)S(1)} %bitcast.53), channel_id=1, source_target_pairs={{0,2},{2,0},{4,6},{6,4},{8,10},{10,8},{12,14},{14,12},{16,18},{18,... | collective-permute-start | bytes 786440 | tf_op jit(solution)/shard_map/ppermute | solution.py:134
  3.7 0.7 %copy-start.3 = (f32[32]{0:T(128)}, f32[32]{0:T(128)S(1)}, u32[]{:S(2)}) copy-start(f32[32]{0:T(128)S(1)} %add_multiply_fusion.2.wave_ref) | copy-start | bytes 388
  4.4 1.0 %copy-start.5 = (bf16[512,256]{1,0:T(8,128)(2,1)S(1)}, bf16[512,256]{1,0:T(8,128)(2,1)}, u32[]{:S(2)}) copy-start(bf16[512,256]{1,0:T(8,128)(2,1)} %param.6) | copy-start | bytes 786436
  5.8 6.6 %collective-permute-start.1 = (f32[4,32,256]{2,1,0:T(8,128)S(1)}, f32[4,32,256]{2,1,0:T(8,128)S(1)}, u32[]{:S(2)}, u32[]{:S(2)}) collective-permute-start(f32[4,32,256]{2,1,0:T(8,128)S(1)} %dynamic-slice_bitcast_fusion), channel_id=1, source_target_pairs={{0,4},{2,6},{4,0},{6,2},{8,12},{10,14},{12,8},{14,10},{16,20},{18,... | collective-permute-start | bytes 393224 | tf_op jit(solution)/shard_map/ppermute | solution.py:140
  12.4 5.5 %collective-permute-start.4 = (f32[32,256]{1,0:T(8,128)S(1)}, f32[32,256]{1,0:T(8,128)S(1)}, u32[]{:S(2)}, u32[]{:S(2)}) collective-permute-start(f32[32,256]{1,0:T(8,128)S(1)} %get-tuple-element.13), channel_id=1, source_target_pairs={{0,24},{2,26},{4,28},{6,30},{8,0},{10,2},{12,4},{14,6},{16,8},{18,... | collective-permute-start | bytes 98312 | tf_op jit(solution)/shard_map/ppermute | solution.py:145
  16.3 4.8 %collective-permute-start.3 = (f32[32,256]{1,0:T(8,128)S(1)}, f32[32,256]{1,0:T(8,128)S(1)}, u32[]{:S(2)}, u32[]{:S(2)}) collective-permute-start(f32[32,256]{1,0:T(8,128)S(1)} %get-tuple-element.14), channel_id=1, source_target_pairs={{0,16},{2,18},{4,20},{6,22},{8,24},{10,26},{12,28},{14,30},{16,0},... | collective-permute-start | bytes 98312 | tf_op jit(solution)/shard_map/ppermute | solution.py:145
  16.3 5.7 %collective-permute-start.2 = (f32[32,256]{1,0:T(8,128)S(1)}, f32[32,256]{1,0:T(8,128)S(1)}, u32[]{:S(2)}, u32[]{:S(2)}) collective-permute-start(f32[32,256]{1,0:T(8,128)S(1)} %get-tuple-element.12), channel_id=1, source_target_pairs={{0,8},{2,10},{4,12},{6,14},{8,16},{10,18},{12,20},{14,22},{16,24},... | collective-permute-start | bytes 98312 | tf_op jit(solution)/shard_map/ppermute | solution.py:145
  22.0 4.3 %collective-permute-start.7 = (f32[32,256]{1,0:T(8,128)S(1)}, f32[32,256]{1,0:T(8,128)S(1)}, u32[]{:S(2)}, u32[]{:S(2)}) collective-permute-start(f32[32,256]{1,0:T(8,128)S(1)} %fusion.20), channel_id=1, source_target_pairs={{0,24},{2,26},{4,28},{6,30},{8,0},{10,2},{12,4},{14,6},{16,8},{18,... | collective-permute-start | bytes 98312 | tf_op jit(solution)/shard_map/ppermute | solution.py:153
  22.7 4.8 %collective-permute-start.6 = (f32[32,256]{1,0:T(8,128)S(1)}, f32[32,256]{1,0:T(8,128)S(1)}, u32[]{:S(2)}, u32[]{:S(2)}) collective-permute-start(f32[32,256]{1,0:T(8,128)S(1)} %fusion.20), channel_id=1, source_target_pairs={{0,16},{2,18},{4,20},{6,22},{8,24},{10,26},{12,28},{14,30},{16,0},... | collective-permute-start | bytes 98312 | tf_op jit(solution)/shard_map/ppermute | solution.py:153
  23.3 5.7 %collective-permute-start.5 = (f32[32,256]{1,0:T(8,128)S(1)}, f32[32,256]{1,0:T(8,128)S(1)}, u32[]{:S(2)}, u32[]{:S(2)}) collective-permute-start(f32[32,256]{1,0:T(8,128)S(1)} %fusion.20), channel_id=1, source_target_pairs={{0,8},{2,10},{4,12},{6,14},{8,16},{10,18},{12,20},{14,22},{16,24},... | collective-permute-start | bytes 98312 | tf_op jit(solution)/shard_map/ppermute | solution.py:153
  29.1 5.0 %collective-permute-start.8 = (f32[4,32,256]{2,1,0:T(8,128)S(1)}, f32[4,32,256]{2,1,0:T(8,128)S(1)}, u32[]{:S(2)}, u32[]{:S(2)}) collective-permute-start(f32[4,32,256]{2,1,0:T(8,128)S(1)} %pad_maximum_fusion.3), channel_id=1, source_target_pairs={{0,4},{2,6},{4,0},{6,2},{8,12},{10,14},{12,8},{14,10},{16,20},{18,... | collective-permute-start | bytes 393224 | tf_op jit(solution)/shard_map/ppermute | solution.py:160
  34.1 1.6 %collective-permute-start.9 = (f32[8,32,256]{2,1,0:T(8,128)S(1)}, f32[8,32,256]{2,1,0:T(8,128)S(1)}, u32[]{:S(2)}, u32[]{:S(2)}) collective-permute-start(f32[8,32,256]{2,1,0:T(8,128)S(1)} %bitcast.45), channel_id=1, source_target_pairs={{0,2},{2,0},{4,6},{6,4},{8,10},{10,8},{12,14},{14,12},{16,18},{18,... | collective-permute-start | bytes 786440 | tf_op jit(solution)/shard_map/ppermute | solution.py:160
  34.3 2.4 %copy-start = (f32[8,64,512]{2,1,0:T(8,128)}, f32[8,64,512]{2,1,0:T(8,128)S(1)}, u32[]{:S(2)}) copy-start(f32[8,64,512]{2,1,0:T(8,128)S(1)} %sqrt_dynamic-update-slice_fusion.geo_ref) | copy-start | bytes 3145732
  47.7 4.2 %copy-start.1 = (f32[32,2,64]{2,1,0:T(2,128)}, f32[32,2,64]{2,1,0:T(2,128)S(1)}, u32[]{:S(2)}) copy-start(f32[32,2,64]{2,1,0:T(2,128)S(1)} %mul.170) | copy-start | bytes 49156
  47.7 3.6 %collective-permute-start.10 = (f32[64]{0:T(128)S(1)}, f32[64]{0:T(128)S(1)}, u32[]{:S(2)}, u32[]{:S(2)}) collective-permute-start(f32[64]{0:T(128)S(1)} %fusion.23), channel_id=1, source_target_pairs={{0,1},{1,0},{2,3},{3,2},{4,5},{5,4},{6,7},{7,6},{8,9},{9,8},{10,11... | collective-permute-start | bytes 776 | tf_op jit(solution)/shard_map/ppermute | solution.py:211

commit v13 on v8

--- a/solution.py
+++ b/solution.py
@@ -70,8 +70,10 @@
     @pl.when(pl.program_id(0) == pl.num_programs(0) - 1)
     def _():
         flat = acc_ref[...].reshape(freqs * 2 * observers, lanes)
+        spread = lax.broadcasted_iota(jnp.int32, (8, lanes), 1) // (lanes // 8)
+        rows = lax.broadcasted_iota(jnp.int32, (8, lanes), 0)
         out_ref[...] = lax.dot_general(
-            jnp.ones((8, lanes), jnp.float32),
+            (spread == rows).astype(jnp.float32),
             flat,
             (((1,), (1,)), ((), ())),
             precision=lax.Precision.HIGHEST,
@@ -117,7 +119,7 @@
         ],
         compiler_params=pltpu.CompilerParams(dimension_semantics=("arbitrary",)),
     )(wave_numbers, geometry, portion)
-    return summed[0].reshape(freqs, 2, observers)
+    return jnp.sum(summed, axis=0).reshape(freqs, 2, observers)
 
 
 def partner_pairs(groups, bit):

time: 51.9 us -> 51.9 us (level)
    mul x1, other arithmetic: 0.95 us -> 0.01 us  [shards(): pressure = summed * (reference_radius / math.sqrt(panel_total))]
    reduce_sum x0 -> x1, other arithmetic: none -> 0.94 us  [far_field(): return jnp.sum(summed, axis=0).reshape(freqs, 2, observers)]
where the time goes in v13:
time: 51.9 us; the launch traced here: 51.6 us
  waiting for transfers between devices  18.4 us (35%)
  starting transfers between devices  14.4 us (28%)
  Pallas kernels  9.93 us (19%)
  other arithmetic  4.73 us (9%)
  local copies, waits for them, and re-layouts  1.59 us (3%)
  matrix products  1.42 us (3%)
  between operations  1.12 us (2%)
    pallas_call x1, Pallas kernels, far_field(): pl.pallas_call(functools.partial(field_kernel, math.gcd(observers // 8, 4...  9.93 us
    ppermute x3, starting transfers between devices, halving_sum(): total = total + lax.ppermute(piece, 'obs', quad_pairs(groups, shift))  4.91 us
    ppermute x2, waiting for transfers between devices, doubling_gather(): other = lax.ppermute(gathered, 'obs', partner_pairs(groups, bit))  4.87 us
    ppermute x3, waiting for transfers between devices, halving_sum(): total = total + lax.ppermute(piece, 'obs', quad_pairs(groups, shift))  4.22 us
    ppermute x2, waiting for transfers between devices, halving_sum(): current = keep + lax.ppermute(send, 'obs', partner_pairs(groups, bit))  3.69 us
    ppermute x3, waiting for transfers between devices, doubling_gather(): lax.ppermute(own, 'obs', quad_pairs(groups, shift))  3.65 us
    ppermute x3, starting transfers between devices, doubling_gather(): lax.ppermute(own, 'obs', quad_pairs(groups, shift))  3.2 us
    ppermute x2, starting transfers between devices, halving_sum(): current = keep + lax.ppermute(send, 'obs', partner_pairs(groups, bit))  3.09 us
  transfers between devices with their start and end apart: 11, of which 10 were waited for; matrix products, arithmetic and copies ran while one was open for 4% of the time, Pallas kernels for 0%

profile of v13, /device:TPU:0, one launch (start us, length us, event | category | flops | bytes accessed | tf_op | source)
XLA Modules:
  0.0 51.6 jit_solution(7438601884769091762)
XLA Ops:
  0.7 0.0 copy-start.7
  0.7 0.0 copy-start.6
  0.7 0.0 copy-start.5
  0.7 0.6 %copy-done.7 = f32[512]{0:T(512)S(1)} copy-done((f32[512]{0:T(512)S(1)}, f32[512]{0:T(512)}, u32[]{:S(2)}) %copy-start.7) | copy-done | bytes 2072
  1.3 0.0 copy-done.6
  1.4 0.0 copy-done.5
  1.4 1.4 %fusion = f32[512,256]{1,0:T(8,128)S(1)} fusion(s32[512]{0:T(512)S(1)} %copy-done.5, s32[512]{0:T(512)S(1)} %bitcast.57, s32[512]{0:T(512)S(1)} %get-tuple-element.15, s32[512]{0:T(512)S(1)} %get-tuple-element.16, bf16[512,256]{1,0:T(8,128)(2,1)} %param.6, f32[512]{0:T(512)S(1)} %copy-done.7), kind=kOutput, calls=%fused_computation | convolution fusion | flops 135397376 | bytes 796672 | tf_op jit(solution)/shard_map/dot_general | solution.py:182
  2.8 0.0 copy-start.2
  2.8 0.5 %collective-permute-start = (f32[8,32,256]{2,1,0:T(8,128)S(1)}, f32[8,32,256]{2,1,0:T(8,128)S(1)}, u32[]{:S(2)}, u32[]{:S(2)}) collective-permute-start(f32[8,32,256]{2,1,0:T(8,128)S(1)} %dynamic-slice_bitcast_fusion), channel_id=1, source_target_pairs={{0,2},{2,0},{4,6},{6,4},{8,10},{10,8},{12,14},{14,12},{16,18},{18,... | collective-permute-start | bytes 786440 | tf_op jit(solution)/shard_map/ppermute | solution.py:143
  3.4 0.1 copy-done.2
  3.5 0.5 %copy-done.4 = f32[3,64]{1,0:T(4,128)S(1)} copy-done((f32[3,64]{1,0:T(4,128)S(1)}, f32[3,64]{1,0:T(4,128)}, u32[]{:S(2)}) %copy-start.4) | copy-done | bytes 792
  4.1 0.1 broadcast_subtract_fusion
  4.1 0.5 %multiply_dynamic-update-slice_fusion.1 = (f32[8,64,512]{2,1,0:T(8,128)S(1)}, f32[1,64,512]{2,1,0:T(8,128)S(1)}) fusion(f32[]{:T(128)S(1)} %bitcast.55, f32[3,64,512]{2,1,0:T(8,128)S(1)} %broadcast_subtract_fusion), kind=kLoop, calls=%fused_computation.32 | loop fusion | flops 262143 | bytes 655364
  4.8 0.0 copy-done.3
  4.8 0.5 multiply_dynamic-update-slice_fusion
  5.3 0.0 collective-permute-done
  5.4 2.6 %collective-permute-start.1 = (f32[4,32,256]{2,1,0:T(8,128)S(1)}, f32[4,32,256]{2,1,0:T(8,128)S(1)}, u32[]{:S(2)}, u32[]{:S(2)}) collective-permute-start(f32[4,32,256]{2,1,0:T(8,128)S(1)} %dynamic-slice_bitcast_fusion.1), channel_id=1, source_target_pairs={{0,4},{2,6},{4,0},{6,2},{8,12},{10,14},{12,8},{14,10},{16,20},{18,... | collective-permute-start | bytes 393224 | tf_op jit(solution)/shard_map/ppermute | solution.py:143
  8.0 0.5 cosine_dynamic-update-slice_fusion
  8.5 3.7 %collective-permute-done.1 = f32[4,32,256]{2,1,0:T(8,128)S(1)} collective-permute-done((f32[4,32,256]{2,1,0:T(8,128)S(1)}, f32[4,32,256]{2,1,0:T(8,128)S(1)}, u32[]{:S(2)}, u32[]{:S(2)}) %collective-permute-start.1) | collective-permute-done | bytes 131104 | tf_op jit(solution)/shard_map/ppermute | solution.py:143
  12.2 3.9 %collective-permute-start.4 = (f32[32,256]{1,0:T(8,128)S(1)}, f32[32,256]{1,0:T(8,128)S(1)}, u32[]{:S(2)}, u32[]{:S(2)}) collective-permute-start(f32[32,256]{1,0:T(8,128)S(1)} %get-tuple-element.13), channel_id=1, source_target_pairs={{0,24},{2,26},{4,28},{6,30},{8,0},{10,2},{12,4},{14,6},{16,8},{18,... | collective-permute-start | bytes 98312 | tf_op jit(solution)/shard_map/ppermute | solution.py:148
  16.1 0.0 collective-permute-start.3
  16.1 1.0 %collective-permute-start.2 = (f32[32,256]{1,0:T(8,128)S(1)}, f32[32,256]{1,0:T(8,128)S(1)}, u32[]{:S(2)}, u32[]{:S(2)}) collective-permute-start(f32[32,256]{1,0:T(8,128)S(1)} %get-tuple-element.12), channel_id=1, source_target_pairs={{0,8},{2,10},{4,12},{6,14},{8,16},{10,18},{12,20},{14,22},{16,24},... | collective-permute-start | bytes 98312 | tf_op jit(solution)/shard_map/ppermute | solution.py:148
  17.1 0.5 sine_dynamic-update-slice_fusion
  17.6 0.1 collective-permute-done.4
  17.7 3.2 %collective-permute-done.3 = f32[32,256]{1,0:T(8,128)S(1)} collective-permute-done((f32[32,256]{1,0:T(8,128)S(1)}, f32[32,256]{1,0:T(8,128)S(1)}, u32[]{:S(2)}, u32[]{:S(2)}) %collective-permute-start.3) | collective-permute-done | bytes 32800 | tf_op jit(solution)/shard_map/ppermute | solution.py:148
  20.9 0.9 %collective-permute-done.2 = f32[32,256]{1,0:T(8,128)S(1)} collective-permute-done((f32[32,256]{1,0:T(8,128)S(1)}, f32[32,256]{1,0:T(8,128)S(1)}, u32[]{:S(2)}, u32[]{:S(2)}) %collective-permute-start.2) | collective-permute-done | bytes 32800 | tf_op jit(solution)/shard_map/ppermute | solution.py:148
  21.8 0.6 %collective-permute-start.7 = (f32[32,256]{1,0:T(8,128)S(1)}, f32[32,256]{1,0:T(8,128)S(1)}, u32[]{:S(2)}, u32[]{:S(2)}) collective-permute-start(f32[32,256]{1,0:T(8,128)S(1)} %fusion.13), channel_id=1, source_target_pairs={{0,24},{2,26},{4,28},{6,30},{8,0},{10,2},{12,4},{14,6},{16,8},{18,... | collective-permute-start | bytes 98312 | tf_op jit(solution)/shard_map/ppermute | solution.py:156
  22.4 0.6 %collective-permute-start.6 = (f32[32,256]{1,0:T(8,128)S(1)}, f32[32,256]{1,0:T(8,128)S(1)}, u32[]{:S(2)}, u32[]{:S(2)}) collective-permute-start(f32[32,256]{1,0:T(8,128)S(1)} %fusion.13), channel_id=1, source_target_pairs={{0,16},{2,18},{4,20},{6,22},{8,24},{10,26},{12,28},{14,30},{16,0},... | collective-permute-start | bytes 98312 | tf_op jit(solution)/shard_map/ppermute | solution.py:156
  23.1 1.9 %collective-permute-start.5 = (f32[32,256]{1,0:T(8,128)S(1)}, f32[32,256]{1,0:T(8,128)S(1)}, u32[]{:S(2)}, u32[]{:S(2)}) collective-permute-start(f32[32,256]{1,0:T(8,128)S(1)} %fusion.13), channel_id=1, source_target_pairs={{0,8},{2,10},{4,12},{6,14},{8,16},{10,18},{12,20},{14,22},{16,24},... | collective-permute-start | bytes 98312 | tf_op jit(solution)/shard_map/ppermute | solution.py:156
  25.1 0.7 %collective-permute-done.7 = f32[32,256]{1,0:T(8,128)S(1)} collective-permute-done((f32[32,256]{1,0:T(8,128)S(1)}, f32[32,256]{1,0:T(8,128)S(1)}, u32[]{:S(2)}, u32[]{:S(2)}) %collective-permute-start.7) | collective-permute-done | bytes 32800 | tf_op jit(solution)/shard_map/ppermute | solution.py:156
  25.8 1.5 %collective-permute-done.6 = f32[32,256]{1,0:T(8,128)S(1)} collective-permute-done((f32[32,256]{1,0:T(8,128)S(1)}, f32[32,256]{1,0:T(8,128)S(1)}, u32[]{:S(2)}, u32[]{:S(2)}) %collective-permute-start.6) | collective-permute-done | bytes 32800 | tf_op jit(solution)/shard_map/ppermute | solution.py:156
  27.2 1.5 %collective-permute-done.5 = f32[32,256]{1,0:T(8,128)S(1)} collective-permute-done((f32[32,256]{1,0:T(8,128)S(1)}, f32[32,256]{1,0:T(8,128)S(1)}, u32[]{:S(2)}, u32[]{:S(2)}) %collective-permute-start.5) | collective-permute-done | bytes 32800 | tf_op jit(solution)/shard_map/ppermute | solution.py:156
  28.8 1.6 %collective-permute-start.8 = (f32[4,32,256]{2,1,0:T(8,128)S(1)}, f32[4,32,256]{2,1,0:T(8,128)S(1)}, u32[]{:S(2)}, u32[]{:S(2)}) collective-permute-start(f32[4,32,256]{2,1,0:T(8,128)S(1)} %pad_maximum_fusion.3), channel_id=1, source_target_pairs={{0,4},{2,6},{4,0},{6,2},{8,12},{10,14},{12,8},{14,10},{16,20},{18,... | collective-permute-start | bytes 393224 | tf_op jit(solution)/shard_map/ppermute | solution.py:163
  30.4 3.4 %collective-permute-done.8 = f32[4,32,256]{2,1,0:T(8,128)S(1)} collective-permute-done((f32[4,32,256]{2,1,0:T(8,128)S(1)}, f32[4,32,256]{2,1,0:T(8,128)S(1)}, u32[]{:S(2)}, u32[]{:S(2)}) %collective-permute-start.8) | collective-permute-done | bytes 131104 | tf_op jit(solution)/shard_map/ppermute | solution.py:163
  33.9 0.1 collective-permute-start.9
  34.1 0.0 copy-start
  34.1 1.4 %collective-permute-done.9 = f32[8,32,256]{2,1,0:T(8,128)S(1)} collective-permute-done((f32[8,32,256]{2,1,0:T(8,128)S(1)}, f32[8,32,256]{2,1,0:T(8,128)S(1)}, u32[]{:S(2)}, u32[]{:S(2)}) %collective-permute-start.9) | collective-permute-done | bytes 262176 | tf_op jit(solution)/shard_map/ppermute | solution.py:163
  35.5 0.1 select_bitcast_fusion.1
  35.6 0.9 %pad_maximum_fusion = f32[8,2,32,256]{3,2,1,0:T(8,128)} fusion(f32[8,1,32,256]{3,2,1,0:T(8,128)S(1)} %get-tuple-element.5, f32[8,1,32,256]{3,2,1,0:T(8,128)S(1)} %get-tuple-element.4), kind=kLoop, calls=%fused_computation.4 | loop fusion | flops 131072 | bytes 1048576 | tf_op jit(solution)/shard_map/stack | solution.py:166
  36.5 9.9 %shard_map.77 = f32[8,4096]{1,0:T(8,128)} custom-call(f32[32]{0:T(128)} %copy-done.3, f32[8,64,512]{2,1,0:T(8,128)} %copy-done, f32[512,256]{1,0:T(8,128)} %bitcast.45), custom_call_target="tpu_custom_call" | custom-call | tf_op jit(solution)/shard_map/pallas_call | solution.py:105
  46.4 0.9 %reduce_sum.18 = f32[4096]{0:T(1024)S(1)} reduce(f32[8,4096]{1,0:T(8,128)} %shard_map.77, f32[]{:T(128)} %constant.175.clone.1), dimensions={0}, to_apply=%region_0.1 | reduce | flops 28672 | bytes 147460 | tf_op jit(solution)/shard_map/reduce_sum | solution.py:122
  47.4 0.1 mul.137
  47.4 0.0 copy-start.1
  47.5 0.1 fusion.15
  47.5 1.6 %collective-permute-start.10 = (f32[64]{0:T(128)S(1)}, f32[64]{0:T(128)S(1)}, u32[]{:S(2)}, u32[]{:S(2)}) collective-permute-start(f32[64]{0:T(128)S(1)} %fusion.15), channel_id=1, source_target_pairs={{0,1},{1,0},{2,3},{3,2},{4,5},{5,4},{6,7},{7,6},{8,9},{9,8},{10,11... | collective-permute-start | bytes 776 | tf_op jit(solution)/shard_map/ppermute | solution.py:201
  49.1 2.0 %collective-permute-done.10 = f32[64]{0:T(128)S(1)} collective-permute-done((f32[64]{0:T(128)S(1)}, f32[64]{0:T(128)S(1)}, u32[]{:S(2)}, u32[]{:S(2)}) %collective-permute-start.10) | collective-permute-done | bytes 288 | tf_op jit(solution)/shard_map/ppermute | solution.py:201
  51.1 0.5 %add_log_fusion = f32[64]{0:T(128)} fusion(f32[64]{0:T(128)S(1)} %fusion.15, f32[64]{0:T(128)S(1)} %collective-permute-done.10), kind=kLoop, calls=%fused_computation.62 | loop fusion | flops 192 | bytes 768 | tf_op jit(solution)/shard_map/log | solution.py:204
  51.6 0.0 copy-done.1
  (21 shorter events, 0.3 us)
Async XLA Ops:
  0.7 0.7 %copy-start.7 = (f32[512]{0:T(512)S(1)}, f32[512]{0:T(512)}, u32[]{:S(2)}) copy-start(f32[512]{0:T(512)} %param.7) | copy-start | bytes 6148
  0.7 0.7 %copy-start.6 = (s32[512,1]{0,1:T(1,128)S(1)}, s32[512,1]{0,1:T(1,128)}, u32[]{:S(2)}) copy-start(s32[512,1]{0,1:T(1,128)} %param.8) | copy-start | bytes 6148
  0.7 0.7 %copy-start.5 = (s32[512]{0:T(512)S(1)}, s32[512]{0:T(512)}, u32[]{:S(2)}) copy-start(s32[512]{0:T(512)} %param.9) | copy-start | bytes 6148
  2.8 0.7 %copy-start.2 = (f32[3,512]{1,0:T(4,128)S(1)}, f32[3,512]{1,0:T(4,128)}, u32[]{:S(2)}) copy-start(f32[3,512]{1,0:T(4,128)} %param.10) | copy-start | bytes 18436
  2.8 2.5 %collective-permute-start = (f32[8,32,256]{2,1,0:T(8,128)S(1)}, f32[8,32,256]{2,1,0:T(8,128)S(1)}, u32[]{:S(2)}, u32[]{:S(2)}) collective-permute-start(f32[8,32,256]{2,1,0:T(8,128)S(1)} %dynamic-slice_bitcast_fusion), channel_id=1, source_target_pairs={{0,2},{2,0},{4,6},{6,4},{8,10},{10,8},{12,14},{14,12},{16,18},{18,... | collective-permute-start | bytes 786440 | tf_op jit(solution)/shard_map/ppermute | solution.py:143
  3.4 0.7 %copy-start.4 = (f32[3,64]{1,0:T(4,128)S(1)}, f32[3,64]{1,0:T(4,128)}, u32[]{:S(2)}) copy-start(f32[3,64]{1,0:T(4,128)} %param.11) | copy-start | bytes 2308
  4.0 0.8 %copy-start.3 = (f32[32]{0:T(128)}, f32[32]{0:T(128)S(1)}, u32[]{:S(2)}) copy-start(f32[32]{0:T(128)S(1)} %add_multiply_fusion.wave_ref) | copy-start | bytes 388
  5.4 6.7 %collective-permute-start.1 = (f32[4,32,256]{2,1,0:T(8,128)S(1)}, f32[4,32,256]{2,1,0:T(8,128)S(1)}, u32[]{:S(2)}, u32[]{:S(2)}) collective-permute-start(f32[4,32,256]{2,1,0:T(8,128)S(1)} %dynamic-slice_bitcast_fusion.1), channel_id=1, source_target_pairs={{0,4},{2,6},{4,0},{6,2},{8,12},{10,14},{12,8},{14,10},{16,20},{18,... | collective-permute-start | bytes 393224 | tf_op jit(solution)/shard_map/ppermute | solution.py:143
  12.2 5.5 %collective-permute-start.4 = (f32[32,256]{1,0:T(8,128)S(1)}, f32[32,256]{1,0:T(8,128)S(1)}, u32[]{:S(2)}, u32[]{:S(2)}) collective-permute-start(f32[32,256]{1,0:T(8,128)S(1)} %get-tuple-element.13), channel_id=1, source_target_pairs={{0,24},{2,26},{4,28},{6,30},{8,0},{10,2},{12,4},{14,6},{16,8},{18,... | collective-permute-start | bytes 98312 | tf_op jit(solution)/shard_map/ppermute | solution.py:148
  16.1 4.8 %collective-permute-start.3 = (f32[32,256]{1,0:T(8,128)S(1)}, f32[32,256]{1,0:T(8,128)S(1)}, u32[]{:S(2)}, u32[]{:S(2)}) collective-permute-start(f32[32,256]{1,0:T(8,128)S(1)} %get-tuple-element.14), channel_id=1, source_target_pairs={{0,16},{2,18},{4,20},{6,22},{8,24},{10,26},{12,28},{14,30},{16,0},... | collective-permute-start | bytes 98312 | tf_op jit(solution)/shard_map/ppermute | solution.py:148
  16.1 5.7 %collective-permute-start.2 = (f32[32,256]{1,0:T(8,128)S(1)}, f32[32,256]{1,0:T(8,128)S(1)}, u32[]{:S(2)}, u32[]{:S(2)}) collective-permute-start(f32[32,256]{1,0:T(8,128)S(1)} %get-tuple-element.12), channel_id=1, source_target_pairs={{0,8},{2,10},{4,12},{6,14},{8,16},{10,18},{12,20},{14,22},{16,24},... | collective-permute-start | bytes 98312 | tf_op jit(solution)/shard_map/ppermute | solution.py:148
  21.8 4.0 %collective-permute-start.7 = (f32[32,256]{1,0:T(8,128)S(1)}, f32[32,256]{1,0:T(8,128)S(1)}, u32[]{:S(2)}, u32[]{:S(2)}) collective-permute-start(f32[32,256]{1,0:T(8,128)S(1)} %fusion.13), channel_id=1, source_target_pairs={{0,24},{2,26},{4,28},{6,30},{8,0},{10,2},{12,4},{14,6},{16,8},{18,... | collective-permute-start | bytes 98312 | tf_op jit(solution)/shard_map/ppermute | solution.py:156
  22.4 4.8 %collective-permute-start.6 = (f32[32,256]{1,0:T(8,128)S(1)}, f32[32,256]{1,0:T(8,128)S(1)}, u32[]{:S(2)}, u32[]{:S(2)}) collective-permute-start(f32[32,256]{1,0:T(8,128)S(1)} %fusion.13), channel_id=1, source_target_pairs={{0,16},{2,18},{4,20},{6,22},{8,24},{10,26},{12,28},{14,30},{16,0},... | collective-permute-start | bytes 98312 | tf_op jit(solution)/shard_map/ppermute | solution.py:156
  23.1 5.7 %collective-permute-start.5 = (f32[32,256]{1,0:T(8,128)S(1)}, f32[32,256]{1,0:T(8,128)S(1)}, u32[]{:S(2)}, u32[]{:S(2)}) collective-permute-start(f32[32,256]{1,0:T(8,128)S(1)} %fusion.13), channel_id=1, source_target_pairs={{0,8},{2,10},{4,12},{6,14},{8,16},{10,18},{12,20},{14,22},{16,24},... | collective-permute-start | bytes 98312 | tf_op jit(solution)/shard_map/ppermute | solution.py:156
  28.8 5.0 %collective-permute-start.8 = (f32[4,32,256]{2,1,0:T(8,128)S(1)}, f32[4,32,256]{2,1,0:T(8,128)S(1)}, u32[]{:S(2)}, u32[]{:S(2)}) collective-permute-start(f32[4,32,256]{2,1,0:T(8,128)S(1)} %pad_maximum_fusion.3), channel_id=1, source_target_pairs={{0,4},{2,6},{4,0},{6,2},{8,12},{10,14},{12,8},{14,10},{16,20},{18,... | collective-permute-start | bytes 393224 | tf_op jit(solution)/shard_map/ppermute | solution.py:163
  33.9 1.6 %collective-permute-start.9 = (f32[8,32,256]{2,1,0:T(8,128)S(1)}, f32[8,32,256]{2,1,0:T(8,128)S(1)}, u32[]{:S(2)}, u32[]{:S(2)}) collective-permute-start(f32[8,32,256]{2,1,0:T(8,128)S(1)} %bitcast.46), channel_id=1, source_target_pairs={{0,2},{2,0},{4,6},{6,4},{8,10},{10,8},{12,14},{14,12},{16,18},{18,... | collective-permute-start | bytes 786440 | tf_op jit(solution)/shard_map/ppermute | solution.py:163
  34.1 2.4 %copy-start = (f32[8,64,512]{2,1,0:T(8,128)}, f32[8,64,512]{2,1,0:T(8,128)S(1)}, u32[]{:S(2)}) copy-start(f32[8,64,512]{2,1,0:T(8,128)S(1)} %sqrt_dynamic-update-slice_fusion.geo_ref) | copy-start | bytes 3145732
  47.4 4.2 %copy-start.1 = (f32[32,2,64]{2,1,0:T(2,128)}, f32[32,2,64]{2,1,0:T(2,128)S(1)}, u32[]{:S(2)}) copy-start(f32[32,2,64]{2,1,0:T(2,128)S(1)} %mul.137) | copy-start | bytes 49156
  47.5 3.6 %collective-permute-start.10 = (f32[64]{0:T(128)S(1)}, f32[64]{0:T(128)S(1)}, u32[]{:S(2)}, u32[]{:S(2)}) collective-permute-start(f32[64]{0:T(128)S(1)} %fusion.15), channel_id=1, source_target_pairs={{0,1},{1,0},{2,3},{3,2},{4,5},{5,4},{6,7},{7,6},{8,9},{9,8},{10,11... | collective-permute-start | bytes 776 | tf_op jit(solution)/shard_map/ppermute | solution.py:201

commit v14 on v8

--- a/solution.py
+++ b/solution.py
@@ -177,6 +177,7 @@
         (panel_number // panels_dev == cell_owner[:, 0][None, :])
         & (panel_number % panels_dev == cell_local[None, :])
     ).astype(jnp.bfloat16)
+    selector, weighted = lax.optimization_barrier((selector, weighted))
     local_source = jnp.dot(selector, weighted, preferred_element_type=jnp.float32)
     group_first = lax.axis_index("freq") * freqs_dev
     wave_numbers = wave_step * (

time: 51.9 us -> 52.8 us (1.017)
  other arithmetic: 4.74 us -> 6.04 us
  matrix products: 1.42 us -> 0.3 us
  local copies, waits for them, and re-layouts: 1.59 us -> 2.26 us
    convert_element_type x0 -> x2, other arithmetic: none -> 1.3 us  [the longest x1 1.08 us: shards(): (cell_weight[:, None] * cell_spectra.astype(jnp.float32)).astype(jnp.bflo...]
    dot_general x1, matrix products: 1.42 us -> 0.3 us  [shards(): jnp.dot(selector, weighted, preferred_element_type=jnp.float32)]
    unnamed x16, local copies, waits for them, and re-layouts: 1.38 us -> 2.05 us
where the time goes in v14:
time: 52.8 us; the launch traced here: 52.5 us
  waiting for transfers between devices  18.5 us (35%)
  starting transfers between devices  14.4 us (27%)
  Pallas kernels  9.93 us (19%)
  other arithmetic  6.04 us (11%)
  local copies, waits for them, and re-layouts  2.26 us (4%)
  between operations  1.13 us (2%)
    pallas_call x1, Pallas kernels, far_field(): pl.pallas_call(functools.partial(field_kernel, math.gcd(observers // 8, 4...  9.93 us
    ppermute x3, starting transfers between devices, halving_sum(): total = total + lax.ppermute(piece, 'obs', quad_pairs(groups, shift))  4.91 us
    ppermute x2, waiting for transfers between devices, doubling_gather(): other = lax.ppermute(gathered, 'obs', partner_pairs(groups, bit))  4.88 us
    ppermute x3, waiting for transfers between devices, halving_sum(): total = total + lax.ppermute(piece, 'obs', quad_pairs(groups, shift))  4.22 us
    ppermute x2, waiting for transfers between devices, halving_sum(): current = keep + lax.ppermute(send, 'obs', partner_pairs(groups, bit))  3.69 us
    ppermute x3, waiting for transfers between devices, doubling_gather(): lax.ppermute(own, 'obs', quad_pairs(groups, shift))  3.65 us
    ppermute x3, starting transfers between devices, doubling_gather(): lax.ppermute(own, 'obs', quad_pairs(groups, shift))  3.2 us
    ppermute x2, starting transfers between devices, halving_sum(): current = keep + lax.ppermute(send, 'obs', partner_pairs(groups, bit))  3.09 us
  transfers between devices with their start and end apart: 11, of which 10 were waited for; matrix products, arithmetic and copies ran while one was open for 4% of the time, Pallas kernels for 0%

profile of v14, /device:TPU:0, one launch (start us, length us, event | category | flops | bytes accessed | tf_op | source)
XLA Modules:
  0.0 52.5 jit_solution(6602592919333985065)
XLA Ops:
  0.6 0.0 copy-start.4
  0.7 0.7 %copy-done.4 = f32[512]{0:T(512)S(1)} copy-done((f32[512]{0:T(512)S(1)}, f32[512]{0:T(512)}, u32[]{:S(2)}) %copy-start.4) | copy-done | bytes 2072
  1.3 1.1 %multiply_convert_fusion = bf16[512,256]{1,0:T(8,128)(2,1)S(1)} fusion(bf16[512,256]{1,0:T(8,128)(2,1)} %param.6, f32[512]{0:T(512)S(1)} %copy-done.4), kind=kLoop, calls=%fused_computation.2 | loop fusion | flops 393216 | bytes 526336 | tf_op jit(solution)/shard_map/convert_element_type | solution.py:174
  2.4 0.0 copy-start.6
  2.4 0.0 copy-start.5
  2.4 0.7 %copy-done.6 = s32[512,1]{0,1:T(1,128)S(1)} copy-done((s32[512,1]{0,1:T(1,128)S(1)}, s32[512,1]{0,1:T(1,128)}, u32[]{:S(2)}) %copy-start.6) | copy-done | bytes 2072
  3.1 0.0 copy-done.5
  3.1 0.2 and_convert_fusion
  3.4 0.3 fusion.15
  3.7 0.0 copy-start.2
  3.7 0.5 collective-permute-start
  4.2 0.1 copy-done.2
  4.4 0.5 %copy-done.7 = f32[3,64]{1,0:T(4,128)S(1)} copy-done((f32[3,64]{1,0:T(4,128)S(1)}, f32[3,64]{1,0:T(4,128)}, u32[]{:S(2)}) %copy-start.7) | copy-done | bytes 792
  4.9 0.1 broadcast_subtract_fusion
  5.0 0.5 %multiply_dynamic-update-slice_fusion.1 = (f32[8,64,512]{2,1,0:T(8,128)S(1)}, f32[1,64,512]{2,1,0:T(8,128)S(1)}) fusion(f32[]{:T(128)S(1)} %bitcast.57, f32[3,64,512]{2,1,0:T(8,128)S(1)} %broadcast_subtract_fusion), kind=kLoop, calls=%fused_computation.24 | loop fusion | flops 262143 | bytes 655364
  5.7 0.0 copy-done.3
  5.7 0.5 multiply_dynamic-update-slice_fusion
  6.2 0.0 collective-permute-done
  6.3 2.6 %collective-permute-start.1 = (f32[4,32,256]{2,1,0:T(8,128)S(1)}, f32[4,32,256]{2,1,0:T(8,128)S(1)}, u32[]{:S(2)}, u32[]{:S(2)}) collective-permute-start(f32[4,32,256]{2,1,0:T(8,128)S(1)} %dynamic-slice_bitcast_fusion.1), channel_id=1, source_target_pairs={{0,4},{2,6},{4,0},{6,2},{8,12},{10,14},{12,8},{14,10},{16,20},{18,... | collective-permute-start | bytes 393224 | tf_op jit(solution)/shard_map/ppermute | solution.py:141
  8.9 0.5 cosine_dynamic-update-slice_fusion
  9.3 3.7 %collective-permute-done.1 = f32[4,32,256]{2,1,0:T(8,128)S(1)} collective-permute-done((f32[4,32,256]{2,1,0:T(8,128)S(1)}, f32[4,32,256]{2,1,0:T(8,128)S(1)}, u32[]{:S(2)}, u32[]{:S(2)}) %collective-permute-start.1) | collective-permute-done | bytes 131104 | tf_op jit(solution)/shard_map/ppermute | solution.py:141
  13.1 3.9 %collective-permute-start.4 = (f32[32,256]{1,0:T(8,128)S(1)}, f32[32,256]{1,0:T(8,128)S(1)}, u32[]{:S(2)}, u32[]{:S(2)}) collective-permute-start(f32[32,256]{1,0:T(8,128)S(1)} %get-tuple-element.17), channel_id=1, source_target_pairs={{0,24},{2,26},{4,28},{6,30},{8,0},{10,2},{12,4},{14,6},{16,8},{18,... | collective-permute-start | bytes 98312 | tf_op jit(solution)/shard_map/ppermute | solution.py:146
  17.0 0.0 collective-permute-start.3
  17.0 1.0 %collective-permute-start.2 = (f32[32,256]{1,0:T(8,128)S(1)}, f32[32,256]{1,0:T(8,128)S(1)}, u32[]{:S(2)}, u32[]{:S(2)}) collective-permute-start(f32[32,256]{1,0:T(8,128)S(1)} %get-tuple-element.16), channel_id=1, source_target_pairs={{0,8},{2,10},{4,12},{6,14},{8,16},{10,18},{12,20},{14,22},{16,24},... | collective-permute-start | bytes 98312 | tf_op jit(solution)/shard_map/ppermute | solution.py:146
  18.0 0.5 sine_dynamic-update-slice_fusion
  18.4 0.1 collective-permute-done.4
  18.6 3.2 %collective-permute-done.3 = f32[32,256]{1,0:T(8,128)S(1)} collective-permute-done((f32[32,256]{1,0:T(8,128)S(1)}, f32[32,256]{1,0:T(8,128)S(1)}, u32[]{:S(2)}, u32[]{:S(2)}) %collective-permute-start.3) | collective-permute-done | bytes 32800 | tf_op jit(solution)/shard_map/ppermute | solution.py:146
  21.8 0.9 %collective-permute-done.2 = f32[32,256]{1,0:T(8,128)S(1)} collective-permute-done((f32[32,256]{1,0:T(8,128)S(1)}, f32[32,256]{1,0:T(8,128)S(1)}, u32[]{:S(2)}, u32[]{:S(2)}) %collective-permute-start.2) | collective-permute-done | bytes 32800 | tf_op jit(solution)/shard_map/ppermute | solution.py:146
  22.7 0.6 %collective-permute-start.7 = (f32[32,256]{1,0:T(8,128)S(1)}, f32[32,256]{1,0:T(8,128)S(1)}, u32[]{:S(2)}, u32[]{:S(2)}) collective-permute-start(f32[32,256]{1,0:T(8,128)S(1)} %fusion.4), channel_id=1, source_target_pairs={{0,24},{2,26},{4,28},{6,30},{8,0},{10,2},{12,4},{14,6},{16,8},{18,... | collective-permute-start | bytes 98312 | tf_op jit(solution)/shard_map/ppermute | solution.py:154
  23.3 0.6 %collective-permute-start.6 = (f32[32,256]{1,0:T(8,128)S(1)}, f32[32,256]{1,0:T(8,128)S(1)}, u32[]{:S(2)}, u32[]{:S(2)}) collective-permute-start(f32[32,256]{1,0:T(8,128)S(1)} %fusion.4), channel_id=1, source_target_pairs={{0,16},{2,18},{4,20},{6,22},{8,24},{10,26},{12,28},{14,30},{16,0},... | collective-permute-start | bytes 98312 | tf_op jit(solution)/shard_map/ppermute | solution.py:154
  23.9 1.9 %collective-permute-start.5 = (f32[32,256]{1,0:T(8,128)S(1)}, f32[32,256]{1,0:T(8,128)S(1)}, u32[]{:S(2)}, u32[]{:S(2)}) collective-permute-start(f32[32,256]{1,0:T(8,128)S(1)} %fusion.4), channel_id=1, source_target_pairs={{0,8},{2,10},{4,12},{6,14},{8,16},{10,18},{12,20},{14,22},{16,24},... | collective-permute-start | bytes 98312 | tf_op jit(solution)/shard_map/ppermute | solution.py:154
  26.0 0.7 %collective-permute-done.7 = f32[32,256]{1,0:T(8,128)S(1)} collective-permute-done((f32[32,256]{1,0:T(8,128)S(1)}, f32[32,256]{1,0:T(8,128)S(1)}, u32[]{:S(2)}, u32[]{:S(2)}) %collective-permute-start.7) | collective-permute-done | bytes 32800 | tf_op jit(solution)/shard_map/ppermute | solution.py:154
  26.7 1.5 %collective-permute-done.6 = f32[32,256]{1,0:T(8,128)S(1)} collective-permute-done((f32[32,256]{1,0:T(8,128)S(1)}, f32[32,256]{1,0:T(8,128)S(1)}, u32[]{:S(2)}, u32[]{:S(2)}) %collective-permute-start.6) | collective-permute-done | bytes 32800 | tf_op jit(solution)/shard_map/ppermute | solution.py:154
  28.1 1.5 %collective-permute-done.5 = f32[32,256]{1,0:T(8,128)S(1)} collective-permute-done((f32[32,256]{1,0:T(8,128)S(1)}, f32[32,256]{1,0:T(8,128)S(1)}, u32[]{:S(2)}, u32[]{:S(2)}) %collective-permute-start.5) | collective-permute-done | bytes 32800 | tf_op jit(solution)/shard_map/ppermute | solution.py:154
  29.7 1.6 %collective-permute-start.8 = (f32[4,32,256]{2,1,0:T(8,128)S(1)}, f32[4,32,256]{2,1,0:T(8,128)S(1)}, u32[]{:S(2)}, u32[]{:S(2)}) collective-permute-start(f32[4,32,256]{2,1,0:T(8,128)S(1)} %pad_maximum_fusion.3), channel_id=1, source_target_pairs={{0,4},{2,6},{4,0},{6,2},{8,12},{10,14},{12,8},{14,10},{16,20},{18,... | collective-permute-start | bytes 393224 | tf_op jit(solution)/shard_map/ppermute | solution.py:161
  31.3 3.5 %collective-permute-done.8 = f32[4,32,256]{2,1,0:T(8,128)S(1)} collective-permute-done((f32[4,32,256]{2,1,0:T(8,128)S(1)}, f32[4,32,256]{2,1,0:T(8,128)S(1)}, u32[]{:S(2)}, u32[]{:S(2)}) %collective-permute-start.8) | collective-permute-done | bytes 131104 | tf_op jit(solution)/shard_map/ppermute | solution.py:161
  34.8 0.1 collective-permute-start.9
  35.0 1.4 %collective-permute-done.9 = f32[8,32,256]{2,1,0:T(8,128)S(1)} collective-permute-done((f32[8,32,256]{2,1,0:T(8,128)S(1)}, f32[8,32,256]{2,1,0:T(8,128)S(1)}, u32[]{:S(2)}, u32[]{:S(2)}) %collective-permute-start.9) | collective-permute-done | bytes 262176 | tf_op jit(solution)/shard_map/ppermute | solution.py:161
  36.4 0.1 select_bitcast_fusion.1
  36.5 0.9 %pad_maximum_fusion = f32[8,2,32,256]{3,2,1,0:T(8,128)} fusion(f32[8,1,32,256]{3,2,1,0:T(8,128)S(1)} %get-tuple-element.9, f32[8,1,32,256]{3,2,1,0:T(8,128)S(1)} %get-tuple-element.8), kind=kLoop, calls=%fused_computation.1 | loop fusion | flops 131072 | bytes 1048576 | tf_op jit(solution)/shard_map/stack | solution.py:164
  37.3 9.9 %shard_map.77 = f32[8,4096]{1,0:T(8,128)} custom-call(f32[32]{0:T(128)} %copy-done.3, f32[8,64,512]{2,1,0:T(8,128)} %copy-done, f32[512,256]{1,0:T(8,128)} %bitcast.49), custom_call_target="tpu_custom_call" | custom-call | tf_op jit(solution)/shard_map/pallas_call | solution.py:103
  47.3 0.9 %fusion.6 = f32[4096]{0:T(1024)S(1)} fusion(f32[8,4096]{1,0:T(8,128)} %shard_map.77), kind=kLoop, calls=%fused_computation.38 | loop fusion | flops 4096 | bytes 32768 | tf_op jit(solution)/shard_map/mul | solution.py:197
  48.2 0.1 mul.137
  48.3 0.0 copy-start.1
  48.3 0.1 fusion.7
  48.4 1.6 %collective-permute-start.10 = (f32[64]{0:T(128)S(1)}, f32[64]{0:T(128)S(1)}, u32[]{:S(2)}, u32[]{:S(2)}) collective-permute-start(f32[64]{0:T(128)S(1)} %fusion.7), channel_id=1, source_target_pairs={{0,1},{1,0},{2,3},{3,2},{4,5},{5,4},{6,7},{7,6},{8,9},{9,8},{10,11... | collective-permute-start | bytes 776 | tf_op jit(solution)/shard_map/ppermute | solution.py:200
  50.0 2.0 %collective-permute-done.10 = f32[64]{0:T(128)S(1)} collective-permute-done((f32[64]{0:T(128)S(1)}, f32[64]{0:T(128)S(1)}, u32[]{:S(2)}, u32[]{:S(2)}) %collective-permute-start.10) | collective-permute-done | bytes 288 | tf_op jit(solution)/shard_map/ppermute | solution.py:200
  52.0 0.5 add_log_fusion
  (22 shorter events, 0.3 us)
Async XLA Ops:
  0.6 0.7 %copy-start.4 = (f32[512]{0:T(512)S(1)}, f32[512]{0:T(512)}, u32[]{:S(2)}) copy-start(f32[512]{0:T(512)} %param.7) | copy-start | bytes 6148
  2.4 0.7 %copy-start.6 = (s32[512,1]{0,1:T(1,128)S(1)}, s32[512,1]{0,1:T(1,128)}, u32[]{:S(2)}) copy-start(s32[512,1]{0,1:T(1,128)} %param.8) | copy-start | bytes 6148
  2.4 0.7 %copy-start.5 = (s32[512]{0:T(512)S(1)}, s32[512]{0:T(512)}, u32[]{:S(2)}) copy-start(s32[512]{0:T(512)} %param.9) | copy-start | bytes 6148
  3.7 0.7 %copy-start.2 = (f32[3,512]{1,0:T(4,128)S(1)}, f32[3,512]{1,0:T(4,128)}, u32[]{:S(2)}) copy-start(f32[3,512]{1,0:T(4,128)} %param.10) | copy-start | bytes 18436
  3.7 2.5 %collective-permute-start = (f32[8,32,256]{2,1,0:T(8,128)S(1)}, f32[8,32,256]{2,1,0:T(8,128)S(1)}, u32[]{:S(2)}, u32[]{:S(2)}) collective-permute-start(f32[8,32,256]{2,1,0:T(8,128)S(1)} %dynamic-slice_bitcast_fusion), channel_id=1, source_target_pairs={{0,2},{2,0},{4,6},{6,4},{8,10},{10,8},{12,14},{14,12},{16,18},{18,... | collective-permute-start | bytes 786440 | tf_op jit(solution)/shard_map/ppermute | solution.py:141
  4.2 0.7 %copy-start.7 = (f32[3,64]{1,0:T(4,128)S(1)}, f32[3,64]{1,0:T(4,128)}, u32[]{:S(2)}) copy-start(f32[3,64]{1,0:T(4,128)} %param.11) | copy-start | bytes 2308
  4.9 0.8 %copy-start.3 = (f32[32]{0:T(128)}, f32[32]{0:T(128)S(1)}, u32[]{:S(2)}) copy-start(f32[32]{0:T(128)S(1)} %add_multiply_fusion.wave_ref) | copy-start | bytes 388
  6.3 6.7 %collective-permute-start.1 = (f32[4,32,256]{2,1,0:T(8,128)S(1)}, f32[4,32,256]{2,1,0:T(8,128)S(1)}, u32[]{:S(2)}, u32[]{:S(2)}) collective-permute-start(f32[4,32,256]{2,1,0:T(8,128)S(1)} %dynamic-slice_bitcast_fusion.1), channel_id=1, source_target_pairs={{0,4},{2,6},{4,0},{6,2},{8,12},{10,14},{12,8},{14,10},{16,20},{18,... | collective-permute-start | bytes 393224 | tf_op jit(solution)/shard_map/ppermute | solution.py:141
  13.1 5.5 %collective-permute-start.4 = (f32[32,256]{1,0:T(8,128)S(1)}, f32[32,256]{1,0:T(8,128)S(1)}, u32[]{:S(2)}, u32[]{:S(2)}) collective-permute-start(f32[32,256]{1,0:T(8,128)S(1)} %get-tuple-element.17), channel_id=1, source_target_pairs={{0,24},{2,26},{4,28},{6,30},{8,0},{10,2},{12,4},{14,6},{16,8},{18,... | collective-permute-start | bytes 98312 | tf_op jit(solution)/shard_map/ppermute | solution.py:146
  17.0 4.8 %collective-permute-start.3 = (f32[32,256]{1,0:T(8,128)S(1)}, f32[32,256]{1,0:T(8,128)S(1)}, u32[]{:S(2)}, u32[]{:S(2)}) collective-permute-start(f32[32,256]{1,0:T(8,128)S(1)} %get-tuple-element.18), channel_id=1, source_target_pairs={{0,16},{2,18},{4,20},{6,22},{8,24},{10,26},{12,28},{14,30},{16,0},... | collective-permute-start | bytes 98312 | tf_op jit(solution)/shard_map/ppermute | solution.py:146
  17.0 5.7 %collective-permute-start.2 = (f32[32,256]{1,0:T(8,128)S(1)}, f32[32,256]{1,0:T(8,128)S(1)}, u32[]{:S(2)}, u32[]{:S(2)}) collective-permute-start(f32[32,256]{1,0:T(8,128)S(1)} %get-tuple-element.16), channel_id=1, source_target_pairs={{0,8},{2,10},{4,12},{6,14},{8,16},{10,18},{12,20},{14,22},{16,24},... | collective-permute-start | bytes 98312 | tf_op jit(solution)/shard_map/ppermute | solution.py:146
  22.7 4.0 %collective-permute-start.7 = (f32[32,256]{1,0:T(8,128)S(1)}, f32[32,256]{1,0:T(8,128)S(1)}, u32[]{:S(2)}, u32[]{:S(2)}) collective-permute-start(f32[32,256]{1,0:T(8,128)S(1)} %fusion.4), channel_id=1, source_target_pairs={{0,24},{2,26},{4,28},{6,30},{8,0},{10,2},{12,4},{14,6},{16,8},{18,... | collective-permute-start | bytes 98312 | tf_op jit(solution)/shard_map/ppermute | solution.py:154
  23.3 4.8 %collective-permute-start.6 = (f32[32,256]{1,0:T(8,128)S(1)}, f32[32,256]{1,0:T(8,128)S(1)}, u32[]{:S(2)}, u32[]{:S(2)}) collective-permute-start(f32[32,256]{1,0:T(8,128)S(1)} %fusion.4), channel_id=1, source_target_pairs={{0,16},{2,18},{4,20},{6,22},{8,24},{10,26},{12,28},{14,30},{16,0},... | collective-permute-start | bytes 98312 | tf_op jit(solution)/shard_map/ppermute | solution.py:154
  23.9 5.7 %collective-permute-start.5 = (f32[32,256]{1,0:T(8,128)S(1)}, f32[32,256]{1,0:T(8,128)S(1)}, u32[]{:S(2)}, u32[]{:S(2)}) collective-permute-start(f32[32,256]{1,0:T(8,128)S(1)} %fusion.4), channel_id=1, source_target_pairs={{0,8},{2,10},{4,12},{6,14},{8,16},{10,18},{12,20},{14,22},{16,24},... | collective-permute-start | bytes 98312 | tf_op jit(solution)/shard_map/ppermute | solution.py:154
  29.7 5.0 %collective-permute-start.8 = (f32[4,32,256]{2,1,0:T(8,128)S(1)}, f32[4,32,256]{2,1,0:T(8,128)S(1)}, u32[]{:S(2)}, u32[]{:S(2)}) collective-permute-start(f32[4,32,256]{2,1,0:T(8,128)S(1)} %pad_maximum_fusion.3), channel_id=1, source_target_pairs={{0,4},{2,6},{4,0},{6,2},{8,12},{10,14},{12,8},{14,10},{16,20},{18,... | collective-permute-start | bytes 393224 | tf_op jit(solution)/shard_map/ppermute | solution.py:161
  34.8 1.6 %collective-permute-start.9 = (f32[8,32,256]{2,1,0:T(8,128)S(1)}, f32[8,32,256]{2,1,0:T(8,128)S(1)}, u32[]{:S(2)}, u32[]{:S(2)}) collective-permute-start(f32[8,32,256]{2,1,0:T(8,128)S(1)} %bitcast.50), channel_id=1, source_target_pairs={{0,2},{2,0},{4,6},{6,4},{8,10},{10,8},{12,14},{14,12},{16,18},{18,... | collective-permute-start | bytes 786440 | tf_op jit(solution)/shard_map/ppermute | solution.py:161
  35.0 2.4 %copy-start = (f32[8,64,512]{2,1,0:T(8,128)}, f32[8,64,512]{2,1,0:T(8,128)S(1)}, u32[]{:S(2)}) copy-start(f32[8,64,512]{2,1,0:T(8,128)S(1)} %sqrt_dynamic-update-slice_fusion.geo_ref) | copy-start | bytes 3145732
  48.3 4.2 %copy-start.1 = (f32[32,2,64]{2,1,0:T(2,128)}, f32[32,2,64]{2,1,0:T(2,128)S(1)}, u32[]{:S(2)}) copy-start(f32[32,2,64]{2,1,0:T(2,128)S(1)} %mul.137) | copy-start | bytes 49156
  48.4 3.6 %collective-permute-start.10 = (f32[64]{0:T(128)S(1)}, f32[64]{0:T(128)S(1)}, u32[]{:S(2)}, u32[]{:S(2)}) collective-permute-start(f32[64]{0:T(128)S(1)} %fusion.7), channel_id=1, source_target_pairs={{0,1},{1,0},{2,3},{3,2},{4,5},{5,4},{6,7},{7,6},{8,9},{9,8},{10,11... | collective-permute-start | bytes 776 | tf_op jit(solution)/shard_map/ppermute | solution.py:200

commit v15 on v11

--- a/solution.py
+++ b/solution.py
@@ -80,8 +80,10 @@
     @pl.when(pl.program_id(0) == pl.num_programs(0) - 1)
     def _():
         flat = acc_ref[...].reshape(freqs * 2 * observers, lanes)
+        spread = lax.broadcasted_iota(jnp.int32, (8, lanes), 1) // (lanes // 8)
+        rows = lax.broadcasted_iota(jnp.int32, (8, lanes), 0)
         out_ref[...] = lax.dot_general(
-            jnp.ones((8, lanes), jnp.float32),
+            (spread == rows).astype(jnp.float32),
             flat,
             (((1,), (1,)), ((), ())),
             precision=lax.Precision.HIGHEST,
@@ -130,7 +132,7 @@
         ],
         compiler_params=pltpu.CompilerParams(dimension_semantics=("arbitrary",)),
     )(wave_numbers, geometry, low, high)
-    return summed[0].reshape(freqs, 2, observers)
+    return jnp.sum(summed, axis=0).reshape(freqs, 2, observers)
 
 
 def partner_pairs(groups, bit):

time: 52 us -> 52 us (level)
    mul x1, other arithmetic: 0.95 us -> 0.01 us  [shards(): pressure = summed * (reference_radius / math.sqrt(panel_total))]
    reduce_sum x0 -> x1, other arithmetic: none -> 0.94 us  [far_field(): return jnp.sum(summed, axis=0).reshape(freqs, 2, observers)]
where the time goes in v15:
time: 52 us; the launch traced here: 51.7 us
  waiting for transfers between devices  17.3 us (33%)
  starting transfers between devices  14.9 us (29%)
  Pallas kernels  10.1 us (19%)
  other arithmetic  3.81 us (7%)
  local copies, waits for them, and re-layouts  3.1 us (6%)
  matrix products  1.41 us (3%)
  between operations  1.13 us (2%)
    pallas_call x1, Pallas kernels, far_field(): pl.pallas_call(functools.partial(field_kernel, math.gcd(observers // 8, 4...  10.1 us
    ppermute x3, starting transfers between devices, halving_sum(): total = total + lax.ppermute(piece, 'obs', quad_pairs(groups, shift))  4.92 us
    ppermute x2, waiting for transfers between devices, doubling_gather(): other = lax.ppermute(gathered, 'obs', partner_pairs(groups, bit))  4.35 us
    ppermute x3, waiting for transfers between devices, halving_sum(): total = total + lax.ppermute(piece, 'obs', quad_pairs(groups, shift))  4.22 us
    ppermute x3, waiting for transfers between devices, doubling_gather(): lax.ppermute(own, 'obs', quad_pairs(groups, shift))  3.65 us
    ppermute x2, starting transfers between devices, halving_sum(): current = keep + lax.ppermute(send, 'obs', partner_pairs(groups, bit))  3.52 us
    ppermute x3, starting transfers between devices, doubling_gather(): lax.ppermute(own, 'obs', quad_pairs(groups, shift))  3.2 us
    ppermute x2, waiting for transfers between devices, halving_sum(): current = keep + lax.ppermute(send, 'obs', partner_pairs(groups, bit))  3.1 us
  transfers between devices with their start and end apart: 11, of which 10 were waited for; matrix products, arithmetic and copies ran while one was open for 5% of the time, Pallas kernels for 0%

profile of v15, /device:TPU:0, one launch (start us, length us, event | category | flops | bytes accessed | tf_op | source)
XLA Modules:
  0.0 51.7 jit_solution(3472601851794998105)
XLA Ops:
  0.7 0.0 copy-start.9
  0.7 0.0 copy-start.8
  0.7 0.0 copy-start.7
  0.7 0.6 %copy-done.9 = f32[512]{0:T(512)S(1)} copy-done((f32[512]{0:T(512)S(1)}, f32[512]{0:T(512)}, u32[]{:S(2)}) %copy-start.9) | copy-done | bytes 2072
  1.3 0.0 copy-done.8
  1.4 0.0 copy-done.7
  1.4 1.4 %fusion = f32[512,256]{1,0:T(8,128)S(1)} fusion(s32[512]{0:T(512)S(1)} %copy-done.7, s32[512]{0:T(512)S(1)} %bitcast.55, s32[512]{0:T(512)S(1)} %get-tuple-element.15, s32[512]{0:T(512)S(1)} %get-tuple-element.16, bf16[512,256]{1,0:T(8,128)(2,1)} %param.6, f32[512]{0:T(512)S(1)} %copy-done.9), kind=kOutput, calls=%fused_computation | convolution fusion | flops 135397376 | bytes 796672 | tf_op jit(solution)/shard_map/dot_general | solution.py:197
  2.8 0.0 copy-start.4
  2.8 0.5 %collective-permute-start = (f32[8,32,256]{2,1,0:T(8,128)S(1)}, f32[8,32,256]{2,1,0:T(8,128)S(1)}, u32[]{:S(2)}, u32[]{:S(2)}) collective-permute-start(f32[8,32,256]{2,1,0:T(8,128)S(1)} %dynamic-slice_bitcast_fusion), channel_id=1, source_target_pairs={{0,2},{2,0},{4,6},{6,4},{8,10},{10,8},{12,14},{14,12},{16,18},{18,... | collective-permute-start | bytes 786440 | tf_op jit(solution)/shard_map/ppermute | solution.py:156
  3.4 0.2 copy-done.4
  3.5 0.1 reshape.79
  3.7 0.0 copy-start.6
  3.7 0.1 sub.49
  3.8 0.6 %copy-done.6 = f32[3,64]{1,0:T(4,128)S(1)} copy-done((f32[3,64]{1,0:T(4,128)S(1)}, f32[3,64]{1,0:T(4,128)}, u32[]{:S(2)}) %copy-start.6) | copy-done | bytes 792
  4.4 0.1 broadcast_subtract_fusion
  4.5 0.5 %multiply_dynamic-update-slice_fusion.1 = (f32[8,64,512]{2,1,0:T(8,128)S(1)}, f32[1,64,512]{2,1,0:T(8,128)S(1)}) fusion(f32[]{:T(128)S(1)} %bitcast.53, f32[3,64,512]{2,1,0:T(8,128)S(1)} %broadcast_subtract_fusion), kind=kLoop, calls=%fused_computation.29 | loop fusion | flops 262143 | bytes 655364
  5.1 0.5 multiply_dynamic-update-slice_fusion
  5.7 3.0 %collective-permute-start.1 = (f32[4,32,256]{2,1,0:T(8,128)S(1)}, f32[4,32,256]{2,1,0:T(8,128)S(1)}, u32[]{:S(2)}, u32[]{:S(2)}) collective-permute-start(f32[4,32,256]{2,1,0:T(8,128)S(1)} %dynamic-slice_bitcast_fusion.1), channel_id=1, source_target_pairs={{0,4},{2,6},{4,0},{6,2},{8,12},{10,14},{12,8},{14,10},{16,20},{18,... | collective-permute-start | bytes 393224 | tf_op jit(solution)/shard_map/ppermute | solution.py:156
  8.7 0.5 cosine_dynamic-update-slice_fusion
  9.2 3.1 %collective-permute-done.1 = f32[4,32,256]{2,1,0:T(8,128)S(1)} collective-permute-done((f32[4,32,256]{2,1,0:T(8,128)S(1)}, f32[4,32,256]{2,1,0:T(8,128)S(1)}, u32[]{:S(2)}, u32[]{:S(2)}) %collective-permute-start.1) | collective-permute-done | bytes 131104 | tf_op jit(solution)/shard_map/ppermute | solution.py:156
  12.3 3.9 %collective-permute-start.4 = (f32[32,256]{1,0:T(8,128)S(1)}, f32[32,256]{1,0:T(8,128)S(1)}, u32[]{:S(2)}, u32[]{:S(2)}) collective-permute-start(f32[32,256]{1,0:T(8,128)S(1)} %get-tuple-element.11), channel_id=1, source_target_pairs={{0,24},{2,26},{4,28},{6,30},{8,0},{10,2},{12,4},{14,6},{16,8},{18,... | collective-permute-start | bytes 98312 | tf_op jit(solution)/shard_map/ppermute | solution.py:161
  16.2 0.0 collective-permute-start.3
  16.2 1.0 %collective-permute-start.2 = (f32[32,256]{1,0:T(8,128)S(1)}, f32[32,256]{1,0:T(8,128)S(1)}, u32[]{:S(2)}, u32[]{:S(2)}) collective-permute-start(f32[32,256]{1,0:T(8,128)S(1)} %get-tuple-element.10), channel_id=1, source_target_pairs={{0,8},{2,10},{4,12},{6,14},{8,16},{10,18},{12,20},{14,22},{16,24},... | collective-permute-start | bytes 98312 | tf_op jit(solution)/shard_map/ppermute | solution.py:161
  17.3 0.5 sine_dynamic-update-slice_fusion
  17.7 0.1 collective-permute-done.4
  17.8 3.2 %collective-permute-done.3 = f32[32,256]{1,0:T(8,128)S(1)} collective-permute-done((f32[32,256]{1,0:T(8,128)S(1)}, f32[32,256]{1,0:T(8,128)S(1)}, u32[]{:S(2)}, u32[]{:S(2)}) %collective-permute-start.3) | collective-permute-done | bytes 32800 | tf_op jit(solution)/shard_map/ppermute | solution.py:161
  21.1 0.9 %collective-permute-done.2 = f32[32,256]{1,0:T(8,128)S(1)} collective-permute-done((f32[32,256]{1,0:T(8,128)S(1)}, f32[32,256]{1,0:T(8,128)S(1)}, u32[]{:S(2)}, u32[]{:S(2)}) %collective-permute-start.2) | collective-permute-done | bytes 32800 | tf_op jit(solution)/shard_map/ppermute | solution.py:161
  22.0 0.7 %collective-permute-start.7 = (f32[32,256]{1,0:T(8,128)S(1)}, f32[32,256]{1,0:T(8,128)S(1)}, u32[]{:S(2)}, u32[]{:S(2)}) collective-permute-start(f32[32,256]{1,0:T(8,128)S(1)} %fusion.13), channel_id=1, source_target_pairs={{0,24},{2,26},{4,28},{6,30},{8,0},{10,2},{12,4},{14,6},{16,8},{18,... | collective-permute-start | bytes 98312 | tf_op jit(solution)/shard_map/ppermute | solution.py:169
  22.7 0.6 %collective-permute-start.6 = (f32[32,256]{1,0:T(8,128)S(1)}, f32[32,256]{1,0:T(8,128)S(1)}, u32[]{:S(2)}, u32[]{:S(2)}) collective-permute-start(f32[32,256]{1,0:T(8,128)S(1)} %fusion.13), channel_id=1, source_target_pairs={{0,16},{2,18},{4,20},{6,22},{8,24},{10,26},{12,28},{14,30},{16,0},... | collective-permute-start | bytes 98312 | tf_op jit(solution)/shard_map/ppermute | solution.py:169
  23.2 1.9 %collective-permute-start.5 = (f32[32,256]{1,0:T(8,128)S(1)}, f32[32,256]{1,0:T(8,128)S(1)}, u32[]{:S(2)}, u32[]{:S(2)}) collective-permute-start(f32[32,256]{1,0:T(8,128)S(1)} %fusion.13), channel_id=1, source_target_pairs={{0,8},{2,10},{4,12},{6,14},{8,16},{10,18},{12,20},{14,22},{16,24},... | collective-permute-start | bytes 98312 | tf_op jit(solution)/shard_map/ppermute | solution.py:169
  25.3 1.0 %collective-permute-done.7 = f32[32,256]{1,0:T(8,128)S(1)} collective-permute-done((f32[32,256]{1,0:T(8,128)S(1)}, f32[32,256]{1,0:T(8,128)S(1)}, u32[]{:S(2)}, u32[]{:S(2)}) %collective-permute-start.7) | collective-permute-done | bytes 32800 | tf_op jit(solution)/shard_map/ppermute | solution.py:169
  26.3 1.2 %collective-permute-done.6 = f32[32,256]{1,0:T(8,128)S(1)} collective-permute-done((f32[32,256]{1,0:T(8,128)S(1)}, f32[32,256]{1,0:T(8,128)S(1)}, u32[]{:S(2)}, u32[]{:S(2)}) %collective-permute-start.6) | collective-permute-done | bytes 32800 | tf_op jit(solution)/shard_map/ppermute | solution.py:169
  27.5 1.5 %collective-permute-done.5 = f32[32,256]{1,0:T(8,128)S(1)} collective-permute-done((f32[32,256]{1,0:T(8,128)S(1)}, f32[32,256]{1,0:T(8,128)S(1)}, u32[]{:S(2)}, u32[]{:S(2)}) %collective-permute-start.5) | collective-permute-done | bytes 32800 | tf_op jit(solution)/shard_map/ppermute | solution.py:169
  29.0 1.6 %collective-permute-start.8 = (f32[4,32,256]{2,1,0:T(8,128)S(1)}, f32[4,32,256]{2,1,0:T(8,128)S(1)}, u32[]{:S(2)}, u32[]{:S(2)}) collective-permute-start(f32[4,32,256]{2,1,0:T(8,128)S(1)} %pad_maximum_fusion.2), channel_id=1, source_target_pairs={{0,4},{2,6},{4,0},{6,2},{8,12},{10,14},{12,8},{14,10},{16,20},{18,... | collective-permute-start | bytes 393224 | tf_op jit(solution)/shard_map/ppermute | solution.py:176
  30.6 3.4 %collective-permute-done.8 = f32[4,32,256]{2,1,0:T(8,128)S(1)} collective-permute-done((f32[4,32,256]{2,1,0:T(8,128)S(1)}, f32[4,32,256]{2,1,0:T(8,128)S(1)}, u32[]{:S(2)}, u32[]{:S(2)}) %collective-permute-start.8) | collective-permute-done | bytes 131104 | tf_op jit(solution)/shard_map/ppermute | solution.py:176
  34.1 0.1 collective-permute-start.9
  34.3 0.5 %copy-done.1 = f32[4,2,32,256]{3,2,1,0:T(8,128)} copy-done((f32[4,2,32,256]{3,2,1,0:T(8,128)}, f32[4,2,32,256]{3,2,1,0:T(8,128)S(1)}, u32[]{:S(2)}) %copy-start.1) | copy-done | bytes 262168
  34.8 0.9 %collective-permute-done.9 = f32[8,32,256]{2,1,0:T(8,128)S(1)} collective-permute-done((f32[8,32,256]{2,1,0:T(8,128)S(1)}, f32[8,32,256]{2,1,0:T(8,128)S(1)}, u32[]{:S(2)}, u32[]{:S(2)}) %collective-permute-start.9) | collective-permute-done | bytes 262176 | tf_op jit(solution)/shard_map/ppermute | solution.py:176
  35.7 0.1 copy-done
  35.8 0.6 %copy-done.2 = f32[8,32,256]{2,1,0:T(8,128)} copy-done((f32[8,32,256]{2,1,0:T(8,128)}, f32[8,32,256]{2,1,0:T(8,128)S(1)}, u32[]{:S(2)}) %copy-start.2) | copy-done | bytes 262168
  36.4 10.1 %shard_map.77 = f32[8,4096]{1,0:T(8,128)} custom-call(f32[32]{0:T(128)} %copy-done.5, f32[8,64,512]{2,1,0:T(8,128)} %copy-done, f32[256,256]{1,0:T(8,128)} %bitcast.41, f32[256,256]{1,0:T(8,128)} %bitcast.46), custom_call_target="tpu_custom_call" | custom-call | tf_op jit(solution)/shard_map/pallas_call | solution.py:117
  46.5 0.9 %reduce_sum.18 = f32[4096]{0:T(1024)S(1)} reduce(f32[8,4096]{1,0:T(8,128)} %shard_map.77, f32[]{:T(128)} %constant.182.clone.1), dimensions={0}, to_apply=%region_0.1 | reduce | flops 28672 | bytes 147460 | tf_op jit(solution)/shard_map/reduce_sum | solution.py:135
  47.4 0.1 mul.137
  47.5 0.0 copy-start.3
  47.5 0.1 fusion.15
  47.6 1.6 %collective-permute-start.10 = (f32[64]{0:T(128)S(1)}, f32[64]{0:T(128)S(1)}, u32[]{:S(2)}, u32[]{:S(2)}) collective-permute-start(f32[64]{0:T(128)S(1)} %fusion.15), channel_id=1, source_target_pairs={{0,1},{1,0},{2,3},{3,2},{4,5},{5,4},{6,7},{7,6},{8,9},{9,8},{10,11... | collective-permute-start | bytes 776 | tf_op jit(solution)/shard_map/ppermute | solution.py:233
  49.2 2.0 %collective-permute-done.10 = f32[64]{0:T(128)S(1)} collective-permute-done((f32[64]{0:T(128)S(1)}, f32[64]{0:T(128)S(1)}, u32[]{:S(2)}, u32[]{:S(2)}) %collective-permute-start.10) | collective-permute-done | bytes 288 | tf_op jit(solution)/shard_map/ppermute | solution.py:233
  51.2 0.5 %add_log_fusion = f32[64]{0:T(128)} fusion(f32[64]{0:T(128)S(1)} %fusion.15, f32[64]{0:T(128)S(1)} %collective-permute-done.10), kind=kLoop, calls=%fused_computation.62 | loop fusion | flops 192 | bytes 768 | tf_op jit(solution)/shard_map/log | solution.py:236
  (27 shorter events, 0.4 us)
Async XLA Ops:
  0.7 0.7 %copy-start.9 = (f32[512]{0:T(512)S(1)}, f32[512]{0:T(512)}, u32[]{:S(2)}) copy-start(f32[512]{0:T(512)} %param.7) | copy-start | bytes 6148
  0.7 0.7 %copy-start.8 = (s32[512,1]{0,1:T(1,128)S(1)}, s32[512,1]{0,1:T(1,128)}, u32[]{:S(2)}) copy-start(s32[512,1]{0,1:T(1,128)} %param.8) | copy-start | bytes 6148
  0.7 0.7 %copy-start.7 = (s32[512]{0:T(512)S(1)}, s32[512]{0:T(512)}, u32[]{:S(2)}) copy-start(s32[512]{0:T(512)} %param.9) | copy-start | bytes 6148
  2.8 0.7 %copy-start.4 = (f32[3,512]{1,0:T(4,128)S(1)}, f32[3,512]{1,0:T(4,128)}, u32[]{:S(2)}) copy-start(f32[3,512]{1,0:T(4,128)} %param.10) | copy-start | bytes 18436
  2.8 2.8 %collective-permute-start = (f32[8,32,256]{2,1,0:T(8,128)S(1)}, f32[8,32,256]{2,1,0:T(8,128)S(1)}, u32[]{:S(2)}, u32[]{:S(2)}) collective-permute-start(f32[8,32,256]{2,1,0:T(8,128)S(1)} %dynamic-slice_bitcast_fusion), channel_id=1, source_target_pairs={{0,2},{2,0},{4,6},{6,4},{8,10},{10,8},{12,14},{14,12},{16,18},{18,... | collective-permute-start | bytes 786440 | tf_op jit(solution)/shard_map/ppermute | solution.py:156
  3.5 1.6 %copy-start.5 = (f32[32]{0:T(128)}, f32[32]{0:T(128)S(1)}, u32[]{:S(2)}) copy-start(f32[32]{0:T(128)S(1)} %add_multiply_fusion.wave_ref) | copy-start | bytes 388
  3.7 0.7 %copy-start.6 = (f32[3,64]{1,0:T(4,128)S(1)}, f32[3,64]{1,0:T(4,128)}, u32[]{:S(2)}) copy-start(f32[3,64]{1,0:T(4,128)} %param.11) | copy-start | bytes 2308
  5.7 6.6 %collective-permute-start.1 = (f32[4,32,256]{2,1,0:T(8,128)S(1)}, f32[4,32,256]{2,1,0:T(8,128)S(1)}, u32[]{:S(2)}, u32[]{:S(2)}) collective-permute-start(f32[4,32,256]{2,1,0:T(8,128)S(1)} %dynamic-slice_bitcast_fusion.1), channel_id=1, source_target_pairs={{0,4},{2,6},{4,0},{6,2},{8,12},{10,14},{12,8},{14,10},{16,20},{18,... | collective-permute-start | bytes 393224 | tf_op jit(solution)/shard_map/ppermute | solution.py:156
  12.3 5.5 %collective-permute-start.4 = (f32[32,256]{1,0:T(8,128)S(1)}, f32[32,256]{1,0:T(8,128)S(1)}, u32[]{:S(2)}, u32[]{:S(2)}) collective-permute-start(f32[32,256]{1,0:T(8,128)S(1)} %get-tuple-element.11), channel_id=1, source_target_pairs={{0,24},{2,26},{4,28},{6,30},{8,0},{10,2},{12,4},{14,6},{16,8},{18,... | collective-permute-start | bytes 98312 | tf_op jit(solution)/shard_map/ppermute | solution.py:161
  16.2 4.8 %collective-permute-start.3 = (f32[32,256]{1,0:T(8,128)S(1)}, f32[32,256]{1,0:T(8,128)S(1)}, u32[]{:S(2)}, u32[]{:S(2)}) collective-permute-start(f32[32,256]{1,0:T(8,128)S(1)} %get-tuple-element.12), channel_id=1, source_target_pairs={{0,16},{2,18},{4,20},{6,22},{8,24},{10,26},{12,28},{14,30},{16,0},... | collective-permute-start | bytes 98312 | tf_op jit(solution)/shard_map/ppermute | solution.py:161
  16.2 5.7 %collective-permute-start.2 = (f32[32,256]{1,0:T(8,128)S(1)}, f32[32,256]{1,0:T(8,128)S(1)}, u32[]{:S(2)}, u32[]{:S(2)}) collective-permute-start(f32[32,256]{1,0:T(8,128)S(1)} %get-tuple-element.10), channel_id=1, source_target_pairs={{0,8},{2,10},{4,12},{6,14},{8,16},{10,18},{12,20},{14,22},{16,24},... | collective-permute-start | bytes 98312 | tf_op jit(solution)/shard_map/ppermute | solution.py:161
  22.0 4.3 %collective-permute-start.7 = (f32[32,256]{1,0:T(8,128)S(1)}, f32[32,256]{1,0:T(8,128)S(1)}, u32[]{:S(2)}, u32[]{:S(2)}) collective-permute-start(f32[32,256]{1,0:T(8,128)S(1)} %fusion.13), channel_id=1, source_target_pairs={{0,24},{2,26},{4,28},{6,30},{8,0},{10,2},{12,4},{14,6},{16,8},{18,... | collective-permute-start | bytes 98312 | tf_op jit(solution)/shard_map/ppermute | solution.py:169
  22.7 4.8 %collective-permute-start.6 = (f32[32,256]{1,0:T(8,128)S(1)}, f32[32,256]{1,0:T(8,128)S(1)}, u32[]{:S(2)}, u32[]{:S(2)}) collective-permute-start(f32[32,256]{1,0:T(8,128)S(1)} %fusion.13), channel_id=1, source_target_pairs={{0,16},{2,18},{4,20},{6,22},{8,24},{10,26},{12,28},{14,30},{16,0},... | collective-permute-start | bytes 98312 | tf_op jit(solution)/shard_map/ppermute | solution.py:169
  23.2 5.7 %collective-permute-start.5 = (f32[32,256]{1,0:T(8,128)S(1)}, f32[32,256]{1,0:T(8,128)S(1)}, u32[]{:S(2)}, u32[]{:S(2)}) collective-permute-start(f32[32,256]{1,0:T(8,128)S(1)} %fusion.13), channel_id=1, source_target_pairs={{0,8},{2,10},{4,12},{6,14},{8,16},{10,18},{12,20},{14,22},{16,24},... | collective-permute-start | bytes 98312 | tf_op jit(solution)/shard_map/ppermute | solution.py:169
  29.0 5.0 %collective-permute-start.8 = (f32[4,32,256]{2,1,0:T(8,128)S(1)}, f32[4,32,256]{2,1,0:T(8,128)S(1)}, u32[]{:S(2)}, u32[]{:S(2)}) collective-permute-start(f32[4,32,256]{2,1,0:T(8,128)S(1)} %pad_maximum_fusion.2), channel_id=1, source_target_pairs={{0,4},{2,6},{4,0},{6,2},{8,12},{10,14},{12,8},{14,10},{16,20},{18,... | collective-permute-start | bytes 393224 | tf_op jit(solution)/shard_map/ppermute | solution.py:176
  34.1 0.7 %copy-start.1 = (f32[4,2,32,256]{3,2,1,0:T(8,128)}, f32[4,2,32,256]{3,2,1,0:T(8,128)S(1)}, u32[]{:S(2)}) copy-start(f32[4,2,32,256]{3,2,1,0:T(8,128)S(1)} %pad_maximum_fusion) | copy-start | bytes 786436
  34.1 1.6 %collective-permute-start.9 = (f32[8,32,256]{2,1,0:T(8,128)S(1)}, f32[8,32,256]{2,1,0:T(8,128)S(1)}, u32[]{:S(2)}, u32[]{:S(2)}) collective-permute-start(f32[8,32,256]{2,1,0:T(8,128)S(1)} %bitcast.40), channel_id=1, source_target_pairs={{0,2},{2,0},{4,6},{6,4},{8,10},{10,8},{12,14},{14,12},{16,18},{18,... | collective-permute-start | bytes 786440 | tf_op jit(solution)/shard_map/ppermute | solution.py:176
  34.8 1.0 %copy-start = (f32[8,64,512]{2,1,0:T(8,128)}, f32[8,64,512]{2,1,0:T(8,128)S(1)}, u32[]{:S(2)}) copy-start(f32[8,64,512]{2,1,0:T(8,128)S(1)} %sqrt_dynamic-update-slice_fusion.geo_ref) | copy-start | bytes 3145732
  35.7 0.7 %copy-start.2 = (f32[8,32,256]{2,1,0:T(8,128)}, f32[8,32,256]{2,1,0:T(8,128)S(1)}, u32[]{:S(2)}) copy-start(f32[8,32,256]{2,1,0:T(8,128)S(1)} %collective-permute-done.9) | copy-start | bytes 786436
  47.5 4.2 %copy-start.3 = (f32[32,2,64]{2,1,0:T(2,128)}, f32[32,2,64]{2,1,0:T(2,128)S(1)}, u32[]{:S(2)}) copy-start(f32[32,2,64]{2,1,0:T(2,128)S(1)} %mul.137) | copy-start | bytes 49156
  47.6 3.6 %collective-permute-start.10 = (f32[64]{0:T(128)S(1)}, f32[64]{0:T(128)S(1)}, u32[]{:S(2)}, u32[]{:S(2)}) collective-permute-start(f32[64]{0:T(128)S(1)} %fusion.15), channel_id=1, source_target_pairs={{0,1},{1,0},{2,3},{3,2},{4,5},{5,4},{6,7},{7,6},{8,9},{9,8},{10,11... | collective-permute-start | bytes 776 | tf_op jit(solution)/shard_map/ppermute | solution.py:233

commit v16 on v8

--- a/solution.py
+++ b/solution.py
@@ -12,7 +12,7 @@
 reference_radius = 10.0
 
 
-def field_kernel(block_group, freq_unroll, wave_ref, geo_ref, src_ref, out_ref, acc_ref, chan_ref, spread_ref):
+def field_kernel(block_group, freq_unroll, wave_ref, geo_ref, src_ref, out_ref, acc_ref, chan_ref):
     freqs, _, observers, lanes = acc_ref.shape
     blocks = observers // 8
 
@@ -22,11 +22,6 @@
 
     chan_ref[...] = jnp.transpose(src_ref[...])
 
-    def spread_body(row, carry):
-        spread_ref[row] = jnp.broadcast_to(chan_ref[pl.ds(row, 1), :], (8, lanes))
-        return carry
-
-    lax.fori_loop(0, chan_ref.shape[0], spread_body, 0, unroll=8)
 
     def block_body(group, carry):
         spans = [
@@ -40,7 +35,7 @@
 
         def freq_body(f, phase):
             base = f * 8
-            channel = [spread_ref[base + c] for c in range(8)]
+            channel = [chan_ref[pl.ds(base + c, 8, stride=0), :] for c in range(8)]
             wave = wave_ref[f]
             turned = []
             for member, rows in enumerate(spans):
@@ -101,7 +96,7 @@
         ]
     )
     summed = pl.pallas_call(
-        functools.partial(field_kernel, math.gcd(observers // 8, 4), 2),
+        functools.partial(field_kernel, math.gcd(observers // 8, 4), 4),
         grid=(panel_total // 128,),
         in_specs=[
             pl.BlockSpec(memory_space=pltpu.SMEM),
@@ -113,7 +108,6 @@
         scratch_shapes=[
             pltpu.VMEM((freqs, 2, observers, 128), jnp.float32),
             pltpu.VMEM((columns, 128), jnp.float32),
-            pltpu.VMEM((columns, 8, 128), jnp.float32),
         ],
         compiler_params=pltpu.CompilerParams(dimension_semantics=("arbitrary",)),
     )(wave_numbers, geometry, portion)

time: 51.9 us -> 50.7 us (0.977)
  Pallas kernels: 9.93 us -> 8.7 us
    pallas_call x1, Pallas kernels: 9.93 us -> 8.7 us  [far_field(): pl.pallas_call(functools.partial(field_kernel, math.gcd(observers // 8, 4...]
where the time goes in v16:
time: 50.7 us; the launch traced here: 50.4 us
  waiting for transfers between devices  18.4 us (36%)
  starting transfers between devices  14.4 us (28%)
  Pallas kernels  8.7 us (17%)
  other arithmetic  4.74 us (9%)
  local copies, waits for them, and re-layouts  1.59 us (3%)
  matrix products  1.42 us (3%)
  between operations  1.11 us (2%)
    pallas_call x1, Pallas kernels, far_field(): pl.pallas_call(functools.partial(field_kernel, math.gcd(observers // 8, 4...  8.7 us
    ppermute x3, starting transfers between devices, halving_sum(): total = total + lax.ppermute(piece, 'obs', quad_pairs(groups, shift))  4.91 us
    ppermute x2, waiting for transfers between devices, doubling_gather(): other = lax.ppermute(gathered, 'obs', partner_pairs(groups, bit))  4.87 us
    ppermute x3, waiting for transfers between devices, halving_sum(): total = total + lax.ppermute(piece, 'obs', quad_pairs(groups, shift))  4.22 us
    ppermute x2, waiting for transfers between devices, halving_sum(): current = keep + lax.ppermute(send, 'obs', partner_pairs(groups, bit))  3.69 us
    ppermute x3, waiting for transfers between devices, doubling_gather(): lax.ppermute(own, 'obs', quad_pairs(groups, shift))  3.65 us
    ppermute x3, starting transfers between devices, doubling_gather(): lax.ppermute(own, 'obs', quad_pairs(groups, shift))  3.2 us
    ppermute x2, starting transfers between devices, halving_sum(): current = keep + lax.ppermute(send, 'obs', partner_pairs(groups, bit))  3.09 us
  transfers between devices with their start and end apart: 11, of which 10 were waited for; matrix products, arithmetic and copies ran while one was open for 4% of the time, Pallas kernels for 0%

profile of v16, /device:TPU:0, one launch (start us, length us, event | category | flops | bytes accessed | tf_op | source)
XLA Modules:
  0.0 50.4 jit_solution(6748939777619530475)
XLA Ops:
  0.7 0.0 copy-start.7
  0.7 0.0 copy-start.6
  0.7 0.0 copy-start.5
  0.7 0.6 %copy-done.7 = f32[512]{0:T(512)S(1)} copy-done((f32[512]{0:T(512)S(1)}, f32[512]{0:T(512)}, u32[]{:S(2)}) %copy-start.7) | copy-done | bytes 2072
  1.3 0.0 copy-done.6
  1.4 0.0 copy-done.5
  1.4 1.4 %fusion = f32[512,256]{1,0:T(8,128)S(1)} fusion(s32[512]{0:T(512)S(1)} %copy-done.5, s32[512]{0:T(512)S(1)} %bitcast.57, s32[512]{0:T(512)S(1)} %get-tuple-element.15, s32[512]{0:T(512)S(1)} %get-tuple-element.16, bf16[512,256]{1,0:T(8,128)(2,1)} %param.6, f32[512]{0:T(512)S(1)} %copy-done.7), kind=kOutput, calls=%fused_computation | convolution fusion | flops 135397376 | bytes 796672 | tf_op jit(solution)/shard_map/dot_general | solution.py:174
  2.8 0.0 copy-start.2
  2.8 0.5 %collective-permute-start = (f32[8,32,256]{2,1,0:T(8,128)S(1)}, f32[8,32,256]{2,1,0:T(8,128)S(1)}, u32[]{:S(2)}, u32[]{:S(2)}) collective-permute-start(f32[8,32,256]{2,1,0:T(8,128)S(1)} %dynamic-slice_bitcast_fusion), channel_id=1, source_target_pairs={{0,2},{2,0},{4,6},{6,4},{8,10},{10,8},{12,14},{14,12},{16,18},{18,... | collective-permute-start | bytes 786440 | tf_op jit(solution)/shard_map/ppermute | solution.py:135
  3.4 0.1 copy-done.2
  3.5 0.5 %copy-done.4 = f32[3,64]{1,0:T(4,128)S(1)} copy-done((f32[3,64]{1,0:T(4,128)S(1)}, f32[3,64]{1,0:T(4,128)}, u32[]{:S(2)}) %copy-start.4) | copy-done | bytes 792
  4.1 0.1 broadcast_subtract_fusion
  4.1 0.5 %multiply_dynamic-update-slice_fusion.1 = (f32[8,64,512]{2,1,0:T(8,128)S(1)}, f32[1,64,512]{2,1,0:T(8,128)S(1)}) fusion(f32[]{:T(128)S(1)} %bitcast.55, f32[3,64,512]{2,1,0:T(8,128)S(1)} %broadcast_subtract_fusion), kind=kLoop, calls=%fused_computation.32 | loop fusion | flops 262143 | bytes 655364
  4.8 0.0 copy-done.3
  4.8 0.5 %multiply_dynamic-update-slice_fusion = f32[8,64,512]{2,1,0:T(8,128)S(1)} fusion(f32[8,64,512]{2,1,0:T(8,128)S(1)} %get-tuple-element.2, f32[1,64,512]{2,1,0:T(8,128)S(1)} %get-tuple-element.3, f32[]{:T(128)S(1)} %bitcast.56), kind=kLoop, calls=%fused_computation.31 | loop fusion | flops 98304 | bytes 262656
  5.3 0.0 collective-permute-done
  5.4 2.6 %collective-permute-start.1 = (f32[4,32,256]{2,1,0:T(8,128)S(1)}, f32[4,32,256]{2,1,0:T(8,128)S(1)}, u32[]{:S(2)}, u32[]{:S(2)}) collective-permute-start(f32[4,32,256]{2,1,0:T(8,128)S(1)} %dynamic-slice_bitcast_fusion.1), channel_id=1, source_target_pairs={{0,4},{2,6},{4,0},{6,2},{8,12},{10,14},{12,8},{14,10},{16,20},{18,... | collective-permute-start | bytes 393224 | tf_op jit(solution)/shard_map/ppermute | solution.py:135
  8.0 0.5 cosine_dynamic-update-slice_fusion
  8.5 3.7 %collective-permute-done.1 = f32[4,32,256]{2,1,0:T(8,128)S(1)} collective-permute-done((f32[4,32,256]{2,1,0:T(8,128)S(1)}, f32[4,32,256]{2,1,0:T(8,128)S(1)}, u32[]{:S(2)}, u32[]{:S(2)}) %collective-permute-start.1) | collective-permute-done | bytes 131104 | tf_op jit(solution)/shard_map/ppermute | solution.py:135
  12.2 3.9 %collective-permute-start.4 = (f32[32,256]{1,0:T(8,128)S(1)}, f32[32,256]{1,0:T(8,128)S(1)}, u32[]{:S(2)}, u32[]{:S(2)}) collective-permute-start(f32[32,256]{1,0:T(8,128)S(1)} %get-tuple-element.13), channel_id=1, source_target_pairs={{0,24},{2,26},{4,28},{6,30},{8,0},{10,2},{12,4},{14,6},{16,8},{18,... | collective-permute-start | bytes 98312 | tf_op jit(solution)/shard_map/ppermute | solution.py:140
  16.1 0.0 collective-permute-start.3
  16.1 1.0 %collective-permute-start.2 = (f32[32,256]{1,0:T(8,128)S(1)}, f32[32,256]{1,0:T(8,128)S(1)}, u32[]{:S(2)}, u32[]{:S(2)}) collective-permute-start(f32[32,256]{1,0:T(8,128)S(1)} %get-tuple-element.12), channel_id=1, source_target_pairs={{0,8},{2,10},{4,12},{6,14},{8,16},{10,18},{12,20},{14,22},{16,24},... | collective-permute-start | bytes 98312 | tf_op jit(solution)/shard_map/ppermute | solution.py:140
  17.1 0.5 sine_dynamic-update-slice_fusion
  17.6 0.1 collective-permute-done.4
  17.7 3.2 %collective-permute-done.3 = f32[32,256]{1,0:T(8,128)S(1)} collective-permute-done((f32[32,256]{1,0:T(8,128)S(1)}, f32[32,256]{1,0:T(8,128)S(1)}, u32[]{:S(2)}, u32[]{:S(2)}) %collective-permute-start.3) | collective-permute-done | bytes 32800 | tf_op jit(solution)/shard_map/ppermute | solution.py:140
  20.9 0.9 %collective-permute-done.2 = f32[32,256]{1,0:T(8,128)S(1)} collective-permute-done((f32[32,256]{1,0:T(8,128)S(1)}, f32[32,256]{1,0:T(8,128)S(1)}, u32[]{:S(2)}, u32[]{:S(2)}) %collective-permute-start.2) | collective-permute-done | bytes 32800 | tf_op jit(solution)/shard_map/ppermute | solution.py:140
  21.8 0.6 %collective-permute-start.7 = (f32[32,256]{1,0:T(8,128)S(1)}, f32[32,256]{1,0:T(8,128)S(1)}, u32[]{:S(2)}, u32[]{:S(2)}) collective-permute-start(f32[32,256]{1,0:T(8,128)S(1)} %fusion.13), channel_id=1, source_target_pairs={{0,24},{2,26},{4,28},{6,30},{8,0},{10,2},{12,4},{14,6},{16,8},{18,... | collective-permute-start | bytes 98312 | tf_op jit(solution)/shard_map/ppermute | solution.py:148
  22.4 0.6 %collective-permute-start.6 = (f32[32,256]{1,0:T(8,128)S(1)}, f32[32,256]{1,0:T(8,128)S(1)}, u32[]{:S(2)}, u32[]{:S(2)}) collective-permute-start(f32[32,256]{1,0:T(8,128)S(1)} %fusion.13), channel_id=1, source_target_pairs={{0,16},{2,18},{4,20},{6,22},{8,24},{10,26},{12,28},{14,30},{16,0},... | collective-permute-start | bytes 98312 | tf_op jit(solution)/shard_map/ppermute | solution.py:148
  23.1 1.9 %collective-permute-start.5 = (f32[32,256]{1,0:T(8,128)S(1)}, f32[32,256]{1,0:T(8,128)S(1)}, u32[]{:S(2)}, u32[]{:S(2)}) collective-permute-start(f32[32,256]{1,0:T(8,128)S(1)} %fusion.13), channel_id=1, source_target_pairs={{0,8},{2,10},{4,12},{6,14},{8,16},{10,18},{12,20},{14,22},{16,24},... | collective-permute-start | bytes 98312 | tf_op jit(solution)/shard_map/ppermute | solution.py:148
  25.1 0.7 %collective-permute-done.7 = f32[32,256]{1,0:T(8,128)S(1)} collective-permute-done((f32[32,256]{1,0:T(8,128)S(1)}, f32[32,256]{1,0:T(8,128)S(1)}, u32[]{:S(2)}, u32[]{:S(2)}) %collective-permute-start.7) | collective-permute-done | bytes 32800 | tf_op jit(solution)/shard_map/ppermute | solution.py:148
  25.8 1.5 %collective-permute-done.6 = f32[32,256]{1,0:T(8,128)S(1)} collective-permute-done((f32[32,256]{1,0:T(8,128)S(1)}, f32[32,256]{1,0:T(8,128)S(1)}, u32[]{:S(2)}, u32[]{:S(2)}) %collective-permute-start.6) | collective-permute-done | bytes 32800 | tf_op jit(solution)/shard_map/ppermute | solution.py:148
  27.2 1.5 %collective-permute-done.5 = f32[32,256]{1,0:T(8,128)S(1)} collective-permute-done((f32[32,256]{1,0:T(8,128)S(1)}, f32[32,256]{1,0:T(8,128)S(1)}, u32[]{:S(2)}, u32[]{:S(2)}) %collective-permute-start.5) | collective-permute-done | bytes 32800 | tf_op jit(solution)/shard_map/ppermute | solution.py:148
  28.8 1.6 %collective-permute-start.8 = (f32[4,32,256]{2,1,0:T(8,128)S(1)}, f32[4,32,256]{2,1,0:T(8,128)S(1)}, u32[]{:S(2)}, u32[]{:S(2)}) collective-permute-start(f32[4,32,256]{2,1,0:T(8,128)S(1)} %pad_maximum_fusion.3), channel_id=1, source_target_pairs={{0,4},{2,6},{4,0},{6,2},{8,12},{10,14},{12,8},{14,10},{16,20},{18,... | collective-permute-start | bytes 393224 | tf_op jit(solution)/shard_map/ppermute | solution.py:155
  30.4 3.4 %collective-permute-done.8 = f32[4,32,256]{2,1,0:T(8,128)S(1)} collective-permute-done((f32[4,32,256]{2,1,0:T(8,128)S(1)}, f32[4,32,256]{2,1,0:T(8,128)S(1)}, u32[]{:S(2)}, u32[]{:S(2)}) %collective-permute-start.8) | collective-permute-done | bytes 131104 | tf_op jit(solution)/shard_map/ppermute | solution.py:155
  33.9 0.1 collective-permute-start.9
  34.1 0.0 copy-start
  34.1 1.4 %collective-permute-done.9 = f32[8,32,256]{2,1,0:T(8,128)S(1)} collective-permute-done((f32[8,32,256]{2,1,0:T(8,128)S(1)}, f32[8,32,256]{2,1,0:T(8,128)S(1)}, u32[]{:S(2)}, u32[]{:S(2)}) %collective-permute-start.9) | collective-permute-done | bytes 262176 | tf_op jit(solution)/shard_map/ppermute | solution.py:155
  35.5 0.1 select_bitcast_fusion.1
  35.6 0.9 %pad_maximum_fusion = f32[8,2,32,256]{3,2,1,0:T(8,128)} fusion(f32[8,1,32,256]{3,2,1,0:T(8,128)S(1)} %get-tuple-element.5, f32[8,1,32,256]{3,2,1,0:T(8,128)S(1)} %get-tuple-element.4), kind=kLoop, calls=%fused_computation.4 | loop fusion | flops 131072 | bytes 1048576 | tf_op jit(solution)/shard_map/stack | solution.py:158
  36.5 0.0 copy-done
  36.5 8.7 %shard_map.77 = f32[8,4096]{1,0:T(8,128)} custom-call(f32[32]{0:T(128)} %copy-done.3, f32[8,64,512]{2,1,0:T(8,128)} %copy-done, f32[512,256]{1,0:T(8,128)} %bitcast.45), custom_call_target="tpu_custom_call" | custom-call | tf_op jit(solution)/shard_map/pallas_call | solution.py:98
  45.2 0.9 %fusion.15 = f32[4096]{0:T(1024)S(1)} fusion(f32[8,4096]{1,0:T(8,128)} %shard_map.77), kind=kLoop, calls=%fused_computation.46 | loop fusion | flops 4096 | bytes 32768 | tf_op jit(solution)/shard_map/mul | solution.py:190
  46.1 0.1 mul.137
  46.2 0.0 copy-start.1
  46.2 0.1 fusion.16
  46.3 1.6 %collective-permute-start.10 = (f32[64]{0:T(128)S(1)}, f32[64]{0:T(128)S(1)}, u32[]{:S(2)}, u32[]{:S(2)}) collective-permute-start(f32[64]{0:T(128)S(1)} %fusion.16), channel_id=1, source_target_pairs={{0,1},{1,0},{2,3},{3,2},{4,5},{5,4},{6,7},{7,6},{8,9},{9,8},{10,11... | collective-permute-start | bytes 776 | tf_op jit(solution)/shard_map/ppermute | solution.py:193
  47.9 2.0 %collective-permute-done.10 = f32[64]{0:T(128)S(1)} collective-permute-done((f32[64]{0:T(128)S(1)}, f32[64]{0:T(128)S(1)}, u32[]{:S(2)}, u32[]{:S(2)}) %collective-permute-start.10) | collective-permute-done | bytes 288 | tf_op jit(solution)/shard_map/ppermute | solution.py:193
  49.9 0.5 %add_log_fusion = f32[64]{0:T(128)} fusion(f32[64]{0:T(128)S(1)} %fusion.16, f32[64]{0:T(128)S(1)} %collective-permute-done.10), kind=kLoop, calls=%fused_computation.63 | loop fusion | flops 192 | bytes 768 | tf_op jit(solution)/shard_map/log | solution.py:196
  (20 shorter events, 0.3 us)
Async XLA Ops:
  0.7 0.7 %copy-start.7 = (f32[512]{0:T(512)S(1)}, f32[512]{0:T(512)}, u32[]{:S(2)}) copy-start(f32[512]{0:T(512)} %param.7) | copy-start | bytes 6148
  0.7 0.7 %copy-start.6 = (s32[512,1]{0,1:T(1,128)S(1)}, s32[512,1]{0,1:T(1,128)}, u32[]{:S(2)}) copy-start(s32[512,1]{0,1:T(1,128)} %param.8) | copy-start | bytes 6148
  0.7 0.7 %copy-start.5 = (s32[512]{0:T(512)S(1)}, s32[512]{0:T(512)}, u32[]{:S(2)}) copy-start(s32[512]{0:T(512)} %param.9) | copy-start | bytes 6148
  2.8 0.7 %copy-start.2 = (f32[3,512]{1,0:T(4,128)S(1)}, f32[3,512]{1,0:T(4,128)}, u32[]{:S(2)}) copy-start(f32[3,512]{1,0:T(4,128)} %param.10) | copy-start | bytes 18436
  2.8 2.5 %collective-permute-start = (f32[8,32,256]{2,1,0:T(8,128)S(1)}, f32[8,32,256]{2,1,0:T(8,128)S(1)}, u32[]{:S(2)}, u32[]{:S(2)}) collective-permute-start(f32[8,32,256]{2,1,0:T(8,128)S(1)} %dynamic-slice_bitcast_fusion), channel_id=1, source_target_pairs={{0,2},{2,0},{4,6},{6,4},{8,10},{10,8},{12,14},{14,12},{16,18},{18,... | collective-permute-start | bytes 786440 | tf_op jit(solution)/shard_map/ppermute | solution.py:135
  3.4 0.7 %copy-start.4 = (f32[3,64]{1,0:T(4,128)S(1)}, f32[3,64]{1,0:T(4,128)}, u32[]{:S(2)}) copy-start(f32[3,64]{1,0:T(4,128)} %param.11) | copy-start | bytes 2308
  4.0 0.8 %copy-start.3 = (f32[32]{0:T(128)}, f32[32]{0:T(128)S(1)}, u32[]{:S(2)}) copy-start(f32[32]{0:T(128)S(1)} %add_multiply_fusion.wave_ref) | copy-start | bytes 388
  5.4 6.7 %collective-permute-start.1 = (f32[4,32,256]{2,1,0:T(8,128)S(1)}, f32[4,32,256]{2,1,0:T(8,128)S(1)}, u32[]{:S(2)}, u32[]{:S(2)}) collective-permute-start(f32[4,32,256]{2,1,0:T(8,128)S(1)} %dynamic-slice_bitcast_fusion.1), channel_id=1, source_target_pairs={{0,4},{2,6},{4,0},{6,2},{8,12},{10,14},{12,8},{14,10},{16,20},{18,... | collective-permute-start | bytes 393224 | tf_op jit(solution)/shard_map/ppermute | solution.py:135
  12.2 5.5 %collective-permute-start.4 = (f32[32,256]{1,0:T(8,128)S(1)}, f32[32,256]{1,0:T(8,128)S(1)}, u32[]{:S(2)}, u32[]{:S(2)}) collective-permute-start(f32[32,256]{1,0:T(8,128)S(1)} %get-tuple-element.13), channel_id=1, source_target_pairs={{0,24},{2,26},{4,28},{6,30},{8,0},{10,2},{12,4},{14,6},{16,8},{18,... | collective-permute-start | bytes 98312 | tf_op jit(solution)/shard_map/ppermute | solution.py:140
  16.1 4.8 %collective-permute-start.3 = (f32[32,256]{1,0:T(8,128)S(1)}, f32[32,256]{1,0:T(8,128)S(1)}, u32[]{:S(2)}, u32[]{:S(2)}) collective-permute-start(f32[32,256]{1,0:T(8,128)S(1)} %get-tuple-element.14), channel_id=1, source_target_pairs={{0,16},{2,18},{4,20},{6,22},{8,24},{10,26},{12,28},{14,30},{16,0},... | collective-permute-start | bytes 98312 | tf_op jit(solution)/shard_map/ppermute | solution.py:140
  16.1 5.7 %collective-permute-start.2 = (f32[32,256]{1,0:T(8,128)S(1)}, f32[32,256]{1,0:T(8,128)S(1)}, u32[]{:S(2)}, u32[]{:S(2)}) collective-permute-start(f32[32,256]{1,0:T(8,128)S(1)} %get-tuple-element.12), channel_id=1, source_target_pairs={{0,8},{2,10},{4,12},{6,14},{8,16},{10,18},{12,20},{14,22},{16,24},... | collective-permute-start | bytes 98312 | tf_op jit(solution)/shard_map/ppermute | solution.py:140
  21.8 4.0 %collective-permute-start.7 = (f32[32,256]{1,0:T(8,128)S(1)}, f32[32,256]{1,0:T(8,128)S(1)}, u32[]{:S(2)}, u32[]{:S(2)}) collective-permute-start(f32[32,256]{1,0:T(8,128)S(1)} %fusion.13), channel_id=1, source_target_pairs={{0,24},{2,26},{4,28},{6,30},{8,0},{10,2},{12,4},{14,6},{16,8},{18,... | collective-permute-start | bytes 98312 | tf_op jit(solution)/shard_map/ppermute | solution.py:148
  22.4 4.8 %collective-permute-start.6 = (f32[32,256]{1,0:T(8,128)S(1)}, f32[32,256]{1,0:T(8,128)S(1)}, u32[]{:S(2)}, u32[]{:S(2)}) collective-permute-start(f32[32,256]{1,0:T(8,128)S(1)} %fusion.13), channel_id=1, source_target_pairs={{0,16},{2,18},{4,20},{6,22},{8,24},{10,26},{12,28},{14,30},{16,0},... | collective-permute-start | bytes 98312 | tf_op jit(solution)/shard_map/ppermute | solution.py:148
  23.1 5.7 %collective-permute-start.5 = (f32[32,256]{1,0:T(8,128)S(1)}, f32[32,256]{1,0:T(8,128)S(1)}, u32[]{:S(2)}, u32[]{:S(2)}) collective-permute-start(f32[32,256]{1,0:T(8,128)S(1)} %fusion.13), channel_id=1, source_target_pairs={{0,8},{2,10},{4,12},{6,14},{8,16},{10,18},{12,20},{14,22},{16,24},... | collective-permute-start | bytes 98312 | tf_op jit(solution)/shard_map/ppermute | solution.py:148
  28.8 5.0 %collective-permute-start.8 = (f32[4,32,256]{2,1,0:T(8,128)S(1)}, f32[4,32,256]{2,1,0:T(8,128)S(1)}, u32[]{:S(2)}, u32[]{:S(2)}) collective-permute-start(f32[4,32,256]{2,1,0:T(8,128)S(1)} %pad_maximum_fusion.3), channel_id=1, source_target_pairs={{0,4},{2,6},{4,0},{6,2},{8,12},{10,14},{12,8},{14,10},{16,20},{18,... | collective-permute-start | bytes 393224 | tf_op jit(solution)/shard_map/ppermute | solution.py:155
  33.9 1.6 %collective-permute-start.9 = (f32[8,32,256]{2,1,0:T(8,128)S(1)}, f32[8,32,256]{2,1,0:T(8,128)S(1)}, u32[]{:S(2)}, u32[]{:S(2)}) collective-permute-start(f32[8,32,256]{2,1,0:T(8,128)S(1)} %bitcast.46), channel_id=1, source_target_pairs={{0,2},{2,0},{4,6},{6,4},{8,10},{10,8},{12,14},{14,12},{16,18},{18,... | collective-permute-start | bytes 786440 | tf_op jit(solution)/shard_map/ppermute | solution.py:155
  34.1 2.4 %copy-start = (f32[8,64,512]{2,1,0:T(8,128)}, f32[8,64,512]{2,1,0:T(8,128)S(1)}, u32[]{:S(2)}) copy-start(f32[8,64,512]{2,1,0:T(8,128)S(1)} %sqrt_dynamic-update-slice_fusion.geo_ref) | copy-start | bytes 3145732
  46.2 4.2 %copy-start.1 = (f32[32,2,64]{2,1,0:T(2,128)}, f32[32,2,64]{2,1,0:T(2,128)S(1)}, u32[]{:S(2)}) copy-start(f32[32,2,64]{2,1,0:T(2,128)S(1)} %mul.137) | copy-start | bytes 49156
  46.3 3.6 %collective-permute-start.10 = (f32[64]{0:T(128)S(1)}, f32[64]{0:T(128)S(1)}, u32[]{:S(2)}, u32[]{:S(2)}) collective-permute-start(f32[64]{0:T(128)S(1)} %fusion.16), channel_id=1, source_target_pairs={{0,1},{1,0},{2,3},{3,2},{4,5},{5,4},{6,7},{7,6},{8,9},{9,8},{10,11... | collective-permute-start | bytes 776 | tf_op jit(solution)/shard_map/ppermute | solution.py:193

commit v17 on v10

--- a/solution.py
+++ b/solution.py
@@ -12,18 +12,13 @@
 reference_radius = 10.0
 
 
-def field_kernel(block_group, freq_unroll, scale, wave_ref, geo_ref, src_ref, out_ref, acc_ref, chan_ref, spread_ref):
+def field_kernel(block_group, freq_unroll, wave_ref, geo_ref, src_ref, out_ref, acc_ref, chan_ref):
     freqs, _, observers, lanes = acc_ref.shape
     blocks = observers // 8
-    chunk = pl.program_id(0)
+
 
     chan_ref[...] = jnp.transpose(src_ref[...])
 
-    def spread_body(row, carry):
-        spread_ref[row] = jnp.broadcast_to(chan_ref[pl.ds(row, 1), :], (8, lanes))
-        return carry
-
-    lax.fori_loop(0, chan_ref.shape[0], spread_body, 0, unroll=8)
 
     def sweep(first):
         def block_body(group, carry):
@@ -38,7 +33,7 @@
 
             def freq_body(f, phase):
                 base = f * 8
-                channel = [spread_ref[base + c] for c in range(8)]
+                channel = [chan_ref[pl.ds(base + c, 8, stride=0), :] for c in range(8)]
                 wave = wave_ref[f]
                 turned = []
                 for member, rows in enumerate(spans):
@@ -71,27 +66,27 @@
 
         lax.fori_loop(0, blocks // block_group, block_body, 0)
 
-    @pl.when(chunk == 0)
+    @pl.when(pl.program_id(0) == 0)
     def _():
         sweep(True)
 
-    @pl.when(chunk > 0)
+    @pl.when(pl.program_id(0) > 0)
     def _():
         sweep(False)
 
-    @pl.when(chunk == pl.num_programs(0) - 1)
+    @pl.when(pl.program_id(0) == pl.num_programs(0) - 1)
     def _():
-        def fold_body(row, carry):
-            f = row // 2
-            part = row % 2
-            flipped = jnp.transpose(acc_ref[f, part])
-            out_ref[f, pl.ds(part, 1), :] = jnp.sum(flipped, axis=0, keepdims=True) * scale
-            return carry
-
-        lax.fori_loop(0, freqs * 2, fold_body, 0)
-
-
-def far_field(portion, panel_position, observer_position, wave_numbers, scale):
+        flat = acc_ref[...].reshape(freqs * 2 * observers, lanes)
+        out_ref[...] = lax.dot_general(
+            jnp.ones((8, lanes), jnp.float32),
+            flat,
+            (((1,), (1,)), ((), ())),
+            precision=lax.Precision.HIGHEST,
+            preferred_element_type=jnp.float32,
+        )
+
+
+def far_field(portion, panel_position, observer_position, wave_numbers):
     panel_total, columns = portion.shape
     freqs = columns // 8
     observers = observer_position.shape[1]
@@ -113,23 +108,22 @@
         ]
     )
     summed = pl.pallas_call(
-        functools.partial(field_kernel, math.gcd(observers // 8, 4), 2, scale),
+        functools.partial(field_kernel, math.gcd(observers // 8, 4), 4),
         grid=(panel_total // 128,),
         in_specs=[
             pl.BlockSpec(memory_space=pltpu.SMEM),
             pl.BlockSpec((8, observers, 128), lambda chunk: (0, 0, chunk)),
             pl.BlockSpec((128, columns), lambda chunk: (chunk, 0)),
         ],
-        out_specs=pl.BlockSpec((freqs, 2, observers), lambda chunk: (0, 0, 0)),
-        out_shape=jax.ShapeDtypeStruct((freqs, 2, observers), jnp.float32),
+        out_specs=pl.BlockSpec((8, freqs * 2 * observers), lambda chunk: (0, 0)),
+        out_shape=jax.ShapeDtypeStruct((8, freqs * 2 * observers), jnp.float32),
         scratch_shapes=[
             pltpu.VMEM((freqs, 2, observers, 128), jnp.float32),
             pltpu.VMEM((columns, 128), jnp.float32),
-            pltpu.VMEM((columns, 8, 128), jnp.float32),
         ],
         compiler_params=pltpu.CompilerParams(dimension_semantics=("arbitrary",)),
     )(wave_numbers, geometry, portion)
-    return summed
+    return summed[0].reshape(freqs, 2, observers)
 
 
 def partner_pairs(groups, bit):
@@ -204,9 +198,8 @@
         portion = lax.all_to_all(
             jnp.broadcast_to(own_source[None], blocks.shape), "obs", 0, 0, tiled=True
         ).reshape(panel_total, columns)
-    pressure = far_field(
-        portion, panel_position, observer_position, wave_numbers, reference_radius / math.sqrt(panel_total)
-    )
+    summed = far_field(portion, panel_position, observer_position, wave_numbers)
+    pressure = summed * (reference_radius / math.sqrt(panel_total))
     energy = jnp.sum(pressure[:, 0] * pressure[:, 0] + pressure[:, 1] * pressure[:, 1], axis=0)
     if lax.axis_size("freq") == 2:
         band_total = energy + lax.ppermute(energy, "freq", [(0, 1), (1, 0)])

time: 56.7 us -> 50.5 us (0.89)
  Pallas kernels: 14.9 us -> 8.49 us
    pallas_call x1, Pallas kernels: 14.9 us -> 8.49 us  [far_field(): pl.pallas_call(functools.partial(field_kernel, math.gcd(observers // 8, 4...]
    mul x0 -> x1, other arithmetic: none -> 0.95 us  [shards(): pressure = summed * (reference_radius / math.sqrt(panel_total))]
    reduce_sum x1, other arithmetic: 0.89 us -> 0.05 us  [shards(): jnp.sum(pressure[:, 0] * pressure[:, 0] + pressure[:, 1] * pressure[:, 1]...]
    unnamed x14 -> x16, local copies, waits for them, and re-layouts: 1.38 us -> 1.38 us
where the time goes in v17:
time: 50.5 us; the launch traced here: 50.2 us
  waiting for transfers between devices  18.4 us (36%)
  starting transfers between devices  14.4 us (29%)
  Pallas kernels  8.49 us (17%)
  other arithmetic  4.74 us (9%)
  local copies, waits for them, and re-layouts  1.59 us (3%)
  matrix products  1.42 us (3%)
  between operations  1.11 us (2%)
    pallas_call x1, Pallas kernels, far_field(): pl.pallas_call(functools.partial(field_kernel, math.gcd(observers // 8, 4...  8.49 us
    ppermute x3, starting transfers between devices, halving_sum(): total = total + lax.ppermute(piece, 'obs', quad_pairs(groups, shift))  4.91 us
    ppermute x2, waiting for transfers between devices, doubling_gather(): other = lax.ppermute(gathered, 'obs', partner_pairs(groups, bit))  4.87 us
    ppermute x3, waiting for transfers between devices, halving_sum(): total = total + lax.ppermute(piece, 'obs', quad_pairs(groups, shift))  4.22 us
    ppermute x2, waiting for transfers between devices, halving_sum(): current = keep + lax.ppermute(send, 'obs', partner_pairs(groups, bit))  3.69 us
    ppermute x3, waiting for transfers between devices, doubling_gather(): lax.ppermute(own, 'obs', quad_pairs(groups, shift))  3.65 us
    ppermute x3, starting transfers between devices, doubling_gather(): lax.ppermute(own, 'obs', quad_pairs(groups, shift))  3.2 us
    ppermute x2, starting transfers between devices, halving_sum(): current = keep + lax.ppermute(send, 'obs', partner_pairs(groups, bit))  3.09 us
  transfers between devices with their start and end apart: 11, of which 10 were waited for; matrix products, arithmetic and copies ran while one was open for 4% of the time, Pallas kernels for 0%

profile of v17, /device:TPU:0, one launch (start us, length us, event | category | flops | bytes accessed | tf_op | source)
XLA Modules:
  0.0 50.2 jit_solution(7837817593826003047)
XLA Ops:
  0.7 0.0 copy-start.7
  0.7 0.0 copy-start.6
  0.7 0.0 copy-start.5
  0.7 0.6 %copy-done.7 = f32[512]{0:T(512)S(1)} copy-done((f32[512]{0:T(512)S(1)}, f32[512]{0:T(512)}, u32[]{:S(2)}) %copy-start.7) | copy-done | bytes 2072
  1.3 0.0 copy-done.6
  1.4 0.0 copy-done.5
  1.4 1.4 %fusion = f32[512,256]{1,0:T(8,128)S(1)} fusion(s32[512]{0:T(512)S(1)} %copy-done.5, s32[512]{0:T(512)S(1)} %bitcast.57, s32[512]{0:T(512)S(1)} %get-tuple-element.15, s32[512]{0:T(512)S(1)} %get-tuple-element.16, bf16[512,256]{1,0:T(8,128)(2,1)} %param.6, f32[512]{0:T(512)S(1)} %copy-done.7), kind=kOutput, calls=%fused_computation | convolution fusion | flops 135397376 | bytes 796672 | tf_op jit(solution)/shard_map/dot_general | solution.py:186
  2.8 0.0 copy-start.2
  2.8 0.5 %collective-permute-start = (f32[8,32,256]{2,1,0:T(8,128)S(1)}, f32[8,32,256]{2,1,0:T(8,128)S(1)}, u32[]{:S(2)}, u32[]{:S(2)}) collective-permute-start(f32[8,32,256]{2,1,0:T(8,128)S(1)} %dynamic-slice_bitcast_fusion), channel_id=1, source_target_pairs={{0,2},{2,0},{4,6},{6,4},{8,10},{10,8},{12,14},{14,12},{16,18},{18,... | collective-permute-start | bytes 786440 | tf_op jit(solution)/shard_map/ppermute | solution.py:147
  3.4 0.1 copy-done.2
  3.5 0.5 %copy-done.4 = f32[3,64]{1,0:T(4,128)S(1)} copy-done((f32[3,64]{1,0:T(4,128)S(1)}, f32[3,64]{1,0:T(4,128)}, u32[]{:S(2)}) %copy-start.4) | copy-done | bytes 792
  4.1 0.1 broadcast_subtract_fusion
  4.1 0.5 %multiply_dynamic-update-slice_fusion.1 = (f32[8,64,512]{2,1,0:T(8,128)S(1)}, f32[1,64,512]{2,1,0:T(8,128)S(1)}) fusion(f32[]{:T(128)S(1)} %bitcast.55, f32[3,64,512]{2,1,0:T(8,128)S(1)} %broadcast_subtract_fusion), kind=kLoop, calls=%fused_computation.32 | loop fusion | flops 262143 | bytes 655364
  4.8 0.0 copy-done.3
  4.8 0.5 %multiply_dynamic-update-slice_fusion = f32[8,64,512]{2,1,0:T(8,128)S(1)} fusion(f32[8,64,512]{2,1,0:T(8,128)S(1)} %get-tuple-element.2, f32[1,64,512]{2,1,0:T(8,128)S(1)} %get-tuple-element.3, f32[]{:T(128)S(1)} %bitcast.56), kind=kLoop, calls=%fused_computation.31 | loop fusion | flops 98304 | bytes 262656
  5.3 0.0 collective-permute-done
  5.4 2.6 %collective-permute-start.1 = (f32[4,32,256]{2,1,0:T(8,128)S(1)}, f32[4,32,256]{2,1,0:T(8,128)S(1)}, u32[]{:S(2)}, u32[]{:S(2)}) collective-permute-start(f32[4,32,256]{2,1,0:T(8,128)S(1)} %dynamic-slice_bitcast_fusion.1), channel_id=1, source_target_pairs={{0,4},{2,6},{4,0},{6,2},{8,12},{10,14},{12,8},{14,10},{16,20},{18,... | collective-permute-start | bytes 393224 | tf_op jit(solution)/shard_map/ppermute | solution.py:147
  8.0 0.5 cosine_dynamic-update-slice_fusion
  8.5 3.7 %collective-permute-done.1 = f32[4,32,256]{2,1,0:T(8,128)S(1)} collective-permute-done((f32[4,32,256]{2,1,0:T(8,128)S(1)}, f32[4,32,256]{2,1,0:T(8,128)S(1)}, u32[]{:S(2)}, u32[]{:S(2)}) %collective-permute-start.1) | collective-permute-done | bytes 131104 | tf_op jit(solution)/shard_map/ppermute | solution.py:147
  12.2 3.9 %collective-permute-start.4 = (f32[32,256]{1,0:T(8,128)S(1)}, f32[32,256]{1,0:T(8,128)S(1)}, u32[]{:S(2)}, u32[]{:S(2)}) collective-permute-start(f32[32,256]{1,0:T(8,128)S(1)} %get-tuple-element.13), channel_id=1, source_target_pairs={{0,24},{2,26},{4,28},{6,30},{8,0},{10,2},{12,4},{14,6},{16,8},{18,... | collective-permute-start | bytes 98312 | tf_op jit(solution)/shard_map/ppermute | solution.py:152
  16.1 0.0 collective-permute-start.3
  16.1 1.0 %collective-permute-start.2 = (f32[32,256]{1,0:T(8,128)S(1)}, f32[32,256]{1,0:T(8,128)S(1)}, u32[]{:S(2)}, u32[]{:S(2)}) collective-permute-start(f32[32,256]{1,0:T(8,128)S(1)} %get-tuple-element.12), channel_id=1, source_target_pairs={{0,8},{2,10},{4,12},{6,14},{8,16},{10,18},{12,20},{14,22},{16,24},... | collective-permute-start | bytes 98312 | tf_op jit(solution)/shard_map/ppermute | solution.py:152
  17.1 0.5 sine_dynamic-update-slice_fusion
  17.6 0.1 collective-permute-done.4
  17.7 3.2 %collective-permute-done.3 = f32[32,256]{1,0:T(8,128)S(1)} collective-permute-done((f32[32,256]{1,0:T(8,128)S(1)}, f32[32,256]{1,0:T(8,128)S(1)}, u32[]{:S(2)}, u32[]{:S(2)}) %collective-permute-start.3) | collective-permute-done | bytes 32800 | tf_op jit(solution)/shard_map/ppermute | solution.py:152
  20.9 0.9 %collective-permute-done.2 = f32[32,256]{1,0:T(8,128)S(1)} collective-permute-done((f32[32,256]{1,0:T(8,128)S(1)}, f32[32,256]{1,0:T(8,128)S(1)}, u32[]{:S(2)}, u32[]{:S(2)}) %collective-permute-start.2) | collective-permute-done | bytes 32800 | tf_op jit(solution)/shard_map/ppermute | solution.py:152
  21.8 0.6 %collective-permute-start.7 = (f32[32,256]{1,0:T(8,128)S(1)}, f32[32,256]{1,0:T(8,128)S(1)}, u32[]{:S(2)}, u32[]{:S(2)}) collective-permute-start(f32[32,256]{1,0:T(8,128)S(1)} %fusion.13), channel_id=1, source_target_pairs={{0,24},{2,26},{4,28},{6,30},{8,0},{10,2},{12,4},{14,6},{16,8},{18,... | collective-permute-start | bytes 98312 | tf_op jit(solution)/shard_map/ppermute | solution.py:160
  22.4 0.6 %collective-permute-start.6 = (f32[32,256]{1,0:T(8,128)S(1)}, f32[32,256]{1,0:T(8,128)S(1)}, u32[]{:S(2)}, u32[]{:S(2)}) collective-permute-start(f32[32,256]{1,0:T(8,128)S(1)} %fusion.13), channel_id=1, source_target_pairs={{0,16},{2,18},{4,20},{6,22},{8,24},{10,26},{12,28},{14,30},{16,0},... | collective-permute-start | bytes 98312 | tf_op jit(solution)/shard_map/ppermute | solution.py:160
  23.1 1.9 %collective-permute-start.5 = (f32[32,256]{1,0:T(8,128)S(1)}, f32[32,256]{1,0:T(8,128)S(1)}, u32[]{:S(2)}, u32[]{:S(2)}) collective-permute-start(f32[32,256]{1,0:T(8,128)S(1)} %fusion.13), channel_id=1, source_target_pairs={{0,8},{2,10},{4,12},{6,14},{8,16},{10,18},{12,20},{14,22},{16,24},... | collective-permute-start | bytes 98312 | tf_op jit(solution)/shard_map/ppermute | solution.py:160
  25.1 0.7 %collective-permute-done.7 = f32[32,256]{1,0:T(8,128)S(1)} collective-permute-done((f32[32,256]{1,0:T(8,128)S(1)}, f32[32,256]{1,0:T(8,128)S(1)}, u32[]{:S(2)}, u32[]{:S(2)}) %collective-permute-start.7) | collective-permute-done | bytes 32800 | tf_op jit(solution)/shard_map/ppermute | solution.py:160
  25.8 1.5 %collective-permute-done.6 = f32[32,256]{1,0:T(8,128)S(1)} collective-permute-done((f32[32,256]{1,0:T(8,128)S(1)}, f32[32,256]{1,0:T(8,128)S(1)}, u32[]{:S(2)}, u32[]{:S(2)}) %collective-permute-start.6) | collective-permute-done | bytes 32800 | tf_op jit(solution)/shard_map/ppermute | solution.py:160
  27.2 1.5 %collective-permute-done.5 = f32[32,256]{1,0:T(8,128)S(1)} collective-permute-done((f32[32,256]{1,0:T(8,128)S(1)}, f32[32,256]{1,0:T(8,128)S(1)}, u32[]{:S(2)}, u32[]{:S(2)}) %collective-permute-start.5) | collective-permute-done | bytes 32800 | tf_op jit(solution)/shard_map/ppermute | solution.py:160
  28.8 1.6 %collective-permute-start.8 = (f32[4,32,256]{2,1,0:T(8,128)S(1)}, f32[4,32,256]{2,1,0:T(8,128)S(1)}, u32[]{:S(2)}, u32[]{:S(2)}) collective-permute-start(f32[4,32,256]{2,1,0:T(8,128)S(1)} %pad_maximum_fusion.3), channel_id=1, source_target_pairs={{0,4},{2,6},{4,0},{6,2},{8,12},{10,14},{12,8},{14,10},{16,20},{18,... | collective-permute-start | bytes 393224 | tf_op jit(solution)/shard_map/ppermute | solution.py:167
  30.4 3.4 %collective-permute-done.8 = f32[4,32,256]{2,1,0:T(8,128)S(1)} collective-permute-done((f32[4,32,256]{2,1,0:T(8,128)S(1)}, f32[4,32,256]{2,1,0:T(8,128)S(1)}, u32[]{:S(2)}, u32[]{:S(2)}) %collective-permute-start.8) | collective-permute-done | bytes 131104 | tf_op jit(solution)/shard_map/ppermute | solution.py:167
  33.9 0.1 collective-permute-start.9
  34.1 0.0 copy-start
  34.1 1.4 %collective-permute-done.9 = f32[8,32,256]{2,1,0:T(8,128)S(1)} collective-permute-done((f32[8,32,256]{2,1,0:T(8,128)S(1)}, f32[8,32,256]{2,1,0:T(8,128)S(1)}, u32[]{:S(2)}, u32[]{:S(2)}) %collective-permute-start.9) | collective-permute-done | bytes 262176 | tf_op jit(solution)/shard_map/ppermute | solution.py:167
  35.5 0.1 select_bitcast_fusion.1
  35.6 0.9 %pad_maximum_fusion = f32[8,2,32,256]{3,2,1,0:T(8,128)} fusion(f32[8,1,32,256]{3,2,1,0:T(8,128)S(1)} %get-tuple-element.5, f32[8,1,32,256]{3,2,1,0:T(8,128)S(1)} %get-tuple-element.4), kind=kLoop, calls=%fused_computation.4 | loop fusion | flops 131072 | bytes 1048576 | tf_op jit(solution)/shard_map/stack | solution.py:170
  36.5 0.0 copy-done
  36.5 8.5 %shard_map.77 = f32[8,4096]{1,0:T(8,128)} custom-call(f32[32]{0:T(128)} %copy-done.3, f32[8,64,512]{2,1,0:T(8,128)} %copy-done, f32[512,256]{1,0:T(8,128)} %bitcast.45), custom_call_target="tpu_custom_call" | custom-call | tf_op jit(solution)/shard_map/pallas_call | solution.py:110
  45.0 0.9 %fusion.15 = f32[4096]{0:T(1024)S(1)} fusion(f32[8,4096]{1,0:T(8,128)} %shard_map.77), kind=kLoop, calls=%fused_computation.46 | loop fusion | flops 4096 | bytes 32768 | tf_op jit(solution)/shard_map/mul | solution.py:202
  45.9 0.1 mul.137
  46.0 0.0 copy-start.1
  46.0 0.1 fusion.16
  46.1 1.6 %collective-permute-start.10 = (f32[64]{0:T(128)S(1)}, f32[64]{0:T(128)S(1)}, u32[]{:S(2)}, u32[]{:S(2)}) collective-permute-start(f32[64]{0:T(128)S(1)} %fusion.16), channel_id=1, source_target_pairs={{0,1},{1,0},{2,3},{3,2},{4,5},{5,4},{6,7},{7,6},{8,9},{9,8},{10,11... | collective-permute-start | bytes 776 | tf_op jit(solution)/shard_map/ppermute | solution.py:205
  47.7 2.0 %collective-permute-done.10 = f32[64]{0:T(128)S(1)} collective-permute-done((f32[64]{0:T(128)S(1)}, f32[64]{0:T(128)S(1)}, u32[]{:S(2)}, u32[]{:S(2)}) %collective-permute-start.10) | collective-permute-done | bytes 288 | tf_op jit(solution)/shard_map/ppermute | solution.py:205
  49.7 0.5 %add_log_fusion = f32[64]{0:T(128)} fusion(f32[64]{0:T(128)S(1)} %fusion.16, f32[64]{0:T(128)S(1)} %collective-permute-done.10), kind=kLoop, calls=%fused_computation.63 | loop fusion | flops 192 | bytes 768 | tf_op jit(solution)/shard_map/log | solution.py:208
  (20 shorter events, 0.3 us)
Async XLA Ops:
  0.7 0.7 %copy-start.7 = (f32[512]{0:T(512)S(1)}, f32[512]{0:T(512)}, u32[]{:S(2)}) copy-start(f32[512]{0:T(512)} %param.7) | copy-start | bytes 6148
  0.7 0.7 %copy-start.6 = (s32[512,1]{0,1:T(1,128)S(1)}, s32[512,1]{0,1:T(1,128)}, u32[]{:S(2)}) copy-start(s32[512,1]{0,1:T(1,128)} %param.8) | copy-start | bytes 6148
  0.7 0.7 %copy-start.5 = (s32[512]{0:T(512)S(1)}, s32[512]{0:T(512)}, u32[]{:S(2)}) copy-start(s32[512]{0:T(512)} %param.9) | copy-start | bytes 6148
  2.8 0.7 %copy-start.2 = (f32[3,512]{1,0:T(4,128)S(1)}, f32[3,512]{1,0:T(4,128)}, u32[]{:S(2)}) copy-start(f32[3,512]{1,0:T(4,128)} %param.10) | copy-start | bytes 18436
  2.8 2.5 %collective-permute-start = (f32[8,32,256]{2,1,0:T(8,128)S(1)}, f32[8,32,256]{2,1,0:T(8,128)S(1)}, u32[]{:S(2)}, u32[]{:S(2)}) collective-permute-start(f32[8,32,256]{2,1,0:T(8,128)S(1)} %dynamic-slice_bitcast_fusion), channel_id=1, source_target_pairs={{0,2},{2,0},{4,6},{6,4},{8,10},{10,8},{12,14},{14,12},{16,18},{18,... | collective-permute-start | bytes 786440 | tf_op jit(solution)/shard_map/ppermute | solution.py:147
  3.4 0.7 %copy-start.4 = (f32[3,64]{1,0:T(4,128)S(1)}, f32[3,64]{1,0:T(4,128)}, u32[]{:S(2)}) copy-start(f32[3,64]{1,0:T(4,128)} %param.11) | copy-start | bytes 2308
  4.0 0.8 %copy-start.3 = (f32[32]{0:T(128)}, f32[32]{0:T(128)S(1)}, u32[]{:S(2)}) copy-start(f32[32]{0:T(128)S(1)} %add_multiply_fusion.wave_ref) | copy-start | bytes 388
  5.4 6.7 %collective-permute-start.1 = (f32[4,32,256]{2,1,0:T(8,128)S(1)}, f32[4,32,256]{2,1,0:T(8,128)S(1)}, u32[]{:S(2)}, u32[]{:S(2)}) collective-permute-start(f32[4,32,256]{2,1,0:T(8,128)S(1)} %dynamic-slice_bitcast_fusion.1), channel_id=1, source_target_pairs={{0,4},{2,6},{4,0},{6,2},{8,12},{10,14},{12,8},{14,10},{16,20},{18,... | collective-permute-start | bytes 393224 | tf_op jit(solution)/shard_map/ppermute | solution.py:147
  12.2 5.5 %collective-permute-start.4 = (f32[32,256]{1,0:T(8,128)S(1)}, f32[32,256]{1,0:T(8,128)S(1)}, u32[]{:S(2)}, u32[]{:S(2)}) collective-permute-start(f32[32,256]{1,0:T(8,128)S(1)} %get-tuple-element.13), channel_id=1, source_target_pairs={{0,24},{2,26},{4,28},{6,30},{8,0},{10,2},{12,4},{14,6},{16,8},{18,... | collective-permute-start | bytes 98312 | tf_op jit(solution)/shard_map/ppermute | solution.py:152
  16.1 4.8 %collective-permute-start.3 = (f32[32,256]{1,0:T(8,128)S(1)}, f32[32,256]{1,0:T(8,128)S(1)}, u32[]{:S(2)}, u32[]{:S(2)}) collective-permute-start(f32[32,256]{1,0:T(8,128)S(1)} %get-tuple-element.14), channel_id=1, source_target_pairs={{0,16},{2,18},{4,20},{6,22},{8,24},{10,26},{12,28},{14,30},{16,0},... | collective-permute-start | bytes 98312 | tf_op jit(solution)/shard_map/ppermute | solution.py:152
  16.1 5.7 %collective-permute-start.2 = (f32[32,256]{1,0:T(8,128)S(1)}, f32[32,256]{1,0:T(8,128)S(1)}, u32[]{:S(2)}, u32[]{:S(2)}) collective-permute-start(f32[32,256]{1,0:T(8,128)S(1)} %get-tuple-element.12), channel_id=1, source_target_pairs={{0,8},{2,10},{4,12},{6,14},{8,16},{10,18},{12,20},{14,22},{16,24},... | collective-permute-start | bytes 98312 | tf_op jit(solution)/shard_map/ppermute | solution.py:152
  21.8 4.0 %collective-permute-start.7 = (f32[32,256]{1,0:T(8,128)S(1)}, f32[32,256]{1,0:T(8,128)S(1)}, u32[]{:S(2)}, u32[]{:S(2)}) collective-permute-start(f32[32,256]{1,0:T(8,128)S(1)} %fusion.13), channel_id=1, source_target_pairs={{0,24},{2,26},{4,28},{6,30},{8,0},{10,2},{12,4},{14,6},{16,8},{18,... | collective-permute-start | bytes 98312 | tf_op jit(solution)/shard_map/ppermute | solution.py:160
  22.4 4.8 %collective-permute-start.6 = (f32[32,256]{1,0:T(8,128)S(1)}, f32[32,256]{1,0:T(8,128)S(1)}, u32[]{:S(2)}, u32[]{:S(2)}) collective-permute-start(f32[32,256]{1,0:T(8,128)S(1)} %fusion.13), channel_id=1, source_target_pairs={{0,16},{2,18},{4,20},{6,22},{8,24},{10,26},{12,28},{14,30},{16,0},... | collective-permute-start | bytes 98312 | tf_op jit(solution)/shard_map/ppermute | solution.py:160
  23.1 5.7 %collective-permute-start.5 = (f32[32,256]{1,0:T(8,128)S(1)}, f32[32,256]{1,0:T(8,128)S(1)}, u32[]{:S(2)}, u32[]{:S(2)}) collective-permute-start(f32[32,256]{1,0:T(8,128)S(1)} %fusion.13), channel_id=1, source_target_pairs={{0,8},{2,10},{4,12},{6,14},{8,16},{10,18},{12,20},{14,22},{16,24},... | collective-permute-start | bytes 98312 | tf_op jit(solution)/shard_map/ppermute | solution.py:160
  28.8 5.0 %collective-permute-start.8 = (f32[4,32,256]{2,1,0:T(8,128)S(1)}, f32[4,32,256]{2,1,0:T(8,128)S(1)}, u32[]{:S(2)}, u32[]{:S(2)}) collective-permute-start(f32[4,32,256]{2,1,0:T(8,128)S(1)} %pad_maximum_fusion.3), channel_id=1, source_target_pairs={{0,4},{2,6},{4,0},{6,2},{8,12},{10,14},{12,8},{14,10},{16,20},{18,... | collective-permute-start | bytes 393224 | tf_op jit(solution)/shard_map/ppermute | solution.py:167
  33.9 1.6 %collective-permute-start.9 = (f32[8,32,256]{2,1,0:T(8,128)S(1)}, f32[8,32,256]{2,1,0:T(8,128)S(1)}, u32[]{:S(2)}, u32[]{:S(2)}) collective-permute-start(f32[8,32,256]{2,1,0:T(8,128)S(1)} %bitcast.46), channel_id=1, source_target_pairs={{0,2},{2,0},{4,6},{6,4},{8,10},{10,8},{12,14},{14,12},{16,18},{18,... | collective-permute-start | bytes 786440 | tf_op jit(solution)/shard_map/ppermute | solution.py:167
  34.1 2.4 %copy-start = (f32[8,64,512]{2,1,0:T(8,128)}, f32[8,64,512]{2,1,0:T(8,128)S(1)}, u32[]{:S(2)}) copy-start(f32[8,64,512]{2,1,0:T(8,128)S(1)} %sqrt_dynamic-update-slice_fusion.geo_ref) | copy-start | bytes 3145732
  46.0 4.2 %copy-start.1 = (f32[32,2,64]{2,1,0:T(2,128)}, f32[32,2,64]{2,1,0:T(2,128)S(1)}, u32[]{:S(2)}) copy-start(f32[32,2,64]{2,1,0:T(2,128)S(1)} %mul.137) | copy-start | bytes 49156
  46.1 3.6 %collective-permute-start.10 = (f32[64]{0:T(128)S(1)}, f32[64]{0:T(128)S(1)}, u32[]{:S(2)}, u32[]{:S(2)}) collective-permute-start(f32[64]{0:T(128)S(1)} %fusion.16), channel_id=1, source_target_pairs={{0,1},{1,0},{2,3},{3,2},{4,5},{5,4},{6,7},{7,6},{8,9},{9,8},{10,11... | collective-permute-start | bytes 776 | tf_op jit(solution)/shard_map/ppermute | solution.py:205

commit v18 on v11

--- a/solution.py
+++ b/solution.py
@@ -13,7 +13,7 @@
 
 
 def field_kernel(
-    block_group, freq_unroll, low_chunks, wave_ref, geo_ref, low_ref, high_ref, out_ref, acc_ref, chan_ref, spread_ref
+    block_group, freq_unroll, low_chunks, wave_ref, geo_ref, low_ref, high_ref, out_ref, acc_ref, chan_ref
 ):
     freqs, _, observers, lanes = acc_ref.shape
     blocks = observers // 8
@@ -32,11 +32,6 @@
     def _():
         chan_ref[...] = jnp.transpose(high_ref[...])
 
-    def spread_body(row, carry):
-        spread_ref[row] = jnp.broadcast_to(chan_ref[pl.ds(row, 1), :], (8, lanes))
-        return carry
-
-    lax.fori_loop(0, chan_ref.shape[0], spread_body, 0, unroll=8)
 
     def block_body(group, carry):
         spans = [
@@ -50,7 +45,7 @@
 
         def freq_body(f, phase):
             base = f * 8
-            channel = [spread_ref[base + c] for c in range(8)]
+            channel = [chan_ref[pl.ds(base + c, 8, stride=0), :] for c in range(8)]
             wave = wave_ref[f]
             turned = []
             for member, rows in enumerate(spans):
@@ -113,7 +108,7 @@
         ]
     )
     summed = pl.pallas_call(
-        functools.partial(field_kernel, math.gcd(observers // 8, 4), 2, low_chunks),
+        functools.partial(field_kernel, math.gcd(observers // 8, 4), 4, low_chunks),
         grid=(panel_total // 128,),
         in_specs=[
             pl.BlockSpec(memory_space=pltpu.SMEM),
@@ -126,7 +121,6 @@
         scratch_shapes=[
             pltpu.VMEM((freqs, 2, observers, 128), jnp.float32),
             pltpu.VMEM((columns, 128), jnp.float32),
-            pltpu.VMEM((columns, 8, 128), jnp.float32),
         ],
         compiler_params=pltpu.CompilerParams(dimension_semantics=("arbitrary",)),
     )(wave_numbers, geometry, low, high)

time: 52 us -> 50.7 us (0.975)
  Pallas kernels: 10.1 us -> 8.83 us
    pallas_call x1, Pallas kernels: 10.1 us -> 8.83 us  [far_field(): pl.pallas_call(functools.partial(field_kernel, math.gcd(observers // 8, 4...]
where the time goes in v18:
time: 50.7 us; the launch traced here: 50.5 us
  waiting for transfers between devices  17.3 us (34%)
  starting transfers between devices  14.9 us (29%)
  Pallas kernels  8.83 us (17%)
  other arithmetic  3.81 us (8%)
  local copies, waits for them, and re-layouts  3.1 us (6%)
  matrix products  1.41 us (3%)
  between operations  1.12 us (2%)
    pallas_call x1, Pallas kernels, far_field(): pl.pallas_call(functools.partial(field_kernel, math.gcd(observers // 8, 4...  8.83 us
    ppermute x3, starting transfers between devices, halving_sum(): total = total + lax.ppermute(piece, 'obs', quad_pairs(groups, shift))  4.92 us
    ppermute x2, waiting for transfers between devices, doubling_gather(): other = lax.ppermute(gathered, 'obs', partner_pairs(groups, bit))  4.35 us
    ppermute x3, waiting for transfers between devices, halving_sum(): total = total + lax.ppermute(piece, 'obs', quad_pairs(groups, shift))  4.22 us
    ppermute x3, waiting for transfers between devices, doubling_gather(): lax.ppermute(own, 'obs', quad_pairs(groups, shift))  3.65 us
    ppermute x2, starting transfers between devices, halving_sum(): current = keep + lax.ppermute(send, 'obs', partner_pairs(groups, bit))  3.52 us
    ppermute x3, starting transfers between devices, doubling_gather(): lax.ppermute(own, 'obs', quad_pairs(groups, shift))  3.2 us
    ppermute x2, waiting for transfers between devices, halving_sum(): current = keep + lax.ppermute(send, 'obs', partner_pairs(groups, bit))  3.1 us
  transfers between devices with their start and end apart: 11, of which 10 were waited for; matrix products, arithmetic and copies ran while one was open for 5% of the time, Pallas kernels for 0%

profile of v18, /device:TPU:0, one launch (start us, length us, event | category | flops | bytes accessed | tf_op | source)
XLA Modules:
  0.0 50.5 jit_solution(7390751054157314079)
XLA Ops:
  0.7 0.0 copy-start.9
  0.7 0.0 copy-start.8
  0.7 0.0 copy-start.7
  0.7 0.6 %copy-done.9 = f32[512]{0:T(512)S(1)} copy-done((f32[512]{0:T(512)S(1)}, f32[512]{0:T(512)}, u32[]{:S(2)}) %copy-start.9) | copy-done | bytes 2072
  1.3 0.0 copy-done.8
  1.4 0.0 copy-done.7
  1.4 1.4 %fusion = f32[512,256]{1,0:T(8,128)S(1)} fusion(s32[512]{0:T(512)S(1)} %copy-done.7, s32[512]{0:T(512)S(1)} %bitcast.55, s32[512]{0:T(512)S(1)} %get-tuple-element.15, s32[512]{0:T(512)S(1)} %get-tuple-element.16, bf16[512,256]{1,0:T(8,128)(2,1)} %param.6, f32[512]{0:T(512)S(1)} %copy-done.9), kind=kOutput, calls=%fused_computation | convolution fusion | flops 135397376 | bytes 796672 | tf_op jit(solution)/shard_map/dot_general | solution.py:189
  2.8 0.0 copy-start.4
  2.8 0.5 %collective-permute-start = (f32[8,32,256]{2,1,0:T(8,128)S(1)}, f32[8,32,256]{2,1,0:T(8,128)S(1)}, u32[]{:S(2)}, u32[]{:S(2)}) collective-permute-start(f32[8,32,256]{2,1,0:T(8,128)S(1)} %dynamic-slice_bitcast_fusion), channel_id=1, source_target_pairs={{0,2},{2,0},{4,6},{6,4},{8,10},{10,8},{12,14},{14,12},{16,18},{18,... | collective-permute-start | bytes 786440 | tf_op jit(solution)/shard_map/ppermute | solution.py:148
  3.4 0.2 copy-done.4
  3.5 0.1 reshape.78
  3.7 0.0 copy-start.6
  3.7 0.1 sub.49
  3.8 0.6 %copy-done.6 = f32[3,64]{1,0:T(4,128)S(1)} copy-done((f32[3,64]{1,0:T(4,128)S(1)}, f32[3,64]{1,0:T(4,128)}, u32[]{:S(2)}) %copy-start.6) | copy-done | bytes 792
  4.4 0.1 broadcast_subtract_fusion
  4.5 0.5 %multiply_dynamic-update-slice_fusion.1 = (f32[8,64,512]{2,1,0:T(8,128)S(1)}, f32[1,64,512]{2,1,0:T(8,128)S(1)}) fusion(f32[]{:T(128)S(1)} %bitcast.53, f32[3,64,512]{2,1,0:T(8,128)S(1)} %broadcast_subtract_fusion), kind=kLoop, calls=%fused_computation.29 | loop fusion | flops 262143 | bytes 655364
  5.1 0.5 %multiply_dynamic-update-slice_fusion = f32[8,64,512]{2,1,0:T(8,128)S(1)} fusion(f32[8,64,512]{2,1,0:T(8,128)S(1)} %get-tuple-element.2, f32[1,64,512]{2,1,0:T(8,128)S(1)} %get-tuple-element.3, f32[]{:T(128)S(1)} %bitcast.54), kind=kLoop, calls=%fused_computation.28 | loop fusion | flops 98304 | bytes 262656
  5.7 3.0 %collective-permute-start.1 = (f32[4,32,256]{2,1,0:T(8,128)S(1)}, f32[4,32,256]{2,1,0:T(8,128)S(1)}, u32[]{:S(2)}, u32[]{:S(2)}) collective-permute-start(f32[4,32,256]{2,1,0:T(8,128)S(1)} %dynamic-slice_bitcast_fusion.1), channel_id=1, source_target_pairs={{0,4},{2,6},{4,0},{6,2},{8,12},{10,14},{12,8},{14,10},{16,20},{18,... | collective-permute-start | bytes 393224 | tf_op jit(solution)/shard_map/ppermute | solution.py:148
  8.7 0.5 cosine_dynamic-update-slice_fusion
  9.2 3.1 %collective-permute-done.1 = f32[4,32,256]{2,1,0:T(8,128)S(1)} collective-permute-done((f32[4,32,256]{2,1,0:T(8,128)S(1)}, f32[4,32,256]{2,1,0:T(8,128)S(1)}, u32[]{:S(2)}, u32[]{:S(2)}) %collective-permute-start.1) | collective-permute-done | bytes 131104 | tf_op jit(solution)/shard_map/ppermute | solution.py:148
  12.3 3.9 %collective-permute-start.4 = (f32[32,256]{1,0:T(8,128)S(1)}, f32[32,256]{1,0:T(8,128)S(1)}, u32[]{:S(2)}, u32[]{:S(2)}) collective-permute-start(f32[32,256]{1,0:T(8,128)S(1)} %get-tuple-element.11), channel_id=1, source_target_pairs={{0,24},{2,26},{4,28},{6,30},{8,0},{10,2},{12,4},{14,6},{16,8},{18,... | collective-permute-start | bytes 98312 | tf_op jit(solution)/shard_map/ppermute | solution.py:153
  16.2 0.0 collective-permute-start.3
  16.2 1.0 %collective-permute-start.2 = (f32[32,256]{1,0:T(8,128)S(1)}, f32[32,256]{1,0:T(8,128)S(1)}, u32[]{:S(2)}, u32[]{:S(2)}) collective-permute-start(f32[32,256]{1,0:T(8,128)S(1)} %get-tuple-element.10), channel_id=1, source_target_pairs={{0,8},{2,10},{4,12},{6,14},{8,16},{10,18},{12,20},{14,22},{16,24},... | collective-permute-start | bytes 98312 | tf_op jit(solution)/shard_map/ppermute | solution.py:153
  17.3 0.5 sine_dynamic-update-slice_fusion
  17.7 0.1 collective-permute-done.4
  17.8 3.2 %collective-permute-done.3 = f32[32,256]{1,0:T(8,128)S(1)} collective-permute-done((f32[32,256]{1,0:T(8,128)S(1)}, f32[32,256]{1,0:T(8,128)S(1)}, u32[]{:S(2)}, u32[]{:S(2)}) %collective-permute-start.3) | collective-permute-done | bytes 32800 | tf_op jit(solution)/shard_map/ppermute | solution.py:153
  21.1 0.9 %collective-permute-done.2 = f32[32,256]{1,0:T(8,128)S(1)} collective-permute-done((f32[32,256]{1,0:T(8,128)S(1)}, f32[32,256]{1,0:T(8,128)S(1)}, u32[]{:S(2)}, u32[]{:S(2)}) %collective-permute-start.2) | collective-permute-done | bytes 32800 | tf_op jit(solution)/shard_map/ppermute | solution.py:153
  22.0 0.7 %collective-permute-start.7 = (f32[32,256]{1,0:T(8,128)S(1)}, f32[32,256]{1,0:T(8,128)S(1)}, u32[]{:S(2)}, u32[]{:S(2)}) collective-permute-start(f32[32,256]{1,0:T(8,128)S(1)} %fusion.13), channel_id=1, source_target_pairs={{0,24},{2,26},{4,28},{6,30},{8,0},{10,2},{12,4},{14,6},{16,8},{18,... | collective-permute-start | bytes 98312 | tf_op jit(solution)/shard_map/ppermute | solution.py:161
  22.7 0.6 %collective-permute-start.6 = (f32[32,256]{1,0:T(8,128)S(1)}, f32[32,256]{1,0:T(8,128)S(1)}, u32[]{:S(2)}, u32[]{:S(2)}) collective-permute-start(f32[32,256]{1,0:T(8,128)S(1)} %fusion.13), channel_id=1, source_target_pairs={{0,16},{2,18},{4,20},{6,22},{8,24},{10,26},{12,28},{14,30},{16,0},... | collective-permute-start | bytes 98312 | tf_op jit(solution)/shard_map/ppermute | solution.py:161
  23.2 1.9 %collective-permute-start.5 = (f32[32,256]{1,0:T(8,128)S(1)}, f32[32,256]{1,0:T(8,128)S(1)}, u32[]{:S(2)}, u32[]{:S(2)}) collective-permute-start(f32[32,256]{1,0:T(8,128)S(1)} %fusion.13), channel_id=1, source_target_pairs={{0,8},{2,10},{4,12},{6,14},{8,16},{10,18},{12,20},{14,22},{16,24},... | collective-permute-start | bytes 98312 | tf_op jit(solution)/shard_map/ppermute | solution.py:161
  25.3 1.0 %collective-permute-done.7 = f32[32,256]{1,0:T(8,128)S(1)} collective-permute-done((f32[32,256]{1,0:T(8,128)S(1)}, f32[32,256]{1,0:T(8,128)S(1)}, u32[]{:S(2)}, u32[]{:S(2)}) %collective-permute-start.7) | collective-permute-done | bytes 32800 | tf_op jit(solution)/shard_map/ppermute | solution.py:161
  26.3 1.2 %collective-permute-done.6 = f32[32,256]{1,0:T(8,128)S(1)} collective-permute-done((f32[32,256]{1,0:T(8,128)S(1)}, f32[32,256]{1,0:T(8,128)S(1)}, u32[]{:S(2)}, u32[]{:S(2)}) %collective-permute-start.6) | collective-permute-done | bytes 32800 | tf_op jit(solution)/shard_map/ppermute | solution.py:161
  27.5 1.5 %collective-permute-done.5 = f32[32,256]{1,0:T(8,128)S(1)} collective-permute-done((f32[32,256]{1,0:T(8,128)S(1)}, f32[32,256]{1,0:T(8,128)S(1)}, u32[]{:S(2)}, u32[]{:S(2)}) %collective-permute-start.5) | collective-permute-done | bytes 32800 | tf_op jit(solution)/shard_map/ppermute | solution.py:161
  29.0 1.6 %collective-permute-start.8 = (f32[4,32,256]{2,1,0:T(8,128)S(1)}, f32[4,32,256]{2,1,0:T(8,128)S(1)}, u32[]{:S(2)}, u32[]{:S(2)}) collective-permute-start(f32[4,32,256]{2,1,0:T(8,128)S(1)} %pad_maximum_fusion.2), channel_id=1, source_target_pairs={{0,4},{2,6},{4,0},{6,2},{8,12},{10,14},{12,8},{14,10},{16,20},{18,... | collective-permute-start | bytes 393224 | tf_op jit(solution)/shard_map/ppermute | solution.py:168
  30.6 3.4 %collective-permute-done.8 = f32[4,32,256]{2,1,0:T(8,128)S(1)} collective-permute-done((f32[4,32,256]{2,1,0:T(8,128)S(1)}, f32[4,32,256]{2,1,0:T(8,128)S(1)}, u32[]{:S(2)}, u32[]{:S(2)}) %collective-permute-start.8) | collective-permute-done | bytes 131104 | tf_op jit(solution)/shard_map/ppermute | solution.py:168
  34.1 0.1 collective-permute-start.9
  34.3 0.5 %copy-done.1 = f32[4,2,32,256]{3,2,1,0:T(8,128)} copy-done((f32[4,2,32,256]{3,2,1,0:T(8,128)}, f32[4,2,32,256]{3,2,1,0:T(8,128)S(1)}, u32[]{:S(2)}) %copy-start.1) | copy-done | bytes 262168
  34.8 0.9 %collective-permute-done.9 = f32[8,32,256]{2,1,0:T(8,128)S(1)} collective-permute-done((f32[8,32,256]{2,1,0:T(8,128)S(1)}, f32[8,32,256]{2,1,0:T(8,128)S(1)}, u32[]{:S(2)}, u32[]{:S(2)}) %collective-permute-start.9) | collective-permute-done | bytes 262176 | tf_op jit(solution)/shard_map/ppermute | solution.py:168
  35.7 0.1 copy-done
  35.8 0.6 %copy-done.2 = f32[8,32,256]{2,1,0:T(8,128)} copy-done((f32[8,32,256]{2,1,0:T(8,128)}, f32[8,32,256]{2,1,0:T(8,128)S(1)}, u32[]{:S(2)}) %copy-start.2) | copy-done | bytes 262168
  36.4 8.8 %shard_map.77 = f32[8,4096]{1,0:T(8,128)} custom-call(f32[32]{0:T(128)} %copy-done.5, f32[8,64,512]{2,1,0:T(8,128)} %copy-done, f32[256,256]{1,0:T(8,128)} %bitcast.41, f32[256,256]{1,0:T(8,128)} %bitcast.46), custom_call_target="tpu_custom_call" | custom-call | tf_op jit(solution)/shard_map/pallas_call | solution.py:110
  45.2 0.9 %fusion.15 = f32[4096]{0:T(1024)S(1)} fusion(f32[8,4096]{1,0:T(8,128)} %shard_map.77), kind=kLoop, calls=%fused_computation.44 | loop fusion | flops 4096 | bytes 32768 | tf_op jit(solution)/shard_map/mul | solution.py:222
  46.2 0.1 mul.137
  46.3 0.0 copy-start.3
  46.3 0.1 fusion.16
  46.3 1.6 %collective-permute-start.10 = (f32[64]{0:T(128)S(1)}, f32[64]{0:T(128)S(1)}, u32[]{:S(2)}, u32[]{:S(2)}) collective-permute-start(f32[64]{0:T(128)S(1)} %fusion.16), channel_id=1, source_target_pairs={{0,1},{1,0},{2,3},{3,2},{4,5},{5,4},{6,7},{7,6},{8,9},{9,8},{10,11... | collective-permute-start | bytes 776 | tf_op jit(solution)/shard_map/ppermute | solution.py:225
  47.9 2.0 %collective-permute-done.10 = f32[64]{0:T(128)S(1)} collective-permute-done((f32[64]{0:T(128)S(1)}, f32[64]{0:T(128)S(1)}, u32[]{:S(2)}, u32[]{:S(2)}) %collective-permute-start.10) | collective-permute-done | bytes 288 | tf_op jit(solution)/shard_map/ppermute | solution.py:225
  49.9 0.5 %add_log_fusion = f32[64]{0:T(128)} fusion(f32[64]{0:T(128)S(1)} %fusion.16, f32[64]{0:T(128)S(1)} %collective-permute-done.10), kind=kLoop, calls=%fused_computation.63 | loop fusion | flops 192 | bytes 768 | tf_op jit(solution)/shard_map/log | solution.py:228
  (26 shorter events, 0.4 us)
Async XLA Ops:
  0.7 0.7 %copy-start.9 = (f32[512]{0:T(512)S(1)}, f32[512]{0:T(512)}, u32[]{:S(2)}) copy-start(f32[512]{0:T(512)} %param.7) | copy-start | bytes 6148
  0.7 0.7 %copy-start.8 = (s32[512,1]{0,1:T(1,128)S(1)}, s32[512,1]{0,1:T(1,128)}, u32[]{:S(2)}) copy-start(s32[512,1]{0,1:T(1,128)} %param.8) | copy-start | bytes 6148
  0.7 0.7 %copy-start.7 = (s32[512]{0:T(512)S(1)}, s32[512]{0:T(512)}, u32[]{:S(2)}) copy-start(s32[512]{0:T(512)} %param.9) | copy-start | bytes 6148
  2.8 0.7 %copy-start.4 = (f32[3,512]{1,0:T(4,128)S(1)}, f32[3,512]{1,0:T(4,128)}, u32[]{:S(2)}) copy-start(f32[3,512]{1,0:T(4,128)} %param.10) | copy-start | bytes 18436
  2.8 2.8 %collective-permute-start = (f32[8,32,256]{2,1,0:T(8,128)S(1)}, f32[8,32,256]{2,1,0:T(8,128)S(1)}, u32[]{:S(2)}, u32[]{:S(2)}) collective-permute-start(f32[8,32,256]{2,1,0:T(8,128)S(1)} %dynamic-slice_bitcast_fusion), channel_id=1, source_target_pairs={{0,2},{2,0},{4,6},{6,4},{8,10},{10,8},{12,14},{14,12},{16,18},{18,... | collective-permute-start | bytes 786440 | tf_op jit(solution)/shard_map/ppermute | solution.py:148
  3.5 1.6 %copy-start.5 = (f32[32]{0:T(128)}, f32[32]{0:T(128)S(1)}, u32[]{:S(2)}) copy-start(f32[32]{0:T(128)S(1)} %add_multiply_fusion.wave_ref) | copy-start | bytes 388
  3.7 0.7 %copy-start.6 = (f32[3,64]{1,0:T(4,128)S(1)}, f32[3,64]{1,0:T(4,128)}, u32[]{:S(2)}) copy-start(f32[3,64]{1,0:T(4,128)} %param.11) | copy-start | bytes 2308
  5.7 6.6 %collective-permute-start.1 = (f32[4,32,256]{2,1,0:T(8,128)S(1)}, f32[4,32,256]{2,1,0:T(8,128)S(1)}, u32[]{:S(2)}, u32[]{:S(2)}) collective-permute-start(f32[4,32,256]{2,1,0:T(8,128)S(1)} %dynamic-slice_bitcast_fusion.1), channel_id=1, source_target_pairs={{0,4},{2,6},{4,0},{6,2},{8,12},{10,14},{12,8},{14,10},{16,20},{18,... | collective-permute-start | bytes 393224 | tf_op jit(solution)/shard_map/ppermute | solution.py:148
  12.3 5.5 %collective-permute-start.4 = (f32[32,256]{1,0:T(8,128)S(1)}, f32[32,256]{1,0:T(8,128)S(1)}, u32[]{:S(2)}, u32[]{:S(2)}) collective-permute-start(f32[32,256]{1,0:T(8,128)S(1)} %get-tuple-element.11), channel_id=1, source_target_pairs={{0,24},{2,26},{4,28},{6,30},{8,0},{10,2},{12,4},{14,6},{16,8},{18,... | collective-permute-start | bytes 98312 | tf_op jit(solution)/shard_map/ppermute | solution.py:153
  16.2 4.8 %collective-permute-start.3 = (f32[32,256]{1,0:T(8,128)S(1)}, f32[32,256]{1,0:T(8,128)S(1)}, u32[]{:S(2)}, u32[]{:S(2)}) collective-permute-start(f32[32,256]{1,0:T(8,128)S(1)} %get-tuple-element.12), channel_id=1, source_target_pairs={{0,16},{2,18},{4,20},{6,22},{8,24},{10,26},{12,28},{14,30},{16,0},... | collective-permute-start | bytes 98312 | tf_op jit(solution)/shard_map/ppermute | solution.py:153
  16.2 5.7 %collective-permute-start.2 = (f32[32,256]{1,0:T(8,128)S(1)}, f32[32,256]{1,0:T(8,128)S(1)}, u32[]{:S(2)}, u32[]{:S(2)}) collective-permute-start(f32[32,256]{1,0:T(8,128)S(1)} %get-tuple-element.10), channel_id=1, source_target_pairs={{0,8},{2,10},{4,12},{6,14},{8,16},{10,18},{12,20},{14,22},{16,24},... | collective-permute-start | bytes 98312 | tf_op jit(solution)/shard_map/ppermute | solution.py:153
  22.0 4.3 %collective-permute-start.7 = (f32[32,256]{1,0:T(8,128)S(1)}, f32[32,256]{1,0:T(8,128)S(1)}, u32[]{:S(2)}, u32[]{:S(2)}) collective-permute-start(f32[32,256]{1,0:T(8,128)S(1)} %fusion.13), channel_id=1, source_target_pairs={{0,24},{2,26},{4,28},{6,30},{8,0},{10,2},{12,4},{14,6},{16,8},{18,... | collective-permute-start | bytes 98312 | tf_op jit(solution)/shard_map/ppermute | solution.py:161
  22.7 4.8 %collective-permute-start.6 = (f32[32,256]{1,0:T(8,128)S(1)}, f32[32,256]{1,0:T(8,128)S(1)}, u32[]{:S(2)}, u32[]{:S(2)}) collective-permute-start(f32[32,256]{1,0:T(8,128)S(1)} %fusion.13), channel_id=1, source_target_pairs={{0,16},{2,18},{4,20},{6,22},{8,24},{10,26},{12,28},{14,30},{16,0},... | collective-permute-start | bytes 98312 | tf_op jit(solution)/shard_map/ppermute | solution.py:161
  23.2 5.7 %collective-permute-start.5 = (f32[32,256]{1,0:T(8,128)S(1)}, f32[32,256]{1,0:T(8,128)S(1)}, u32[]{:S(2)}, u32[]{:S(2)}) collective-permute-start(f32[32,256]{1,0:T(8,128)S(1)} %fusion.13), channel_id=1, source_target_pairs={{0,8},{2,10},{4,12},{6,14},{8,16},{10,18},{12,20},{14,22},{16,24},... | collective-permute-start | bytes 98312 | tf_op jit(solution)/shard_map/ppermute | solution.py:161
  29.0 5.0 %collective-permute-start.8 = (f32[4,32,256]{2,1,0:T(8,128)S(1)}, f32[4,32,256]{2,1,0:T(8,128)S(1)}, u32[]{:S(2)}, u32[]{:S(2)}) collective-permute-start(f32[4,32,256]{2,1,0:T(8,128)S(1)} %pad_maximum_fusion.2), channel_id=1, source_target_pairs={{0,4},{2,6},{4,0},{6,2},{8,12},{10,14},{12,8},{14,10},{16,20},{18,... | collective-permute-start | bytes 393224 | tf_op jit(solution)/shard_map/ppermute | solution.py:168
  34.1 0.7 %copy-start.1 = (f32[4,2,32,256]{3,2,1,0:T(8,128)}, f32[4,2,32,256]{3,2,1,0:T(8,128)S(1)}, u32[]{:S(2)}) copy-start(f32[4,2,32,256]{3,2,1,0:T(8,128)S(1)} %pad_maximum_fusion) | copy-start | bytes 786436
  34.1 1.6 %collective-permute-start.9 = (f32[8,32,256]{2,1,0:T(8,128)S(1)}, f32[8,32,256]{2,1,0:T(8,128)S(1)}, u32[]{:S(2)}, u32[]{:S(2)}) collective-permute-start(f32[8,32,256]{2,1,0:T(8,128)S(1)} %bitcast.40), channel_id=1, source_target_pairs={{0,2},{2,0},{4,6},{6,4},{8,10},{10,8},{12,14},{14,12},{16,18},{18,... | collective-permute-start | bytes 786440 | tf_op jit(solution)/shard_map/ppermute | solution.py:168
  34.8 1.0 %copy-start = (f32[8,64,512]{2,1,0:T(8,128)}, f32[8,64,512]{2,1,0:T(8,128)S(1)}, u32[]{:S(2)}) copy-start(f32[8,64,512]{2,1,0:T(8,128)S(1)} %sqrt_dynamic-update-slice_fusion.geo_ref) | copy-start | bytes 3145732
  35.7 0.7 %copy-start.2 = (f32[8,32,256]{2,1,0:T(8,128)}, f32[8,32,256]{2,1,0:T(8,128)S(1)}, u32[]{:S(2)}) copy-start(f32[8,32,256]{2,1,0:T(8,128)S(1)} %collective-permute-done.9) | copy-start | bytes 786436
  46.3 4.2 %copy-start.3 = (f32[32,2,64]{2,1,0:T(2,128)}, f32[32,2,64]{2,1,0:T(2,128)S(1)}, u32[]{:S(2)}) copy-start(f32[32,2,64]{2,1,0:T(2,128)S(1)} %mul.137) | copy-start | bytes 49156
  46.3 3.6 %collective-permute-start.10 = (f32[64]{0:T(128)S(1)}, f32[64]{0:T(128)S(1)}, u32[]{:S(2)}, u32[]{:S(2)}) collective-permute-start(f32[64]{0:T(128)S(1)} %fusion.16), channel_id=1, source_target_pairs={{0,1},{1,0},{2,3},{3,2},{4,5},{5,4},{6,7},{7,6},{8,9},{9,8},{10,11... | collective-permute-start | bytes 776 | tf_op jit(solution)/shard_map/ppermute | solution.py:225

commit v19 on v16

--- a/solution.py
+++ b/solution.py
@@ -69,7 +69,7 @@
             jnp.ones((8, lanes), jnp.float32),
             flat,
             (((1,), (1,)), ((), ())),
-            precision=lax.Precision.HIGHEST,
+            precision=lax.Precision.HIGH,
             preferred_element_type=jnp.float32,
         )
 

time: 50.7 us -> 49.9 us (0.984)
  Pallas kernels: 8.7 us -> 7.9 us
    pallas_call x1, Pallas kernels: 8.7 us -> 7.9 us  [far_field(): pl.pallas_call(functools.partial(field_kernel, math.gcd(observers // 8, 4...]
where the time goes in v19:
time: 49.9 us; the launch traced here: 49.6 us
  waiting for transfers between devices  18.4 us (37%)
  starting transfers between devices  14.4 us (29%)
  Pallas kernels  7.9 us (16%)
  other arithmetic  4.74 us (9%)
  local copies, waits for them, and re-layouts  1.59 us (3%)
  matrix products  1.42 us (3%)
  between operations  1.11 us (2%)
    pallas_call x1, Pallas kernels, far_field(): pl.pallas_call(functools.partial(field_kernel, math.gcd(observers // 8, 4...  7.9 us
    ppermute x3, starting transfers between devices, halving_sum(): total = total + lax.ppermute(piece, 'obs', quad_pairs(groups, shift))  4.91 us
    ppermute x2, waiting for transfers between devices, doubling_gather(): other = lax.ppermute(gathered, 'obs', partner_pairs(groups, bit))  4.87 us
    ppermute x3, waiting for transfers between devices, halving_sum(): total = total + lax.ppermute(piece, 'obs', quad_pairs(groups, shift))  4.22 us
    ppermute x2, waiting for transfers between devices, halving_sum(): current = keep + lax.ppermute(send, 'obs', partner_pairs(groups, bit))  3.69 us
    ppermute x3, waiting for transfers between devices, doubling_gather(): lax.ppermute(own, 'obs', quad_pairs(groups, shift))  3.65 us
    ppermute x3, starting transfers between devices, doubling_gather(): lax.ppermute(own, 'obs', quad_pairs(groups, shift))  3.2 us
    ppermute x2, starting transfers between devices, halving_sum(): current = keep + lax.ppermute(send, 'obs', partner_pairs(groups, bit))  3.09 us
  transfers between devices with their start and end apart: 11, of which 10 were waited for; matrix products, arithmetic and copies ran while one was open for 4% of the time, Pallas kernels for 0%

profile of v19, /device:TPU:0, one launch (start us, length us, event | category | flops | bytes accessed | tf_op | source)
XLA Modules:
  0.0 49.6 jit_solution(13947214056364082129)
XLA Ops:
  0.7 0.0 copy-start.7
  0.7 0.0 copy-start.6
  0.7 0.0 copy-start.5
  0.7 0.6 %copy-done.7 = f32[512]{0:T(512)S(1)} copy-done((f32[512]{0:T(512)S(1)}, f32[512]{0:T(512)}, u32[]{:S(2)}) %copy-start.7) | copy-done | bytes 2072
  1.3 0.0 copy-done.6
  1.4 0.0 copy-done.5
  1.4 1.4 %fusion = f32[512,256]{1,0:T(8,128)S(1)} fusion(s32[512]{0:T(512)S(1)} %copy-done.5, s32[512]{0:T(512)S(1)} %bitcast.57, s32[512]{0:T(512)S(1)} %get-tuple-element.15, s32[512]{0:T(512)S(1)} %get-tuple-element.16, bf16[512,256]{1,0:T(8,128)(2,1)} %param.6, f32[512]{0:T(512)S(1)} %copy-done.7), kind=kOutput, calls=%fused_computation | convolution fusion | flops 135397376 | bytes 796672 | tf_op jit(solution)/shard_map/dot_general | solution.py:174
  2.8 0.0 copy-start.2
  2.8 0.5 %collective-permute-start = (f32[8,32,256]{2,1,0:T(8,128)S(1)}, f32[8,32,256]{2,1,0:T(8,128)S(1)}, u32[]{:S(2)}, u32[]{:S(2)}) collective-permute-start(f32[8,32,256]{2,1,0:T(8,128)S(1)} %dynamic-slice_bitcast_fusion), channel_id=1, source_target_pairs={{0,2},{2,0},{4,6},{6,4},{8,10},{10,8},{12,14},{14,12},{16,18},{18,... | collective-permute-start | bytes 786440 | tf_op jit(solution)/shard_map/ppermute | solution.py:135
  3.4 0.1 copy-done.2
  3.5 0.5 %copy-done.4 = f32[3,64]{1,0:T(4,128)S(1)} copy-done((f32[3,64]{1,0:T(4,128)S(1)}, f32[3,64]{1,0:T(4,128)}, u32[]{:S(2)}) %copy-start.4) | copy-done | bytes 792
  4.1 0.1 broadcast_subtract_fusion
  4.1 0.5 %multiply_dynamic-update-slice_fusion.1 = (f32[8,64,512]{2,1,0:T(8,128)S(1)}, f32[1,64,512]{2,1,0:T(8,128)S(1)}) fusion(f32[]{:T(128)S(1)} %bitcast.55, f32[3,64,512]{2,1,0:T(8,128)S(1)} %broadcast_subtract_fusion), kind=kLoop, calls=%fused_computation.32 | loop fusion | flops 262143 | bytes 655364
  4.8 0.0 copy-done.3
  4.8 0.5 %multiply_dynamic-update-slice_fusion = f32[8,64,512]{2,1,0:T(8,128)S(1)} fusion(f32[8,64,512]{2,1,0:T(8,128)S(1)} %get-tuple-element.2, f32[1,64,512]{2,1,0:T(8,128)S(1)} %get-tuple-element.3, f32[]{:T(128)S(1)} %bitcast.56), kind=kLoop, calls=%fused_computation.31 | loop fusion | flops 98304 | bytes 262656
  5.3 0.0 collective-permute-done
  5.4 2.6 %collective-permute-start.1 = (f32[4,32,256]{2,1,0:T(8,128)S(1)}, f32[4,32,256]{2,1,0:T(8,128)S(1)}, u32[]{:S(2)}, u32[]{:S(2)}) collective-permute-start(f32[4,32,256]{2,1,0:T(8,128)S(1)} %dynamic-slice_bitcast_fusion.1), channel_id=1, source_target_pairs={{0,4},{2,6},{4,0},{6,2},{8,12},{10,14},{12,8},{14,10},{16,20},{18,... | collective-permute-start | bytes 393224 | tf_op jit(solution)/shard_map/ppermute | solution.py:135
  8.0 0.5 cosine_dynamic-update-slice_fusion
  8.5 3.7 %collective-permute-done.1 = f32[4,32,256]{2,1,0:T(8,128)S(1)} collective-permute-done((f32[4,32,256]{2,1,0:T(8,128)S(1)}, f32[4,32,256]{2,1,0:T(8,128)S(1)}, u32[]{:S(2)}, u32[]{:S(2)}) %collective-permute-start.1) | collective-permute-done | bytes 131104 | tf_op jit(solution)/shard_map/ppermute | solution.py:135
  12.2 3.9 %collective-permute-start.4 = (f32[32,256]{1,0:T(8,128)S(1)}, f32[32,256]{1,0:T(8,128)S(1)}, u32[]{:S(2)}, u32[]{:S(2)}) collective-permute-start(f32[32,256]{1,0:T(8,128)S(1)} %get-tuple-element.13), channel_id=1, source_target_pairs={{0,24},{2,26},{4,28},{6,30},{8,0},{10,2},{12,4},{14,6},{16,8},{18,... | collective-permute-start | bytes 98312 | tf_op jit(solution)/shard_map/ppermute | solution.py:140
  16.1 0.0 collective-permute-start.3
  16.1 1.0 %collective-permute-start.2 = (f32[32,256]{1,0:T(8,128)S(1)}, f32[32,256]{1,0:T(8,128)S(1)}, u32[]{:S(2)}, u32[]{:S(2)}) collective-permute-start(f32[32,256]{1,0:T(8,128)S(1)} %get-tuple-element.12), channel_id=1, source_target_pairs={{0,8},{2,10},{4,12},{6,14},{8,16},{10,18},{12,20},{14,22},{16,24},... | collective-permute-start | bytes 98312 | tf_op jit(solution)/shard_map/ppermute | solution.py:140
  17.1 0.5 sine_dynamic-update-slice_fusion
  17.6 0.1 collective-permute-done.4
  17.7 3.2 %collective-permute-done.3 = f32[32,256]{1,0:T(8,128)S(1)} collective-permute-done((f32[32,256]{1,0:T(8,128)S(1)}, f32[32,256]{1,0:T(8,128)S(1)}, u32[]{:S(2)}, u32[]{:S(2)}) %collective-permute-start.3) | collective-permute-done | bytes 32800 | tf_op jit(solution)/shard_map/ppermute | solution.py:140
  20.9 0.9 %collective-permute-done.2 = f32[32,256]{1,0:T(8,128)S(1)} collective-permute-done((f32[32,256]{1,0:T(8,128)S(1)}, f32[32,256]{1,0:T(8,128)S(1)}, u32[]{:S(2)}, u32[]{:S(2)}) %collective-permute-start.2) | collective-permute-done | bytes 32800 | tf_op jit(solution)/shard_map/ppermute | solution.py:140
  21.8 0.6 %collective-permute-start.7 = (f32[32,256]{1,0:T(8,128)S(1)}, f32[32,256]{1,0:T(8,128)S(1)}, u32[]{:S(2)}, u32[]{:S(2)}) collective-permute-start(f32[32,256]{1,0:T(8,128)S(1)} %fusion.13), channel_id=1, source_target_pairs={{0,24},{2,26},{4,28},{6,30},{8,0},{10,2},{12,4},{14,6},{16,8},{18,... | collective-permute-start | bytes 98312 | tf_op jit(solution)/shard_map/ppermute | solution.py:148
  22.4 0.6 %collective-permute-start.6 = (f32[32,256]{1,0:T(8,128)S(1)}, f32[32,256]{1,0:T(8,128)S(1)}, u32[]{:S(2)}, u32[]{:S(2)}) collective-permute-start(f32[32,256]{1,0:T(8,128)S(1)} %fusion.13), channel_id=1, source_target_pairs={{0,16},{2,18},{4,20},{6,22},{8,24},{10,26},{12,28},{14,30},{16,0},... | collective-permute-start | bytes 98312 | tf_op jit(solution)/shard_map/ppermute | solution.py:148
  23.1 1.9 %collective-permute-start.5 = (f32[32,256]{1,0:T(8,128)S(1)}, f32[32,256]{1,0:T(8,128)S(1)}, u32[]{:S(2)}, u32[]{:S(2)}) collective-permute-start(f32[32,256]{1,0:T(8,128)S(1)} %fusion.13), channel_id=1, source_target_pairs={{0,8},{2,10},{4,12},{6,14},{8,16},{10,18},{12,20},{14,22},{16,24},... | collective-permute-start | bytes 98312 | tf_op jit(solution)/shard_map/ppermute | solution.py:148
  25.1 0.7 %collective-permute-done.7 = f32[32,256]{1,0:T(8,128)S(1)} collective-permute-done((f32[32,256]{1,0:T(8,128)S(1)}, f32[32,256]{1,0:T(8,128)S(1)}, u32[]{:S(2)}, u32[]{:S(2)}) %collective-permute-start.7) | collective-permute-done | bytes 32800 | tf_op jit(solution)/shard_map/ppermute | solution.py:148
  25.8 1.5 %collective-permute-done.6 = f32[32,256]{1,0:T(8,128)S(1)} collective-permute-done((f32[32,256]{1,0:T(8,128)S(1)}, f32[32,256]{1,0:T(8,128)S(1)}, u32[]{:S(2)}, u32[]{:S(2)}) %collective-permute-start.6) | collective-permute-done | bytes 32800 | tf_op jit(solution)/shard_map/ppermute | solution.py:148
  27.2 1.5 %collective-permute-done.5 = f32[32,256]{1,0:T(8,128)S(1)} collective-permute-done((f32[32,256]{1,0:T(8,128)S(1)}, f32[32,256]{1,0:T(8,128)S(1)}, u32[]{:S(2)}, u32[]{:S(2)}) %collective-permute-start.5) | collective-permute-done | bytes 32800 | tf_op jit(solution)/shard_map/ppermute | solution.py:148
  28.8 1.6 %collective-permute-start.8 = (f32[4,32,256]{2,1,0:T(8,128)S(1)}, f32[4,32,256]{2,1,0:T(8,128)S(1)}, u32[]{:S(2)}, u32[]{:S(2)}) collective-permute-start(f32[4,32,256]{2,1,0:T(8,128)S(1)} %pad_maximum_fusion.3), channel_id=1, source_target_pairs={{0,4},{2,6},{4,0},{6,2},{8,12},{10,14},{12,8},{14,10},{16,20},{18,... | collective-permute-start | bytes 393224 | tf_op jit(solution)/shard_map/ppermute | solution.py:155
  30.4 3.4 %collective-permute-done.8 = f32[4,32,256]{2,1,0:T(8,128)S(1)} collective-permute-done((f32[4,32,256]{2,1,0:T(8,128)S(1)}, f32[4,32,256]{2,1,0:T(8,128)S(1)}, u32[]{:S(2)}, u32[]{:S(2)}) %collective-permute-start.8) | collective-permute-done | bytes 131104 | tf_op jit(solution)/shard_map/ppermute | solution.py:155
  33.9 0.1 collective-permute-start.9
  34.1 0.0 copy-start
  34.1 1.4 %collective-permute-done.9 = f32[8,32,256]{2,1,0:T(8,128)S(1)} collective-permute-done((f32[8,32,256]{2,1,0:T(8,128)S(1)}, f32[8,32,256]{2,1,0:T(8,128)S(1)}, u32[]{:S(2)}, u32[]{:S(2)}) %collective-permute-start.9) | collective-permute-done | bytes 262176 | tf_op jit(solution)/shard_map/ppermute | solution.py:155
  35.5 0.1 select_bitcast_fusion.1
  35.6 0.9 %pad_maximum_fusion = f32[8,2,32,256]{3,2,1,0:T(8,128)} fusion(f32[8,1,32,256]{3,2,1,0:T(8,128)S(1)} %get-tuple-element.5, f32[8,1,32,256]{3,2,1,0:T(8,128)S(1)} %get-tuple-element.4), kind=kLoop, calls=%fused_computation.4 | loop fusion | flops 131072 | bytes 1048576 | tf_op jit(solution)/shard_map/stack | solution.py:158
  36.5 0.0 copy-done
  36.5 7.9 %shard_map.77 = f32[8,4096]{1,0:T(8,128)} custom-call(f32[32]{0:T(128)} %copy-done.3, f32[8,64,512]{2,1,0:T(8,128)} %copy-done, f32[512,256]{1,0:T(8,128)} %bitcast.45), custom_call_target="tpu_custom_call" | custom-call | tf_op jit(solution)/shard_map/pallas_call | solution.py:98
  44.4 0.9 %fusion.15 = f32[4096]{0:T(1024)S(1)} fusion(f32[8,4096]{1,0:T(8,128)} %shard_map.77), kind=kLoop, calls=%fused_computation.46 | loop fusion | flops 4096 | bytes 32768 | tf_op jit(solution)/shard_map/mul | solution.py:190
  45.3 0.1 mul.137
  45.4 0.0 copy-start.1
  45.4 0.1 fusion.16
  45.5 1.6 %collective-permute-start.10 = (f32[64]{0:T(128)S(1)}, f32[64]{0:T(128)S(1)}, u32[]{:S(2)}, u32[]{:S(2)}) collective-permute-start(f32[64]{0:T(128)S(1)} %fusion.16), channel_id=1, source_target_pairs={{0,1},{1,0},{2,3},{3,2},{4,5},{5,4},{6,7},{7,6},{8,9},{9,8},{10,11... | collective-permute-start | bytes 776 | tf_op jit(solution)/shard_map/ppermute | solution.py:193
  47.1 2.0 %collective-permute-done.10 = f32[64]{0:T(128)S(1)} collective-permute-done((f32[64]{0:T(128)S(1)}, f32[64]{0:T(128)S(1)}, u32[]{:S(2)}, u32[]{:S(2)}) %collective-permute-start.10) | collective-permute-done | bytes 288 | tf_op jit(solution)/shard_map/ppermute | solution.py:193
  49.1 0.5 %add_log_fusion = f32[64]{0:T(128)} fusion(f32[64]{0:T(128)S(1)} %fusion.16, f32[64]{0:T(128)S(1)} %collective-permute-done.10), kind=kLoop, calls=%fused_computation.63 | loop fusion | flops 192 | bytes 768 | tf_op jit(solution)/shard_map/log | solution.py:196
  (20 shorter events, 0.3 us)
Async XLA Ops:
  0.7 0.7 %copy-start.7 = (f32[512]{0:T(512)S(1)}, f32[512]{0:T(512)}, u32[]{:S(2)}) copy-start(f32[512]{0:T(512)} %param.7) | copy-start | bytes 6148
  0.7 0.7 %copy-start.6 = (s32[512,1]{0,1:T(1,128)S(1)}, s32[512,1]{0,1:T(1,128)}, u32[]{:S(2)}) copy-start(s32[512,1]{0,1:T(1,128)} %param.8) | copy-start | bytes 6148
  0.7 0.7 %copy-start.5 = (s32[512]{0:T(512)S(1)}, s32[512]{0:T(512)}, u32[]{:S(2)}) copy-start(s32[512]{0:T(512)} %param.9) | copy-start | bytes 6148
  2.8 0.7 %copy-start.2 = (f32[3,512]{1,0:T(4,128)S(1)}, f32[3,512]{1,0:T(4,128)}, u32[]{:S(2)}) copy-start(f32[3,512]{1,0:T(4,128)} %param.10) | copy-start | bytes 18436
  2.8 2.5 %collective-permute-start = (f32[8,32,256]{2,1,0:T(8,128)S(1)}, f32[8,32,256]{2,1,0:T(8,128)S(1)}, u32[]{:S(2)}, u32[]{:S(2)}) collective-permute-start(f32[8,32,256]{2,1,0:T(8,128)S(1)} %dynamic-slice_bitcast_fusion), channel_id=1, source_target_pairs={{0,2},{2,0},{4,6},{6,4},{8,10},{10,8},{12,14},{14,12},{16,18},{18,... | collective-permute-start | bytes 786440 | tf_op jit(solution)/shard_map/ppermute | solution.py:135
  3.4 0.7 %copy-start.4 = (f32[3,64]{1,0:T(4,128)S(1)}, f32[3,64]{1,0:T(4,128)}, u32[]{:S(2)}) copy-start(f32[3,64]{1,0:T(4,128)} %param.11) | copy-start | bytes 2308
  4.0 0.8 %copy-start.3 = (f32[32]{0:T(128)}, f32[32]{0:T(128)S(1)}, u32[]{:S(2)}) copy-start(f32[32]{0:T(128)S(1)} %add_multiply_fusion.wave_ref) | copy-start | bytes 388
  5.4 6.7 %collective-permute-start.1 = (f32[4,32,256]{2,1,0:T(8,128)S(1)}, f32[4,32,256]{2,1,0:T(8,128)S(1)}, u32[]{:S(2)}, u32[]{:S(2)}) collective-permute-start(f32[4,32,256]{2,1,0:T(8,128)S(1)} %dynamic-slice_bitcast_fusion.1), channel_id=1, source_target_pairs={{0,4},{2,6},{4,0},{6,2},{8,12},{10,14},{12,8},{14,10},{16,20},{18,... | collective-permute-start | bytes 393224 | tf_op jit(solution)/shard_map/ppermute | solution.py:135
  12.2 5.5 %collective-permute-start.4 = (f32[32,256]{1,0:T(8,128)S(1)}, f32[32,256]{1,0:T(8,128)S(1)}, u32[]{:S(2)}, u32[]{:S(2)}) collective-permute-start(f32[32,256]{1,0:T(8,128)S(1)} %get-tuple-element.13), channel_id=1, source_target_pairs={{0,24},{2,26},{4,28},{6,30},{8,0},{10,2},{12,4},{14,6},{16,8},{18,... | collective-permute-start | bytes 98312 | tf_op jit(solution)/shard_map/ppermute | solution.py:140
  16.1 4.8 %collective-permute-start.3 = (f32[32,256]{1,0:T(8,128)S(1)}, f32[32,256]{1,0:T(8,128)S(1)}, u32[]{:S(2)}, u32[]{:S(2)}) collective-permute-start(f32[32,256]{1,0:T(8,128)S(1)} %get-tuple-element.14), channel_id=1, source_target_pairs={{0,16},{2,18},{4,20},{6,22},{8,24},{10,26},{12,28},{14,30},{16,0},... | collective-permute-start | bytes 98312 | tf_op jit(solution)/shard_map/ppermute | solution.py:140
  16.1 5.7 %collective-permute-start.2 = (f32[32,256]{1,0:T(8,128)S(1)}, f32[32,256]{1,0:T(8,128)S(1)}, u32[]{:S(2)}, u32[]{:S(2)}) collective-permute-start(f32[32,256]{1,0:T(8,128)S(1)} %get-tuple-element.12), channel_id=1, source_target_pairs={{0,8},{2,10},{4,12},{6,14},{8,16},{10,18},{12,20},{14,22},{16,24},... | collective-permute-start | bytes 98312 | tf_op jit(solution)/shard_map/ppermute | solution.py:140
  21.8 4.0 %collective-permute-start.7 = (f32[32,256]{1,0:T(8,128)S(1)}, f32[32,256]{1,0:T(8,128)S(1)}, u32[]{:S(2)}, u32[]{:S(2)}) collective-permute-start(f32[32,256]{1,0:T(8,128)S(1)} %fusion.13), channel_id=1, source_target_pairs={{0,24},{2,26},{4,28},{6,30},{8,0},{10,2},{12,4},{14,6},{16,8},{18,... | collective-permute-start | bytes 98312 | tf_op jit(solution)/shard_map/ppermute | solution.py:148
  22.4 4.8 %collective-permute-start.6 = (f32[32,256]{1,0:T(8,128)S(1)}, f32[32,256]{1,0:T(8,128)S(1)}, u32[]{:S(2)}, u32[]{:S(2)}) collective-permute-start(f32[32,256]{1,0:T(8,128)S(1)} %fusion.13), channel_id=1, source_target_pairs={{0,16},{2,18},{4,20},{6,22},{8,24},{10,26},{12,28},{14,30},{16,0},... | collective-permute-start | bytes 98312 | tf_op jit(solution)/shard_map/ppermute | solution.py:148
  23.1 5.7 %collective-permute-start.5 = (f32[32,256]{1,0:T(8,128)S(1)}, f32[32,256]{1,0:T(8,128)S(1)}, u32[]{:S(2)}, u32[]{:S(2)}) collective-permute-start(f32[32,256]{1,0:T(8,128)S(1)} %fusion.13), channel_id=1, source_target_pairs={{0,8},{2,10},{4,12},{6,14},{8,16},{10,18},{12,20},{14,22},{16,24},... | collective-permute-start | bytes 98312 | tf_op jit(solution)/shard_map/ppermute | solution.py:148
  28.8 5.0 %collective-permute-start.8 = (f32[4,32,256]{2,1,0:T(8,128)S(1)}, f32[4,32,256]{2,1,0:T(8,128)S(1)}, u32[]{:S(2)}, u32[]{:S(2)}) collective-permute-start(f32[4,32,256]{2,1,0:T(8,128)S(1)} %pad_maximum_fusion.3), channel_id=1, source_target_pairs={{0,4},{2,6},{4,0},{6,2},{8,12},{10,14},{12,8},{14,10},{16,20},{18,... | collective-permute-start | bytes 393224 | tf_op jit(solution)/shard_map/ppermute | solution.py:155
  33.9 1.6 %collective-permute-start.9 = (f32[8,32,256]{2,1,0:T(8,128)S(1)}, f32[8,32,256]{2,1,0:T(8,128)S(1)}, u32[]{:S(2)}, u32[]{:S(2)}) collective-permute-start(f32[8,32,256]{2,1,0:T(8,128)S(1)} %bitcast.46), channel_id=1, source_target_pairs={{0,2},{2,0},{4,6},{6,4},{8,10},{10,8},{12,14},{14,12},{16,18},{18,... | collective-permute-start | bytes 786440 | tf_op jit(solution)/shard_map/ppermute | solution.py:155
  34.1 2.4 %copy-start = (f32[8,64,512]{2,1,0:T(8,128)}, f32[8,64,512]{2,1,0:T(8,128)S(1)}, u32[]{:S(2)}) copy-start(f32[8,64,512]{2,1,0:T(8,128)S(1)} %sqrt_dynamic-update-slice_fusion.geo_ref) | copy-start | bytes 3145732
  45.4 4.2 %copy-start.1 = (f32[32,2,64]{2,1,0:T(2,128)}, f32[32,2,64]{2,1,0:T(2,128)S(1)}, u32[]{:S(2)}) copy-start(f32[32,2,64]{2,1,0:T(2,128)S(1)} %mul.137) | copy-start | bytes 49156
  45.5 3.6 %collective-permute-start.10 = (f32[64]{0:T(128)S(1)}, f32[64]{0:T(128)S(1)}, u32[]{:S(2)}, u32[]{:S(2)}) collective-permute-start(f32[64]{0:T(128)S(1)} %fusion.16), channel_id=1, source_target_pairs={{0,1},{1,0},{2,3},{3,2},{4,5},{5,4},{6,7},{7,6},{8,9},{9,8},{10,11... | collective-permute-start | bytes 776 | tf_op jit(solution)/shard_map/ppermute | solution.py:193

commit v20 on v19

--- a/solution.py
+++ b/solution.py
@@ -96,7 +96,7 @@
         ]
     )
     summed = pl.pallas_call(
-        functools.partial(field_kernel, math.gcd(observers // 8, 4), 4),
+        functools.partial(field_kernel, math.gcd(observers // 8, 4), 8),
         grid=(panel_total // 128,),
         in_specs=[
             pl.BlockSpec(memory_space=pltpu.SMEM),

time: 49.9 us -> 49.7 us (level)
  no operation moved by 1% of the time
where the time goes in v20:
time: 49.7 us; the launch traced here: 49.4 us
  waiting for transfers between devices  18.4 us (37%)
  starting transfers between devices  14.4 us (29%)
  Pallas kernels  7.73 us (16%)
  other arithmetic  4.74 us (10%)
  local copies, waits for them, and re-layouts  1.59 us (3%)
  matrix products  1.42 us (3%)
  between operations  1.11 us (2%)
    pallas_call x1, Pallas kernels, far_field(): pl.pallas_call(functools.partial(field_kernel, math.gcd(observers // 8, 4...  7.73 us
    ppermute x3, starting transfers between devices, halving_sum(): total = total + lax.ppermute(piece, 'obs', quad_pairs(groups, shift))  4.91 us
    ppermute x2, waiting for transfers between devices, doubling_gather(): other = lax.ppermute(gathered, 'obs', partner_pairs(groups, bit))  4.87 us
    ppermute x3, waiting for transfers between devices, halving_sum(): total = total + lax.ppermute(piece, 'obs', quad_pairs(groups, shift))  4.22 us
    ppermute x2, waiting for transfers between devices, halving_sum(): current = keep + lax.ppermute(send, 'obs', partner_pairs(groups, bit))  3.69 us
    ppermute x3, waiting for transfers between devices, doubling_gather(): lax.ppermute(own, 'obs', quad_pairs(groups, shift))  3.65 us
    ppermute x3, starting transfers between devices, doubling_gather(): lax.ppermute(own, 'obs', quad_pairs(groups, shift))  3.2 us
    ppermute x2, starting transfers between devices, halving_sum(): current = keep + lax.ppermute(send, 'obs', partner_pairs(groups, bit))  3.09 us
  transfers between devices with their start and end apart: 11, of which 10 were waited for; matrix products, arithmetic and copies ran while one was open for 4% of the time, Pallas kernels for 0%

profile of v20, /device:TPU:0, one launch (start us, length us, event | category | flops | bytes accessed | tf_op | source)
XLA Modules:
  0.0 49.4 jit_solution(13257368056528173622)
XLA Ops:
  0.7 0.0 copy-start.7
  0.7 0.0 copy-start.6
  0.7 0.0 copy-start.5
  0.7 0.6 %copy-done.7 = f32[512]{0:T(512)S(1)} copy-done((f32[512]{0:T(512)S(1)}, f32[512]{0:T(512)}, u32[]{:S(2)}) %copy-start.7) | copy-done | bytes 2072
  1.3 0.0 copy-done.6
  1.4 0.0 copy-done.5
  1.4 1.4 %fusion = f32[512,256]{1,0:T(8,128)S(1)} fusion(s32[512]{0:T(512)S(1)} %copy-done.5, s32[512]{0:T(512)S(1)} %bitcast.57, s32[512]{0:T(512)S(1)} %get-tuple-element.15, s32[512]{0:T(512)S(1)} %get-tuple-element.16, bf16[512,256]{1,0:T(8,128)(2,1)} %param.6, f32[512]{0:T(512)S(1)} %copy-done.7), kind=kOutput, calls=%fused_computation | convolution fusion | flops 135397376 | bytes 796672 | tf_op jit(solution)/shard_map/dot_general | solution.py:174
  2.8 0.0 copy-start.2
  2.8 0.5 %collective-permute-start = (f32[8,32,256]{2,1,0:T(8,128)S(1)}, f32[8,32,256]{2,1,0:T(8,128)S(1)}, u32[]{:S(2)}, u32[]{:S(2)}) collective-permute-start(f32[8,32,256]{2,1,0:T(8,128)S(1)} %dynamic-slice_bitcast_fusion), channel_id=1, source_target_pairs={{0,2},{2,0},{4,6},{6,4},{8,10},{10,8},{12,14},{14,12},{16,18},{18,... | collective-permute-start | bytes 786440 | tf_op jit(solution)/shard_map/ppermute | solution.py:135
  3.4 0.1 copy-done.2
  3.5 0.5 %copy-done.4 = f32[3,64]{1,0:T(4,128)S(1)} copy-done((f32[3,64]{1,0:T(4,128)S(1)}, f32[3,64]{1,0:T(4,128)}, u32[]{:S(2)}) %copy-start.4) | copy-done | bytes 792
  4.1 0.1 broadcast_subtract_fusion
  4.1 0.5 %multiply_dynamic-update-slice_fusion.1 = (f32[8,64,512]{2,1,0:T(8,128)S(1)}, f32[1,64,512]{2,1,0:T(8,128)S(1)}) fusion(f32[]{:T(128)S(1)} %bitcast.55, f32[3,64,512]{2,1,0:T(8,128)S(1)} %broadcast_subtract_fusion), kind=kLoop, calls=%fused_computation.32 | loop fusion | flops 262143 | bytes 655364
  4.8 0.0 copy-done.3
  4.8 0.5 %multiply_dynamic-update-slice_fusion = f32[8,64,512]{2,1,0:T(8,128)S(1)} fusion(f32[8,64,512]{2,1,0:T(8,128)S(1)} %get-tuple-element.2, f32[1,64,512]{2,1,0:T(8,128)S(1)} %get-tuple-element.3, f32[]{:T(128)S(1)} %bitcast.56), kind=kLoop, calls=%fused_computation.31 | loop fusion | flops 98304 | bytes 262656
  5.3 0.0 collective-permute-done
  5.4 2.6 %collective-permute-start.1 = (f32[4,32,256]{2,1,0:T(8,128)S(1)}, f32[4,32,256]{2,1,0:T(8,128)S(1)}, u32[]{:S(2)}, u32[]{:S(2)}) collective-permute-start(f32[4,32,256]{2,1,0:T(8,128)S(1)} %dynamic-slice_bitcast_fusion.1), channel_id=1, source_target_pairs={{0,4},{2,6},{4,0},{6,2},{8,12},{10,14},{12,8},{14,10},{16,20},{18,... | collective-permute-start | bytes 393224 | tf_op jit(solution)/shard_map/ppermute | solution.py:135
  8.0 0.5 cosine_dynamic-update-slice_fusion
  8.5 3.7 %collective-permute-done.1 = f32[4,32,256]{2,1,0:T(8,128)S(1)} collective-permute-done((f32[4,32,256]{2,1,0:T(8,128)S(1)}, f32[4,32,256]{2,1,0:T(8,128)S(1)}, u32[]{:S(2)}, u32[]{:S(2)}) %collective-permute-start.1) | collective-permute-done | bytes 131104 | tf_op jit(solution)/shard_map/ppermute | solution.py:135
  12.2 3.9 %collective-permute-start.4 = (f32[32,256]{1,0:T(8,128)S(1)}, f32[32,256]{1,0:T(8,128)S(1)}, u32[]{:S(2)}, u32[]{:S(2)}) collective-permute-start(f32[32,256]{1,0:T(8,128)S(1)} %get-tuple-element.13), channel_id=1, source_target_pairs={{0,24},{2,26},{4,28},{6,30},{8,0},{10,2},{12,4},{14,6},{16,8},{18,... | collective-permute-start | bytes 98312 | tf_op jit(solution)/shard_map/ppermute | solution.py:140
  16.1 0.0 collective-permute-start.3
  16.1 1.0 %collective-permute-start.2 = (f32[32,256]{1,0:T(8,128)S(1)}, f32[32,256]{1,0:T(8,128)S(1)}, u32[]{:S(2)}, u32[]{:S(2)}) collective-permute-start(f32[32,256]{1,0:T(8,128)S(1)} %get-tuple-element.12), channel_id=1, source_target_pairs={{0,8},{2,10},{4,12},{6,14},{8,16},{10,18},{12,20},{14,22},{16,24},... | collective-permute-start | bytes 98312 | tf_op jit(solution)/shard_map/ppermute | solution.py:140
  17.1 0.5 sine_dynamic-update-slice_fusion
  17.6 0.1 collective-permute-done.4
  17.7 3.2 %collective-permute-done.3 = f32[32,256]{1,0:T(8,128)S(1)} collective-permute-done((f32[32,256]{1,0:T(8,128)S(1)}, f32[32,256]{1,0:T(8,128)S(1)}, u32[]{:S(2)}, u32[]{:S(2)}) %collective-permute-start.3) | collective-permute-done | bytes 32800 | tf_op jit(solution)/shard_map/ppermute | solution.py:140
  20.9 0.9 %collective-permute-done.2 = f32[32,256]{1,0:T(8,128)S(1)} collective-permute-done((f32[32,256]{1,0:T(8,128)S(1)}, f32[32,256]{1,0:T(8,128)S(1)}, u32[]{:S(2)}, u32[]{:S(2)}) %collective-permute-start.2) | collective-permute-done | bytes 32800 | tf_op jit(solution)/shard_map/ppermute | solution.py:140
  21.8 0.6 %collective-permute-start.7 = (f32[32,256]{1,0:T(8,128)S(1)}, f32[32,256]{1,0:T(8,128)S(1)}, u32[]{:S(2)}, u32[]{:S(2)}) collective-permute-start(f32[32,256]{1,0:T(8,128)S(1)} %fusion.13), channel_id=1, source_target_pairs={{0,24},{2,26},{4,28},{6,30},{8,0},{10,2},{12,4},{14,6},{16,8},{18,... | collective-permute-start | bytes 98312 | tf_op jit(solution)/shard_map/ppermute | solution.py:148
  22.4 0.6 %collective-permute-start.6 = (f32[32,256]{1,0:T(8,128)S(1)}, f32[32,256]{1,0:T(8,128)S(1)}, u32[]{:S(2)}, u32[]{:S(2)}) collective-permute-start(f32[32,256]{1,0:T(8,128)S(1)} %fusion.13), channel_id=1, source_target_pairs={{0,16},{2,18},{4,20},{6,22},{8,24},{10,26},{12,28},{14,30},{16,0},... | collective-permute-start | bytes 98312 | tf_op jit(solution)/shard_map/ppermute | solution.py:148
  23.1 1.9 %collective-permute-start.5 = (f32[32,256]{1,0:T(8,128)S(1)}, f32[32,256]{1,0:T(8,128)S(1)}, u32[]{:S(2)}, u32[]{:S(2)}) collective-permute-start(f32[32,256]{1,0:T(8,128)S(1)} %fusion.13), channel_id=1, source_target_pairs={{0,8},{2,10},{4,12},{6,14},{8,16},{10,18},{12,20},{14,22},{16,24},... | collective-permute-start | bytes 98312 | tf_op jit(solution)/shard_map/ppermute | solution.py:148
  25.1 0.7 %collective-permute-done.7 = f32[32,256]{1,0:T(8,128)S(1)} collective-permute-done((f32[32,256]{1,0:T(8,128)S(1)}, f32[32,256]{1,0:T(8,128)S(1)}, u32[]{:S(2)}, u32[]{:S(2)}) %collective-permute-start.7) | collective-permute-done | bytes 32800 | tf_op jit(solution)/shard_map/ppermute | solution.py:148
  25.8 1.5 %collective-permute-done.6 = f32[32,256]{1,0:T(8,128)S(1)} collective-permute-done((f32[32,256]{1,0:T(8,128)S(1)}, f32[32,256]{1,0:T(8,128)S(1)}, u32[]{:S(2)}, u32[]{:S(2)}) %collective-permute-start.6) | collective-permute-done | bytes 32800 | tf_op jit(solution)/shard_map/ppermute | solution.py:148
  27.2 1.5 %collective-permute-done.5 = f32[32,256]{1,0:T(8,128)S(1)} collective-permute-done((f32[32,256]{1,0:T(8,128)S(1)}, f32[32,256]{1,0:T(8,128)S(1)}, u32[]{:S(2)}, u32[]{:S(2)}) %collective-permute-start.5) | collective-permute-done | bytes 32800 | tf_op jit(solution)/shard_map/ppermute | solution.py:148
  28.8 1.6 %collective-permute-start.8 = (f32[4,32,256]{2,1,0:T(8,128)S(1)}, f32[4,32,256]{2,1,0:T(8,128)S(1)}, u32[]{:S(2)}, u32[]{:S(2)}) collective-permute-start(f32[4,32,256]{2,1,0:T(8,128)S(1)} %pad_maximum_fusion.3), channel_id=1, source_target_pairs={{0,4},{2,6},{4,0},{6,2},{8,12},{10,14},{12,8},{14,10},{16,20},{18,... | collective-permute-start | bytes 393224 | tf_op jit(solution)/shard_map/ppermute | solution.py:155
  30.4 3.4 %collective-permute-done.8 = f32[4,32,256]{2,1,0:T(8,128)S(1)} collective-permute-done((f32[4,32,256]{2,1,0:T(8,128)S(1)}, f32[4,32,256]{2,1,0:T(8,128)S(1)}, u32[]{:S(2)}, u32[]{:S(2)}) %collective-permute-start.8) | collective-permute-done | bytes 131104 | tf_op jit(solution)/shard_map/ppermute | solution.py:155
  33.9 0.1 collective-permute-start.9
  34.1 0.0 copy-start
  34.1 1.4 %collective-permute-done.9 = f32[8,32,256]{2,1,0:T(8,128)S(1)} collective-permute-done((f32[8,32,256]{2,1,0:T(8,128)S(1)}, f32[8,32,256]{2,1,0:T(8,128)S(1)}, u32[]{:S(2)}, u32[]{:S(2)}) %collective-permute-start.9) | collective-permute-done | bytes 262176 | tf_op jit(solution)/shard_map/ppermute | solution.py:155
  35.5 0.1 select_bitcast_fusion.1
  35.6 0.9 %pad_maximum_fusion = f32[8,2,32,256]{3,2,1,0:T(8,128)} fusion(f32[8,1,32,256]{3,2,1,0:T(8,128)S(1)} %get-tuple-element.5, f32[8,1,32,256]{3,2,1,0:T(8,128)S(1)} %get-tuple-element.4), kind=kLoop, calls=%fused_computation.4 | loop fusion | flops 131072 | bytes 1048576 | tf_op jit(solution)/shard_map/stack | solution.py:158
  36.5 7.7 %shard_map.77 = f32[8,4096]{1,0:T(8,128)} custom-call(f32[32]{0:T(128)} %copy-done.3, f32[8,64,512]{2,1,0:T(8,128)} %copy-done, f32[512,256]{1,0:T(8,128)} %bitcast.45), custom_call_target="tpu_custom_call" | custom-call | tf_op jit(solution)/shard_map/pallas_call | solution.py:98
  44.2 0.9 %fusion.15 = f32[4096]{0:T(1024)S(1)} fusion(f32[8,4096]{1,0:T(8,128)} %shard_map.77), kind=kLoop, calls=%fused_computation.46 | loop fusion | flops 4096 | bytes 32768 | tf_op jit(solution)/shard_map/mul | solution.py:190
  45.2 0.1 mul.137
  45.2 0.0 copy-start.1
  45.3 0.1 fusion.16
  45.3 1.6 %collective-permute-start.10 = (f32[64]{0:T(128)S(1)}, f32[64]{0:T(128)S(1)}, u32[]{:S(2)}, u32[]{:S(2)}) collective-permute-start(f32[64]{0:T(128)S(1)} %fusion.16), channel_id=1, source_target_pairs={{0,1},{1,0},{2,3},{3,2},{4,5},{5,4},{6,7},{7,6},{8,9},{9,8},{10,11... | collective-permute-start | bytes 776 | tf_op jit(solution)/shard_map/ppermute | solution.py:193
  46.9 2.0 %collective-permute-done.10 = f32[64]{0:T(128)S(1)} collective-permute-done((f32[64]{0:T(128)S(1)}, f32[64]{0:T(128)S(1)}, u32[]{:S(2)}, u32[]{:S(2)}) %collective-permute-start.10) | collective-permute-done | bytes 288 | tf_op jit(solution)/shard_map/ppermute | solution.py:193
  48.9 0.5 %add_log_fusion = f32[64]{0:T(128)} fusion(f32[64]{0:T(128)S(1)} %fusion.16, f32[64]{0:T(128)S(1)} %collective-permute-done.10), kind=kLoop, calls=%fused_computation.63 | loop fusion | flops 192 | bytes 768 | tf_op jit(solution)/shard_map/log | solution.py:196
  49.4 0.0 copy-done.1
  (20 shorter events, 0.3 us)
Async XLA Ops:
  0.7 0.7 %copy-start.7 = (f32[512]{0:T(512)S(1)}, f32[512]{0:T(512)}, u32[]{:S(2)}) copy-start(f32[512]{0:T(512)} %param.7) | copy-start | bytes 6148
  0.7 0.7 %copy-start.6 = (s32[512,1]{0,1:T(1,128)S(1)}, s32[512,1]{0,1:T(1,128)}, u32[]{:S(2)}) copy-start(s32[512,1]{0,1:T(1,128)} %param.8) | copy-start | bytes 6148
  0.7 0.7 %copy-start.5 = (s32[512]{0:T(512)S(1)}, s32[512]{0:T(512)}, u32[]{:S(2)}) copy-start(s32[512]{0:T(512)} %param.9) | copy-start | bytes 6148
  2.8 0.7 %copy-start.2 = (f32[3,512]{1,0:T(4,128)S(1)}, f32[3,512]{1,0:T(4,128)}, u32[]{:S(2)}) copy-start(f32[3,512]{1,0:T(4,128)} %param.10) | copy-start | bytes 18436
  2.8 2.5 %collective-permute-start = (f32[8,32,256]{2,1,0:T(8,128)S(1)}, f32[8,32,256]{2,1,0:T(8,128)S(1)}, u32[]{:S(2)}, u32[]{:S(2)}) collective-permute-start(f32[8,32,256]{2,1,0:T(8,128)S(1)} %dynamic-slice_bitcast_fusion), channel_id=1, source_target_pairs={{0,2},{2,0},{4,6},{6,4},{8,10},{10,8},{12,14},{14,12},{16,18},{18,... | collective-permute-start | bytes 786440 | tf_op jit(solution)/shard_map/ppermute | solution.py:135
  3.4 0.7 %copy-start.4 = (f32[3,64]{1,0:T(4,128)S(1)}, f32[3,64]{1,0:T(4,128)}, u32[]{:S(2)}) copy-start(f32[3,64]{1,0:T(4,128)} %param.11) | copy-start | bytes 2308
  4.0 0.8 %copy-start.3 = (f32[32]{0:T(128)}, f32[32]{0:T(128)S(1)}, u32[]{:S(2)}) copy-start(f32[32]{0:T(128)S(1)} %add_multiply_fusion.wave_ref) | copy-start | bytes 388
  5.4 6.7 %collective-permute-start.1 = (f32[4,32,256]{2,1,0:T(8,128)S(1)}, f32[4,32,256]{2,1,0:T(8,128)S(1)}, u32[]{:S(2)}, u32[]{:S(2)}) collective-permute-start(f32[4,32,256]{2,1,0:T(8,128)S(1)} %dynamic-slice_bitcast_fusion.1), channel_id=1, source_target_pairs={{0,4},{2,6},{4,0},{6,2},{8,12},{10,14},{12,8},{14,10},{16,20},{18,... | collective-permute-start | bytes 393224 | tf_op jit(solution)/shard_map/ppermute | solution.py:135
  12.2 5.5 %collective-permute-start.4 = (f32[32,256]{1,0:T(8,128)S(1)}, f32[32,256]{1,0:T(8,128)S(1)}, u32[]{:S(2)}, u32[]{:S(2)}) collective-permute-start(f32[32,256]{1,0:T(8,128)S(1)} %get-tuple-element.13), channel_id=1, source_target_pairs={{0,24},{2,26},{4,28},{6,30},{8,0},{10,2},{12,4},{14,6},{16,8},{18,... | collective-permute-start | bytes 98312 | tf_op jit(solution)/shard_map/ppermute | solution.py:140
  16.1 4.8 %collective-permute-start.3 = (f32[32,256]{1,0:T(8,128)S(1)}, f32[32,256]{1,0:T(8,128)S(1)}, u32[]{:S(2)}, u32[]{:S(2)}) collective-permute-start(f32[32,256]{1,0:T(8,128)S(1)} %get-tuple-element.14), channel_id=1, source_target_pairs={{0,16},{2,18},{4,20},{6,22},{8,24},{10,26},{12,28},{14,30},{16,0},... | collective-permute-start | bytes 98312 | tf_op jit(solution)/shard_map/ppermute | solution.py:140
  16.1 5.7 %collective-permute-start.2 = (f32[32,256]{1,0:T(8,128)S(1)}, f32[32,256]{1,0:T(8,128)S(1)}, u32[]{:S(2)}, u32[]{:S(2)}) collective-permute-start(f32[32,256]{1,0:T(8,128)S(1)} %get-tuple-element.12), channel_id=1, source_target_pairs={{0,8},{2,10},{4,12},{6,14},{8,16},{10,18},{12,20},{14,22},{16,24},... | collective-permute-start | bytes 98312 | tf_op jit(solution)/shard_map/ppermute | solution.py:140
  21.8 4.0 %collective-permute-start.7 = (f32[32,256]{1,0:T(8,128)S(1)}, f32[32,256]{1,0:T(8,128)S(1)}, u32[]{:S(2)}, u32[]{:S(2)}) collective-permute-start(f32[32,256]{1,0:T(8,128)S(1)} %fusion.13), channel_id=1, source_target_pairs={{0,24},{2,26},{4,28},{6,30},{8,0},{10,2},{12,4},{14,6},{16,8},{18,... | collective-permute-start | bytes 98312 | tf_op jit(solution)/shard_map/ppermute | solution.py:148
  22.4 4.8 %collective-permute-start.6 = (f32[32,256]{1,0:T(8,128)S(1)}, f32[32,256]{1,0:T(8,128)S(1)}, u32[]{:S(2)}, u32[]{:S(2)}) collective-permute-start(f32[32,256]{1,0:T(8,128)S(1)} %fusion.13), channel_id=1, source_target_pairs={{0,16},{2,18},{4,20},{6,22},{8,24},{10,26},{12,28},{14,30},{16,0},... | collective-permute-start | bytes 98312 | tf_op jit(solution)/shard_map/ppermute | solution.py:148
  23.1 5.7 %collective-permute-start.5 = (f32[32,256]{1,0:T(8,128)S(1)}, f32[32,256]{1,0:T(8,128)S(1)}, u32[]{:S(2)}, u32[]{:S(2)}) collective-permute-start(f32[32,256]{1,0:T(8,128)S(1)} %fusion.13), channel_id=1, source_target_pairs={{0,8},{2,10},{4,12},{6,14},{8,16},{10,18},{12,20},{14,22},{16,24},... | collective-permute-start | bytes 98312 | tf_op jit(solution)/shard_map/ppermute | solution.py:148
  28.8 5.0 %collective-permute-start.8 = (f32[4,32,256]{2,1,0:T(8,128)S(1)}, f32[4,32,256]{2,1,0:T(8,128)S(1)}, u32[]{:S(2)}, u32[]{:S(2)}) collective-permute-start(f32[4,32,256]{2,1,0:T(8,128)S(1)} %pad_maximum_fusion.3), channel_id=1, source_target_pairs={{0,4},{2,6},{4,0},{6,2},{8,12},{10,14},{12,8},{14,10},{16,20},{18,... | collective-permute-start | bytes 393224 | tf_op jit(solution)/shard_map/ppermute | solution.py:155
  33.9 1.6 %collective-permute-start.9 = (f32[8,32,256]{2,1,0:T(8,128)S(1)}, f32[8,32,256]{2,1,0:T(8,128)S(1)}, u32[]{:S(2)}, u32[]{:S(2)}) collective-permute-start(f32[8,32,256]{2,1,0:T(8,128)S(1)} %bitcast.46), channel_id=1, source_target_pairs={{0,2},{2,0},{4,6},{6,4},{8,10},{10,8},{12,14},{14,12},{16,18},{18,... | collective-permute-start | bytes 786440 | tf_op jit(solution)/shard_map/ppermute | solution.py:155
  34.1 2.4 %copy-start = (f32[8,64,512]{2,1,0:T(8,128)}, f32[8,64,512]{2,1,0:T(8,128)S(1)}, u32[]{:S(2)}) copy-start(f32[8,64,512]{2,1,0:T(8,128)S(1)} %sqrt_dynamic-update-slice_fusion.geo_ref) | copy-start | bytes 3145732
  45.2 4.2 %copy-start.1 = (f32[32,2,64]{2,1,0:T(2,128)}, f32[32,2,64]{2,1,0:T(2,128)S(1)}, u32[]{:S(2)}) copy-start(f32[32,2,64]{2,1,0:T(2,128)S(1)} %mul.137) | copy-start | bytes 49156
  45.3 3.6 %collective-permute-start.10 = (f32[64]{0:T(128)S(1)}, f32[64]{0:T(128)S(1)}, u32[]{:S(2)}, u32[]{:S(2)}) collective-permute-start(f32[64]{0:T(128)S(1)} %fusion.16), channel_id=1, source_target_pairs={{0,1},{1,0},{2,3},{3,2},{4,5},{5,4},{6,7},{7,6},{8,9},{9,8},{10,11... | collective-permute-start | bytes 776 | tf_op jit(solution)/shard_map/ppermute | solution.py:193

commit v21 on v20

--- a/solution.py
+++ b/solution.py
@@ -96,7 +96,7 @@
         ]
     )
     summed = pl.pallas_call(
-        functools.partial(field_kernel, math.gcd(observers // 8, 4), 8),
+        functools.partial(field_kernel, math.gcd(observers // 8, 4), 16),
         grid=(panel_total // 128,),
         in_specs=[
             pl.BlockSpec(memory_space=pltpu.SMEM),

time: 49.7 us -> 49.6 us (level)
  no operation moved by 1% of the time
where the time goes in v21:
time: 49.6 us; the launch traced here: 49.4 us
  waiting for transfers between devices  18.4 us (37%)
  starting transfers between devices  14.4 us (29%)
  Pallas kernels  7.64 us (15%)
  other arithmetic  4.74 us (10%)
  local copies, waits for them, and re-layouts  1.59 us (3%)
  matrix products  1.42 us (3%)
  between operations  1.11 us (2%)
    pallas_call x1, Pallas kernels, far_field(): pl.pallas_call(functools.partial(field_kernel, math.gcd(observers // 8, 4...  7.64 us
    ppermute x3, starting transfers between devices, halving_sum(): total = total + lax.ppermute(piece, 'obs', quad_pairs(groups, shift))  4.91 us
    ppermute x2, waiting for transfers between devices, doubling_gather(): other = lax.ppermute(gathered, 'obs', partner_pairs(groups, bit))  4.87 us
    ppermute x3, waiting for transfers between devices, halving_sum(): total = total + lax.ppermute(piece, 'obs', quad_pairs(groups, shift))  4.22 us
    ppermute x2, waiting for transfers between devices, halving_sum(): current = keep + lax.ppermute(send, 'obs', partner_pairs(groups, bit))  3.69 us
    ppermute x3, waiting for transfers between devices, doubling_gather(): lax.ppermute(own, 'obs', quad_pairs(groups, shift))  3.65 us
    ppermute x3, starting transfers between devices, doubling_gather(): lax.ppermute(own, 'obs', quad_pairs(groups, shift))  3.2 us
    ppermute x2, starting transfers between devices, halving_sum(): current = keep + lax.ppermute(send, 'obs', partner_pairs(groups, bit))  3.09 us
  transfers between devices with their start and end apart: 11, of which 10 were waited for; matrix products, arithmetic and copies ran while one was open for 4% of the time, Pallas kernels for 0%

profile of v21, /device:TPU:0, one launch (start us, length us, event | category | flops | bytes accessed | tf_op | source)
XLA Modules:
  0.0 49.4 jit_solution(8200450738695192473)
XLA Ops:
  0.7 0.0 copy-start.7
  0.7 0.0 copy-start.6
  0.7 0.0 copy-start.5
  0.7 0.6 %copy-done.7 = f32[512]{0:T(512)S(1)} copy-done((f32[512]{0:T(512)S(1)}, f32[512]{0:T(512)}, u32[]{:S(2)}) %copy-start.7) | copy-done | bytes 2072
  1.3 0.0 copy-done.6
  1.4 0.0 copy-done.5
  1.4 1.4 %fusion = f32[512,256]{1,0:T(8,128)S(1)} fusion(s32[512]{0:T(512)S(1)} %copy-done.5, s32[512]{0:T(512)S(1)} %bitcast.57, s32[512]{0:T(512)S(1)} %get-tuple-element.15, s32[512]{0:T(512)S(1)} %get-tuple-element.16, bf16[512,256]{1,0:T(8,128)(2,1)} %param.6, f32[512]{0:T(512)S(1)} %copy-done.7), kind=kOutput, calls=%fused_computation | convolution fusion | flops 135397376 | bytes 796672 | tf_op jit(solution)/shard_map/dot_general | solution.py:174
  2.8 0.0 copy-start.2
  2.8 0.5 %collective-permute-start = (f32[8,32,256]{2,1,0:T(8,128)S(1)}, f32[8,32,256]{2,1,0:T(8,128)S(1)}, u32[]{:S(2)}, u32[]{:S(2)}) collective-permute-start(f32[8,32,256]{2,1,0:T(8,128)S(1)} %dynamic-slice_bitcast_fusion), channel_id=1, source_target_pairs={{0,2},{2,0},{4,6},{6,4},{8,10},{10,8},{12,14},{14,12},{16,18},{18,... | collective-permute-start | bytes 786440 | tf_op jit(solution)/shard_map/ppermute | solution.py:135
  3.4 0.1 copy-done.2
  3.5 0.5 %copy-done.4 = f32[3,64]{1,0:T(4,128)S(1)} copy-done((f32[3,64]{1,0:T(4,128)S(1)}, f32[3,64]{1,0:T(4,128)}, u32[]{:S(2)}) %copy-start.4) | copy-done | bytes 792
  4.1 0.1 broadcast_subtract_fusion
  4.1 0.5 %multiply_dynamic-update-slice_fusion.1 = (f32[8,64,512]{2,1,0:T(8,128)S(1)}, f32[1,64,512]{2,1,0:T(8,128)S(1)}) fusion(f32[]{:T(128)S(1)} %bitcast.55, f32[3,64,512]{2,1,0:T(8,128)S(1)} %broadcast_subtract_fusion), kind=kLoop, calls=%fused_computation.32 | loop fusion | flops 262143 | bytes 655364
  4.8 0.0 copy-done.3
  4.8 0.5 %multiply_dynamic-update-slice_fusion = f32[8,64,512]{2,1,0:T(8,128)S(1)} fusion(f32[8,64,512]{2,1,0:T(8,128)S(1)} %get-tuple-element.2, f32[1,64,512]{2,1,0:T(8,128)S(1)} %get-tuple-element.3, f32[]{:T(128)S(1)} %bitcast.56), kind=kLoop, calls=%fused_computation.31 | loop fusion | flops 98304 | bytes 262656
  5.3 0.0 collective-permute-done
  5.4 2.6 %collective-permute-start.1 = (f32[4,32,256]{2,1,0:T(8,128)S(1)}, f32[4,32,256]{2,1,0:T(8,128)S(1)}, u32[]{:S(2)}, u32[]{:S(2)}) collective-permute-start(f32[4,32,256]{2,1,0:T(8,128)S(1)} %dynamic-slice_bitcast_fusion.1), channel_id=1, source_target_pairs={{0,4},{2,6},{4,0},{6,2},{8,12},{10,14},{12,8},{14,10},{16,20},{18,... | collective-permute-start | bytes 393224 | tf_op jit(solution)/shard_map/ppermute | solution.py:135
  8.0 0.5 cosine_dynamic-update-slice_fusion
  8.5 3.7 %collective-permute-done.1 = f32[4,32,256]{2,1,0:T(8,128)S(1)} collective-permute-done((f32[4,32,256]{2,1,0:T(8,128)S(1)}, f32[4,32,256]{2,1,0:T(8,128)S(1)}, u32[]{:S(2)}, u32[]{:S(2)}) %collective-permute-start.1) | collective-permute-done | bytes 131104 | tf_op jit(solution)/shard_map/ppermute | solution.py:135
  12.2 3.9 %collective-permute-start.4 = (f32[32,256]{1,0:T(8,128)S(1)}, f32[32,256]{1,0:T(8,128)S(1)}, u32[]{:S(2)}, u32[]{:S(2)}) collective-permute-start(f32[32,256]{1,0:T(8,128)S(1)} %get-tuple-element.13), channel_id=1, source_target_pairs={{0,24},{2,26},{4,28},{6,30},{8,0},{10,2},{12,4},{14,6},{16,8},{18,... | collective-permute-start | bytes 98312 | tf_op jit(solution)/shard_map/ppermute | solution.py:140
  16.1 0.0 collective-permute-start.3
  16.1 1.0 %collective-permute-start.2 = (f32[32,256]{1,0:T(8,128)S(1)}, f32[32,256]{1,0:T(8,128)S(1)}, u32[]{:S(2)}, u32[]{:S(2)}) collective-permute-start(f32[32,256]{1,0:T(8,128)S(1)} %get-tuple-element.12), channel_id=1, source_target_pairs={{0,8},{2,10},{4,12},{6,14},{8,16},{10,18},{12,20},{14,22},{16,24},... | collective-permute-start | bytes 98312 | tf_op jit(solution)/shard_map/ppermute | solution.py:140
  17.1 0.5 sine_dynamic-update-slice_fusion
  17.6 0.1 collective-permute-done.4
  17.7 3.2 %collective-permute-done.3 = f32[32,256]{1,0:T(8,128)S(1)} collective-permute-done((f32[32,256]{1,0:T(8,128)S(1)}, f32[32,256]{1,0:T(8,128)S(1)}, u32[]{:S(2)}, u32[]{:S(2)}) %collective-permute-start.3) | collective-permute-done | bytes 32800 | tf_op jit(solution)/shard_map/ppermute | solution.py:140
  20.9 0.9 %collective-permute-done.2 = f32[32,256]{1,0:T(8,128)S(1)} collective-permute-done((f32[32,256]{1,0:T(8,128)S(1)}, f32[32,256]{1,0:T(8,128)S(1)}, u32[]{:S(2)}, u32[]{:S(2)}) %collective-permute-start.2) | collective-permute-done | bytes 32800 | tf_op jit(solution)/shard_map/ppermute | solution.py:140
  21.8 0.6 %collective-permute-start.7 = (f32[32,256]{1,0:T(8,128)S(1)}, f32[32,256]{1,0:T(8,128)S(1)}, u32[]{:S(2)}, u32[]{:S(2)}) collective-permute-start(f32[32,256]{1,0:T(8,128)S(1)} %fusion.13), channel_id=1, source_target_pairs={{0,24},{2,26},{4,28},{6,30},{8,0},{10,2},{12,4},{14,6},{16,8},{18,... | collective-permute-start | bytes 98312 | tf_op jit(solution)/shard_map/ppermute | solution.py:148
  22.4 0.6 %collective-permute-start.6 = (f32[32,256]{1,0:T(8,128)S(1)}, f32[32,256]{1,0:T(8,128)S(1)}, u32[]{:S(2)}, u32[]{:S(2)}) collective-permute-start(f32[32,256]{1,0:T(8,128)S(1)} %fusion.13), channel_id=1, source_target_pairs={{0,16},{2,18},{4,20},{6,22},{8,24},{10,26},{12,28},{14,30},{16,0},... | collective-permute-start | bytes 98312 | tf_op jit(solution)/shard_map/ppermute | solution.py:148
  23.1 1.9 %collective-permute-start.5 = (f32[32,256]{1,0:T(8,128)S(1)}, f32[32,256]{1,0:T(8,128)S(1)}, u32[]{:S(2)}, u32[]{:S(2)}) collective-permute-start(f32[32,256]{1,0:T(8,128)S(1)} %fusion.13), channel_id=1, source_target_pairs={{0,8},{2,10},{4,12},{6,14},{8,16},{10,18},{12,20},{14,22},{16,24},... | collective-permute-start | bytes 98312 | tf_op jit(solution)/shard_map/ppermute | solution.py:148
  25.1 0.7 %collective-permute-done.7 = f32[32,256]{1,0:T(8,128)S(1)} collective-permute-done((f32[32,256]{1,0:T(8,128)S(1)}, f32[32,256]{1,0:T(8,128)S(1)}, u32[]{:S(2)}, u32[]{:S(2)}) %collective-permute-start.7) | collective-permute-done | bytes 32800 | tf_op jit(solution)/shard_map/ppermute | solution.py:148
  25.8 1.5 %collective-permute-done.6 = f32[32,256]{1,0:T(8,128)S(1)} collective-permute-done((f32[32,256]{1,0:T(8,128)S(1)}, f32[32,256]{1,0:T(8,128)S(1)}, u32[]{:S(2)}, u32[]{:S(2)}) %collective-permute-start.6) | collective-permute-done | bytes 32800 | tf_op jit(solution)/shard_map/ppermute | solution.py:148
  27.2 1.5 %collective-permute-done.5 = f32[32,256]{1,0:T(8,128)S(1)} collective-permute-done((f32[32,256]{1,0:T(8,128)S(1)}, f32[32,256]{1,0:T(8,128)S(1)}, u32[]{:S(2)}, u32[]{:S(2)}) %collective-permute-start.5) | collective-permute-done | bytes 32800 | tf_op jit(solution)/shard_map/ppermute | solution.py:148
  28.8 1.6 %collective-permute-start.8 = (f32[4,32,256]{2,1,0:T(8,128)S(1)}, f32[4,32,256]{2,1,0:T(8,128)S(1)}, u32[]{:S(2)}, u32[]{:S(2)}) collective-permute-start(f32[4,32,256]{2,1,0:T(8,128)S(1)} %pad_maximum_fusion.3), channel_id=1, source_target_pairs={{0,4},{2,6},{4,0},{6,2},{8,12},{10,14},{12,8},{14,10},{16,20},{18,... | collective-permute-start | bytes 393224 | tf_op jit(solution)/shard_map/ppermute | solution.py:155
  30.4 3.4 %collective-permute-done.8 = f32[4,32,256]{2,1,0:T(8,128)S(1)} collective-permute-done((f32[4,32,256]{2,1,0:T(8,128)S(1)}, f32[4,32,256]{2,1,0:T(8,128)S(1)}, u32[]{:S(2)}, u32[]{:S(2)}) %collective-permute-start.8) | collective-permute-done | bytes 131104 | tf_op jit(solution)/shard_map/ppermute | solution.py:155
  33.9 0.1 collective-permute-start.9
  34.1 0.0 copy-start
  34.1 1.4 %collective-permute-done.9 = f32[8,32,256]{2,1,0:T(8,128)S(1)} collective-permute-done((f32[8,32,256]{2,1,0:T(8,128)S(1)}, f32[8,32,256]{2,1,0:T(8,128)S(1)}, u32[]{:S(2)}, u32[]{:S(2)}) %collective-permute-start.9) | collective-permute-done | bytes 262176 | tf_op jit(solution)/shard_map/ppermute | solution.py:155
  35.5 0.1 select_bitcast_fusion.1
  35.6 0.9 %pad_maximum_fusion = f32[8,2,32,256]{3,2,1,0:T(8,128)} fusion(f32[8,1,32,256]{3,2,1,0:T(8,128)S(1)} %get-tuple-element.5, f32[8,1,32,256]{3,2,1,0:T(8,128)S(1)} %get-tuple-element.4), kind=kLoop, calls=%fused_computation.4 | loop fusion | flops 131072 | bytes 1048576 | tf_op jit(solution)/shard_map/stack | solution.py:158
  36.5 0.0 copy-done
  36.5 7.6 %shard_map.77 = f32[8,4096]{1,0:T(8,128)} custom-call(f32[32]{0:T(128)} %copy-done.3, f32[8,64,512]{2,1,0:T(8,128)} %copy-done, f32[512,256]{1,0:T(8,128)} %bitcast.45), custom_call_target="tpu_custom_call" | custom-call | tf_op jit(solution)/shard_map/pallas_call | solution.py:98
  44.1 0.9 %fusion.15 = f32[4096]{0:T(1024)S(1)} fusion(f32[8,4096]{1,0:T(8,128)} %shard_map.77), kind=kLoop, calls=%fused_computation.46 | loop fusion | flops 4096 | bytes 32768 | tf_op jit(solution)/shard_map/mul | solution.py:190
  45.1 0.1 mul.137
  45.2 0.0 copy-start.1
  45.2 0.1 fusion.16
  45.2 1.6 %collective-permute-start.10 = (f32[64]{0:T(128)S(1)}, f32[64]{0:T(128)S(1)}, u32[]{:S(2)}, u32[]{:S(2)}) collective-permute-start(f32[64]{0:T(128)S(1)} %fusion.16), channel_id=1, source_target_pairs={{0,1},{1,0},{2,3},{3,2},{4,5},{5,4},{6,7},{7,6},{8,9},{9,8},{10,11... | collective-permute-start | bytes 776 | tf_op jit(solution)/shard_map/ppermute | solution.py:193
  46.8 2.0 %collective-permute-done.10 = f32[64]{0:T(128)S(1)} collective-permute-done((f32[64]{0:T(128)S(1)}, f32[64]{0:T(128)S(1)}, u32[]{:S(2)}, u32[]{:S(2)}) %collective-permute-start.10) | collective-permute-done | bytes 288 | tf_op jit(solution)/shard_map/ppermute | solution.py:193
  48.8 0.5 %add_log_fusion = f32[64]{0:T(128)} fusion(f32[64]{0:T(128)S(1)} %fusion.16, f32[64]{0:T(128)S(1)} %collective-permute-done.10), kind=kLoop, calls=%fused_computation.63 | loop fusion | flops 192 | bytes 768 | tf_op jit(solution)/shard_map/log | solution.py:196
  (20 shorter events, 0.3 us)
Async XLA Ops:
  0.7 0.7 %copy-start.7 = (f32[512]{0:T(512)S(1)}, f32[512]{0:T(512)}, u32[]{:S(2)}) copy-start(f32[512]{0:T(512)} %param.7) | copy-start | bytes 6148
  0.7 0.7 %copy-start.6 = (s32[512,1]{0,1:T(1,128)S(1)}, s32[512,1]{0,1:T(1,128)}, u32[]{:S(2)}) copy-start(s32[512,1]{0,1:T(1,128)} %param.8) | copy-start | bytes 6148
  0.7 0.7 %copy-start.5 = (s32[512]{0:T(512)S(1)}, s32[512]{0:T(512)}, u32[]{:S(2)}) copy-start(s32[512]{0:T(512)} %param.9) | copy-start | bytes 6148
  2.8 0.7 %copy-start.2 = (f32[3,512]{1,0:T(4,128)S(1)}, f32[3,512]{1,0:T(4,128)}, u32[]{:S(2)}) copy-start(f32[3,512]{1,0:T(4,128)} %param.10) | copy-start | bytes 18436
  2.8 2.5 %collective-permute-start = (f32[8,32,256]{2,1,0:T(8,128)S(1)}, f32[8,32,256]{2,1,0:T(8,128)S(1)}, u32[]{:S(2)}, u32[]{:S(2)}) collective-permute-start(f32[8,32,256]{2,1,0:T(8,128)S(1)} %dynamic-slice_bitcast_fusion), channel_id=1, source_target_pairs={{0,2},{2,0},{4,6},{6,4},{8,10},{10,8},{12,14},{14,12},{16,18},{18,... | collective-permute-start | bytes 786440 | tf_op jit(solution)/shard_map/ppermute | solution.py:135
  3.4 0.7 %copy-start.4 = (f32[3,64]{1,0:T(4,128)S(1)}, f32[3,64]{1,0:T(4,128)}, u32[]{:S(2)}) copy-start(f32[3,64]{1,0:T(4,128)} %param.11) | copy-start | bytes 2308
  4.0 0.8 %copy-start.3 = (f32[32]{0:T(128)}, f32[32]{0:T(128)S(1)}, u32[]{:S(2)}) copy-start(f32[32]{0:T(128)S(1)} %add_multiply_fusion.wave_ref) | copy-start | bytes 388
  5.4 6.7 %collective-permute-start.1 = (f32[4,32,256]{2,1,0:T(8,128)S(1)}, f32[4,32,256]{2,1,0:T(8,128)S(1)}, u32[]{:S(2)}, u32[]{:S(2)}) collective-permute-start(f32[4,32,256]{2,1,0:T(8,128)S(1)} %dynamic-slice_bitcast_fusion.1), channel_id=1, source_target_pairs={{0,4},{2,6},{4,0},{6,2},{8,12},{10,14},{12,8},{14,10},{16,20},{18,... | collective-permute-start | bytes 393224 | tf_op jit(solution)/shard_map/ppermute | solution.py:135
  12.2 5.5 %collective-permute-start.4 = (f32[32,256]{1,0:T(8,128)S(1)}, f32[32,256]{1,0:T(8,128)S(1)}, u32[]{:S(2)}, u32[]{:S(2)}) collective-permute-start(f32[32,256]{1,0:T(8,128)S(1)} %get-tuple-element.13), channel_id=1, source_target_pairs={{0,24},{2,26},{4,28},{6,30},{8,0},{10,2},{12,4},{14,6},{16,8},{18,... | collective-permute-start | bytes 98312 | tf_op jit(solution)/shard_map/ppermute | solution.py:140
  16.1 4.8 %collective-permute-start.3 = (f32[32,256]{1,0:T(8,128)S(1)}, f32[32,256]{1,0:T(8,128)S(1)}, u32[]{:S(2)}, u32[]{:S(2)}) collective-permute-start(f32[32,256]{1,0:T(8,128)S(1)} %get-tuple-element.14), channel_id=1, source_target_pairs={{0,16},{2,18},{4,20},{6,22},{8,24},{10,26},{12,28},{14,30},{16,0},... | collective-permute-start | bytes 98312 | tf_op jit(solution)/shard_map/ppermute | solution.py:140
  16.1 5.7 %collective-permute-start.2 = (f32[32,256]{1,0:T(8,128)S(1)}, f32[32,256]{1,0:T(8,128)S(1)}, u32[]{:S(2)}, u32[]{:S(2)}) collective-permute-start(f32[32,256]{1,0:T(8,128)S(1)} %get-tuple-element.12), channel_id=1, source_target_pairs={{0,8},{2,10},{4,12},{6,14},{8,16},{10,18},{12,20},{14,22},{16,24},... | collective-permute-start | bytes 98312 | tf_op jit(solution)/shard_map/ppermute | solution.py:140
  21.8 4.0 %collective-permute-start.7 = (f32[32,256]{1,0:T(8,128)S(1)}, f32[32,256]{1,0:T(8,128)S(1)}, u32[]{:S(2)}, u32[]{:S(2)}) collective-permute-start(f32[32,256]{1,0:T(8,128)S(1)} %fusion.13), channel_id=1, source_target_pairs={{0,24},{2,26},{4,28},{6,30},{8,0},{10,2},{12,4},{14,6},{16,8},{18,... | collective-permute-start | bytes 98312 | tf_op jit(solution)/shard_map/ppermute | solution.py:148
  22.4 4.8 %collective-permute-start.6 = (f32[32,256]{1,0:T(8,128)S(1)}, f32[32,256]{1,0:T(8,128)S(1)}, u32[]{:S(2)}, u32[]{:S(2)}) collective-permute-start(f32[32,256]{1,0:T(8,128)S(1)} %fusion.13), channel_id=1, source_target_pairs={{0,16},{2,18},{4,20},{6,22},{8,24},{10,26},{12,28},{14,30},{16,0},... | collective-permute-start | bytes 98312 | tf_op jit(solution)/shard_map/ppermute | solution.py:148
  23.1 5.7 %collective-permute-start.5 = (f32[32,256]{1,0:T(8,128)S(1)}, f32[32,256]{1,0:T(8,128)S(1)}, u32[]{:S(2)}, u32[]{:S(2)}) collective-permute-start(f32[32,256]{1,0:T(8,128)S(1)} %fusion.13), channel_id=1, source_target_pairs={{0,8},{2,10},{4,12},{6,14},{8,16},{10,18},{12,20},{14,22},{16,24},... | collective-permute-start | bytes 98312 | tf_op jit(solution)/shard_map/ppermute | solution.py:148
  28.8 5.0 %collective-permute-start.8 = (f32[4,32,256]{2,1,0:T(8,128)S(1)}, f32[4,32,256]{2,1,0:T(8,128)S(1)}, u32[]{:S(2)}, u32[]{:S(2)}) collective-permute-start(f32[4,32,256]{2,1,0:T(8,128)S(1)} %pad_maximum_fusion.3), channel_id=1, source_target_pairs={{0,4},{2,6},{4,0},{6,2},{8,12},{10,14},{12,8},{14,10},{16,20},{18,... | collective-permute-start | bytes 393224 | tf_op jit(solution)/shard_map/ppermute | solution.py:155
  33.9 1.6 %collective-permute-start.9 = (f32[8,32,256]{2,1,0:T(8,128)S(1)}, f32[8,32,256]{2,1,0:T(8,128)S(1)}, u32[]{:S(2)}, u32[]{:S(2)}) collective-permute-start(f32[8,32,256]{2,1,0:T(8,128)S(1)} %bitcast.46), channel_id=1, source_target_pairs={{0,2},{2,0},{4,6},{6,4},{8,10},{10,8},{12,14},{14,12},{16,18},{18,... | collective-permute-start | bytes 786440 | tf_op jit(solution)/shard_map/ppermute | solution.py:155
  34.1 2.4 %copy-start = (f32[8,64,512]{2,1,0:T(8,128)}, f32[8,64,512]{2,1,0:T(8,128)S(1)}, u32[]{:S(2)}) copy-start(f32[8,64,512]{2,1,0:T(8,128)S(1)} %sqrt_dynamic-update-slice_fusion.geo_ref) | copy-start | bytes 3145732
  45.2 4.2 %copy-start.1 = (f32[32,2,64]{2,1,0:T(2,128)}, f32[32,2,64]{2,1,0:T(2,128)S(1)}, u32[]{:S(2)}) copy-start(f32[32,2,64]{2,1,0:T(2,128)S(1)} %mul.137) | copy-start | bytes 49156
  45.2 3.6 %collective-permute-start.10 = (f32[64]{0:T(128)S(1)}, f32[64]{0:T(128)S(1)}, u32[]{:S(2)}, u32[]{:S(2)}) collective-permute-start(f32[64]{0:T(128)S(1)} %fusion.16), channel_id=1, source_target_pairs={{0,1},{1,0},{2,3},{3,2},{4,5},{5,4},{6,7},{7,6},{8,9},{9,8},{10,11... | collective-permute-start | bytes 776 | tf_op jit(solution)/shard_map/ppermute | solution.py:193

commit v22 on v21

--- a/solution.py
+++ b/solution.py
@@ -96,7 +96,7 @@
         ]
     )
     summed = pl.pallas_call(
-        functools.partial(field_kernel, math.gcd(observers // 8, 4), 16),
+        functools.partial(field_kernel, math.gcd(observers // 8, 4), 32),
         grid=(panel_total // 128,),
         in_specs=[
             pl.BlockSpec(memory_space=pltpu.SMEM),

time: 49.6 us -> 49.5 us (level)
  no operation moved by 1% of the time
where the time goes in v22:
time: 49.5 us; the launch traced here: 49.2 us
  waiting for transfers between devices  18.4 us (37%)
  starting transfers between devices  14.4 us (29%)
  Pallas kernels  7.54 us (15%)
  other arithmetic  4.74 us (10%)
  local copies, waits for them, and re-layouts  1.59 us (3%)
  matrix products  1.42 us (3%)
  between operations  1.11 us (2%)
    pallas_call x1, Pallas kernels, far_field(): pl.pallas_call(functools.partial(field_kernel, math.gcd(observers // 8, 4...  7.54 us
    ppermute x3, starting transfers between devices, halving_sum(): total = total + lax.ppermute(piece, 'obs', quad_pairs(groups, shift))  4.91 us
    ppermute x2, waiting for transfers between devices, doubling_gather(): other = lax.ppermute(gathered, 'obs', partner_pairs(groups, bit))  4.87 us
    ppermute x3, waiting for transfers between devices, halving_sum(): total = total + lax.ppermute(piece, 'obs', quad_pairs(groups, shift))  4.22 us
    ppermute x2, waiting for transfers between devices, halving_sum(): current = keep + lax.ppermute(send, 'obs', partner_pairs(groups, bit))  3.69 us
    ppermute x3, waiting for transfers between devices, doubling_gather(): lax.ppermute(own, 'obs', quad_pairs(groups, shift))  3.65 us
    ppermute x3, starting transfers between devices, doubling_gather(): lax.ppermute(own, 'obs', quad_pairs(groups, shift))  3.2 us
    ppermute x2, starting transfers between devices, halving_sum(): current = keep + lax.ppermute(send, 'obs', partner_pairs(groups, bit))  3.09 us
  transfers between devices with their start and end apart: 11, of which 10 were waited for; matrix products, arithmetic and copies ran while one was open for 4% of the time, Pallas kernels for 0%

profile of v22, /device:TPU:0, one launch (start us, length us, event | category | flops | bytes accessed | tf_op | source)
XLA Modules:
  0.0 49.2 jit_solution(8113719367460249315)
XLA Ops:
  0.7 0.0 copy-start.7
  0.7 0.0 copy-start.6
  0.7 0.0 copy-start.5
  0.7 0.6 %copy-done.7 = f32[512]{0:T(512)S(1)} copy-done((f32[512]{0:T(512)S(1)}, f32[512]{0:T(512)}, u32[]{:S(2)}) %copy-start.7) | copy-done | bytes 2072
  1.3 0.0 copy-done.6
  1.4 0.0 copy-done.5
  1.4 1.4 %fusion = f32[512,256]{1,0:T(8,128)S(1)} fusion(s32[512]{0:T(512)S(1)} %copy-done.5, s32[512]{0:T(512)S(1)} %bitcast.57, s32[512]{0:T(512)S(1)} %get-tuple-element.15, s32[512]{0:T(512)S(1)} %get-tuple-element.16, bf16[512,256]{1,0:T(8,128)(2,1)} %param.6, f32[512]{0:T(512)S(1)} %copy-done.7), kind=kOutput, calls=%fused_computation | convolution fusion | flops 135397376 | bytes 796672 | tf_op jit(solution)/shard_map/dot_general | solution.py:174
  2.8 0.0 copy-start.2
  2.8 0.5 %collective-permute-start = (f32[8,32,256]{2,1,0:T(8,128)S(1)}, f32[8,32,256]{2,1,0:T(8,128)S(1)}, u32[]{:S(2)}, u32[]{:S(2)}) collective-permute-start(f32[8,32,256]{2,1,0:T(8,128)S(1)} %dynamic-slice_bitcast_fusion), channel_id=1, source_target_pairs={{0,2},{2,0},{4,6},{6,4},{8,10},{10,8},{12,14},{14,12},{16,18},{18,... | collective-permute-start | bytes 786440 | tf_op jit(solution)/shard_map/ppermute | solution.py:135
  3.4 0.1 copy-done.2
  3.5 0.5 %copy-done.4 = f32[3,64]{1,0:T(4,128)S(1)} copy-done((f32[3,64]{1,0:T(4,128)S(1)}, f32[3,64]{1,0:T(4,128)}, u32[]{:S(2)}) %copy-start.4) | copy-done | bytes 792
  4.1 0.1 broadcast_subtract_fusion
  4.1 0.5 %multiply_dynamic-update-slice_fusion.1 = (f32[8,64,512]{2,1,0:T(8,128)S(1)}, f32[1,64,512]{2,1,0:T(8,128)S(1)}) fusion(f32[]{:T(128)S(1)} %bitcast.55, f32[3,64,512]{2,1,0:T(8,128)S(1)} %broadcast_subtract_fusion), kind=kLoop, calls=%fused_computation.32 | loop fusion | flops 262143 | bytes 655364
  4.8 0.0 copy-done.3
  4.8 0.5 %multiply_dynamic-update-slice_fusion = f32[8,64,512]{2,1,0:T(8,128)S(1)} fusion(f32[8,64,512]{2,1,0:T(8,128)S(1)} %get-tuple-element.2, f32[1,64,512]{2,1,0:T(8,128)S(1)} %get-tuple-element.3, f32[]{:T(128)S(1)} %bitcast.56), kind=kLoop, calls=%fused_computation.31 | loop fusion | flops 98304 | bytes 262656
  5.3 0.0 collective-permute-done
  5.4 2.6 %collective-permute-start.1 = (f32[4,32,256]{2,1,0:T(8,128)S(1)}, f32[4,32,256]{2,1,0:T(8,128)S(1)}, u32[]{:S(2)}, u32[]{:S(2)}) collective-permute-start(f32[4,32,256]{2,1,0:T(8,128)S(1)} %dynamic-slice_bitcast_fusion.1), channel_id=1, source_target_pairs={{0,4},{2,6},{4,0},{6,2},{8,12},{10,14},{12,8},{14,10},{16,20},{18,... | collective-permute-start | bytes 393224 | tf_op jit(solution)/shard_map/ppermute | solution.py:135
  8.0 0.5 cosine_dynamic-update-slice_fusion
  8.5 3.7 %collective-permute-done.1 = f32[4,32,256]{2,1,0:T(8,128)S(1)} collective-permute-done((f32[4,32,256]{2,1,0:T(8,128)S(1)}, f32[4,32,256]{2,1,0:T(8,128)S(1)}, u32[]{:S(2)}, u32[]{:S(2)}) %collective-permute-start.1) | collective-permute-done | bytes 131104 | tf_op jit(solution)/shard_map/ppermute | solution.py:135
  12.2 3.9 %collective-permute-start.4 = (f32[32,256]{1,0:T(8,128)S(1)}, f32[32,256]{1,0:T(8,128)S(1)}, u32[]{:S(2)}, u32[]{:S(2)}) collective-permute-start(f32[32,256]{1,0:T(8,128)S(1)} %get-tuple-element.13), channel_id=1, source_target_pairs={{0,24},{2,26},{4,28},{6,30},{8,0},{10,2},{12,4},{14,6},{16,8},{18,... | collective-permute-start | bytes 98312 | tf_op jit(solution)/shard_map/ppermute | solution.py:140
  16.1 0.0 collective-permute-start.3
  16.1 1.0 %collective-permute-start.2 = (f32[32,256]{1,0:T(8,128)S(1)}, f32[32,256]{1,0:T(8,128)S(1)}, u32[]{:S(2)}, u32[]{:S(2)}) collective-permute-start(f32[32,256]{1,0:T(8,128)S(1)} %get-tuple-element.12), channel_id=1, source_target_pairs={{0,8},{2,10},{4,12},{6,14},{8,16},{10,18},{12,20},{14,22},{16,24},... | collective-permute-start | bytes 98312 | tf_op jit(solution)/shard_map/ppermute | solution.py:140
  17.1 0.5 sine_dynamic-update-slice_fusion
  17.6 0.1 collective-permute-done.4
  17.7 3.2 %collective-permute-done.3 = f32[32,256]{1,0:T(8,128)S(1)} collective-permute-done((f32[32,256]{1,0:T(8,128)S(1)}, f32[32,256]{1,0:T(8,128)S(1)}, u32[]{:S(2)}, u32[]{:S(2)}) %collective-permute-start.3) | collective-permute-done | bytes 32800 | tf_op jit(solution)/shard_map/ppermute | solution.py:140
  20.9 0.9 %collective-permute-done.2 = f32[32,256]{1,0:T(8,128)S(1)} collective-permute-done((f32[32,256]{1,0:T(8,128)S(1)}, f32[32,256]{1,0:T(8,128)S(1)}, u32[]{:S(2)}, u32[]{:S(2)}) %collective-permute-start.2) | collective-permute-done | bytes 32800 | tf_op jit(solution)/shard_map/ppermute | solution.py:140
  21.8 0.6 %collective-permute-start.7 = (f32[32,256]{1,0:T(8,128)S(1)}, f32[32,256]{1,0:T(8,128)S(1)}, u32[]{:S(2)}, u32[]{:S(2)}) collective-permute-start(f32[32,256]{1,0:T(8,128)S(1)} %fusion.13), channel_id=1, source_target_pairs={{0,24},{2,26},{4,28},{6,30},{8,0},{10,2},{12,4},{14,6},{16,8},{18,... | collective-permute-start | bytes 98312 | tf_op jit(solution)/shard_map/ppermute | solution.py:148
  22.4 0.6 %collective-permute-start.6 = (f32[32,256]{1,0:T(8,128)S(1)}, f32[32,256]{1,0:T(8,128)S(1)}, u32[]{:S(2)}, u32[]{:S(2)}) collective-permute-start(f32[32,256]{1,0:T(8,128)S(1)} %fusion.13), channel_id=1, source_target_pairs={{0,16},{2,18},{4,20},{6,22},{8,24},{10,26},{12,28},{14,30},{16,0},... | collective-permute-start | bytes 98312 | tf_op jit(solution)/shard_map/ppermute | solution.py:148
  23.1 1.9 %collective-permute-start.5 = (f32[32,256]{1,0:T(8,128)S(1)}, f32[32,256]{1,0:T(8,128)S(1)}, u32[]{:S(2)}, u32[]{:S(2)}) collective-permute-start(f32[32,256]{1,0:T(8,128)S(1)} %fusion.13), channel_id=1, source_target_pairs={{0,8},{2,10},{4,12},{6,14},{8,16},{10,18},{12,20},{14,22},{16,24},... | collective-permute-start | bytes 98312 | tf_op jit(solution)/shard_map/ppermute | solution.py:148
  25.1 0.7 %collective-permute-done.7 = f32[32,256]{1,0:T(8,128)S(1)} collective-permute-done((f32[32,256]{1,0:T(8,128)S(1)}, f32[32,256]{1,0:T(8,128)S(1)}, u32[]{:S(2)}, u32[]{:S(2)}) %collective-permute-start.7) | collective-permute-done | bytes 32800 | tf_op jit(solution)/shard_map/ppermute | solution.py:148
  25.8 1.5 %collective-permute-done.6 = f32[32,256]{1,0:T(8,128)S(1)} collective-permute-done((f32[32,256]{1,0:T(8,128)S(1)}, f32[32,256]{1,0:T(8,128)S(1)}, u32[]{:S(2)}, u32[]{:S(2)}) %collective-permute-start.6) | collective-permute-done | bytes 32800 | tf_op jit(solution)/shard_map/ppermute | solution.py:148
  27.2 1.5 %collective-permute-done.5 = f32[32,256]{1,0:T(8,128)S(1)} collective-permute-done((f32[32,256]{1,0:T(8,128)S(1)}, f32[32,256]{1,0:T(8,128)S(1)}, u32[]{:S(2)}, u32[]{:S(2)}) %collective-permute-start.5) | collective-permute-done | bytes 32800 | tf_op jit(solution)/shard_map/ppermute | solution.py:148
  28.8 1.6 %collective-permute-start.8 = (f32[4,32,256]{2,1,0:T(8,128)S(1)}, f32[4,32,256]{2,1,0:T(8,128)S(1)}, u32[]{:S(2)}, u32[]{:S(2)}) collective-permute-start(f32[4,32,256]{2,1,0:T(8,128)S(1)} %pad_maximum_fusion.3), channel_id=1, source_target_pairs={{0,4},{2,6},{4,0},{6,2},{8,12},{10,14},{12,8},{14,10},{16,20},{18,... | collective-permute-start | bytes 393224 | tf_op jit(solution)/shard_map/ppermute | solution.py:155
  30.4 3.4 %collective-permute-done.8 = f32[4,32,256]{2,1,0:T(8,128)S(1)} collective-permute-done((f32[4,32,256]{2,1,0:T(8,128)S(1)}, f32[4,32,256]{2,1,0:T(8,128)S(1)}, u32[]{:S(2)}, u32[]{:S(2)}) %collective-permute-start.8) | collective-permute-done | bytes 131104 | tf_op jit(solution)/shard_map/ppermute | solution.py:155
  33.9 0.1 collective-permute-start.9
  34.1 0.0 copy-start
  34.1 1.4 %collective-permute-done.9 = f32[8,32,256]{2,1,0:T(8,128)S(1)} collective-permute-done((f32[8,32,256]{2,1,0:T(8,128)S(1)}, f32[8,32,256]{2,1,0:T(8,128)S(1)}, u32[]{:S(2)}, u32[]{:S(2)}) %collective-permute-start.9) | collective-permute-done | bytes 262176 | tf_op jit(solution)/shard_map/ppermute | solution.py:155
  35.5 0.1 select_bitcast_fusion.1
  35.6 0.9 %pad_maximum_fusion = f32[8,2,32,256]{3,2,1,0:T(8,128)} fusion(f32[8,1,32,256]{3,2,1,0:T(8,128)S(1)} %get-tuple-element.5, f32[8,1,32,256]{3,2,1,0:T(8,128)S(1)} %get-tuple-element.4), kind=kLoop, calls=%fused_computation.4 | loop fusion | flops 131072 | bytes 1048576 | tf_op jit(solution)/shard_map/stack | solution.py:158
  36.5 0.0 copy-done
  36.5 7.5 %shard_map.77 = f32[8,4096]{1,0:T(8,128)} custom-call(f32[32]{0:T(128)} %copy-done.3, f32[8,64,512]{2,1,0:T(8,128)} %copy-done, f32[512,256]{1,0:T(8,128)} %bitcast.45), custom_call_target="tpu_custom_call" | custom-call | tf_op jit(solution)/shard_map/pallas_call | solution.py:98
  44.0 0.9 %fusion.15 = f32[4096]{0:T(1024)S(1)} fusion(f32[8,4096]{1,0:T(8,128)} %shard_map.77), kind=kLoop, calls=%fused_computation.46 | loop fusion | flops 4096 | bytes 32768 | tf_op jit(solution)/shard_map/mul | solution.py:190
  45.0 0.1 mul.137
  45.1 0.0 copy-start.1
  45.1 0.1 fusion.16
  45.1 1.6 %collective-permute-start.10 = (f32[64]{0:T(128)S(1)}, f32[64]{0:T(128)S(1)}, u32[]{:S(2)}, u32[]{:S(2)}) collective-permute-start(f32[64]{0:T(128)S(1)} %fusion.16), channel_id=1, source_target_pairs={{0,1},{1,0},{2,3},{3,2},{4,5},{5,4},{6,7},{7,6},{8,9},{9,8},{10,11... | collective-permute-start | bytes 776 | tf_op jit(solution)/shard_map/ppermute | solution.py:193
  46.7 2.0 %collective-permute-done.10 = f32[64]{0:T(128)S(1)} collective-permute-done((f32[64]{0:T(128)S(1)}, f32[64]{0:T(128)S(1)}, u32[]{:S(2)}, u32[]{:S(2)}) %collective-permute-start.10) | collective-permute-done | bytes 288 | tf_op jit(solution)/shard_map/ppermute | solution.py:193
  48.7 0.5 %add_log_fusion = f32[64]{0:T(128)} fusion(f32[64]{0:T(128)S(1)} %fusion.16, f32[64]{0:T(128)S(1)} %collective-permute-done.10), kind=kLoop, calls=%fused_computation.63 | loop fusion | flops 192 | bytes 768 | tf_op jit(solution)/shard_map/log | solution.py:196
  (20 shorter events, 0.3 us)
Async XLA Ops:
  0.7 0.7 %copy-start.7 = (f32[512]{0:T(512)S(1)}, f32[512]{0:T(512)}, u32[]{:S(2)}) copy-start(f32[512]{0:T(512)} %param.7) | copy-start | bytes 6148
  0.7 0.7 %copy-start.6 = (s32[512,1]{0,1:T(1,128)S(1)}, s32[512,1]{0,1:T(1,128)}, u32[]{:S(2)}) copy-start(s32[512,1]{0,1:T(1,128)} %param.8) | copy-start | bytes 6148
  0.7 0.7 %copy-start.5 = (s32[512]{0:T(512)S(1)}, s32[512]{0:T(512)}, u32[]{:S(2)}) copy-start(s32[512]{0:T(512)} %param.9) | copy-start | bytes 6148
  2.8 0.7 %copy-start.2 = (f32[3,512]{1,0:T(4,128)S(1)}, f32[3,512]{1,0:T(4,128)}, u32[]{:S(2)}) copy-start(f32[3,512]{1,0:T(4,128)} %param.10) | copy-start | bytes 18436
  2.8 2.5 %collective-permute-start = (f32[8,32,256]{2,1,0:T(8,128)S(1)}, f32[8,32,256]{2,1,0:T(8,128)S(1)}, u32[]{:S(2)}, u32[]{:S(2)}) collective-permute-start(f32[8,32,256]{2,1,0:T(8,128)S(1)} %dynamic-slice_bitcast_fusion), channel_id=1, source_target_pairs={{0,2},{2,0},{4,6},{6,4},{8,10},{10,8},{12,14},{14,12},{16,18},{18,... | collective-permute-start | bytes 786440 | tf_op jit(solution)/shard_map/ppermute | solution.py:135
  3.4 0.7 %copy-start.4 = (f32[3,64]{1,0:T(4,128)S(1)}, f32[3,64]{1,0:T(4,128)}, u32[]{:S(2)}) copy-start(f32[3,64]{1,0:T(4,128)} %param.11) | copy-start | bytes 2308
  4.0 0.8 %copy-start.3 = (f32[32]{0:T(128)}, f32[32]{0:T(128)S(1)}, u32[]{:S(2)}) copy-start(f32[32]{0:T(128)S(1)} %add_multiply_fusion.wave_ref) | copy-start | bytes 388
  5.4 6.7 %collective-permute-start.1 = (f32[4,32,256]{2,1,0:T(8,128)S(1)}, f32[4,32,256]{2,1,0:T(8,128)S(1)}, u32[]{:S(2)}, u32[]{:S(2)}) collective-permute-start(f32[4,32,256]{2,1,0:T(8,128)S(1)} %dynamic-slice_bitcast_fusion.1), channel_id=1, source_target_pairs={{0,4},{2,6},{4,0},{6,2},{8,12},{10,14},{12,8},{14,10},{16,20},{18,... | collective-permute-start | bytes 393224 | tf_op jit(solution)/shard_map/ppermute | solution.py:135
  12.2 5.5 %collective-permute-start.4 = (f32[32,256]{1,0:T(8,128)S(1)}, f32[32,256]{1,0:T(8,128)S(1)}, u32[]{:S(2)}, u32[]{:S(2)}) collective-permute-start(f32[32,256]{1,0:T(8,128)S(1)} %get-tuple-element.13), channel_id=1, source_target_pairs={{0,24},{2,26},{4,28},{6,30},{8,0},{10,2},{12,4},{14,6},{16,8},{18,... | collective-permute-start | bytes 98312 | tf_op jit(solution)/shard_map/ppermute | solution.py:140
  16.1 4.8 %collective-permute-start.3 = (f32[32,256]{1,0:T(8,128)S(1)}, f32[32,256]{1,0:T(8,128)S(1)}, u32[]{:S(2)}, u32[]{:S(2)}) collective-permute-start(f32[32,256]{1,0:T(8,128)S(1)} %get-tuple-element.14), channel_id=1, source_target_pairs={{0,16},{2,18},{4,20},{6,22},{8,24},{10,26},{12,28},{14,30},{16,0},... | collective-permute-start | bytes 98312 | tf_op jit(solution)/shard_map/ppermute | solution.py:140
  16.1 5.7 %collective-permute-start.2 = (f32[32,256]{1,0:T(8,128)S(1)}, f32[32,256]{1,0:T(8,128)S(1)}, u32[]{:S(2)}, u32[]{:S(2)}) collective-permute-start(f32[32,256]{1,0:T(8,128)S(1)} %get-tuple-element.12), channel_id=1, source_target_pairs={{0,8},{2,10},{4,12},{6,14},{8,16},{10,18},{12,20},{14,22},{16,24},... | collective-permute-start | bytes 98312 | tf_op jit(solution)/shard_map/ppermute | solution.py:140
  21.8 4.0 %collective-permute-start.7 = (f32[32,256]{1,0:T(8,128)S(1)}, f32[32,256]{1,0:T(8,128)S(1)}, u32[]{:S(2)}, u32[]{:S(2)}) collective-permute-start(f32[32,256]{1,0:T(8,128)S(1)} %fusion.13), channel_id=1, source_target_pairs={{0,24},{2,26},{4,28},{6,30},{8,0},{10,2},{12,4},{14,6},{16,8},{18,... | collective-permute-start | bytes 98312 | tf_op jit(solution)/shard_map/ppermute | solution.py:148
  22.4 4.8 %collective-permute-start.6 = (f32[32,256]{1,0:T(8,128)S(1)}, f32[32,256]{1,0:T(8,128)S(1)}, u32[]{:S(2)}, u32[]{:S(2)}) collective-permute-start(f32[32,256]{1,0:T(8,128)S(1)} %fusion.13), channel_id=1, source_target_pairs={{0,16},{2,18},{4,20},{6,22},{8,24},{10,26},{12,28},{14,30},{16,0},... | collective-permute-start | bytes 98312 | tf_op jit(solution)/shard_map/ppermute | solution.py:148
  23.1 5.7 %collective-permute-start.5 = (f32[32,256]{1,0:T(8,128)S(1)}, f32[32,256]{1,0:T(8,128)S(1)}, u32[]{:S(2)}, u32[]{:S(2)}) collective-permute-start(f32[32,256]{1,0:T(8,128)S(1)} %fusion.13), channel_id=1, source_target_pairs={{0,8},{2,10},{4,12},{6,14},{8,16},{10,18},{12,20},{14,22},{16,24},... | collective-permute-start | bytes 98312 | tf_op jit(solution)/shard_map/ppermute | solution.py:148
  28.8 5.0 %collective-permute-start.8 = (f32[4,32,256]{2,1,0:T(8,128)S(1)}, f32[4,32,256]{2,1,0:T(8,128)S(1)}, u32[]{:S(2)}, u32[]{:S(2)}) collective-permute-start(f32[4,32,256]{2,1,0:T(8,128)S(1)} %pad_maximum_fusion.3), channel_id=1, source_target_pairs={{0,4},{2,6},{4,0},{6,2},{8,12},{10,14},{12,8},{14,10},{16,20},{18,... | collective-permute-start | bytes 393224 | tf_op jit(solution)/shard_map/ppermute | solution.py:155
  33.9 1.6 %collective-permute-start.9 = (f32[8,32,256]{2,1,0:T(8,128)S(1)}, f32[8,32,256]{2,1,0:T(8,128)S(1)}, u32[]{:S(2)}, u32[]{:S(2)}) collective-permute-start(f32[8,32,256]{2,1,0:T(8,128)S(1)} %bitcast.46), channel_id=1, source_target_pairs={{0,2},{2,0},{4,6},{6,4},{8,10},{10,8},{12,14},{14,12},{16,18},{18,... | collective-permute-start | bytes 786440 | tf_op jit(solution)/shard_map/ppermute | solution.py:155
  34.1 2.4 %copy-start = (f32[8,64,512]{2,1,0:T(8,128)}, f32[8,64,512]{2,1,0:T(8,128)S(1)}, u32[]{:S(2)}) copy-start(f32[8,64,512]{2,1,0:T(8,128)S(1)} %sqrt_dynamic-update-slice_fusion.geo_ref) | copy-start | bytes 3145732
  45.1 4.2 %copy-start.1 = (f32[32,2,64]{2,1,0:T(2,128)}, f32[32,2,64]{2,1,0:T(2,128)S(1)}, u32[]{:S(2)}) copy-start(f32[32,2,64]{2,1,0:T(2,128)S(1)} %mul.137) | copy-start | bytes 49156
  45.1 3.6 %collective-permute-start.10 = (f32[64]{0:T(128)S(1)}, f32[64]{0:T(128)S(1)}, u32[]{:S(2)}, u32[]{:S(2)}) collective-permute-start(f32[64]{0:T(128)S(1)} %fusion.16), channel_id=1, source_target_pairs={{0,1},{1,0},{2,3},{3,2},{4,5},{5,4},{6,7},{7,6},{8,9},{9,8},{10,11... | collective-permute-start | bytes 776 | tf_op jit(solution)/shard_map/ppermute | solution.py:193
